TPU v7x, 32 devices: a whole 2x2x4 slice. The times are simulated.
32 devices in a mesh: groups: 1, gx: 4 (over z), gy: 4 (over y, x), gz: 2 (over core).
Axes of the slice: x: 2, y: 2, z: 4, core: 2. Of those that a mesh axis runs over, the one named last changes fastest.
Arguments:
- modes: float32 [3, 16, 32, 8, 128], P('groups', 'gx', 'gy', 'gz'), may hold values from -6 to 6
- cell_weight: float32 [16, 32, 8], P('gx', 'gy', 'gz'), may hold values from 0.25 to 4
- pair_owner: int32 [32], replicated, may hold values from 0 to 31, each once
Outputs:
- convective: float32 [64, 8256], P('groups', ('gx', 'gy', 'gz'))
All inputs are finite; a program needn't handle non-finite values.
Results may differ from a plain program's by a relative error of at most 0.000098.
Values sent between devices are 32-bit elements; how exact they have to be, the bound alone decides.
No kernel may reach another device: no remote copies, remote signals or barrier semaphores. Data moves between devices by JAX's collectives and lax.ppermute only.
A program may use at most 64 MiB of HBM per device.

v0:
```python
import jax
import jax.numpy as jnp
import numpy as np
from jax import lax
from jax.sharding import PartitionSpec as P

TEST = 64


def extended(value, sides, width):
    for axis, dim in sides:
        peers, length = (lax.axis_size(axis), value.shape[dim])
        up = [(i, (i + 1) % peers) for i in range(peers)]
        down = [(j, i) for i, j in up]
        last = lax.slice_in_dim(value, length - width, length, axis=dim)
        leading = lax.slice_in_dim(value, 0, width, axis=dim)
        before = lax.ppermute(last, axis, up)
        after = lax.ppermute(leading, axis, down)
        value = jnp.concatenate([before, value, after], axis=dim)
    return value


def gradients(padded):
    step_x = (padded[:, 2:, 1:-1, 1:-1] - padded[:, :-2, 1:-1, 1:-1]) * 0.5
    step_y = (padded[:, 1:-1, 2:, 1:-1] - padded[:, 1:-1, :-2, 1:-1]) * 0.5
    step_z = (padded[:, 1:-1, 1:-1, 2:] - padded[:, 1:-1, 1:-1, :-2]) * 0.5
    return jnp.stack([step_x, step_y, step_z], axis=1)


def assemble(mode_flat, grad_flat, weight_flat, test_count, block_size):
    weighted = mode_flat[:, :, :test_count] * weight_flat[None, :, None]
    cells = weighted.shape[1]
    blocks = weighted.reshape(3, cells, test_count // block_size, block_size).transpose(2, 0, 1, 3)

    def one_block(chosen):
        zeta = jnp.einsum("axi,abxk->ibxk", chosen, grad_flat, precision=lax.Precision.HIGHEST)
        return jnp.einsum("ibxk,bxj->ijk", zeta, mode_flat, precision=lax.Precision.HIGHEST)

    result = lax.map(one_block, blocks)
    width = mode_flat.shape[2]
    return result.reshape(test_count, width, width)


def shards(modes, cell_weight, pair_owner):
    width = modes.shape[4]
    size_x = lax.axis_size("gx")
    size_y = lax.axis_size("gy")
    size_z = lax.axis_size("gz")
    owners = size_x * size_y * size_z
    padded = extended(modes, (("gx", 1), ("gy", 2), ("gz", 3)), 1)
    depth = padded.shape[3]
    layer = lax.broadcasted_iota(jnp.int32, (1, 1, 1, depth, 1), 3)
    level = lax.axis_index("gz")
    outside = (layer == 0) & (level == 0) | (layer == depth - 1) & (level == size_z - 1)
    padded = jnp.where(outside, jnp.float32(0.0), padded)
    grads = gradients(padded)
    mode_flat = modes.reshape(3, -1, width)
    grad_flat = grads.reshape(3, 3, -1, width)
    weight_flat = cell_weight.reshape(-1)
    total_cells = modes.shape[1] * modes.shape[2] * modes.shape[3] * owners
    scale = 1.0 / jnp.sqrt(jnp.float32(3.0 * total_cells))
    tensor = assemble(mode_flat, grad_flat, weight_flat, TEST, 8) * scale
    pair_total = width * (width + 1) // 2
    block_len = (pair_total + owners - 1) // owners
    upper_j, upper_k = np.triu_indices(width)
    table_j = jnp.asarray(upper_j.astype(np.int32))
    table_k = jnp.asarray(upper_k.astype(np.int32))
    slots = jnp.arange(block_len * owners, dtype=jnp.int32)
    position = slots // block_len
    within = slots % block_len
    pair_index = jnp.take(pair_owner, position) * block_len + within
    valid = pair_index < pair_total
    clipped = jnp.minimum(pair_index, pair_total - 1)
    index_j = jnp.take(table_j, clipped)
    index_k = jnp.take(table_k, clipped)
    flattened = tensor.reshape(TEST, width * width)
    summed = jnp.take(flattened, index_j * width + index_k, axis=1) + jnp.take(
        flattened, index_k * width + index_j, axis=1
    )
    partial_terms = jnp.where(valid[None, :], summed, jnp.float32(0.0))
    owned = lax.psum_scatter(partial_terms, ("gx", "gy", "gz"), scatter_dimension=1, tiled=True)
    return owned


def solution(mesh):
    placed = (P("groups", "gx", "gy", "gz", None), P("gx", "gy", "gz"), P())
    return jax.shard_map(
        shards,
        mesh=mesh,
        in_specs=placed,
        out_specs=P("groups", ("gx", "gy", "gz")),
        check_vma=False,
    )
```

profile of v0, /device:TPU:0, one launch (start us, length us, event | category | flops | bytes accessed | tf_op | source)
XLA Modules:
  0.0 340.5 jit_solution(8372125762917601217)
XLA Ops:
  0.0 0.8 fusion.27
  0.8 3.1 collective-permute-start
  3.9 2.1 collective-permute-start.1
  6.0 1.8 fusion.29
  7.8 2.1 fusion.28
  9.9 0.2 compare_reduce_fusion
  10.1 0.2 compare_reduce_fusion.1
  10.3 0.2 compare_reduce_fusion.10
  10.5 0.2 compare_reduce_fusion.11
  10.6 0.2 compare_reduce_fusion.12
  10.8 0.2 compare_reduce_fusion.13
  11.0 0.2 compare_reduce_fusion.14
  11.2 0.2 compare_reduce_fusion.15
  11.4 0.2 compare_reduce_fusion.16
  11.6 0.2 compare_reduce_fusion.17
  11.7 0.2 compare_reduce_fusion.18
  11.9 0.2 compare_reduce_fusion.19
  12.1 0.2 compare_reduce_fusion.2
  12.3 0.2 compare_reduce_fusion.20
  12.8 0.2 compare_reduce_fusion.23
  13.2 0.2 compare_reduce_fusion.3
  14.1 0.2 compare_reduce_fusion.8
  14.5 4.6 %fusion.24 = s32[8256]{0:T(1024)S(1)} fusion(s32[]{:T(128)} %bitcast.34, s32[]{:T(128)} %bitcast.35, s32[]{:T(128)} %bitcast.36, s32[]{:T(128)} %bitcast.37, s32[]{:T(128)} %bitcast.38, s32[]{:T(128)} %bitcast.40, s32[]{:T(128)} %bitcast.39), kind=kLoop, calls=%fused_computation.88 | loop fusion | flops 189888 | bytes 33052 | tf_op jit(solution)/shard_map/jit(_take)/gather | solution.py:71
  19.1 15.8 %broadcast_compare_fusion = (pred[8256]{0:T(1024)(128)(4,1)S(1)}, s32[8256]{0:T(1024)S(1)}) fusion(pred[8256]{0:T(1024)(128)(4,1)S(1)} %compare_reduce_fusion, pred[8256]{0:T(1024)(128)(4,1)S(1)} %compare_reduce_fusion.1, pred[8256]{0:T(1024)(128)(4,1)S(1)} %compare_reduce_fusion.2, pred[8256]{0:T(1024)(128)(4,1)S(1)} %compare_reduce_fusion.3, ...), kind=kLoop, calls=%fused_computation.89 | loop fusion | flops 388032 | bytes 280804 | tf_op jit(solution)/shard_map/lt | solution.py:72
  35.0 42.8 %gather_fusion = s32[8256]{0:T(1024)S(1)} fusion(s32[8256]{0:T(1024)S(1)} %copy-done, s32[9216]{0:T(1024)S(1)} %pad_clamp_fusion.2), kind=kCustom, calls=%fused_computation.clone | custom fusion | bytes 99072 | tf_op jit(solution)/shard_map/jit(_take)/gather | solution.py:74
  77.8 42.8 %gather_fusion.1 = s32[8256]{0:T(1024)S(1)} fusion(s32[8256]{0:T(1024)S(1)} %copy-done.1, s32[9216]{0:T(1024)S(1)} %pad_clamp_fusion.2), kind=kCustom, calls=%fused_computation.2.clone | custom fusion | bytes 99072 | tf_op jit(solution)/shard_map/jit(_take)/gather | solution.py:75
  121.2 1.7 collective-permute-start.2
  122.9 1.3 collective-permute-start.3
  124.2 2.1 collective-permute-done.2
  126.3 0.5 collective-permute-done.3
  127.1 0.5 collective-permute-start.5
  127.6 0.8 collective-permute-done.4
  128.5 0.3 maximum_select_fusion
  128.8 0.2 fusion.14
  129.6 47.1 %while.10 = (s32[]{:T(128)}, f32[8,8,128,128]{2,3,1,0:T(8,128)}, f32[8,3,128,8]{2,3,0,1:T(8,128)S(1)}, f32[3,3,128,128]{3,0,1,2:T(4,128)S(1)}, f32[3,128,128]{2,1,0:T(8,128)S(1)}, /*index=5*/s32[]{:T(128)}) while((s32[]{:T(128)}, f32[8,8,128,128]{2,3,1,0:T(8,128)}, f32[8,3,128,8]{2,3,0,1:T(8,128)S(1)}, f32[3,3,128,128]{3,0,1,2:T(4,128)S(1)}, ...), condition=%wide.region_1.2_spmd, body=%wide.region_0.1_spmd.sunk | while | flops 618135552 | bytes 4518473 | solution.py:39
  129.8 2.2 convolution_bitcast_fusion.2
  132.0 3.5 %fusion.40 = f32[8,8,128,128]{2,3,1,0:T(8,128)} fusion(f32[8,8,128,128]{2,3,1,0:T(8,128)} %get-tuple-element.151, s32[]{:T(128)} %get-tuple-element.150, f32[8,3,128,128]{3,0,1,2:T(8,128)S(1)} %convolution_bitcast_fusion.2, f32[3,128,128]{2,1,0:T(8,128)S(1)} %get-tuple-element.160), kind=kOutput, calls=%fused_computation.8.clone.1 | convolution fusion | flops 603979776 | bytes 2294272 | tf_op jit(solution)/shard_map/while/body/eval_jaxpr/ibxk,bxj->ijk/dot_general | solution.py:37
  135.6 2.2 convolution_bitcast_fusion.2
  137.8 3.5 %fusion.40 = f32[8,8,128,128]{2,3,1,0:T(8,128)} fusion(f32[8,8,128,128]{2,3,1,0:T(8,128)} %get-tuple-element.151, s32[]{:T(128)} %get-tuple-element.150, f32[8,3,128,128]{3,0,1,2:T(8,128)S(1)} %convolution_bitcast_fusion.2, f32[3,128,128]{2,1,0:T(8,128)S(1)} %get-tuple-element.160), kind=kOutput, calls=%fused_computation.8.clone.1 | convolution fusion | flops 603979776 | bytes 2294272 | tf_op jit(solution)/shard_map/while/body/eval_jaxpr/ibxk,bxj->ijk/dot_general | solution.py:37
  141.5 2.2 convolution_bitcast_fusion.2
  143.7 3.5 %fusion.40 = f32[8,8,128,128]{2,3,1,0:T(8,128)} fusion(f32[8,8,128,128]{2,3,1,0:T(8,128)} %get-tuple-element.151, s32[]{:T(128)} %get-tuple-element.150, f32[8,3,128,128]{3,0,1,2:T(8,128)S(1)} %convolution_bitcast_fusion.2, f32[3,128,128]{2,1,0:T(8,128)S(1)} %get-tuple-element.160), kind=kOutput, calls=%fused_computation.8.clone.1 | convolution fusion | flops 603979776 | bytes 2294272 | tf_op jit(solution)/shard_map/while/body/eval_jaxpr/ibxk,bxj->ijk/dot_general | solution.py:37
  147.4 2.2 convolution_bitcast_fusion.2
  149.6 3.5 %fusion.40 = f32[8,8,128,128]{2,3,1,0:T(8,128)} fusion(f32[8,8,128,128]{2,3,1,0:T(8,128)} %get-tuple-element.151, s32[]{:T(128)} %get-tuple-element.150, f32[8,3,128,128]{3,0,1,2:T(8,128)S(1)} %convolution_bitcast_fusion.2, f32[3,128,128]{2,1,0:T(8,128)S(1)} %get-tuple-element.160), kind=kOutput, calls=%fused_computation.8.clone.1 | convolution fusion | flops 603979776 | bytes 2294272 | tf_op jit(solution)/shard_map/while/body/eval_jaxpr/ibxk,bxj->ijk/dot_general | solution.py:37
  153.3 2.2 convolution_bitcast_fusion.2
  155.5 3.5 %fusion.40 = f32[8,8,128,128]{2,3,1,0:T(8,128)} fusion(f32[8,8,128,128]{2,3,1,0:T(8,128)} %get-tuple-element.151, s32[]{:T(128)} %get-tuple-element.150, f32[8,3,128,128]{3,0,1,2:T(8,128)S(1)} %convolution_bitcast_fusion.2, f32[3,128,128]{2,1,0:T(8,128)S(1)} %get-tuple-element.160), kind=kOutput, calls=%fused_computation.8.clone.1 | convolution fusion | flops 603979776 | bytes 2294272 | tf_op jit(solution)/shard_map/while/body/eval_jaxpr/ibxk,bxj->ijk/dot_general | solution.py:37
  159.2 2.2 convolution_bitcast_fusion.2
  161.4 3.5 %fusion.40 = f32[8,8,128,128]{2,3,1,0:T(8,128)} fusion(f32[8,8,128,128]{2,3,1,0:T(8,128)} %get-tuple-element.151, s32[]{:T(128)} %get-tuple-element.150, f32[8,3,128,128]{3,0,1,2:T(8,128)S(1)} %convolution_bitcast_fusion.2, f32[3,128,128]{2,1,0:T(8,128)S(1)} %get-tuple-element.160), kind=kOutput, calls=%fused_computation.8.clone.1 | convolution fusion | flops 603979776 | bytes 2294272 | tf_op jit(solution)/shard_map/while/body/eval_jaxpr/ibxk,bxj->ijk/dot_general | solution.py:37
  165.1 2.2 convolution_bitcast_fusion.2
  167.3 3.5 %fusion.40 = f32[8,8,128,128]{2,3,1,0:T(8,128)} fusion(f32[8,8,128,128]{2,3,1,0:T(8,128)} %get-tuple-element.151, s32[]{:T(128)} %get-tuple-element.150, f32[8,3,128,128]{3,0,1,2:T(8,128)S(1)} %convolution_bitcast_fusion.2, f32[3,128,128]{2,1,0:T(8,128)S(1)} %get-tuple-element.160), kind=kOutput, calls=%fused_computation.8.clone.1 | convolution fusion | flops 603979776 | bytes 2294272 | tf_op jit(solution)/shard_map/while/body/eval_jaxpr/ibxk,bxj->ijk/dot_general | solution.py:37
  171.0 2.2 convolution_bitcast_fusion.2
  173.2 3.5 %fusion.40 = f32[8,8,128,128]{2,3,1,0:T(8,128)} fusion(f32[8,8,128,128]{2,3,1,0:T(8,128)} %get-tuple-element.151, s32[]{:T(128)} %get-tuple-element.150, f32[8,3,128,128]{3,0,1,2:T(8,128)S(1)} %convolution_bitcast_fusion.2, f32[3,128,128]{2,1,0:T(8,128)S(1)} %get-tuple-element.160), kind=kOutput, calls=%fused_computation.8.clone.1 | convolution fusion | flops 603979776 | bytes 2294272 | tf_op jit(solution)/shard_map/while/body/eval_jaxpr/ibxk,bxj->ijk/dot_general | solution.py:37
  176.7 4.9 %broadcast_multiply_fusion = f32[8,8,128,128]{2,3,1,0:T(8,128)} fusion(f32[8,8,128,128]{2,3,1,0:T(8,128)} %get-tuple-element.34), kind=kLoop, calls=%fused_computation.15 | loop fusion | flops 1048576 | bytes 8388608 | tf_op jit(solution)/shard_map/mul | solution.py:62
  181.6 5.3 %copy.47 = f32[8,8,128,128]{3,2,1,0:T(8,128)} copy(f32[8,8,128,128]{2,3,1,0:T(8,128)} %broadcast_multiply_fusion) | data formatting | bytes 8388608 | tf_op jit(solution)/shard_map/mul | solution.py:62
  186.9 6.5 %copy.63 = f32[8,8,128,128]{3,1,2,0:T(8,128)} copy(f32[8,8,128,128]{3,2,1,0:T(8,128)} %copy.47) | data formatting | bytes 8388608
  193.5 6.9 %copy.48 = f32[64,16384]{0,1:T(8,128)} copy(f32[64,16384]{1,0:T(8,128)} %bitcast.83) | data formatting | bytes 8388608 | tf_op jit(solution)/shard_map/mul | solution.py:62
  200.4 19.6 %gather_fusion.2 = f32[8256,64]{1,0:T(8,128)} fusion(f32[64,16384]{0,1:T(8,128)} %copy.48, s32[9216]{0:T(1024)S(1)} %pad_clamp_fusion.1), kind=kCustom, calls=%fused_computation.1.clone | custom fusion | bytes 4260096 | tf_op jit(solution)/shard_map/jit(_take)/gather | solution.py:77
  220.0 19.7 %gather_fusion.3 = f32[8256,64]{1,0:T(8,128)} fusion(f32[64,16384]{0,1:T(8,128)} %copy.48, s32[9216]{0:T(1024)S(1)} %pad_clamp_fusion), kind=kCustom, calls=%fused_computation.3.clone | custom fusion | bytes 4260096 | tf_op jit(solution)/shard_map/jit(_take)/gather | solution.py:77
  239.6 12.0 %fusion.11 = f32[64,8256]{0,1:T(8,128)} fusion(f32[8256,64]{1,0:T(8,128)} %gather_fusion.3, f32[8256,64]{1,0:T(8,128)} %gather_fusion.2, pred[8256]{0:T(1024)(128)(4,1)S(1)} %get-tuple-element.70, pred[8256]{0:T(1024)(128)(4,1)S(1)} %get-tuple-element.67, pred[8256]{0:T(1024)(128)(4,1)S(1)} %get-tuple-element.65), kind=kLoop, calls=%fused_computation.13 | loop fusion | flops 2113536 | bytes 6365376 | tf_op jit(solution)/shard_map/jit(_where)/select_n | solution.py:80
  251.7 82.5 %fusion = f32[64,272]{0,1:T(8,128)S(1)} fusion(f32[64,8256]{0,1:T(8,128)} %fusion.11), kind=kCustom, calls=%all-reduce-scatter | all-reduce-scatter fusion | flops 557057 | bytes 2183168
  334.2 1.3 collective-permute-start.6
  335.6 1.3 collective-permute-start.7
  336.9 2.1 collective-permute-done.7
  338.9 0.8 concatenate.13
  339.7 0.8 copy.50
  (60 shorter events, 4.2 us)
Async XLA Ops:
  0.0 35.0 %copy-start = (s32[8256]{0:T(1024)S(1)}, s32[8256]{0:T(1024)}, u32[]{:S(2)}) copy-start(s32[8256]{0:T(1024)} %constant.91.clone2.1) | copy-start | bytes 99076
  0.8 120.2 %collective-permute-start = (f32[3,1,8,4,128]{4,3,2,1,0:T(4,128)S(1)}, f32[3,1,8,4,128]{4,3,2,1,0:T(4,128)S(1)}, u32[]{:S(2)}, u32[]{:S(2)}) collective-permute-start(f32[3,1,8,4,128]{4,3,2,1,0:T(4,128)S(1)} %get-tuple-element.80), channel_id=1, source_target_pairs={{0,8},{8,16},{16,24},{24,0},{1,9},{9,17},{17,25},{25,1},{2,10},{10... | collective-permute-start | bytes 147464 | tf_op jit(solution)/shard_map/ppermute | solution.py:17
  3.9 117.2 %collective-permute-start.1 = (f32[3,1,8,4,128]{4,3,2,1,0:T(4,128)S(1)}, f32[3,1,8,4,128]{4,3,2,1,0:T(4,128)S(1)}, u32[]{:S(2)}, u32[]{:S(2)}) collective-permute-start(f32[3,1,8,4,128]{4,3,2,1,0:T(4,128)S(1)} %get-tuple-element.79), channel_id=1, source_target_pairs={{8,0},{16,8},{24,16},{0,24},{9,1},{17,9},{25,17},{1,25},{10,2},{18... | collective-permute-start | bytes 147464 | tf_op jit(solution)/shard_map/ppermute | solution.py:18
  35.0 42.8 %copy-start.1 = (s32[8256]{0:T(1024)S(1)}, s32[8256]{0:T(1024)}, u32[]{:S(2)}) copy-start(s32[8256]{0:T(1024)} %constant.92.clone2.1) | copy-start | bytes 99076
  77.8 42.8 %copy-start.2 = (f32[3,4,8,4,128]{4,3,2,1,0:T(4,128)S(1)}, f32[3,4,8,4,128]{4,3,2,1,0:T(4,128)}, u32[]{:S(2)}) copy-start(f32[3,4,8,4,128]{4,3,2,1,0:T(4,128)} %param.11) | copy-start | bytes 589828
  77.8 42.9 %copy-start.3 = (f32[4,8,4]{1,2,0:T(4,128)S(1)}, f32[4,8,4]{1,2,0:T(4,128)}, u32[]{:S(2)}) copy-start(f32[4,8,4]{1,2,0:T(4,128)} %param.12) | copy-start | bytes 1540
  121.2 5.2 %collective-permute-start.2 = (f32[3,6,1,4,128]{4,3,2,1,0:T(4,128)S(1)}, f32[3,6,1,4,128]{4,3,2,1,0:T(4,128)S(1)}, u32[]{:S(2)}, u32[]{:S(2)}) collective-permute-start(f32[3,6,1,4,128]{4,3,2,1,0:T(4,128)S(1)} %get-tuple-element.77), channel_id=1, source_target_pairs={{0,2},{2,4},{4,6},{6,0},{1,3},{3,5},{5,7},{7,1},{8,10},{10,12},{12... | collective-permute-start | bytes 110600 | tf_op jit(solution)/shard_map/ppermute | solution.py:17
  122.9 4.0 %collective-permute-start.3 = (f32[3,6,1,4,128]{4,3,2,1,0:T(4,128)S(1)}, f32[3,6,1,4,128]{4,3,2,1,0:T(4,128)S(1)}, u32[]{:S(2)}, u32[]{:S(2)}) collective-permute-start(f32[3,6,1,4,128]{4,3,2,1,0:T(4,128)S(1)} %get-tuple-element.78), channel_id=1, source_target_pairs={{2,0},{4,2},{6,4},{0,6},{3,1},{5,3},{7,5},{1,7},{10,8},{12,10},{14... | collective-permute-start | bytes 110600 | tf_op jit(solution)/shard_map/ppermute | solution.py:18
  127.0 1.4 collective-permute-start.4
  127.1 1.4 collective-permute-start.5
  334.2 4.7 %collective-permute-start.6 = (f32[64,272]{0,1:T(8,128)S(1)}, f32[64,272]{0,1:T(8,128)S(1)}, u32[]{:S(2)}, u32[]{:S(2)}) collective-permute-start(f32[64,272]{0,1:T(8,128)S(1)} %fusion), channel_id=1, source_target_pairs={{0,1},{1,2},{2,3},{3,4},{4,5},{5,6},{6,7},{7,8},{8,9},{9,10},{10,1... | collective-permute-start | bytes 208904
  335.6 3.4 collective-permute-start.7
where the time goes:
time: 342 us; the launch traced here: 340 us
  local copies, waits for them, and re-layouts  152 us (44%)
  blocking collectives  82.5 us (24%)
  matrix products  45.8 us (13%)
  other arithmetic  42.8 us (13%)
  starting transfers between devices  11.3 us (3%)
  waiting for transfers between devices  5.65 us (2%)
    unnamed x1, blocking collectives  82.5 us
    gather x1, local copies, waits for them, and re-layouts, shards(): index_j = jnp.take(table_j, clipped)  42.8 us
    gather x1, local copies, waits for them, and re-layouts, shards(): index_k = jnp.take(table_k, clipped)  42.8 us
    dot_general x8, matrix products, one_block(): jnp.einsum('ibxk,bxj->ijk', zeta, mode_flat, precision=lax.Precision.HIGH...  28.2 us
    gather x1, local copies, waits for them, and re-layouts, shards(): jnp.take(flattened, index_k * width + index_j, axis=1)  19.7 us
    gather x1, local copies, waits for them, and re-layouts, shards(): jnp.take(flattened, index_j * width + index_k, axis=1)  19.6 us
    dot_general x8, matrix products, one_block(): jnp.einsum('axi,abxk->ibxk', chosen, grad_flat, precision=lax.Precision.H...  17.6 us
    lt x1, other arithmetic, shards(): valid = pair_index < pair_total  15.8 us
  transfers between devices with their start and end apart: 8, of which 5 were waited for; matrix products, arithmetic and copies ran while one was open for 34% of the time, Pallas kernels for 0%

commit v1 on v0

--- a/solution.py
+++ b/solution.py
@@ -27,20 +27,6 @@
     return jnp.stack([step_x, step_y, step_z], axis=1)
 
 
-def assemble(mode_flat, grad_flat, weight_flat, test_count, block_size):
-    weighted = mode_flat[:, :, :test_count] * weight_flat[None, :, None]
-    cells = weighted.shape[1]
-    blocks = weighted.reshape(3, cells, test_count // block_size, block_size).transpose(2, 0, 1, 3)
-
-    def one_block(chosen):
-        zeta = jnp.einsum("axi,abxk->ibxk", chosen, grad_flat, precision=lax.Precision.HIGHEST)
-        return jnp.einsum("ibxk,bxj->ijk", zeta, mode_flat, precision=lax.Precision.HIGHEST)
-
-    result = lax.map(one_block, blocks)
-    width = mode_flat.shape[2]
-    return result.reshape(test_count, width, width)
-
-
 def shards(modes, cell_weight, pair_owner):
     width = modes.shape[4]
     size_x = lax.axis_size("gx")
@@ -59,27 +45,21 @@
     weight_flat = cell_weight.reshape(-1)
     total_cells = modes.shape[1] * modes.shape[2] * modes.shape[3] * owners
     scale = 1.0 / jnp.sqrt(jnp.float32(3.0 * total_cells))
-    tensor = assemble(mode_flat, grad_flat, weight_flat, TEST, 8) * scale
+    weighted = mode_flat[:, :, :TEST] * weight_flat[None, :, None]
+    zeta = jnp.einsum("axi,abxk->ibxk", weighted, grad_flat, precision=lax.Precision.HIGHEST)
+    tensor = jnp.einsum("ibxk,bxj->ijk", zeta, mode_flat, precision=lax.Precision.HIGHEST)
+    sym = (tensor + jnp.swapaxes(tensor, 1, 2)) * scale
     pair_total = width * (width + 1) // 2
     block_len = (pair_total + owners - 1) // owners
-    upper_j, upper_k = np.triu_indices(width)
-    table_j = jnp.asarray(upper_j.astype(np.int32))
-    table_k = jnp.asarray(upper_k.astype(np.int32))
-    slots = jnp.arange(block_len * owners, dtype=jnp.int32)
-    position = slots // block_len
-    within = slots % block_len
-    pair_index = jnp.take(pair_owner, position) * block_len + within
-    valid = pair_index < pair_total
-    clipped = jnp.minimum(pair_index, pair_total - 1)
-    index_j = jnp.take(table_j, clipped)
-    index_k = jnp.take(table_k, clipped)
-    flattened = tensor.reshape(TEST, width * width)
-    summed = jnp.take(flattened, index_j * width + index_k, axis=1) + jnp.take(
-        flattened, index_k * width + index_j, axis=1
-    )
-    partial_terms = jnp.where(valid[None, :], summed, jnp.float32(0.0))
-    owned = lax.psum_scatter(partial_terms, ("gx", "gy", "gz"), scatter_dimension=1, tiled=True)
-    return owned
+    rows = [sym[:, j, j:] for j in range(width)]
+    slack = block_len * owners - pair_total
+    if slack:
+        rows.append(jnp.zeros((TEST, slack), jnp.float32))
+    canon = jnp.concatenate(rows, axis=1)
+    blocks = canon.reshape(TEST, owners, block_len).transpose(1, 0, 2)
+    partial_terms = jnp.take(blocks, pair_owner, axis=0)
+    owned = lax.psum_scatter(partial_terms, ("gx", "gy", "gz"), scatter_dimension=0, tiled=True)
+    return owned.reshape(TEST, block_len)
 
 
 def solution(mesh):

time: 342 us -> 229 us (0.67)
  waiting for transfers between devices: 5.65 us -> 105 us
  local copies, waits for them, and re-layouts: 152 us -> 64.8 us
  blocking collectives: 82.5 us -> 0 us
  other arithmetic: 42.8 us -> 9.3 us
  matrix products: 45.8 us -> 26.6 us
  between operations: 0.33 us -> 14.3 us
    gather x6 -> x1, local copies, waits for them, and re-layouts: 129 us -> 2.64 us  [shards(): partial_terms = jnp.take(blocks, pair_owner, axis=0)]
    reduce_scatter x0 -> x1, waiting for transfers between devices: none -> 101 us  [shards(): lax.psum_scatter(partial_terms, ('gx', 'gy', 'gz'), scatter_dimension=0,...]
    unnamed x1 -> x0, blocking collectives: 82.5 us -> none
    slice x0 -> x128, local copies, waits for them, and re-layouts: none -> 29.4 us  [shards(): rows = [sym[:, j, j:] for j in range(width)]]
    dot_general x16 -> x2, matrix products: 45.8 us -> 26.6 us  [the longest x1 13.8 us: shards(): jnp.einsum('ibxk,bxj->ijk', zeta, mode_flat, precision=lax.Precision.HIGH...]
    dot_general x0 -> x2, local copies, waits for them, and re-layouts: none -> 18.3 us  [the longest x1 12.6 us: shards(): jnp.einsum('axi,abxk->ibxk', weighted, grad_flat, precision=lax.Precision...]
    lt x1 -> x0, other arithmetic: 15.8 us -> none  [shards(): valid = pair_index < pair_total]
    mul x6 -> x1, local copies, waits for them, and re-layouts: 12.8 us -> 0.1 us  [shards(): weighted = mode_flat[:, :, :TEST] * weight_flat[None, :, None]]
  transfers between devices with their start and end apart: 8 -> 7, of which waited for: 5 -> 5; matrix products, arithmetic and copies ran while one was open for 34% -> 2% of each run, Pallas kernels for 0% -> 0%
where the time goes in v1:
time: 229 us
  waiting for transfers between devices  105 us (46%)
  local copies, waits for them, and re-layouts  64.8 us (28%)
  matrix products  26.6 us (12%)
  between operations  14.3 us (6%)
  other arithmetic  9.3 us (4%)
  starting transfers between devices  8.7 us (4%)
    reduce_scatter x1, waiting for transfers between devices, shards(): lax.psum_scatter(partial_terms, ('gx', 'gy', 'gz'), scatter_dimension=0,...  101 us
    slice x128, local copies, waits for them, and re-layouts, shards(): rows = [sym[:, j, j:] for j in range(width)]  29.4 us
    dot_general x1, matrix products, shards(): jnp.einsum('ibxk,bxj->ijk', zeta, mode_flat, precision=lax.Precision.HIGH...  13.8 us
    dot_general x1, matrix products, shards(): jnp.einsum('axi,abxk->ibxk', weighted, grad_flat, precision=lax.Precision...  12.8 us
    dot_general x1, local copies, waits for them, and re-layouts, shards(): jnp.einsum('axi,abxk->ibxk', weighted, grad_flat, precision=lax.Precision...  12.6 us
    reshape x2, local copies, waits for them, and re-layouts, shards(): blocks = canon.reshape(TEST, owners, block_len).transpose(1, 0, 2)  7.71 us
    dot_general x1, local copies, waits for them, and re-layouts, shards(): jnp.einsum('ibxk,bxj->ijk', zeta, mode_flat, precision=lax.Precision.HIGH...  5.62 us
    ppermute x3, starting transfers between devices, extended(): before = lax.ppermute(last, axis, up)  4.83 us
  transfers between devices with their start and end apart: 7, of which 5 were waited for; matrix products, arithmetic and copies ran while one was open for 2% of the time, Pallas kernels for 0%

profile of v1, /device:TPU:0, one launch (start us, length us, event | category | flops | bytes accessed | tf_op | source)
XLA Modules:
  0.0 228.6 jit_solution(6659245132652291671)
XLA Ops:
  6.5 0.8 fusion.14
  7.4 3.1 %collective-permute-start = (f32[3,1,8,4,128]{4,3,2,1,0:T(4,128)S(1)}, f32[3,1,8,4,128]{4,3,2,1,0:T(4,128)S(1)}, u32[]{:S(2)}, u32[]{:S(2)}) collective-permute-start(f32[3,1,8,4,128]{4,3,2,1,0:T(4,128)S(1)} %get-tuple-element.13), channel_id=1, source_target_pairs={{0,8},{8,16},{16,24},{24,0},{1,9},{9,17},{17,25},{25,1},{2,10},{10... | collective-permute-start | bytes 147464 | tf_op jit(solution)/shard_map/ppermute | solution.py:17
  10.4 2.1 collective-permute-start.1
  12.5 0.8 copy.9
  13.4 0.7 compare_select_fusion
  14.1 1.0 fusion.9
  15.1 0.7 compare_and_fusion
  15.8 1.0 constant_dynamic-update-slice_fusion.1
  16.8 1.7 collective-permute-start.2
  18.5 1.3 collective-permute-start.3
  19.8 2.2 collective-permute-done.2
  21.9 0.5 collective-permute-done.3
  22.4 0.1 pad_maximum_fusion.3
  22.7 0.5 collective-permute-start.5
  23.2 0.8 collective-permute-done.4
  23.9 0.2 collective-permute-done.5
  24.1 0.3 maximum_select_fusion
  24.4 0.2 fusion.12
  24.6 12.8 %fusion.6 = f32[128,3,128,64]{2,3,1,0:T(8,128)} fusion(f32[3,3,128,128]{3,2,0,1:T(8,128)S(1)} %pad_maximum_fusion, f32[3,128,64,1]{2,1,0,3:T(8,128)S(1)} %fusion.9), kind=kOutput, calls=%fused_computation.8 | convolution fusion | flops 113246208 | bytes 13271040 | tf_op jit(solution)/shard_map/axi,abxk->ibxk/dot_general | solution.py:49
  37.4 12.6 %copy.17 = f32[128,3,128,64]{0,2,1,3:T(8,128)} copy(f32[128,3,128,64]{2,3,1,0:T(8,128)} %fusion.6) | data formatting | bytes 25165824 | tf_op jit(solution)/shard_map/axi,abxk->ibxk/dot_general | solution.py:49
  50.1 13.8 %fusion.3 = f32[64,128,128]{2,1,0:T(8,128)} fusion(f32[3,128,128,1]{2,1,0,3:T(8,128)S(1)} %bitcast.155, f32[128,3,128,64]{0,2,1,3:T(8,128)} %copy.17), kind=kOutput, calls=%fused_computation.6 | convolution fusion | flops 4831838208 | bytes 16973824 | tf_op jit(solution)/shard_map/ibxk,bxj->ijk/dot_general | solution.py:50
  63.9 5.6 %copy.10 = f32[64,128,128]{1,2,0:T(8,128)} copy(f32[64,128,128]{2,1,0:T(8,128)} %fusion.3) | data formatting | bytes 8388608 | tf_op jit(solution)/shard_map/ibxk,bxj->ijk/dot_general | solution.py:50
  69.5 4.3 %fusion.2 = f32[64,128,128]{2,1,0:T(8,128)S(1)} fusion(f32[64,128,128]{2,1,0:T(8,128)} %fusion.3, f32[64,128,128]{1,2,0:T(8,128)} %copy.10), kind=kLoop, calls=%fused_computation.4 | loop fusion | flops 2097152 | bytes 12582912 | tf_op jit(solution)/shard_map/mul | solution.py:51
  73.9 0.1 slice.665
  74.3 0.1 slice.668
  74.7 0.1 slice.671
  76.0 0.1 slice.679
  77.2 0.1 slice.687
  78.5 0.1 slice.695
  80.2 0.1 slice.583
  81.3 0.1 slice.591
  82.5 0.1 slice.599
  83.6 0.1 slice.607
  84.7 0.1 slice.615
  85.9 0.1 slice.623
  87.0 0.1 slice.631
  87.6 0.4 slice.635
  88.3 0.1 slice.639
  89.2 0.8 slice.645
  89.9 0.7 slice.646
  90.7 0.7 slice.647
  91.4 0.7 slice.648
  92.2 0.7 slice.649
  92.9 0.7 slice.650
  93.7 0.7 slice.651
  94.4 0.7 slice.652
  95.1 0.7 slice.653
  95.9 0.7 slice.654
  96.6 0.7 slice.655
  97.4 0.7 slice.656
  98.1 0.7 slice.657
  98.8 0.7 slice.658
  99.6 0.7 slice.659
  100.3 0.7 slice.660
  101.1 0.8 slice.661
  101.8 0.7 slice.662
  102.6 0.7 slice.663
  103.3 0.7 slice.664
  104.0 4.1 %concatenate.16 = f32[64,8256]{1,0:T(8,128)} concatenate(f32[64,128]{1,0:T(8,128)S(1)} %bitcast.159, f32[64,127]{1,0:T(8,128)S(1)} %bitcast.170, f32[64,126]{1,0:T(8,128)S(1)} %bitcast.181, f32[64,125]{1,0:T(8,128)S(1)} %bitcast.192, f32[64,124]{1,0:T(8,128)S(1)} %bitcast.201, f32[64,123]{1,0:T(8,128)S(1)} %bitcast.202, f32[64,122]{1,0:T(8,128)S(1)} %bitcast.203, ...), dimensions={1} | concatenate | bytes 4227072 | tf_op jit(solution)/shard_map/concatenate | solution.py:58
  108.2 4.3 %reshape.38 = f32[64,32,258]{2,1,0:T(8,128)S(1)} reshape(f32[64,8256]{1,0:T(8,128)} %concatenate.16) | data formatting | bytes 4227072 | tf_op jit(solution)/shard_map/reshape | solution.py:59
  112.5 3.4 %copy.25 = f32[64,32,258]{2,0,1:T(8,128)} copy(f32[64,32,258]{2,1,0:T(8,128)S(1)} %reshape.38) | data formatting | bytes 4227072 | tf_op jit(solution)/shard_map/reshape | solution.py:59
  115.9 2.6 %gather_fusion = f32[32,64,258]{2,1,0:T(8,128)S(1)} fusion(f32[32,64,258]{2,1,0:T(8,128)} %bitcast.153, s32[1024]{0:T(1024)S(1)} %pad_clamp_fusion), kind=kCustom, calls=%fused_computation | custom fusion | bytes 4227200 | tf_op jit(solution)/shard_map/jit(_take)/gather | solution.py:60
  118.5 2.0 broadcast_select_fusion
  120.6 101.1 %reduce-scatter.2.cloned.1.call-done = f32[1,64,258]{2,1,0:T(8,128)} async-done(((f32[32,64,258]{2,1,0:T(8,128)}), f32[1,64,258]{2,1,0:T(8,128)}) %reduce-scatter.2.cloned.1.call-update) | async-done | bytes 66064 | tf_op jit(solution)/shard_map/reduce_scatter | solution.py:61
  (107 shorter events, 12.5 us)
Async XLA Ops:
  6.5 215.2 %reduce-scatter.2.cloned.1.call-start = ((), (), s32[]{:S(2)}) async-start(), calls=%async_computation.1 | async-start | bytes 3244032 | tf_op jit(solution)/shard_map/reduce_scatter | solution.py:61
  7.4 8.4 %collective-permute-start = (f32[3,1,8,4,128]{4,3,2,1,0:T(4,128)S(1)}, f32[3,1,8,4,128]{4,3,2,1,0:T(4,128)S(1)}, u32[]{:S(2)}, u32[]{:S(2)}) collective-permute-start(f32[3,1,8,4,128]{4,3,2,1,0:T(4,128)S(1)} %get-tuple-element.13), channel_id=1, source_target_pairs={{0,8},{8,16},{16,24},{24,0},{1,9},{9,17},{17,25},{25,1},{2,10},{10... | collective-permute-start | bytes 147464 | tf_op jit(solution)/shard_map/ppermute | solution.py:17
  10.4 6.3 %collective-permute-start.1 = (f32[3,1,8,4,128]{4,3,2,1,0:T(4,128)S(1)}, f32[3,1,8,4,128]{4,3,2,1,0:T(4,128)S(1)}, u32[]{:S(2)}, u32[]{:S(2)}) collective-permute-start(f32[3,1,8,4,128]{4,3,2,1,0:T(4,128)S(1)} %get-tuple-element.12), channel_id=1, source_target_pairs={{8,0},{16,8},{24,16},{0,24},{9,1},{17,9},{25,17},{1,25},{10,2},{18... | collective-permute-start | bytes 147464 | tf_op jit(solution)/shard_map/ppermute | solution.py:18
  16.8 5.2 %collective-permute-start.2 = (f32[3,6,1,4,128]{4,3,2,1,0:T(4,128)S(1)}, f32[3,6,1,4,128]{4,3,2,1,0:T(4,128)S(1)}, u32[]{:S(2)}, u32[]{:S(2)}) collective-permute-start(f32[3,6,1,4,128]{4,3,2,1,0:T(4,128)S(1)} %get-tuple-element.10), channel_id=1, source_target_pairs={{0,2},{2,4},{4,6},{6,0},{1,3},{3,5},{5,7},{7,1},{8,10},{10,12},{12... | collective-permute-start | bytes 110600 | tf_op jit(solution)/shard_map/ppermute | solution.py:17
  18.5 4.0 %collective-permute-start.3 = (f32[3,6,1,4,128]{4,3,2,1,0:T(4,128)S(1)}, f32[3,6,1,4,128]{4,3,2,1,0:T(4,128)S(1)}, u32[]{:S(2)}, u32[]{:S(2)}) collective-permute-start(f32[3,6,1,4,128]{4,3,2,1,0:T(4,128)S(1)} %get-tuple-element.11), channel_id=1, source_target_pairs={{2,0},{4,2},{6,4},{0,6},{3,1},{5,3},{7,5},{1,7},{10,8},{12,10},{14... | collective-permute-start | bytes 110600 | tf_op jit(solution)/shard_map/ppermute | solution.py:18
  22.6 1.4 collective-permute-start.4
  22.7 1.4 collective-permute-start.5
  37.4 12.7 %copy-start = (f32[3,4,8,4,128]{4,3,2,1,0:T(4,128)S(1)}, f32[3,4,8,4,128]{4,3,2,1,0:T(4,128)}, u32[]{:S(2)}) copy-start(f32[3,4,8,4,128]{4,3,2,1,0:T(4,128)} %param.3) | copy-start | bytes 589828
Sparse Core Ops, SparseCore 0:
  120.7 100.9 reduce-scatter.1

commit v2 on v1

--- a/solution.py
+++ b/solution.py
@@ -25,6 +25,48 @@
     step_y = (padded[:, 1:-1, 2:, 1:-1] - padded[:, 1:-1, :-2, 1:-1]) * 0.5
     step_z = (padded[:, 1:-1, 1:-1, 2:] - padded[:, 1:-1, 1:-1, :-2]) * 0.5
     return jnp.stack([step_x, step_y, step_z], axis=1)
+
+
+def halving_stages(axes):
+    stages = []
+    for axis in axes:
+        size = lax.axis_size(axis)
+        bit = size // 2
+        while bit >= 1:
+            stages.append((axis, bit, size))
+            bit //= 2
+    return stages
+
+
+def halve(value, axis, bit, size, dim):
+    pairs = [(i, i ^ bit) for i in range(size)]
+    mine = (lax.axis_index(axis) // bit) % 2
+    keep = lax.dynamic_index_in_dim(value, mine, dim, keepdims=True)
+    other = lax.dynamic_index_in_dim(value, 1 - mine, dim, keepdims=True)
+    return keep + lax.ppermute(other, axis, pairs)
+
+
+def scatter_sum(payload, axes):
+    sizes = [lax.axis_size(a) for a in axes]
+    if any(s & (s - 1) for s in sizes):
+        return lax.psum_scatter(payload, tuple(axes), scatter_dimension=0, tiled=True)
+    stages = halving_stages(axes)
+    rows, lanes = payload.shape[1], payload.shape[2]
+    value = payload.reshape((2,) * len(stages) + (rows, lanes))
+    first = [k for k, s in enumerate(stages) if s[0] == axes[-1]]
+    for k in first:
+        value = halve(value, *stages[k], k)
+    rest = [k for k in range(len(stages)) if k not in first]
+    count = min(3, len(rest), rows)
+    cuts = np.array_split(np.arange(rows), count) if count else [np.arange(rows)]
+    parts = []
+    for p, cut in enumerate(cuts):
+        part = value[..., int(cut[0]) : int(cut[-1]) + 1, :]
+        for k in rest[p:] + rest[:p]:
+            part = halve(part, *stages[k], k)
+        parts.append(part)
+    value = jnp.concatenate(parts, axis=-2) if len(parts) > 1 else parts[0]
+    return value.reshape(1, rows, lanes)
 
 
 def shards(modes, cell_weight, pair_owner):
@@ -57,9 +99,12 @@
         rows.append(jnp.zeros((TEST, slack), jnp.float32))
     canon = jnp.concatenate(rows, axis=1)
     blocks = canon.reshape(TEST, owners, block_len).transpose(1, 0, 2)
-    partial_terms = jnp.take(blocks, pair_owner, axis=0)
-    owned = lax.psum_scatter(partial_terms, ("gx", "gy", "gz"), scatter_dimension=0, tiled=True)
-    return owned.reshape(TEST, block_len)
+    partial_terms = jnp.take(blocks, pair_owner, axis=0).reshape(owners, TEST * block_len)
+    lanes = 128
+    rows = -(-TEST * block_len // lanes)
+    partial_terms = jnp.pad(partial_terms, ((0, 0), (0, rows * lanes - TEST * block_len)))
+    owned = scatter_sum(partial_terms.reshape(owners, rows, lanes), ("gx", "gy", "gz"))
+    return owned.reshape(-1)[: TEST * block_len].reshape(TEST, block_len)
 
 
 def solution(mesh):

time: 229 us -> 212 us (0.926); the launches traced: 229 us -> 208 us
  waiting for transfers between devices: 105 us -> 19.5 us
  local copies, waits for them, and re-layouts: 64.8 us -> 100 us
  matrix products: 26.6 us -> 53.3 us
  starting transfers between devices: 8.7 us -> 24.7 us
  between operations: 14.3 us -> 0.91 us
    reduce_scatter x1 -> x0, waiting for transfers between devices: 101 us -> none  [shards(): lax.psum_scatter(partial_terms, ('gx', 'gy', 'gz'), scatter_dimension=0,...]
    slice x128, local copies, waits for them, and re-layouts: 29.4 us -> 69.6 us  [shards(): rows = [sym[:, j, j:] for j in range(width)]]
    dot_general x1, matrix products: 13.8 us -> 43.1 us  [shards(): jnp.einsum('ibxk,bxj->ijk', zeta, mode_flat, precision=lax.Precision.HIGH...]
    ppermute x0 -> x13, waiting for transfers between devices: none -> 16.1 us  [halve(): return keep + lax.ppermute(other, axis, pairs)]
    ppermute x0 -> x13, starting transfers between devices: none -> 16 us  [halve(): return keep + lax.ppermute(other, axis, pairs)]
    dot_general x1 -> x0, local copies, waits for them, and re-layouts: 12.6 us -> none  [shards(): jnp.einsum('axi,abxk->ibxk', weighted, grad_flat, precision=lax.Precision...]
    gather x1 -> x2, local copies, waits for them, and re-layouts: 2.64 us -> 7.24 us  [shards(): jnp.take(blocks, pair_owner, axis=0).reshape(owners, TEST * block_len)]
    dot_general x1, matrix products: 12.8 us -> 10.2 us  [shards(): jnp.einsum('axi,abxk->ibxk', weighted, grad_flat, precision=lax.Precision...]
  transfers between devices with their start and end apart: 7 -> 19, of which waited for: 5 -> 11; matrix products, arithmetic and copies ran while one was open for 2% -> 2% of each run, Pallas kernels for 0% -> 0%
where the time goes in v2:
time: 212 us; the launch traced here: 208 us
  local copies, waits for them, and re-layouts  100 us (47%)
  matrix products  53.3 us (25%)
  starting transfers between devices  24.7 us (12%)
  waiting for transfers between devices  19.5 us (9%)
  other arithmetic  9.6 us (5%)
    slice x128, local copies, waits for them, and re-layouts, shards(): rows = [sym[:, j, j:] for j in range(width)]  69.6 us
    dot_general x1, matrix products, shards(): jnp.einsum('ibxk,bxj->ijk', zeta, mode_flat, precision=lax.Precision.HIGH...  43.1 us
    ppermute x13, waiting for transfers between devices, halve(): return keep + lax.ppermute(other, axis, pairs)  16.1 us
    ppermute x13, starting transfers between devices, halve(): return keep + lax.ppermute(other, axis, pairs)  16 us
    dot_general x1, matrix products, shards(): jnp.einsum('axi,abxk->ibxk', weighted, grad_flat, precision=lax.Precision...  10.2 us
    reshape x2, local copies, waits for them, and re-layouts, shards(): blocks = canon.reshape(TEST, owners, block_len).transpose(1, 0, 2)  7.9 us
    gather x2, local copies, waits for them, and re-layouts, shards(): jnp.take(blocks, pair_owner, axis=0).reshape(owners, TEST * block_len)  7.24 us
    dot_general x1, local copies, waits for them, and re-layouts, shards(): jnp.einsum('ibxk,bxj->ijk', zeta, mode_flat, precision=lax.Precision.HIGH...  5.68 us
  transfers between devices with their start and end apart: 19, of which 11 were waited for; matrix products, arithmetic and copies ran while one was open for 2% of the time, Pallas kernels for 0%

profile of v2, /device:TPU:0, one launch (start us, length us, event | category | flops | bytes accessed | tf_op | source)
XLA Modules:
  0.0 208.4 jit_solution(1668810999479573188)
XLA Ops:
  0.0 0.8 fusion.17
  0.8 3.1 %collective-permute-start = (f32[3,1,8,4,128]{4,3,2,1,0:T(4,128)S(1)}, f32[3,1,8,4,128]{4,3,2,1,0:T(4,128)S(1)}, u32[]{:S(2)}, u32[]{:S(2)}) collective-permute-start(f32[3,1,8,4,128]{4,3,2,1,0:T(4,128)S(1)} %get-tuple-element.16), channel_id=1, source_target_pairs={{0,8},{8,16},{16,24},{24,0},{1,9},{9,17},{17,25},{25,1},{2,10},{10... | collective-permute-start | bytes 147464 | tf_op jit(solution)/shard_map/ppermute | solution.py:17
  3.9 2.1 %collective-permute-start.1 = (f32[3,1,8,4,128]{4,3,2,1,0:T(4,128)S(1)}, f32[3,1,8,4,128]{4,3,2,1,0:T(4,128)S(1)}, u32[]{:S(2)}, u32[]{:S(2)}) collective-permute-start(f32[3,1,8,4,128]{4,3,2,1,0:T(4,128)S(1)} %get-tuple-element.15), channel_id=1, source_target_pairs={{8,0},{16,8},{24,16},{0,24},{9,1},{17,9},{25,17},{1,25},{10,2},{18... | collective-permute-start | bytes 147464 | tf_op jit(solution)/shard_map/ppermute | solution.py:18
  6.0 1.0 copy.62
  7.0 0.8 copy.47
  9.3 1.0 constant_dynamic-update-slice_fusion.1
  10.3 1.7 collective-permute-start.2
  12.0 1.3 collective-permute-start.3
  13.5 1.9 collective-permute-done.2
  16.7 0.8 collective-permute-done.4
  18.5 10.2 %convolution_bitcast_fusion = f32[64,3,128,128]{3,0,1,2:T(8,128)S(1)} fusion(f32[3,128,64,1]{2,0,3,1:T(4,128)S(1)} %copy.57, f32[3,1,128,128]{3,0,1,2:T(4,128)S(1)} %bitcast.156, f32[3,1,128,128]{3,0,1,2:T(4,128)S(1)} %bitcast.155, f32[3,1,128,128]{3,0,1,2:T(4,128)S(1)} %bitcast.154), kind=kOutput, calls=%fused_computation.3 | convolution fusion | flops 113541120 | bytes 13271040 | tf_op jit(solution)/shard_map/axi,abxk->ibxk/dot_general | solution.py:91
  28.7 43.1 %fusion.3 = f32[64,128,128]{2,1,0:T(8,128)} fusion(f32[3,128,128,1]{2,1,0,3:T(8,128)S(1)} %bitcast.153, f32[64,3,128,128]{3,0,1,2:T(8,128)S(1)} %convolution_bitcast_fusion), kind=kOutput, calls=%fused_computation.7 | convolution fusion | flops 4831838208 | bytes 16973824 | tf_op jit(solution)/shard_map/ibxk,bxj->ijk/dot_general | solution.py:92
  71.8 5.7 %copy.50 = f32[64,128,128]{1,2,0:T(8,128)} copy(f32[64,128,128]{2,1,0:T(8,128)} %fusion.3) | data formatting | bytes 8388608 | tf_op jit(solution)/shard_map/ibxk,bxj->ijk/dot_general | solution.py:92
  77.5 4.3 %fusion.2 = f32[64,128,128]{2,1,0:T(8,128)S(1)} fusion(f32[64,128,128]{2,1,0:T(8,128)} %fusion.3, f32[64,128,128]{1,2,0:T(8,128)} %copy.50), kind=kLoop, calls=%fused_computation.5 | loop fusion | flops 2097152 | bytes 12582912 | tf_op jit(solution)/shard_map/mul | solution.py:93
  87.8 0.8 slice.592
  88.5 0.8 slice.593
  92.3 0.8 slice.598
  93.0 0.8 slice.599
  100.5 0.8 slice.609
  103.5 0.8 slice.613
  104.3 0.8 slice.614
  105.8 0.8 slice.616
  107.3 0.8 slice.618
  113.3 0.8 slice.626
  117.0 0.8 slice.631
  119.3 0.8 slice.634
  123.0 0.8 slice.639
  124.5 0.8 slice.641
  125.3 0.8 slice.642
  126.1 0.8 slice.643
  127.6 0.8 slice.645
  128.3 0.8 slice.646
  131.3 0.8 slice.650
  132.8 0.8 slice.652
  135.8 0.8 slice.656
  137.3 0.8 slice.658
  138.8 0.9 slice.660
  142.0 0.8 slice.664
  144.2 0.8 slice.667
  149.5 0.8 slice.674
  151.7 3.9 %concatenate.19 = f32[64,8256]{1,0:T(8,128)S(1)} concatenate(f32[64,128]{1,0:T(8,128)S(1)} %bitcast.157, f32[64,127]{1,0:T(8,128)S(1)} %bitcast.168, f32[64,126]{1,0:T(8,128)S(1)} %bitcast.179, f32[64,125]{1,0:T(8,128)S(1)} %bitcast.190, f32[64,124]{1,0:T(8,128)S(1)} %bitcast.199, f32[64,123]{1,0:T(8,128)} %bitcast.200, f32[64,122]{1,0:T(8,128)} %bitcast.201, ...), dimensions={1} | concatenate | bytes 4227072 | tf_op jit(solution)/shard_map/concatenate | solution.py:100
  155.7 4.2 %reshape.40 = f32[64,32,258]{2,1,0:T(8,128)} reshape(f32[64,8256]{1,0:T(8,128)S(1)} %concatenate.19) | data formatting | bytes 4227072 | tf_op jit(solution)/shard_map/reshape | solution.py:101
  159.9 3.7 %copy.69 = f32[64,32,258]{2,0,1:T(8,128)S(1)} copy(f32[64,32,258]{2,1,0:T(8,128)} %reshape.40) | data formatting | bytes 4227072 | tf_op jit(solution)/shard_map/reshape | solution.py:101
  163.6 2.4 %gather_fusion = f32[32,64,258]{2,1,0:T(8,128)} fusion(f32[32,64,258]{2,1,0:T(8,128)S(1)} %bitcast.151, s32[1024]{0:T(1024)S(1)} %pad_clamp_fusion), kind=kCustom, calls=%fused_computation | custom fusion | bytes 4227200 | tf_op jit(solution)/shard_map/jit(_take)/gather | solution.py:102
  166.0 4.9 %gather.7 = f32[2,2,2,2,2,129,128]{6,5,4,3,2,1,0:T(8,128)} reshape(f32[32,64,258]{2,1,0:T(8,128)} %gather_fusion) | data formatting | bytes 4227072 | tf_op jit(solution)/shard_map/jit(_take)/gather | solution.py:102
  170.8 1.8 broadcast_select_fusion
  173.7 2.5 %collective-permute-done.6 = f32[2,2,2,2,1,129,128]{6,3,5,4,2,1,0:T(2,128)} collective-permute-done((f32[2,2,2,2,1,129,128]{6,3,5,4,2,1,0:T(2,128)S(1)}, f32[2,2,2,2,1,129,128]{6,3,5,4,2,1,0:T(2,128)}, u32[]{:S(2)}, u32[]{:S(2)}) %collective-permute-start.6) | collective-permute-done | bytes 1056800 | tf_op jit(solution)/shard_map/ppermute | solution.py:46
  176.2 1.3 copy_add_fusion
  177.7 0.9 collective-permute-start.7
  178.5 1.7 collective-permute-start.11
  180.2 1.6 collective-permute-start.15
  181.8 7.6 %collective-permute-done.7 = f32[1,2,2,2,1,43,128]{6,5,4,3,2,1,0:T(8,128)S(1)} collective-permute-done((f32[1,2,2,2,1,43,128]{6,5,4,3,2,1,0:T(8,128)S(1)}, f32[1,2,2,2,1,43,128]{6,5,4,3,2,1,0:T(8,128)S(1)}, u32[]{:S(2)}, u32[]{:S(2)}) %collective-permute-start.7) | collective-permute-done | bytes 176160 | tf_op jit(solution)/shard_map/ppermute | solution.py:46
  189.8 1.6 collective-permute-start.12
  191.5 1.4 collective-permute-start.16
  192.9 1.3 collective-permute-done.8
  194.3 1.6 collective-permute-start.9
  195.9 1.5 collective-permute-start.13
  197.4 2.4 %collective-permute-start.17 = (f32[1,2,1,1,1,43,128]{6,5,4,3,2,1,0:T(8,128)S(1)}, f32[1,2,1,1,1,43,128]{6,5,4,3,2,1,0:T(8,128)S(1)}, u32[]{:S(2)}, u32[]{:S(2)}) collective-permute-start(f32[1,2,1,1,1,43,128]{6,5,4,3,2,1,0:T(8,128)S(1)} %constant_dynamic-slice_fusion.1), channel_id=1, source_target_pairs={{0,16},{8,24},{16,0},{24,8},{1,17},{9,25},{17,1},{25,9},{2,18},{10... | collective-permute-start | bytes 132104 | tf_op jit(solution)/shard_map/ppermute | solution.py:46
  199.8 1.1 collective-permute-start.10
  200.9 1.3 collective-permute-start.14
  202.3 1.2 collective-permute-done.17
  204.1 1.6 collective-permute-done.14
  205.7 1.6 collective-permute-done.18
  207.4 0.8 reshape_reshape_reshape.3
  (165 shorter events, 56.2 us)
Async XLA Ops:
  0.8 8.4 %collective-permute-start = (f32[3,1,8,4,128]{4,3,2,1,0:T(4,128)S(1)}, f32[3,1,8,4,128]{4,3,2,1,0:T(4,128)S(1)}, u32[]{:S(2)}, u32[]{:S(2)}) collective-permute-start(f32[3,1,8,4,128]{4,3,2,1,0:T(4,128)S(1)} %get-tuple-element.16), channel_id=1, source_target_pairs={{0,8},{8,16},{16,24},{24,0},{1,9},{9,17},{17,25},{25,1},{2,10},{10... | collective-permute-start | bytes 147464 | tf_op jit(solution)/shard_map/ppermute | solution.py:17
  3.9 6.3 %collective-permute-start.1 = (f32[3,1,8,4,128]{4,3,2,1,0:T(4,128)S(1)}, f32[3,1,8,4,128]{4,3,2,1,0:T(4,128)S(1)}, u32[]{:S(2)}, u32[]{:S(2)}) collective-permute-start(f32[3,1,8,4,128]{4,3,2,1,0:T(4,128)S(1)} %get-tuple-element.15), channel_id=1, source_target_pairs={{8,0},{16,8},{24,16},{0,24},{9,1},{17,9},{25,17},{1,25},{10,2},{18... | collective-permute-start | bytes 147464 | tf_op jit(solution)/shard_map/ppermute | solution.py:18
  10.3 5.2 %collective-permute-start.2 = (f32[3,6,1,4,128]{4,3,2,1,0:T(4,128)S(1)}, f32[3,6,1,4,128]{4,3,2,1,0:T(4,128)S(1)}, u32[]{:S(2)}, u32[]{:S(2)}) collective-permute-start(f32[3,6,1,4,128]{4,3,2,1,0:T(4,128)S(1)} %get-tuple-element.13), channel_id=1, source_target_pairs={{0,2},{2,4},{4,6},{6,0},{1,3},{3,5},{5,7},{7,1},{8,10},{10,12},{12... | collective-permute-start | bytes 110600 | tf_op jit(solution)/shard_map/ppermute | solution.py:17
  12.0 4.0 %collective-permute-start.3 = (f32[3,6,1,4,128]{4,3,2,1,0:T(4,128)S(1)}, f32[3,6,1,4,128]{4,3,2,1,0:T(4,128)S(1)}, u32[]{:S(2)}, u32[]{:S(2)}) collective-permute-start(f32[3,6,1,4,128]{4,3,2,1,0:T(4,128)S(1)} %get-tuple-element.14), channel_id=1, source_target_pairs={{2,0},{4,2},{6,4},{0,6},{3,1},{5,3},{7,5},{1,7},{10,8},{12,10},{14... | collective-permute-start | bytes 110600 | tf_op jit(solution)/shard_map/ppermute | solution.py:18
  16.1 1.4 collective-permute-start.4
  16.2 1.4 collective-permute-start.5
  18.5 10.2 %copy-start = (f32[3,4,8,4,128]{4,3,2,1,0:T(4,128)S(1)}, f32[3,4,8,4,128]{4,3,2,1,0:T(4,128)}, u32[]{:S(2)}) copy-start(f32[3,4,8,4,128]{4,3,2,1,0:T(4,128)} %param.3) | copy-start | bytes 589828
  173.3 2.9 %collective-permute-start.6 = (f32[2,2,2,2,1,129,128]{6,3,5,4,2,1,0:T(2,128)S(1)}, f32[2,2,2,2,1,129,128]{6,3,5,4,2,1,0:T(2,128)}, u32[]{:S(2)}, u32[]{:S(2)}) collective-permute-start(f32[2,2,2,2,1,129,128]{6,3,5,4,2,1,0:T(2,128)S(1)} %copy.55), channel_id=1, source_target_pairs={{0,1},{1,0},{2,3},{3,2},{4,5},{5,4},{6,7},{7,6},{8,9},{9,8},{10,11... | collective-permute-start | bytes 3170312 | tf_op jit(solution)/shard_map/ppermute | solution.py:46
  177.7 11.7 %collective-permute-start.7 = (f32[1,2,2,2,1,43,128]{6,5,4,3,2,1,0:T(8,128)S(1)}, f32[1,2,2,2,1,43,128]{6,5,4,3,2,1,0:T(8,128)S(1)}, u32[]{:S(2)}, u32[]{:S(2)}) collective-permute-start(f32[1,2,2,2,1,43,128]{6,5,4,3,2,1,0:T(8,128)S(1)} %constant_dynamic-slice_fusion.11), channel_id=1, source_target_pairs={{0,16},{8,24},{16,0},{24,8},{1,17},{9,25},{17,1},{25,9},{2,18},{10... | collective-permute-start | bytes 528392 | tf_op jit(solution)/shard_map/ppermute | solution.py:46
  178.5 11.2 %collective-permute-start.11 = (f32[2,1,2,2,1,43,128]{6,5,4,3,2,1,0:T(8,128)S(1)}, f32[2,1,2,2,1,43,128]{6,5,4,3,2,1,0:T(8,128)S(1)}, u32[]{:S(2)}, u32[]{:S(2)}) collective-permute-start(f32[2,1,2,2,1,43,128]{6,5,4,3,2,1,0:T(8,128)S(1)} %constant_dynamic-slice_fusion.7), channel_id=1, source_target_pairs={{0,8},{8,0},{16,24},{24,16},{1,9},{9,1},{17,25},{25,17},{2,10},{10... | collective-permute-start | bytes 528392 | tf_op jit(solution)/shard_map/ppermute | solution.py:46
  180.2 11.2 %collective-permute-start.15 = (f32[2,2,1,2,1,43,128]{6,5,4,3,2,1,0:T(8,128)S(1)}, f32[2,2,1,2,1,43,128]{6,5,4,3,2,1,0:T(8,128)S(1)}, u32[]{:S(2)}, u32[]{:S(2)}) collective-permute-start(f32[2,2,1,2,1,43,128]{6,5,4,3,2,1,0:T(8,128)S(1)} %constant_dynamic-slice_fusion.3), channel_id=1, source_target_pairs={{0,4},{2,6},{4,0},{6,2},{1,5},{3,7},{5,1},{7,3},{8,12},{10,14},{12... | collective-permute-start | bytes 528392 | tf_op jit(solution)/shard_map/ppermute | solution.py:46
  189.5 4.8 %collective-permute-start.8 = (f32[1,1,2,2,1,43,128]{6,5,4,3,2,1,0:T(8,128)S(1)}, f32[1,1,2,2,1,43,128]{6,5,4,3,2,1,0:T(8,128)S(1)}, u32[]{:S(2)}, u32[]{:S(2)}) collective-permute-start(f32[1,1,2,2,1,43,128]{6,5,4,3,2,1,0:T(8,128)S(1)} %constant_dynamic-slice_fusion.10), channel_id=1, source_target_pairs={{0,8},{8,0},{16,24},{24,16},{1,9},{9,1},{17,25},{25,17},{2,10},{10... | collective-permute-start | bytes 264200 | tf_op jit(solution)/shard_map/ppermute | solution.py:46
  189.8 6.0 %collective-permute-start.12 = (f32[2,1,1,2,1,43,128]{6,5,4,3,2,1,0:T(8,128)S(1)}, f32[2,1,1,2,1,43,128]{6,5,4,3,2,1,0:T(8,128)S(1)}, u32[]{:S(2)}, u32[]{:S(2)}) collective-permute-start(f32[2,1,1,2,1,43,128]{6,5,4,3,2,1,0:T(8,128)S(1)} %constant_dynamic-slice_fusion.6), channel_id=1, source_target_pairs={{0,4},{2,6},{4,0},{6,2},{1,5},{3,7},{5,1},{7,3},{8,12},{10,14},{12... | collective-permute-start | bytes 264200 | tf_op jit(solution)/shard_map/ppermute | solution.py:46
  191.5 5.9 %collective-permute-start.16 = (f32[2,2,1,1,1,43,128]{6,5,4,3,2,1,0:T(8,128)S(1)}, f32[2,2,1,1,1,43,128]{6,5,4,3,2,1,0:T(8,128)S(1)}, u32[]{:S(2)}, u32[]{:S(2)}) collective-permute-start(f32[2,2,1,1,1,43,128]{6,5,4,3,2,1,0:T(8,128)S(1)} %constant_dynamic-slice_fusion.2), channel_id=1, source_target_pairs={{0,2},{2,0},{4,6},{6,4},{1,3},{3,1},{5,7},{7,5},{8,10},{10,8},{12,... | collective-permute-start | bytes 264200 | tf_op jit(solution)/shard_map/ppermute | solution.py:46
  194.3 5.5 %collective-permute-start.9 = (f32[1,1,1,2,1,43,128]{6,5,4,3,2,1,0:T(8,128)S(1)}, f32[1,1,1,2,1,43,128]{6,5,4,3,2,1,0:T(8,128)S(1)}, u32[]{:S(2)}, u32[]{:S(2)}) collective-permute-start(f32[1,1,1,2,1,43,128]{6,5,4,3,2,1,0:T(8,128)S(1)} %constant_dynamic-slice_fusion.9), channel_id=1, source_target_pairs={{0,4},{2,6},{4,0},{6,2},{1,5},{3,7},{5,1},{7,3},{8,12},{10,14},{12... | collective-permute-start | bytes 132104 | tf_op jit(solution)/shard_map/ppermute | solution.py:46
  195.9 5.0 %collective-permute-start.13 = (f32[2,1,1,1,1,43,128]{6,5,4,3,2,1,0:T(8,128)S(1)}, f32[2,1,1,1,1,43,128]{6,5,4,3,2,1,0:T(8,128)S(1)}, u32[]{:S(2)}, u32[]{:S(2)}) collective-permute-start(f32[2,1,1,1,1,43,128]{6,5,4,3,2,1,0:T(8,128)S(1)} %constant_dynamic-slice_fusion.5), channel_id=1, source_target_pairs={{0,2},{2,0},{4,6},{6,4},{1,3},{3,1},{5,7},{7,5},{8,10},{10,8},{12,... | collective-permute-start | bytes 132104 | tf_op jit(solution)/shard_map/ppermute | solution.py:46
  197.4 6.1 %collective-permute-start.17 = (f32[1,2,1,1,1,43,128]{6,5,4,3,2,1,0:T(8,128)S(1)}, f32[1,2,1,1,1,43,128]{6,5,4,3,2,1,0:T(8,128)S(1)}, u32[]{:S(2)}, u32[]{:S(2)}) collective-permute-start(f32[1,2,1,1,1,43,128]{6,5,4,3,2,1,0:T(8,128)S(1)} %constant_dynamic-slice_fusion.1), channel_id=1, source_target_pairs={{0,16},{8,24},{16,0},{24,8},{1,17},{9,25},{17,1},{25,9},{2,18},{10... | collective-permute-start | bytes 132104 | tf_op jit(solution)/shard_map/ppermute | solution.py:46
  199.8 4.3 %collective-permute-start.10 = (f32[1,1,1,1,1,43,128]{6,5,4,3,2,1,0:T(8,128)S(1)}, f32[1,1,1,1,1,43,128]{6,5,4,3,2,1,0:T(8,128)S(1)}, u32[]{:S(2)}, u32[]{:S(2)}) collective-permute-start(f32[1,1,1,1,1,43,128]{6,5,4,3,2,1,0:T(8,128)S(1)} %constant_dynamic-slice_fusion.8), channel_id=1, source_target_pairs={{0,2},{2,0},{4,6},{6,4},{1,3},{3,1},{5,7},{7,5},{8,10},{10,8},{12,... | collective-permute-start | bytes 66056 | tf_op jit(solution)/shard_map/ppermute | solution.py:46
  200.9 4.8 %collective-permute-start.14 = (f32[1,1,1,1,1,43,128]{6,5,4,3,2,1,0:T(8,128)S(1)}, f32[1,1,1,1,1,43,128]{6,5,4,3,2,1,0:T(8,128)S(1)}, u32[]{:S(2)}, u32[]{:S(2)}) collective-permute-start(f32[1,1,1,1,1,43,128]{6,5,4,3,2,1,0:T(8,128)S(1)} %constant_dynamic-slice_fusion.4), channel_id=1, source_target_pairs={{0,16},{8,24},{16,0},{24,8},{1,17},{9,25},{17,1},{25,9},{2,18},{10... | collective-permute-start | bytes 66056 | tf_op jit(solution)/shard_map/ppermute | solution.py:46
  203.5 3.9 %collective-permute-start.18 = (f32[1,1,1,1,1,43,128]{6,5,4,3,2,1,0:T(8,128)S(1)}, f32[1,1,1,1,1,43,128]{6,5,4,3,2,1,0:T(8,128)S(1)}, u32[]{:S(2)}, u32[]{:S(2)}) collective-permute-start(f32[1,1,1,1,1,43,128]{6,5,4,3,2,1,0:T(8,128)S(1)} %constant_dynamic-slice_fusion), channel_id=1, source_target_pairs={{0,8},{8,0},{16,24},{24,16},{1,9},{9,1},{17,25},{25,17},{2,10},{10... | collective-permute-start | bytes 66056 | tf_op jit(solution)/shard_map/ppermute | solution.py:46

commit v3 on v2

--- a/solution.py
+++ b/solution.py
@@ -2,6 +2,8 @@
 import jax.numpy as jnp
 import numpy as np
 from jax import lax
+from jax.experimental import pallas as pl
+from jax.experimental.pallas import tpu as pltpu
 from jax.sharding import PartitionSpec as P
 
 TEST = 64
@@ -69,6 +71,49 @@
     return value.reshape(1, rows, lanes)
 
 
+def triangle_kernel(w_ref, g_ref, m_ref, out_ref, sym_ref):
+    test, width = w_ref.shape[1], m_ref.shape[1]
+    out_ref[...] = jnp.zeros(out_ref.shape, out_ref.dtype)
+
+    def contract(i, carry):
+        zt = w_ref[0, pl.ds(i, 1), :] * g_ref[0]
+        zt = zt + w_ref[1, pl.ds(i, 1), :] * g_ref[1]
+        zt = zt + w_ref[2, pl.ds(i, 1), :] * g_ref[2]
+        part = jnp.dot(zt, m_ref[...], precision=lax.Precision.HIGHEST, preferred_element_type=jnp.float32)
+        start = pl.multiple_of(i * width, width)
+        sym_ref[pl.ds(start, width), :] = part + part.T
+        return carry
+
+    lax.fori_loop(0, test, contract, 0)
+    lane = lax.broadcasted_iota(jnp.int32, (test, 128), 1)
+
+    def place(j, carry):
+        slab = sym_ref[pl.ds(j, test, stride=width), :]
+        offset = j * width - (j * (j - 1)) // 2
+        end = offset % 128 + width - j
+        rolled = pltpu.roll(slab, (offset - j) % 128, 1)
+        first = pl.multiple_of((offset // 128) * 128, 128)
+        second = pl.multiple_of(first + 128, 128)
+        low = lane >= offset % 128
+        out_ref[:, pl.ds(first, 128)] = jnp.where(low & (lane < end), rolled, out_ref[:, pl.ds(first, 128)])
+        out_ref[:, pl.ds(second, 128)] = jnp.where(lane < end - 128, rolled, out_ref[:, pl.ds(second, 128)])
+        return carry
+
+    lax.fori_loop(0, width, place, 0)
+
+
+def triangle(weighted, grads, modes_flat, pair_total, slots):
+    test, width = weighted.shape[1], modes_flat.shape[1]
+    tiles = max(pair_total // 128 + 2, -(-slots // 128))
+    return pl.pallas_call(
+        triangle_kernel,
+        out_shape=jax.ShapeDtypeStruct((test, tiles * 128), jnp.float32),
+        in_specs=[pl.BlockSpec(memory_space=pltpu.VMEM)] * 3,
+        out_specs=pl.BlockSpec(memory_space=pltpu.VMEM),
+        scratch_shapes=[pltpu.VMEM((test * width, width), jnp.float32)],
+    )(weighted, grads, modes_flat)
+
+
 def shards(modes, cell_weight, pair_owner):
     width = modes.shape[4]
     size_x = lax.axis_size("gx")
@@ -87,19 +132,15 @@
     weight_flat = cell_weight.reshape(-1)
     total_cells = modes.shape[1] * modes.shape[2] * modes.shape[3] * owners
     scale = 1.0 / jnp.sqrt(jnp.float32(3.0 * total_cells))
-    weighted = mode_flat[:, :, :TEST] * weight_flat[None, :, None]
-    zeta = jnp.einsum("axi,abxk->ibxk", weighted, grad_flat, precision=lax.Precision.HIGHEST)
-    tensor = jnp.einsum("ibxk,bxj->ijk", zeta, mode_flat, precision=lax.Precision.HIGHEST)
-    sym = (tensor + jnp.swapaxes(tensor, 1, 2)) * scale
+    cells = mode_flat.shape[1]
+    weighted = mode_flat[:, :, :TEST] * (weight_flat * scale)[None, :, None]
+    weighted = jnp.tile(jnp.swapaxes(weighted, 1, 2), (1, 1, 3))
+    grads_t = grad_flat.transpose(0, 3, 1, 2).reshape(3, width, 3 * cells)
     pair_total = width * (width + 1) // 2
     block_len = (pair_total + owners - 1) // owners
-    rows = [sym[:, j, j:] for j in range(width)]
-    slack = block_len * owners - pair_total
-    if slack:
-        rows.append(jnp.zeros((TEST, slack), jnp.float32))
-    canon = jnp.concatenate(rows, axis=1)
+    canon = triangle(weighted, grads_t, mode_flat.reshape(3 * cells, width), pair_total, owners * block_len)[:, : owners * block_len]
     blocks = canon.reshape(TEST, owners, block_len).transpose(1, 0, 2)
-    partial_terms = jnp.take(blocks, pair_owner, axis=0).reshape(owners, TEST * block_len)
+    partial_terms = jnp.take(blocks, pair_owner, axis=0, mode="clip").reshape(owners, TEST * block_len)
     lanes = 128
     rows = -(-TEST * block_len // lanes)
     partial_terms = jnp.pad(partial_terms, ((0, 0), (0, rows * lanes - TEST * block_len)))

time: 212 us -> 111 us (0.52); the launches traced: 208 us -> 111 us
  local copies, waits for them, and re-layouts: 100 us -> 21.5 us
  matrix products: 53.3 us -> 0 us
  Pallas kernels: 0 us -> 42.9 us
  other arithmetic: 9.6 us -> 4.53 us
  starting transfers between devices: 24.7 us -> 22.3 us
    slice x128 -> x2, local copies, waits for them, and re-layouts: 69.6 us -> 1.6 us  [shards(): triangle(weighted, grads_t, mode_flat.reshape(3 * cells, width), pair_tot...]
    dot_general x2 -> x0, matrix products: 53.3 us -> none  [the longest x1 43.1 us: shards(): jnp.einsum('ibxk,bxj->ijk', zeta, mode_flat, precision=lax.Precision.HIGH...]
    pallas_call x0 -> x1, Pallas kernels: none -> 42.9 us  [triangle(): pl.pallas_call(triangle_kernel, out_shape=jax.ShapeDtypeStruct((test, til...]
    dot_general x1 -> x0, local copies, waits for them, and re-layouts: 5.68 us -> none  [shards(): jnp.einsum('ibxk,bxj->ijk', zeta, mode_flat, precision=lax.Precision.HIGH...]
    gather x2 -> x1, local copies, waits for them, and re-layouts: 7.24 us -> 2.38 us  [shards(): jnp.take(blocks, pair_owner, axis=0, mode='clip')]
    another operation x0 -> x3, local copies, waits for them, and re-layouts: none -> 4.71 us  [the longest x1 3.77 us: scatter_sum(): value = payload.reshape((2,) * len(stages) + (rows, lanes))]
    concatenate x1 -> x0, local copies, waits for them, and re-layouts: 3.91 us -> none  [shards(): canon = jnp.concatenate(rows, axis=1)]
    mul x2 -> x1, other arithmetic: 4.32 us -> 0.7 us  [shards(): weighted = mode_flat[:, :, :TEST] * (weight_flat * scale)[None, :, None]]
  transfers between devices with their start and end apart: 19 -> 19, of which waited for: 11 -> 11; matrix products, arithmetic and copies ran while one was open for 2% -> 4% of each run, Pallas kernels for 0% -> 0%
where the time goes in v3:
time: 111 us
  Pallas kernels  42.9 us (39%)
  starting transfers between devices  22.3 us (20%)
  local copies, waits for them, and re-layouts  21.5 us (19%)
  waiting for transfers between devices  19.5 us (18%)
  other arithmetic  4.53 us (4%)
    pallas_call x1, Pallas kernels, triangle(): pl.pallas_call(triangle_kernel, out_shape=jax.ShapeDtypeStruct((test, til...  42.9 us
    ppermute x13, waiting for transfers between devices, halve(): return keep + lax.ppermute(other, axis, pairs)  15.3 us
    ppermute x13, starting transfers between devices, halve(): return keep + lax.ppermute(other, axis, pairs)  13.7 us
    reshape x2, local copies, waits for them, and re-layouts, shards(): blocks = canon.reshape(TEST, owners, block_len).transpose(1, 0, 2)  7.88 us
    ppermute x3, starting transfers between devices, extended(): after = lax.ppermute(leading, axis, down)  5 us
    another operation x1, local copies, waits for them, and re-layouts, scatter_sum(): value = payload.reshape((2,) * len(stages) + (rows, lanes))  3.77 us
    ppermute x3, starting transfers between devices, extended(): before = lax.ppermute(last, axis, up)  3.56 us
    ppermute x3, waiting for transfers between devices, extended(): before = lax.ppermute(last, axis, up)  3.46 us
  transfers between devices with their start and end apart: 19, of which 11 were waited for; matrix products, arithmetic and copies ran while one was open for 4% of the time, Pallas kernels for 0%

profile of v3, /device:TPU:0, one launch (start us, length us, event | category | flops | bytes accessed | tf_op | source)
XLA Modules:
  0.0 111.0 jit_solution(17075983472516166019)
XLA Ops:
  0.0 0.8 fusion.6
  0.8 3.1 %collective-permute-start = (f32[3,1,8,4,128]{4,3,2,1,0:T(4,128)S(1)}, f32[3,1,8,4,128]{4,3,2,1,0:T(4,128)S(1)}, u32[]{:S(2)}, u32[]{:S(2)}) collective-permute-start(f32[3,1,8,4,128]{4,3,2,1,0:T(4,128)S(1)} %get-tuple-element.16), channel_id=1, source_target_pairs={{0,8},{8,16},{16,24},{24,0},{1,9},{9,17},{17,25},{25,1},{2,10},{10... | collective-permute-start | bytes 147464 | tf_op jit(solution)/shard_map/ppermute | solution.py:19
  3.9 2.1 %collective-permute-start.1 = (f32[3,1,8,4,128]{4,3,2,1,0:T(4,128)S(1)}, f32[3,1,8,4,128]{4,3,2,1,0:T(4,128)S(1)}, u32[]{:S(2)}, u32[]{:S(2)}) collective-permute-start(f32[3,1,8,4,128]{4,3,2,1,0:T(4,128)S(1)} %get-tuple-element.15), channel_id=1, source_target_pairs={{8,0},{16,8},{24,16},{0,24},{9,1},{17,9},{25,17},{1,25},{10,2},{18... | collective-permute-start | bytes 147464 | tf_op jit(solution)/shard_map/ppermute | solution.py:20
  6.0 0.7 broadcast_multiply_fusion
  6.7 0.1 copy.13
  6.8 0.1 mul.32
  6.9 1.0 fusion.3
  7.9 0.2 collective-permute-done
  8.1 1.0 constant_dynamic-update-slice_fusion.1
  9.1 0.0 collective-permute-done.1
  9.1 2.8 %collective-permute-start.3 = (f32[3,6,1,4,128]{4,3,2,1,0:T(4,128)S(1)}, f32[3,6,1,4,128]{4,3,2,1,0:T(4,128)S(1)}, u32[]{:S(2)}, u32[]{:S(2)}) collective-permute-start(f32[3,6,1,4,128]{4,3,2,1,0:T(4,128)S(1)} %get-tuple-element.14), channel_id=1, source_target_pairs={{2,0},{4,2},{6,4},{0,6},{3,1},{5,3},{7,5},{1,7},{10,8},{12,10},{14... | collective-permute-start | bytes 110600 | tf_op jit(solution)/shard_map/ppermute | solution.py:20
  11.9 0.0 collective-permute-start.2
  11.9 0.7 pad_clamp_fusion
  12.6 0.1 copy.14
  12.7 0.1 tile.4
  12.8 0.9 tile.10.w_ref
  13.7 0.0 collective-permute-done.3
  13.7 3.1 %collective-permute-done.2 = f32[3,6,1,4,128]{4,3,2,1,0:T(4,128)S(1)} collective-permute-done((f32[3,6,1,4,128]{4,3,2,1,0:T(4,128)S(1)}, f32[3,6,1,4,128]{4,3,2,1,0:T(4,128)S(1)}, u32[]{:S(2)}, u32[]{:S(2)}) %collective-permute-start.2) | collective-permute-done | bytes 36896 | tf_op jit(solution)/shard_map/ppermute | solution.py:19
  16.8 0.1 pad_maximum_fusion.3
  17.0 0.1 collective-permute-start.5
  17.0 0.5 collective-permute-start.4
  17.5 0.8 collective-permute-done.5
  18.3 0.2 collective-permute-done.4
  18.5 0.3 maximum_select_fusion
  18.7 0.2 fusion.2
  19.0 1.1 copy.15.g_ref
  20.0 42.9 %shard_map.37 = f32[64,8448]{1,0:T(8,128)} custom-call(f32[3,64,384]{2,1,0:T(8,128)} %tile.10.w_ref, f32[3,128,384]{2,1,0:T(8,128)} %copy.15.g_ref, f32[384,128]{1,0:T(8,128)} %bitcast.15), custom_call_target="tpu_custom_call" | custom-call | tf_op jit(solution)/shard_map/pallas_call | solution.py:108
  63.0 0.0 slice-start
  63.0 1.6 %slice-done = f32[64,8256]{1,0:T(8,128)S(1)} async-done(((f32[64,8448]{1,0:T(8,128)}), f32[64,8256]{1,0:T(8,128)S(1)}, s32[]{:S(2)}) %slice-start) | async-done | bytes 2113560 | tf_op jit(solution)/shard_map/slice | solution.py:141
  64.6 4.2 %reshape.47 = f32[64,32,258]{2,1,0:T(8,128)} reshape(f32[64,8256]{1,0:T(8,128)S(1)} %slice-done) | data formatting | bytes 4227072 | tf_op jit(solution)/shard_map/reshape | solution.py:142
  68.7 3.7 %copy.21 = f32[64,32,258]{2,0,1:T(8,128)S(1)} copy(f32[64,32,258]{2,1,0:T(8,128)} %reshape.47) | data formatting | bytes 4227072 | tf_op jit(solution)/shard_map/reshape | solution.py:142
  72.5 2.4 %gather_fusion = f32[32,64,258]{2,1,0:T(8,128)} fusion(f32[32,64,258]{2,1,0:T(8,128)S(1)} %bitcast.13, s32[1024]{0:T(1024)S(1)} %pad_clamp_fusion), kind=kCustom, calls=%fused_computation | custom fusion | bytes 4227200 | tf_op jit(solution)/shard_map/jit(_take)/gather | solution.py:143
  74.8 3.8 %reshape_reshape.7 = f32[2,2,2,2,2,129,128]{6,5,4,3,2,1,0:T(8,128)S(1)} reshape(f32[32,64,258]{2,1,0:T(8,128)} %gather_fusion) | data formatting | bytes 4227072 | tf_op jit(solution)/shard_map/reshape;reshape | solution.py:57
  78.6 0.1 constant_dynamic-slice_fusion.12
  78.7 0.5 copy.17
  79.3 0.4 collective-permute-start.6
  79.7 2.5 %collective-permute-done.6 = f32[2,2,2,2,1,129,128]{6,3,5,4,2,1,0:T(2,128)} collective-permute-done((f32[2,2,2,2,1,129,128]{6,3,5,4,2,1,0:T(2,128)S(1)}, f32[2,2,2,2,1,129,128]{6,3,5,4,2,1,0:T(2,128)}, u32[]{:S(2)}, u32[]{:S(2)}) %collective-permute-start.6) | collective-permute-done | bytes 1056800 | tf_op jit(solution)/shard_map/ppermute | solution.py:48
  82.1 1.3 %copy_add_fusion = f32[2,2,2,2,1,129,128]{6,5,4,3,2,1,0:T(8,128)S(1)} fusion(f32[2,2,2,2,1,129,128]{6,3,5,4,2,1,0:T(2,128)} %collective-permute-done.6, f32[2,2,2,2,2,129,128]{6,5,4,3,2,1,0:T(8,128)S(1)} %reshape_reshape.7, s32[]{:T(128)S(6)} %select_n.122), kind=kLoop, calls=%fused_computation.2 | loop fusion | flops 264192 | bytes 3170308 | tf_op jit(solution)/shard_map/add | solution.py:48
  83.5 0.1 fusion.4
  83.6 0.6 collective-permute-start.15
  84.2 0.2 collective-permute-start.11
  84.4 3.1 %collective-permute-start.7 = (f32[1,2,2,2,1,43,128]{6,5,4,3,2,1,0:T(8,128)S(1)}, f32[1,2,2,2,1,43,128]{6,5,4,3,2,1,0:T(8,128)S(1)}, u32[]{:S(2)}, u32[]{:S(2)}) collective-permute-start(f32[1,2,2,2,1,43,128]{6,5,4,3,2,1,0:T(8,128)S(1)} %constant_dynamic-slice_fusion.11), channel_id=1, source_target_pairs={{0,16},{8,24},{16,0},{24,8},{1,17},{9,25},{17,1},{25,9},{2,18},{10... | collective-permute-start | bytes 528392 | tf_op jit(solution)/shard_map/ppermute | solution.py:48
  87.5 3.3 %collective-permute-done.15 = f32[2,2,1,2,1,43,128]{6,5,4,3,2,1,0:T(8,128)S(1)} collective-permute-done((f32[2,2,1,2,1,43,128]{6,5,4,3,2,1,0:T(8,128)S(1)}, f32[2,2,1,2,1,43,128]{6,5,4,3,2,1,0:T(8,128)S(1)}, u32[]{:S(2)}, u32[]{:S(2)}) %collective-permute-start.15) | collective-permute-done | bytes 176160 | tf_op jit(solution)/shard_map/ppermute | solution.py:48
  90.9 0.1 collective-permute-start.16
  91.0 4.1 %collective-permute-done.11 = f32[2,1,2,2,1,43,128]{6,5,4,3,2,1,0:T(8,128)S(1)} collective-permute-done((f32[2,1,2,2,1,43,128]{6,5,4,3,2,1,0:T(8,128)S(1)}, f32[2,1,2,2,1,43,128]{6,5,4,3,2,1,0:T(8,128)S(1)}, u32[]{:S(2)}, u32[]{:S(2)}) %collective-permute-start.11) | collective-permute-done | bytes 176160 | tf_op jit(solution)/shard_map/ppermute | solution.py:48
  95.2 1.5 %collective-permute-start.12 = (f32[2,1,1,2,1,43,128]{6,5,4,3,2,1,0:T(8,128)S(1)}, f32[2,1,1,2,1,43,128]{6,5,4,3,2,1,0:T(8,128)S(1)}, u32[]{:S(2)}, u32[]{:S(2)}) collective-permute-start(f32[2,1,1,2,1,43,128]{6,5,4,3,2,1,0:T(8,128)S(1)} %constant_dynamic-slice_fusion.6), channel_id=1, source_target_pairs={{0,4},{2,6},{4,0},{6,2},{1,5},{3,7},{5,1},{7,3},{8,12},{10,14},{12... | collective-permute-start | bytes 264200 | tf_op jit(solution)/shard_map/ppermute | solution.py:48
  96.7 0.0 collective-permute-done.7
  96.8 0.3 collective-permute-start.8
  97.1 0.0 collective-permute-done.16
  97.2 2.8 %collective-permute-start.17 = (f32[1,2,1,1,1,43,128]{6,5,4,3,2,1,0:T(8,128)S(1)}, f32[1,2,1,1,1,43,128]{6,5,4,3,2,1,0:T(8,128)S(1)}, u32[]{:S(2)}, u32[]{:S(2)}) collective-permute-start(f32[1,2,1,1,1,43,128]{6,5,4,3,2,1,0:T(8,128)S(1)} %constant_dynamic-slice_fusion.1), channel_id=1, source_target_pairs={{0,16},{8,24},{16,0},{24,8},{1,17},{9,25},{17,1},{25,9},{2,18},{10... | collective-permute-start | bytes 132104 | tf_op jit(solution)/shard_map/ppermute | solution.py:48
  99.9 0.0 collective-permute-done.12
  100.0 0.1 collective-permute-start.13
  100.1 1.5 %collective-permute-done.8 = f32[1,1,2,2,1,43,128]{6,5,4,3,2,1,0:T(8,128)S(1)} collective-permute-done((f32[1,1,2,2,1,43,128]{6,5,4,3,2,1,0:T(8,128)S(1)}, f32[1,1,2,2,1,43,128]{6,5,4,3,2,1,0:T(8,128)S(1)}, u32[]{:S(2)}, u32[]{:S(2)}) %collective-permute-start.8) | collective-permute-done | bytes 88096 | tf_op jit(solution)/shard_map/ppermute | solution.py:48
  101.6 1.5 %collective-permute-start.9 = (f32[1,1,1,2,1,43,128]{6,5,4,3,2,1,0:T(8,128)S(1)}, f32[1,1,1,2,1,43,128]{6,5,4,3,2,1,0:T(8,128)S(1)}, u32[]{:S(2)}, u32[]{:S(2)}) collective-permute-start(f32[1,1,1,2,1,43,128]{6,5,4,3,2,1,0:T(8,128)S(1)} %constant_dynamic-slice_fusion.9), channel_id=1, source_target_pairs={{0,4},{2,6},{4,0},{6,2},{1,5},{3,7},{5,1},{7,3},{8,12},{10,14},{12... | collective-permute-start | bytes 132104 | tf_op jit(solution)/shard_map/ppermute | solution.py:48
  103.2 0.0 collective-permute-done.17
  103.2 0.9 collective-permute-start.18
  104.1 0.0 collective-permute-done.13
  104.1 2.1 %collective-permute-start.14 = (f32[1,1,1,1,1,43,128]{6,5,4,3,2,1,0:T(8,128)S(1)}, f32[1,1,1,1,1,43,128]{6,5,4,3,2,1,0:T(8,128)S(1)}, u32[]{:S(2)}, u32[]{:S(2)}) collective-permute-start(f32[1,1,1,1,1,43,128]{6,5,4,3,2,1,0:T(8,128)S(1)} %constant_dynamic-slice_fusion.4), channel_id=1, source_target_pairs={{0,16},{8,24},{16,0},{24,8},{1,17},{9,25},{17,1},{25,9},{2,18},{10... | collective-permute-start | bytes 66056 | tf_op jit(solution)/shard_map/ppermute | solution.py:48
  106.2 0.0 collective-permute-done.9
  106.3 0.1 collective-permute-start.10
  106.4 0.7 collective-permute-done.18
  107.1 1.8 %collective-permute-done.14 = f32[1,1,1,1,1,43,128]{6,5,4,3,2,1,0:T(8,128)S(1)} collective-permute-done((f32[1,1,1,1,1,43,128]{6,5,4,3,2,1,0:T(8,128)S(1)}, f32[1,1,1,1,1,43,128]{6,5,4,3,2,1,0:T(8,128)S(1)}, u32[]{:S(2)}, u32[]{:S(2)}) %collective-permute-start.14) | collective-permute-done | bytes 22048 | tf_op jit(solution)/shard_map/ppermute | solution.py:48
  108.9 1.2 %collective-permute-done.10 = f32[1,1,1,1,1,43,128]{6,5,4,3,2,1,0:T(8,128)S(1)} collective-permute-done((f32[1,1,1,1,1,43,128]{6,5,4,3,2,1,0:T(8,128)S(1)}, f32[1,1,1,1,1,43,128]{6,5,4,3,2,1,0:T(8,128)S(1)}, u32[]{:S(2)}, u32[]{:S(2)}) %collective-permute-start.10) | collective-permute-done | bytes 22048 | tf_op jit(solution)/shard_map/ppermute | solution.py:48
  110.2 0.8 reshape_reshape_reshape.3
  (30 shorter events, 0.4 us)
Async XLA Ops:
  0.8 7.3 %collective-permute-start = (f32[3,1,8,4,128]{4,3,2,1,0:T(4,128)S(1)}, f32[3,1,8,4,128]{4,3,2,1,0:T(4,128)S(1)}, u32[]{:S(2)}, u32[]{:S(2)}) collective-permute-start(f32[3,1,8,4,128]{4,3,2,1,0:T(4,128)S(1)} %get-tuple-element.16), channel_id=1, source_target_pairs={{0,8},{8,16},{16,24},{24,0},{1,9},{9,17},{17,25},{25,1},{2,10},{10... | collective-permute-start | bytes 147464 | tf_op jit(solution)/shard_map/ppermute | solution.py:19
  3.9 5.2 %collective-permute-start.1 = (f32[3,1,8,4,128]{4,3,2,1,0:T(4,128)S(1)}, f32[3,1,8,4,128]{4,3,2,1,0:T(4,128)S(1)}, u32[]{:S(2)}, u32[]{:S(2)}) collective-permute-start(f32[3,1,8,4,128]{4,3,2,1,0:T(4,128)S(1)} %get-tuple-element.15), channel_id=1, source_target_pairs={{8,0},{16,8},{24,16},{0,24},{9,1},{17,9},{25,17},{1,25},{10,2},{18... | collective-permute-start | bytes 147464 | tf_op jit(solution)/shard_map/ppermute | solution.py:20
  9.1 4.6 %collective-permute-start.3 = (f32[3,6,1,4,128]{4,3,2,1,0:T(4,128)S(1)}, f32[3,6,1,4,128]{4,3,2,1,0:T(4,128)S(1)}, u32[]{:S(2)}, u32[]{:S(2)}) collective-permute-start(f32[3,6,1,4,128]{4,3,2,1,0:T(4,128)S(1)} %get-tuple-element.14), channel_id=1, source_target_pairs={{2,0},{4,2},{6,4},{0,6},{3,1},{5,3},{7,5},{1,7},{10,8},{12,10},{14... | collective-permute-start | bytes 110600 | tf_op jit(solution)/shard_map/ppermute | solution.py:20
  11.9 4.9 %collective-permute-start.2 = (f32[3,6,1,4,128]{4,3,2,1,0:T(4,128)S(1)}, f32[3,6,1,4,128]{4,3,2,1,0:T(4,128)S(1)}, u32[]{:S(2)}, u32[]{:S(2)}) collective-permute-start(f32[3,6,1,4,128]{4,3,2,1,0:T(4,128)S(1)} %get-tuple-element.13), channel_id=1, source_target_pairs={{0,2},{2,4},{4,6},{6,0},{1,3},{3,5},{5,7},{7,1},{8,10},{10,12},{12... | collective-permute-start | bytes 110600 | tf_op jit(solution)/shard_map/ppermute | solution.py:19
  17.0 1.4 %collective-permute-start.5 = (f32[3,6,10,1,128]{4,3,2,1,0:T(1,128)S(1)}, f32[3,6,10,1,128]{4,3,2,1,0:T(1,128)S(1)}, u32[]{:S(2)}, u32[]{:S(2)}) collective-permute-start(f32[3,6,10,1,128]{4,3,2,1,0:T(1,128)S(1)} %get-tuple-element.12), channel_id=1, source_target_pairs={{1,0},{0,1},{3,2},{2,3},{5,4},{4,5},{7,6},{6,7},{9,8},{8,9},{11,10... | collective-permute-start | bytes 276488 | tf_op jit(solution)/shard_map/ppermute | solution.py:20
  17.0 1.4 %collective-permute-start.4 = (f32[3,6,10,1,128]{4,3,2,1,0:T(1,128)S(1)}, f32[3,6,10,1,128]{4,3,2,1,0:T(1,128)S(1)}, u32[]{:S(2)}, u32[]{:S(2)}) collective-permute-start(f32[3,6,10,1,128]{4,3,2,1,0:T(1,128)S(1)} %get-tuple-element.11), channel_id=1, source_target_pairs={{0,1},{1,0},{2,3},{3,2},{4,5},{5,4},{6,7},{7,6},{8,9},{9,8},{10,11... | collective-permute-start | bytes 276488 | tf_op jit(solution)/shard_map/ppermute | solution.py:19
  63.0 1.6 %slice-start = ((f32[64,8448]{1,0:T(8,128)}), f32[64,8256]{1,0:T(8,128)S(1)}, s32[]{:S(2)}) async-start(f32[64,8448]{1,0:T(8,128)} %shard_map.37), calls=%async_computation | async-start | bytes 4259840 | tf_op jit(solution)/shard_map/slice | solution.py:141
  79.3 2.9 %collective-permute-start.6 = (f32[2,2,2,2,1,129,128]{6,3,5,4,2,1,0:T(2,128)S(1)}, f32[2,2,2,2,1,129,128]{6,3,5,4,2,1,0:T(2,128)}, u32[]{:S(2)}, u32[]{:S(2)}) collective-permute-start(f32[2,2,2,2,1,129,128]{6,3,5,4,2,1,0:T(2,128)S(1)} %copy.17), channel_id=1, source_target_pairs={{0,1},{1,0},{2,3},{3,2},{4,5},{5,4},{6,7},{7,6},{8,9},{9,8},{10,11... | collective-permute-start | bytes 3170312 | tf_op jit(solution)/shard_map/ppermute | solution.py:48
  83.6 7.3 %collective-permute-start.15 = (f32[2,2,1,2,1,43,128]{6,5,4,3,2,1,0:T(8,128)S(1)}, f32[2,2,1,2,1,43,128]{6,5,4,3,2,1,0:T(8,128)S(1)}, u32[]{:S(2)}, u32[]{:S(2)}) collective-permute-start(f32[2,2,1,2,1,43,128]{6,5,4,3,2,1,0:T(8,128)S(1)} %constant_dynamic-slice_fusion.3), channel_id=1, source_target_pairs={{0,4},{2,6},{4,0},{6,2},{1,5},{3,7},{5,1},{7,3},{8,12},{10,14},{12... | collective-permute-start | bytes 528392 | tf_op jit(solution)/shard_map/ppermute | solution.py:48
  84.2 10.9 %collective-permute-start.11 = (f32[2,1,2,2,1,43,128]{6,5,4,3,2,1,0:T(8,128)S(1)}, f32[2,1,2,2,1,43,128]{6,5,4,3,2,1,0:T(8,128)S(1)}, u32[]{:S(2)}, u32[]{:S(2)}) collective-permute-start(f32[2,1,2,2,1,43,128]{6,5,4,3,2,1,0:T(8,128)S(1)} %constant_dynamic-slice_fusion.7), channel_id=1, source_target_pairs={{0,8},{8,0},{16,24},{24,16},{1,9},{9,1},{17,25},{25,17},{2,10},{10... | collective-permute-start | bytes 528392 | tf_op jit(solution)/shard_map/ppermute | solution.py:48
  84.4 12.3 %collective-permute-start.7 = (f32[1,2,2,2,1,43,128]{6,5,4,3,2,1,0:T(8,128)S(1)}, f32[1,2,2,2,1,43,128]{6,5,4,3,2,1,0:T(8,128)S(1)}, u32[]{:S(2)}, u32[]{:S(2)}) collective-permute-start(f32[1,2,2,2,1,43,128]{6,5,4,3,2,1,0:T(8,128)S(1)} %constant_dynamic-slice_fusion.11), channel_id=1, source_target_pairs={{0,16},{8,24},{16,0},{24,8},{1,17},{9,25},{17,1},{25,9},{2,18},{10... | collective-permute-start | bytes 528392 | tf_op jit(solution)/shard_map/ppermute | solution.py:48
  90.9 6.2 %collective-permute-start.16 = (f32[2,2,1,1,1,43,128]{6,5,4,3,2,1,0:T(8,128)S(1)}, f32[2,2,1,1,1,43,128]{6,5,4,3,2,1,0:T(8,128)S(1)}, u32[]{:S(2)}, u32[]{:S(2)}) collective-permute-start(f32[2,2,1,1,1,43,128]{6,5,4,3,2,1,0:T(8,128)S(1)} %constant_dynamic-slice_fusion.2), channel_id=1, source_target_pairs={{0,2},{2,0},{4,6},{6,4},{1,3},{3,1},{5,7},{7,5},{8,10},{10,8},{12,... | collective-permute-start | bytes 264200 | tf_op jit(solution)/shard_map/ppermute | solution.py:48
  95.2 4.7 %collective-permute-start.12 = (f32[2,1,1,2,1,43,128]{6,5,4,3,2,1,0:T(8,128)S(1)}, f32[2,1,1,2,1,43,128]{6,5,4,3,2,1,0:T(8,128)S(1)}, u32[]{:S(2)}, u32[]{:S(2)}) collective-permute-start(f32[2,1,1,2,1,43,128]{6,5,4,3,2,1,0:T(8,128)S(1)} %constant_dynamic-slice_fusion.6), channel_id=1, source_target_pairs={{0,4},{2,6},{4,0},{6,2},{1,5},{3,7},{5,1},{7,3},{8,12},{10,14},{12... | collective-permute-start | bytes 264200 | tf_op jit(solution)/shard_map/ppermute | solution.py:48
  96.8 4.8 %collective-permute-start.8 = (f32[1,1,2,2,1,43,128]{6,5,4,3,2,1,0:T(8,128)S(1)}, f32[1,1,2,2,1,43,128]{6,5,4,3,2,1,0:T(8,128)S(1)}, u32[]{:S(2)}, u32[]{:S(2)}) collective-permute-start(f32[1,1,2,2,1,43,128]{6,5,4,3,2,1,0:T(8,128)S(1)} %constant_dynamic-slice_fusion.10), channel_id=1, source_target_pairs={{0,8},{8,0},{16,24},{24,16},{1,9},{9,1},{17,25},{25,17},{2,10},{10... | collective-permute-start | bytes 264200 | tf_op jit(solution)/shard_map/ppermute | solution.py:48
  97.2 6.0 %collective-permute-start.17 = (f32[1,2,1,1,1,43,128]{6,5,4,3,2,1,0:T(8,128)S(1)}, f32[1,2,1,1,1,43,128]{6,5,4,3,2,1,0:T(8,128)S(1)}, u32[]{:S(2)}, u32[]{:S(2)}) collective-permute-start(f32[1,2,1,1,1,43,128]{6,5,4,3,2,1,0:T(8,128)S(1)} %constant_dynamic-slice_fusion.1), channel_id=1, source_target_pairs={{0,16},{8,24},{16,0},{24,8},{1,17},{9,25},{17,1},{25,9},{2,18},{10... | collective-permute-start | bytes 132104 | tf_op jit(solution)/shard_map/ppermute | solution.py:48
  100.0 4.2 %collective-permute-start.13 = (f32[2,1,1,1,1,43,128]{6,5,4,3,2,1,0:T(8,128)S(1)}, f32[2,1,1,1,1,43,128]{6,5,4,3,2,1,0:T(8,128)S(1)}, u32[]{:S(2)}, u32[]{:S(2)}) collective-permute-start(f32[2,1,1,1,1,43,128]{6,5,4,3,2,1,0:T(8,128)S(1)} %constant_dynamic-slice_fusion.5), channel_id=1, source_target_pairs={{0,2},{2,0},{4,6},{6,4},{1,3},{3,1},{5,7},{7,5},{8,10},{10,8},{12,... | collective-permute-start | bytes 132104 | tf_op jit(solution)/shard_map/ppermute | solution.py:48
  101.6 4.6 %collective-permute-start.9 = (f32[1,1,1,2,1,43,128]{6,5,4,3,2,1,0:T(8,128)S(1)}, f32[1,1,1,2,1,43,128]{6,5,4,3,2,1,0:T(8,128)S(1)}, u32[]{:S(2)}, u32[]{:S(2)}) collective-permute-start(f32[1,1,1,2,1,43,128]{6,5,4,3,2,1,0:T(8,128)S(1)} %constant_dynamic-slice_fusion.9), channel_id=1, source_target_pairs={{0,4},{2,6},{4,0},{6,2},{1,5},{3,7},{5,1},{7,3},{8,12},{10,14},{12... | collective-permute-start | bytes 132104 | tf_op jit(solution)/shard_map/ppermute | solution.py:48
  103.2 3.9 %collective-permute-start.18 = (f32[1,1,1,1,1,43,128]{6,5,4,3,2,1,0:T(8,128)S(1)}, f32[1,1,1,1,1,43,128]{6,5,4,3,2,1,0:T(8,128)S(1)}, u32[]{:S(2)}, u32[]{:S(2)}) collective-permute-start(f32[1,1,1,1,1,43,128]{6,5,4,3,2,1,0:T(8,128)S(1)} %constant_dynamic-slice_fusion), channel_id=1, source_target_pairs={{0,8},{8,0},{16,24},{24,16},{1,9},{9,1},{17,25},{25,17},{2,10},{10... | collective-permute-start | bytes 66056 | tf_op jit(solution)/shard_map/ppermute | solution.py:48
  104.1 4.8 %collective-permute-start.14 = (f32[1,1,1,1,1,43,128]{6,5,4,3,2,1,0:T(8,128)S(1)}, f32[1,1,1,1,1,43,128]{6,5,4,3,2,1,0:T(8,128)S(1)}, u32[]{:S(2)}, u32[]{:S(2)}) collective-permute-start(f32[1,1,1,1,1,43,128]{6,5,4,3,2,1,0:T(8,128)S(1)} %constant_dynamic-slice_fusion.4), channel_id=1, source_target_pairs={{0,16},{8,24},{16,0},{24,8},{1,17},{9,25},{17,1},{25,9},{2,18},{10... | collective-permute-start | bytes 66056 | tf_op jit(solution)/shard_map/ppermute | solution.py:48
  106.3 3.9 %collective-permute-start.10 = (f32[1,1,1,1,1,43,128]{6,5,4,3,2,1,0:T(8,128)S(1)}, f32[1,1,1,1,1,43,128]{6,5,4,3,2,1,0:T(8,128)S(1)}, u32[]{:S(2)}, u32[]{:S(2)}) collective-permute-start(f32[1,1,1,1,1,43,128]{6,5,4,3,2,1,0:T(8,128)S(1)} %constant_dynamic-slice_fusion.8), channel_id=1, source_target_pairs={{0,2},{2,0},{4,6},{6,4},{1,3},{3,1},{5,7},{7,5},{8,10},{10,8},{12,... | collective-permute-start | bytes 66056 | tf_op jit(solution)/shard_map/ppermute | solution.py:48

commit v4 on v3

--- a/solution.py
+++ b/solution.py
@@ -73,18 +73,26 @@
 
 def triangle_kernel(w_ref, g_ref, m_ref, out_ref, sym_ref):
     test, width = w_ref.shape[1], m_ref.shape[1]
+    group = 4
     out_ref[...] = jnp.zeros(out_ref.shape, out_ref.dtype)
 
-    def contract(i, carry):
-        zt = w_ref[0, pl.ds(i, 1), :] * g_ref[0]
-        zt = zt + w_ref[1, pl.ds(i, 1), :] * g_ref[1]
-        zt = zt + w_ref[2, pl.ds(i, 1), :] * g_ref[2]
+    def contract(step, carry):
+        slabs = []
+        for u in range(group):
+            i = step * group + u
+            zt = w_ref[0, pl.ds(i, 1), :] * g_ref[0]
+            zt = zt + w_ref[1, pl.ds(i, 1), :] * g_ref[1]
+            zt = zt + w_ref[2, pl.ds(i, 1), :] * g_ref[2]
+            slabs.append(zt)
+        zt = jnp.concatenate(slabs, axis=0)
         part = jnp.dot(zt, m_ref[...], precision=lax.Precision.HIGHEST, preferred_element_type=jnp.float32)
-        start = pl.multiple_of(i * width, width)
-        sym_ref[pl.ds(start, width), :] = part + part.T
+        for u in range(group):
+            piece = part[u * width : (u + 1) * width, :]
+            start = pl.multiple_of((step * group + u) * width, width)
+            sym_ref[pl.ds(start, width), :] = piece + piece.T
         return carry
 
-    lax.fori_loop(0, test, contract, 0)
+    lax.fori_loop(0, test // group, contract, 0)
     lane = lax.broadcasted_iota(jnp.int32, (test, 128), 1)
 
     def place(j, carry):

time: 111 us -> 99.9 us (0.900)
  Pallas kernels: 42.9 us -> 31.3 us
    pallas_call x1, Pallas kernels: 42.9 us -> 31.3 us  [triangle(): pl.pallas_call(triangle_kernel, out_shape=jax.ShapeDtypeStruct((test, til...]
  transfers between devices with their start and end apart: 19 -> 19, of which waited for: 11 -> 11; matrix products, arithmetic and copies ran while one was open for 4% -> 5% of each run, Pallas kernels for 0% -> 0%
where the time goes in v4:
time: 99.9 us; the launch traced here: 99.4 us
  Pallas kernels  31.3 us (31%)
  starting transfers between devices  22.4 us (22%)
  local copies, waits for them, and re-layouts  21.5 us (22%)
  waiting for transfers between devices  19.4 us (19%)
  other arithmetic  4.53 us (5%)
    pallas_call x1, Pallas kernels, triangle(): pl.pallas_call(triangle_kernel, out_shape=jax.ShapeDtypeStruct((test, til...  31.3 us
    ppermute x13, waiting for transfers between devices, halve(): return keep + lax.ppermute(other, axis, pairs)  15.1 us
    ppermute x13, starting transfers between devices, halve(): return keep + lax.ppermute(other, axis, pairs)  13.8 us
    reshape x2, local copies, waits for them, and re-layouts, shards(): blocks = canon.reshape(TEST, owners, block_len).transpose(1, 0, 2)  7.88 us
    ppermute x3, starting transfers between devices, extended(): after = lax.ppermute(leading, axis, down)  5 us
    another operation x1, local copies, waits for them, and re-layouts, scatter_sum(): value = payload.reshape((2,) * len(stages) + (rows, lanes))  3.77 us
    ppermute x3, starting transfers between devices, extended(): before = lax.ppermute(last, axis, up)  3.56 us
    ppermute x3, waiting for transfers between devices, extended(): before = lax.ppermute(last, axis, up)  3.46 us
  transfers between devices with their start and end apart: 19, of which 11 were waited for; matrix products, arithmetic and copies ran while one was open for 5% of the time, Pallas kernels for 0%

profile of v4, /device:TPU:0, one launch (start us, length us, event | category | flops | bytes accessed | tf_op | source)
XLA Modules:
  0.0 99.4 jit_solution(11327140909500571057)
XLA Ops:
  0.0 0.8 fusion.6
  0.8 3.1 %collective-permute-start = (f32[3,1,8,4,128]{4,3,2,1,0:T(4,128)S(1)}, f32[3,1,8,4,128]{4,3,2,1,0:T(4,128)S(1)}, u32[]{:S(2)}, u32[]{:S(2)}) collective-permute-start(f32[3,1,8,4,128]{4,3,2,1,0:T(4,128)S(1)} %get-tuple-element.16), channel_id=1, source_target_pairs={{0,8},{8,16},{16,24},{24,0},{1,9},{9,17},{17,25},{25,1},{2,10},{10... | collective-permute-start | bytes 147464 | tf_op jit(solution)/shard_map/ppermute | solution.py:19
  3.9 2.1 %collective-permute-start.1 = (f32[3,1,8,4,128]{4,3,2,1,0:T(4,128)S(1)}, f32[3,1,8,4,128]{4,3,2,1,0:T(4,128)S(1)}, u32[]{:S(2)}, u32[]{:S(2)}) collective-permute-start(f32[3,1,8,4,128]{4,3,2,1,0:T(4,128)S(1)} %get-tuple-element.15), channel_id=1, source_target_pairs={{8,0},{16,8},{24,16},{0,24},{9,1},{17,9},{25,17},{1,25},{10,2},{18... | collective-permute-start | bytes 147464 | tf_op jit(solution)/shard_map/ppermute | solution.py:20
  6.0 0.7 broadcast_multiply_fusion
  6.7 0.1 copy.13
  6.8 0.1 mul.32
  6.9 1.0 %fusion.3 = f32[3,64,128]{1,2,0:T(8,128)S(1)} fusion(f32[3,128,128]{2,1,0:T(8,128)} %bitcast.14, f32[128]{0:T(128)S(1)} %mul.32), kind=kLoop, calls=%fused_computation.12 | loop fusion | flops 24576 | bytes 197120 | tf_op jit(solution)/shard_map/transpose | solution.py:145
  7.9 0.2 collective-permute-done
  8.1 1.0 constant_dynamic-update-slice_fusion.1
  9.1 0.0 collective-permute-done.1
  9.1 2.8 %collective-permute-start.3 = (f32[3,6,1,4,128]{4,3,2,1,0:T(4,128)S(1)}, f32[3,6,1,4,128]{4,3,2,1,0:T(4,128)S(1)}, u32[]{:S(2)}, u32[]{:S(2)}) collective-permute-start(f32[3,6,1,4,128]{4,3,2,1,0:T(4,128)S(1)} %get-tuple-element.14), channel_id=1, source_target_pairs={{2,0},{4,2},{6,4},{0,6},{3,1},{5,3},{7,5},{1,7},{10,8},{12,10},{14... | collective-permute-start | bytes 110600 | tf_op jit(solution)/shard_map/ppermute | solution.py:20
  11.9 0.0 collective-permute-start.2
  11.9 0.7 pad_clamp_fusion
  12.6 0.1 copy.14
  12.7 0.1 tile.4
  12.8 0.9 tile.10.w_ref
  13.7 0.0 collective-permute-done.3
  13.7 3.1 %collective-permute-done.2 = f32[3,6,1,4,128]{4,3,2,1,0:T(4,128)S(1)} collective-permute-done((f32[3,6,1,4,128]{4,3,2,1,0:T(4,128)S(1)}, f32[3,6,1,4,128]{4,3,2,1,0:T(4,128)S(1)}, u32[]{:S(2)}, u32[]{:S(2)}) %collective-permute-start.2) | collective-permute-done | bytes 36896 | tf_op jit(solution)/shard_map/ppermute | solution.py:19
  16.8 0.1 pad_maximum_fusion.3
  17.0 0.1 collective-permute-start.5
  17.0 0.5 collective-permute-start.4
  17.5 0.8 collective-permute-done.5
  18.3 0.2 collective-permute-done.4
  18.5 0.3 maximum_select_fusion
  18.7 0.2 fusion.2
  19.0 1.1 %copy.15.g_ref = f32[3,128,384]{2,1,0:T(8,128)} copy(f32[3,128,384]{1,2,0:T(8,128)S(1)} %bitcast.16) | data formatting | bytes 1179648 | tf_op jit(solution)/shard_map/reshape | solution.py:146
  20.0 31.3 %shard_map.37 = f32[64,8448]{1,0:T(8,128)} custom-call(f32[3,64,384]{2,1,0:T(8,128)} %tile.10.w_ref, f32[3,128,384]{2,1,0:T(8,128)} %copy.15.g_ref, f32[384,128]{1,0:T(8,128)} %bitcast.15), custom_call_target="tpu_custom_call" | custom-call | tf_op jit(solution)/shard_map/pallas_call | solution.py:116
  51.3 0.0 slice-start
  51.3 1.6 %slice-done = f32[64,8256]{1,0:T(8,128)S(1)} async-done(((f32[64,8448]{1,0:T(8,128)}), f32[64,8256]{1,0:T(8,128)S(1)}, s32[]{:S(2)}) %slice-start) | async-done | bytes 2113560 | tf_op jit(solution)/shard_map/slice | solution.py:149
  52.9 4.2 %reshape.47 = f32[64,32,258]{2,1,0:T(8,128)} reshape(f32[64,8256]{1,0:T(8,128)S(1)} %slice-done) | data formatting | bytes 4227072 | tf_op jit(solution)/shard_map/reshape | solution.py:150
  57.1 3.7 %copy.21 = f32[64,32,258]{2,0,1:T(8,128)S(1)} copy(f32[64,32,258]{2,1,0:T(8,128)} %reshape.47) | data formatting | bytes 4227072 | tf_op jit(solution)/shard_map/reshape | solution.py:150
  60.8 2.4 %gather_fusion = f32[32,64,258]{2,1,0:T(8,128)} fusion(f32[32,64,258]{2,1,0:T(8,128)S(1)} %bitcast.13, s32[1024]{0:T(1024)S(1)} %pad_clamp_fusion), kind=kCustom, calls=%fused_computation | custom fusion | bytes 4227200 | tf_op jit(solution)/shard_map/jit(_take)/gather | solution.py:151
  63.2 3.8 %reshape_reshape.7 = f32[2,2,2,2,2,129,128]{6,5,4,3,2,1,0:T(8,128)S(1)} reshape(f32[32,64,258]{2,1,0:T(8,128)} %gather_fusion) | data formatting | bytes 4227072 | tf_op jit(solution)/shard_map/reshape;reshape | solution.py:57
  67.0 0.1 constant_dynamic-slice_fusion.12
  67.0 0.5 copy.17
  67.6 0.4 collective-permute-start.6
  68.0 2.4 %collective-permute-done.6 = f32[2,2,2,2,1,129,128]{6,3,5,4,2,1,0:T(2,128)} collective-permute-done((f32[2,2,2,2,1,129,128]{6,3,5,4,2,1,0:T(2,128)S(1)}, f32[2,2,2,2,1,129,128]{6,3,5,4,2,1,0:T(2,128)}, u32[]{:S(2)}, u32[]{:S(2)}) %collective-permute-start.6) | collective-permute-done | bytes 1056800 | tf_op jit(solution)/shard_map/ppermute | solution.py:48
  70.5 1.3 %copy_add_fusion = f32[2,2,2,2,1,129,128]{6,5,4,3,2,1,0:T(8,128)S(1)} fusion(f32[2,2,2,2,1,129,128]{6,3,5,4,2,1,0:T(2,128)} %collective-permute-done.6, f32[2,2,2,2,2,129,128]{6,5,4,3,2,1,0:T(8,128)S(1)} %reshape_reshape.7, s32[]{:T(128)S(6)} %select_n.122), kind=kLoop, calls=%fused_computation.2 | loop fusion | flops 264192 | bytes 3170308 | tf_op jit(solution)/shard_map/add | solution.py:48
  71.8 0.1 fusion.4
  72.0 0.6 collective-permute-start.15
  72.6 0.2 collective-permute-start.11
  72.8 3.1 %collective-permute-start.7 = (f32[1,2,2,2,1,43,128]{6,5,4,3,2,1,0:T(8,128)S(1)}, f32[1,2,2,2,1,43,128]{6,5,4,3,2,1,0:T(8,128)S(1)}, u32[]{:S(2)}, u32[]{:S(2)}) collective-permute-start(f32[1,2,2,2,1,43,128]{6,5,4,3,2,1,0:T(8,128)S(1)} %constant_dynamic-slice_fusion.11), channel_id=1, source_target_pairs={{0,16},{8,24},{16,0},{24,8},{1,17},{9,25},{17,1},{25,9},{2,18},{10... | collective-permute-start | bytes 528392 | tf_op jit(solution)/shard_map/ppermute | solution.py:48
  75.9 3.4 %collective-permute-done.15 = f32[2,2,1,2,1,43,128]{6,5,4,3,2,1,0:T(8,128)S(1)} collective-permute-done((f32[2,2,1,2,1,43,128]{6,5,4,3,2,1,0:T(8,128)S(1)}, f32[2,2,1,2,1,43,128]{6,5,4,3,2,1,0:T(8,128)S(1)}, u32[]{:S(2)}, u32[]{:S(2)}) %collective-permute-start.15) | collective-permute-done | bytes 176160 | tf_op jit(solution)/shard_map/ppermute | solution.py:48
  79.3 0.1 collective-permute-start.16
  79.4 4.0 %collective-permute-done.11 = f32[2,1,2,2,1,43,128]{6,5,4,3,2,1,0:T(8,128)S(1)} collective-permute-done((f32[2,1,2,2,1,43,128]{6,5,4,3,2,1,0:T(8,128)S(1)}, f32[2,1,2,2,1,43,128]{6,5,4,3,2,1,0:T(8,128)S(1)}, u32[]{:S(2)}, u32[]{:S(2)}) %collective-permute-start.11) | collective-permute-done | bytes 176160 | tf_op jit(solution)/shard_map/ppermute | solution.py:48
  83.5 1.6 %collective-permute-start.12 = (f32[2,1,1,2,1,43,128]{6,5,4,3,2,1,0:T(8,128)S(1)}, f32[2,1,1,2,1,43,128]{6,5,4,3,2,1,0:T(8,128)S(1)}, u32[]{:S(2)}, u32[]{:S(2)}) collective-permute-start(f32[2,1,1,2,1,43,128]{6,5,4,3,2,1,0:T(8,128)S(1)} %constant_dynamic-slice_fusion.6), channel_id=1, source_target_pairs={{0,4},{2,6},{4,0},{6,2},{1,5},{3,7},{5,1},{7,3},{8,12},{10,14},{12... | collective-permute-start | bytes 264200 | tf_op jit(solution)/shard_map/ppermute | solution.py:48
  85.1 0.0 collective-permute-done.7
  85.2 0.2 collective-permute-start.8
  85.4 0.0 collective-permute-done.16
  85.5 2.8 %collective-permute-start.17 = (f32[1,2,1,1,1,43,128]{6,5,4,3,2,1,0:T(8,128)S(1)}, f32[1,2,1,1,1,43,128]{6,5,4,3,2,1,0:T(8,128)S(1)}, u32[]{:S(2)}, u32[]{:S(2)}) collective-permute-start(f32[1,2,1,1,1,43,128]{6,5,4,3,2,1,0:T(8,128)S(1)} %constant_dynamic-slice_fusion.1), channel_id=1, source_target_pairs={{0,16},{8,24},{16,0},{24,8},{1,17},{9,25},{17,1},{25,9},{2,18},{10... | collective-permute-start | bytes 132104 | tf_op jit(solution)/shard_map/ppermute | solution.py:48
  88.2 0.0 collective-permute-done.12
  88.3 0.1 collective-permute-start.13
  88.4 1.5 %collective-permute-done.8 = f32[1,1,2,2,1,43,128]{6,5,4,3,2,1,0:T(8,128)S(1)} collective-permute-done((f32[1,1,2,2,1,43,128]{6,5,4,3,2,1,0:T(8,128)S(1)}, f32[1,1,2,2,1,43,128]{6,5,4,3,2,1,0:T(8,128)S(1)}, u32[]{:S(2)}, u32[]{:S(2)}) %collective-permute-start.8) | collective-permute-done | bytes 88096 | tf_op jit(solution)/shard_map/ppermute | solution.py:48
  89.9 1.7 %collective-permute-start.9 = (f32[1,1,1,2,1,43,128]{6,5,4,3,2,1,0:T(8,128)S(1)}, f32[1,1,1,2,1,43,128]{6,5,4,3,2,1,0:T(8,128)S(1)}, u32[]{:S(2)}, u32[]{:S(2)}) collective-permute-start(f32[1,1,1,2,1,43,128]{6,5,4,3,2,1,0:T(8,128)S(1)} %constant_dynamic-slice_fusion.9), channel_id=1, source_target_pairs={{0,4},{2,6},{4,0},{6,2},{1,5},{3,7},{5,1},{7,3},{8,12},{10,14},{12... | collective-permute-start | bytes 132104 | tf_op jit(solution)/shard_map/ppermute | solution.py:48
  91.6 0.0 collective-permute-done.17
  91.6 0.9 collective-permute-start.18
  92.5 0.0 collective-permute-done.13
  92.5 2.1 %collective-permute-start.14 = (f32[1,1,1,1,1,43,128]{6,5,4,3,2,1,0:T(8,128)S(1)}, f32[1,1,1,1,1,43,128]{6,5,4,3,2,1,0:T(8,128)S(1)}, u32[]{:S(2)}, u32[]{:S(2)}) collective-permute-start(f32[1,1,1,1,1,43,128]{6,5,4,3,2,1,0:T(8,128)S(1)} %constant_dynamic-slice_fusion.4), channel_id=1, source_target_pairs={{0,16},{8,24},{16,0},{24,8},{1,17},{9,25},{17,1},{25,9},{2,18},{10... | collective-permute-start | bytes 66056 | tf_op jit(solution)/shard_map/ppermute | solution.py:48
  94.6 0.0 collective-permute-done.9
  94.6 0.1 collective-permute-start.10
  94.7 0.8 collective-permute-done.18
  95.5 1.8 %collective-permute-done.14 = f32[1,1,1,1,1,43,128]{6,5,4,3,2,1,0:T(8,128)S(1)} collective-permute-done((f32[1,1,1,1,1,43,128]{6,5,4,3,2,1,0:T(8,128)S(1)}, f32[1,1,1,1,1,43,128]{6,5,4,3,2,1,0:T(8,128)S(1)}, u32[]{:S(2)}, u32[]{:S(2)}) %collective-permute-start.14) | collective-permute-done | bytes 22048 | tf_op jit(solution)/shard_map/ppermute | solution.py:48
  97.3 1.2 %collective-permute-done.10 = f32[1,1,1,1,1,43,128]{6,5,4,3,2,1,0:T(8,128)S(1)} collective-permute-done((f32[1,1,1,1,1,43,128]{6,5,4,3,2,1,0:T(8,128)S(1)}, f32[1,1,1,1,1,43,128]{6,5,4,3,2,1,0:T(8,128)S(1)}, u32[]{:S(2)}, u32[]{:S(2)}) %collective-permute-start.10) | collective-permute-done | bytes 22048 | tf_op jit(solution)/shard_map/ppermute | solution.py:48
  98.5 0.8 reshape_reshape_reshape.3
  (30 shorter events, 0.4 us)
Async XLA Ops:
  0.8 7.3 %collective-permute-start = (f32[3,1,8,4,128]{4,3,2,1,0:T(4,128)S(1)}, f32[3,1,8,4,128]{4,3,2,1,0:T(4,128)S(1)}, u32[]{:S(2)}, u32[]{:S(2)}) collective-permute-start(f32[3,1,8,4,128]{4,3,2,1,0:T(4,128)S(1)} %get-tuple-element.16), channel_id=1, source_target_pairs={{0,8},{8,16},{16,24},{24,0},{1,9},{9,17},{17,25},{25,1},{2,10},{10... | collective-permute-start | bytes 147464 | tf_op jit(solution)/shard_map/ppermute | solution.py:19
  3.9 5.2 %collective-permute-start.1 = (f32[3,1,8,4,128]{4,3,2,1,0:T(4,128)S(1)}, f32[3,1,8,4,128]{4,3,2,1,0:T(4,128)S(1)}, u32[]{:S(2)}, u32[]{:S(2)}) collective-permute-start(f32[3,1,8,4,128]{4,3,2,1,0:T(4,128)S(1)} %get-tuple-element.15), channel_id=1, source_target_pairs={{8,0},{16,8},{24,16},{0,24},{9,1},{17,9},{25,17},{1,25},{10,2},{18... | collective-permute-start | bytes 147464 | tf_op jit(solution)/shard_map/ppermute | solution.py:20
  9.1 4.6 %collective-permute-start.3 = (f32[3,6,1,4,128]{4,3,2,1,0:T(4,128)S(1)}, f32[3,6,1,4,128]{4,3,2,1,0:T(4,128)S(1)}, u32[]{:S(2)}, u32[]{:S(2)}) collective-permute-start(f32[3,6,1,4,128]{4,3,2,1,0:T(4,128)S(1)} %get-tuple-element.14), channel_id=1, source_target_pairs={{2,0},{4,2},{6,4},{0,6},{3,1},{5,3},{7,5},{1,7},{10,8},{12,10},{14... | collective-permute-start | bytes 110600 | tf_op jit(solution)/shard_map/ppermute | solution.py:20
  11.9 4.9 %collective-permute-start.2 = (f32[3,6,1,4,128]{4,3,2,1,0:T(4,128)S(1)}, f32[3,6,1,4,128]{4,3,2,1,0:T(4,128)S(1)}, u32[]{:S(2)}, u32[]{:S(2)}) collective-permute-start(f32[3,6,1,4,128]{4,3,2,1,0:T(4,128)S(1)} %get-tuple-element.13), channel_id=1, source_target_pairs={{0,2},{2,4},{4,6},{6,0},{1,3},{3,5},{5,7},{7,1},{8,10},{10,12},{12... | collective-permute-start | bytes 110600 | tf_op jit(solution)/shard_map/ppermute | solution.py:19
  17.0 1.4 %collective-permute-start.5 = (f32[3,6,10,1,128]{4,3,2,1,0:T(1,128)S(1)}, f32[3,6,10,1,128]{4,3,2,1,0:T(1,128)S(1)}, u32[]{:S(2)}, u32[]{:S(2)}) collective-permute-start(f32[3,6,10,1,128]{4,3,2,1,0:T(1,128)S(1)} %get-tuple-element.12), channel_id=1, source_target_pairs={{1,0},{0,1},{3,2},{2,3},{5,4},{4,5},{7,6},{6,7},{9,8},{8,9},{11,10... | collective-permute-start | bytes 276488 | tf_op jit(solution)/shard_map/ppermute | solution.py:20
  17.0 1.4 %collective-permute-start.4 = (f32[3,6,10,1,128]{4,3,2,1,0:T(1,128)S(1)}, f32[3,6,10,1,128]{4,3,2,1,0:T(1,128)S(1)}, u32[]{:S(2)}, u32[]{:S(2)}) collective-permute-start(f32[3,6,10,1,128]{4,3,2,1,0:T(1,128)S(1)} %get-tuple-element.11), channel_id=1, source_target_pairs={{0,1},{1,0},{2,3},{3,2},{4,5},{5,4},{6,7},{7,6},{8,9},{9,8},{10,11... | collective-permute-start | bytes 276488 | tf_op jit(solution)/shard_map/ppermute | solution.py:19
  51.3 1.6 %slice-start = ((f32[64,8448]{1,0:T(8,128)}), f32[64,8256]{1,0:T(8,128)S(1)}, s32[]{:S(2)}) async-start(f32[64,8448]{1,0:T(8,128)} %shard_map.37), calls=%async_computation | async-start | bytes 4259840 | tf_op jit(solution)/shard_map/slice | solution.py:149
  67.6 2.9 %collective-permute-start.6 = (f32[2,2,2,2,1,129,128]{6,3,5,4,2,1,0:T(2,128)S(1)}, f32[2,2,2,2,1,129,128]{6,3,5,4,2,1,0:T(2,128)}, u32[]{:S(2)}, u32[]{:S(2)}) collective-permute-start(f32[2,2,2,2,1,129,128]{6,3,5,4,2,1,0:T(2,128)S(1)} %copy.17), channel_id=1, source_target_pairs={{0,1},{1,0},{2,3},{3,2},{4,5},{5,4},{6,7},{7,6},{8,9},{9,8},{10,11... | collective-permute-start | bytes 3170312 | tf_op jit(solution)/shard_map/ppermute | solution.py:48
  72.0 7.3 %collective-permute-start.15 = (f32[2,2,1,2,1,43,128]{6,5,4,3,2,1,0:T(8,128)S(1)}, f32[2,2,1,2,1,43,128]{6,5,4,3,2,1,0:T(8,128)S(1)}, u32[]{:S(2)}, u32[]{:S(2)}) collective-permute-start(f32[2,2,1,2,1,43,128]{6,5,4,3,2,1,0:T(8,128)S(1)} %constant_dynamic-slice_fusion.3), channel_id=1, source_target_pairs={{0,4},{2,6},{4,0},{6,2},{1,5},{3,7},{5,1},{7,3},{8,12},{10,14},{12... | collective-permute-start | bytes 528392 | tf_op jit(solution)/shard_map/ppermute | solution.py:48
  72.6 10.9 %collective-permute-start.11 = (f32[2,1,2,2,1,43,128]{6,5,4,3,2,1,0:T(8,128)S(1)}, f32[2,1,2,2,1,43,128]{6,5,4,3,2,1,0:T(8,128)S(1)}, u32[]{:S(2)}, u32[]{:S(2)}) collective-permute-start(f32[2,1,2,2,1,43,128]{6,5,4,3,2,1,0:T(8,128)S(1)} %constant_dynamic-slice_fusion.7), channel_id=1, source_target_pairs={{0,8},{8,0},{16,24},{24,16},{1,9},{9,1},{17,25},{25,17},{2,10},{10... | collective-permute-start | bytes 528392 | tf_op jit(solution)/shard_map/ppermute | solution.py:48
  72.8 12.3 %collective-permute-start.7 = (f32[1,2,2,2,1,43,128]{6,5,4,3,2,1,0:T(8,128)S(1)}, f32[1,2,2,2,1,43,128]{6,5,4,3,2,1,0:T(8,128)S(1)}, u32[]{:S(2)}, u32[]{:S(2)}) collective-permute-start(f32[1,2,2,2,1,43,128]{6,5,4,3,2,1,0:T(8,128)S(1)} %constant_dynamic-slice_fusion.11), channel_id=1, source_target_pairs={{0,16},{8,24},{16,0},{24,8},{1,17},{9,25},{17,1},{25,9},{2,18},{10... | collective-permute-start | bytes 528392 | tf_op jit(solution)/shard_map/ppermute | solution.py:48
  79.3 6.1 %collective-permute-start.16 = (f32[2,2,1,1,1,43,128]{6,5,4,3,2,1,0:T(8,128)S(1)}, f32[2,2,1,1,1,43,128]{6,5,4,3,2,1,0:T(8,128)S(1)}, u32[]{:S(2)}, u32[]{:S(2)}) collective-permute-start(f32[2,2,1,1,1,43,128]{6,5,4,3,2,1,0:T(8,128)S(1)} %constant_dynamic-slice_fusion.2), channel_id=1, source_target_pairs={{0,2},{2,0},{4,6},{6,4},{1,3},{3,1},{5,7},{7,5},{8,10},{10,8},{12,... | collective-permute-start | bytes 264200 | tf_op jit(solution)/shard_map/ppermute | solution.py:48
  83.5 4.7 %collective-permute-start.12 = (f32[2,1,1,2,1,43,128]{6,5,4,3,2,1,0:T(8,128)S(1)}, f32[2,1,1,2,1,43,128]{6,5,4,3,2,1,0:T(8,128)S(1)}, u32[]{:S(2)}, u32[]{:S(2)}) collective-permute-start(f32[2,1,1,2,1,43,128]{6,5,4,3,2,1,0:T(8,128)S(1)} %constant_dynamic-slice_fusion.6), channel_id=1, source_target_pairs={{0,4},{2,6},{4,0},{6,2},{1,5},{3,7},{5,1},{7,3},{8,12},{10,14},{12... | collective-permute-start | bytes 264200 | tf_op jit(solution)/shard_map/ppermute | solution.py:48
  85.2 4.7 %collective-permute-start.8 = (f32[1,1,2,2,1,43,128]{6,5,4,3,2,1,0:T(8,128)S(1)}, f32[1,1,2,2,1,43,128]{6,5,4,3,2,1,0:T(8,128)S(1)}, u32[]{:S(2)}, u32[]{:S(2)}) collective-permute-start(f32[1,1,2,2,1,43,128]{6,5,4,3,2,1,0:T(8,128)S(1)} %constant_dynamic-slice_fusion.10), channel_id=1, source_target_pairs={{0,8},{8,0},{16,24},{24,16},{1,9},{9,1},{17,25},{25,17},{2,10},{10... | collective-permute-start | bytes 264200 | tf_op jit(solution)/shard_map/ppermute | solution.py:48
  85.5 6.1 %collective-permute-start.17 = (f32[1,2,1,1,1,43,128]{6,5,4,3,2,1,0:T(8,128)S(1)}, f32[1,2,1,1,1,43,128]{6,5,4,3,2,1,0:T(8,128)S(1)}, u32[]{:S(2)}, u32[]{:S(2)}) collective-permute-start(f32[1,2,1,1,1,43,128]{6,5,4,3,2,1,0:T(8,128)S(1)} %constant_dynamic-slice_fusion.1), channel_id=1, source_target_pairs={{0,16},{8,24},{16,0},{24,8},{1,17},{9,25},{17,1},{25,9},{2,18},{10... | collective-permute-start | bytes 132104 | tf_op jit(solution)/shard_map/ppermute | solution.py:48
  88.3 4.2 %collective-permute-start.13 = (f32[2,1,1,1,1,43,128]{6,5,4,3,2,1,0:T(8,128)S(1)}, f32[2,1,1,1,1,43,128]{6,5,4,3,2,1,0:T(8,128)S(1)}, u32[]{:S(2)}, u32[]{:S(2)}) collective-permute-start(f32[2,1,1,1,1,43,128]{6,5,4,3,2,1,0:T(8,128)S(1)} %constant_dynamic-slice_fusion.5), channel_id=1, source_target_pairs={{0,2},{2,0},{4,6},{6,4},{1,3},{3,1},{5,7},{7,5},{8,10},{10,8},{12,... | collective-permute-start | bytes 132104 | tf_op jit(solution)/shard_map/ppermute | solution.py:48
  89.9 4.7 %collective-permute-start.9 = (f32[1,1,1,2,1,43,128]{6,5,4,3,2,1,0:T(8,128)S(1)}, f32[1,1,1,2,1,43,128]{6,5,4,3,2,1,0:T(8,128)S(1)}, u32[]{:S(2)}, u32[]{:S(2)}) collective-permute-start(f32[1,1,1,2,1,43,128]{6,5,4,3,2,1,0:T(8,128)S(1)} %constant_dynamic-slice_fusion.9), channel_id=1, source_target_pairs={{0,4},{2,6},{4,0},{6,2},{1,5},{3,7},{5,1},{7,3},{8,12},{10,14},{12... | collective-permute-start | bytes 132104 | tf_op jit(solution)/shard_map/ppermute | solution.py:48
  91.6 3.9 %collective-permute-start.18 = (f32[1,1,1,1,1,43,128]{6,5,4,3,2,1,0:T(8,128)S(1)}, f32[1,1,1,1,1,43,128]{6,5,4,3,2,1,0:T(8,128)S(1)}, u32[]{:S(2)}, u32[]{:S(2)}) collective-permute-start(f32[1,1,1,1,1,43,128]{6,5,4,3,2,1,0:T(8,128)S(1)} %constant_dynamic-slice_fusion), channel_id=1, source_target_pairs={{0,8},{8,0},{16,24},{24,16},{1,9},{9,1},{17,25},{25,17},{2,10},{10... | collective-permute-start | bytes 66056 | tf_op jit(solution)/shard_map/ppermute | solution.py:48
  92.5 4.8 %collective-permute-start.14 = (f32[1,1,1,1,1,43,128]{6,5,4,3,2,1,0:T(8,128)S(1)}, f32[1,1,1,1,1,43,128]{6,5,4,3,2,1,0:T(8,128)S(1)}, u32[]{:S(2)}, u32[]{:S(2)}) collective-permute-start(f32[1,1,1,1,1,43,128]{6,5,4,3,2,1,0:T(8,128)S(1)} %constant_dynamic-slice_fusion.4), channel_id=1, source_target_pairs={{0,16},{8,24},{16,0},{24,8},{1,17},{9,25},{17,1},{25,9},{2,18},{10... | collective-permute-start | bytes 66056 | tf_op jit(solution)/shard_map/ppermute | solution.py:48
  94.6 3.9 %collective-permute-start.10 = (f32[1,1,1,1,1,43,128]{6,5,4,3,2,1,0:T(8,128)S(1)}, f32[1,1,1,1,1,43,128]{6,5,4,3,2,1,0:T(8,128)S(1)}, u32[]{:S(2)}, u32[]{:S(2)}) collective-permute-start(f32[1,1,1,1,1,43,128]{6,5,4,3,2,1,0:T(8,128)S(1)} %constant_dynamic-slice_fusion.8), channel_id=1, source_target_pairs={{0,2},{2,0},{4,6},{6,4},{1,3},{3,1},{5,7},{7,5},{8,10},{10,8},{12,... | collective-permute-start | bytes 66056 | tf_op jit(solution)/shard_map/ppermute | solution.py:48

commit v5 on v4

--- a/solution.py
+++ b/solution.py
@@ -27,6 +27,25 @@
     step_y = (padded[:, 1:-1, 2:, 1:-1] - padded[:, 1:-1, :-2, 1:-1]) * 0.5
     step_z = (padded[:, 1:-1, 1:-1, 2:] - padded[:, 1:-1, 1:-1, :-2]) * 0.5
     return jnp.stack([step_x, step_y, step_z], axis=1)
+
+
+def face_gradients(value):
+    steps = []
+    for axis, dim in (("gx", 1), ("gy", 2), ("gz", 3)):
+        peers, length = lax.axis_size(axis), value.shape[dim]
+        up = [(i, (i + 1) % peers) for i in range(peers)]
+        down = [(j, i) for i, j in up]
+        before = lax.ppermute(lax.slice_in_dim(value, length - 1, length, axis=dim), axis, up)
+        after = lax.ppermute(lax.slice_in_dim(value, 0, 1, axis=dim), axis, down)
+        if axis == "gz":
+            level = lax.axis_index(axis)
+            before = jnp.where(level == 0, jnp.float32(0.0), before)
+            after = jnp.where(level == peers - 1, jnp.float32(0.0), after)
+        ext = jnp.concatenate([before, value, after], axis=dim)
+        high = lax.slice_in_dim(ext, 2, length + 2, axis=dim)
+        low = lax.slice_in_dim(ext, 0, length, axis=dim)
+        steps.append((high - low) * 0.5)
+    return jnp.stack(steps, axis=1)
 
 
 def halving_stages(axes):
@@ -128,13 +147,7 @@
     size_y = lax.axis_size("gy")
     size_z = lax.axis_size("gz")
     owners = size_x * size_y * size_z
-    padded = extended(modes, (("gx", 1), ("gy", 2), ("gz", 3)), 1)
-    depth = padded.shape[3]
-    layer = lax.broadcasted_iota(jnp.int32, (1, 1, 1, depth, 1), 3)
-    level = lax.axis_index("gz")
-    outside = (layer == 0) & (level == 0) | (layer == depth - 1) & (level == size_z - 1)
-    padded = jnp.where(outside, jnp.float32(0.0), padded)
-    grads = gradients(padded)
+    grads = face_gradients(modes)
     mode_flat = modes.reshape(3, -1, width)
     grad_flat = grads.reshape(3, 3, -1, width)
     weight_flat = cell_weight.reshape(-1)

time: 99.9 us -> 97.6 us (0.977)
  waiting for transfers between devices: 19.4 us -> 16.8 us
  local copies, waits for them, and re-layouts: 21.5 us -> 22.5 us
    ppermute x6, waiting for transfers between devices: 4.24 us -> 0.84 us  [the longest x3 0.84 us: face_gradients(): after = lax.ppermute(lax.slice_in_dim(value, 0, 1, axis=dim), axis, down)]
    slice x2 -> x3, local copies, waits for them, and re-layouts: 0.85 us -> 2.76 us  [face_gradients(): after = lax.ppermute(lax.slice_in_dim(value, 0, 1, axis=dim), axis, down)]
  transfers between devices with their start and end apart: 19 -> 19, of which waited for: 11 -> 10; matrix products, arithmetic and copies ran while one was open for 5% -> 6% of each run, Pallas kernels for 0% -> 0%
where the time goes in v5:
time: 97.6 us; the launch traced here: 97.1 us
  Pallas kernels  31.3 us (32%)
  local copies, waits for them, and re-layouts  22.5 us (23%)
  starting transfers between devices  21.9 us (22%)
  waiting for transfers between devices  16.8 us (17%)
  other arithmetic  4.3 us (4%)
    pallas_call x1, Pallas kernels, triangle(): pl.pallas_call(triangle_kernel, out_shape=jax.ShapeDtypeStruct((test, til...  31.3 us
    ppermute x13, waiting for transfers between devices, halve(): return keep + lax.ppermute(other, axis, pairs)  16 us
    ppermute x13, starting transfers between devices, halve(): return keep + lax.ppermute(other, axis, pairs)  13.3 us
    reshape x2, local copies, waits for them, and re-layouts, shards(): blocks = canon.reshape(TEST, owners, block_len).transpose(1, 0, 2)  7.88 us
    ppermute x3, starting transfers between devices, face_gradients(): lax.ppermute(lax.slice_in_dim(value, length - 1, length, axis=dim), axis,...  4.79 us
    ppermute x3, starting transfers between devices, face_gradients(): after = lax.ppermute(lax.slice_in_dim(value, 0, 1, axis=dim), axis, down)  3.86 us
    another operation x1, local copies, waits for them, and re-layouts, scatter_sum(): value = payload.reshape((2,) * len(stages) + (rows, lanes))  3.77 us
    slice x3, local copies, waits for them, and re-layouts, face_gradients(): after = lax.ppermute(lax.slice_in_dim(value, 0, 1, axis=dim), axis, down)  2.76 us
  transfers between devices with their start and end apart: 19, of which 10 were waited for; matrix products, arithmetic and copies ran while one was open for 6% of the time, Pallas kernels for 0%

profile of v5, /device:TPU:0, one launch (start us, length us, event | category | flops | bytes accessed | tf_op | source)
XLA Modules:
  0.0 97.1 jit_solution(2485223685617560973)
XLA Ops:
  0.0 0.0 copy-start
  0.0 0.9 fusion.8
  0.9 3.1 %collective-permute-start.1 = (f32[3,1,8,4,128]{4,3,2,1,0:T(4,128)S(1)}, f32[3,1,8,4,128]{4,3,2,1,0:T(4,128)S(1)}, u32[]{:S(2)}, u32[]{:S(2)}) collective-permute-start(f32[3,1,8,4,128]{4,3,2,1,0:T(4,128)S(1)} %get-tuple-element.12), channel_id=1, source_target_pairs={{0,8},{8,16},{16,24},{24,0},{1,9},{9,17},{17,25},{25,1},{2,10},{10... | collective-permute-start | bytes 147464 | tf_op jit(solution)/shard_map/ppermute | solution.py:38
  4.0 2.1 %collective-permute-start = (f32[3,1,8,4,128]{4,3,2,1,0:T(4,128)S(1)}, f32[3,1,8,4,128]{4,3,2,1,0:T(4,128)S(1)}, u32[]{:S(2)}, u32[]{:S(2)}) collective-permute-start(f32[3,1,8,4,128]{4,3,2,1,0:T(4,128)S(1)} %get-tuple-element.11), channel_id=1, source_target_pairs={{8,0},{16,8},{24,16},{0,24},{9,1},{17,9},{25,17},{1,25},{10,2},{18... | collective-permute-start | bytes 147464 | tf_op jit(solution)/shard_map/ppermute | solution.py:39
  6.0 0.8 fusion.9
  6.8 1.6 %collective-permute-start.3 = (f32[3,4,1,4,128]{4,3,2,1,0:T(4,128)S(1)}, f32[3,4,1,4,128]{4,3,2,1,0:T(4,128)S(1)}, u32[]{:S(2)}, u32[]{:S(2)}) collective-permute-start(f32[3,4,1,4,128]{4,3,2,1,0:T(4,128)S(1)} %get-tuple-element.14), channel_id=1, source_target_pairs={{0,2},{2,4},{4,6},{6,0},{1,3},{3,5},{5,7},{7,1},{8,10},{10,12},{12... | collective-permute-start | bytes 73736 | tf_op jit(solution)/shard_map/ppermute | solution.py:38
  8.5 1.3 %collective-permute-start.2 = (f32[3,4,1,4,128]{4,3,2,1,0:T(4,128)S(1)}, f32[3,4,1,4,128]{4,3,2,1,0:T(4,128)S(1)}, u32[]{:S(2)}, u32[]{:S(2)}) collective-permute-start(f32[3,4,1,4,128]{4,3,2,1,0:T(4,128)S(1)} %get-tuple-element.13), channel_id=1, source_target_pairs={{2,0},{4,2},{6,4},{0,6},{3,1},{5,3},{7,5},{1,7},{10,8},{12,10},{14... | collective-permute-start | bytes 73736 | tf_op jit(solution)/shard_map/ppermute | solution.py:39
  9.7 1.1 %fusion.10 = (f32[3,4,8,1,128]{4,3,2,1,0:T(1,128)S(1)}, f32[3,4,8,1,128]{4,3,2,1,0:T(1,128)S(1)}) fusion(f32[3,4,8,4,128]{4,3,2,1,0:T(4,128)} %param.3), kind=kLoop, calls=%fused_computation.51 | loop fusion | bytes 196608 | tf_op jit(solution)/shard_map/slice | solution.py:39
  10.9 0.1 collective-permute-start.5
  10.9 0.7 broadcast_multiply_fusion
  11.6 0.1 copy.13
  11.7 0.1 mul.32
  11.8 1.0 %fusion.6 = f32[3,64,128]{1,2,0:T(8,128)S(1)} fusion(f32[3,128,128]{2,1,0:T(8,128)} %bitcast.14, f32[128]{0:T(128)S(1)} %mul.32), kind=kLoop, calls=%fused_computation.17 | loop fusion | flops 24576 | bytes 197120 | tf_op jit(solution)/shard_map/transpose | solution.py:158
  12.9 0.7 pad_clamp_fusion
  13.5 0.1 copy.14
  13.6 0.1 tile.4
  13.7 0.9 tile.10.w_ref
  14.6 0.0 collective-permute-done.5
  14.6 0.5 collective-permute-start.4
  15.1 0.8 collective-permute-done.4
  16.0 0.0 collective-permute-done.3
  16.0 0.0 collective-permute-done.2
  16.0 0.0 collective-permute-done.1
  16.0 0.0 collective-permute-done
  16.1 0.0 copy-done
  16.1 0.3 fusion.5
  16.4 1.1 %copy.15.g_ref = f32[3,128,384]{2,1,0:T(8,128)} copy(f32[3,128,384]{1,2,0:T(8,128)S(1)} %bitcast.16) | data formatting | bytes 1179648 | tf_op jit(solution)/shard_map/reshape | solution.py:159
  17.4 31.3 %shard_map.37 = f32[64,8448]{1,0:T(8,128)} custom-call(f32[3,64,384]{2,1,0:T(8,128)} %tile.10.w_ref, f32[3,128,384]{2,1,0:T(8,128)} %copy.15.g_ref, f32[384,128]{1,0:T(8,128)} %bitcast.15), custom_call_target="tpu_custom_call" | custom-call | tf_op jit(solution)/shard_map/pallas_call | solution.py:135
  48.7 1.6 %slice-done = f32[64,8256]{1,0:T(8,128)S(1)} async-done(((f32[64,8448]{1,0:T(8,128)}), f32[64,8256]{1,0:T(8,128)S(1)}, s32[]{:S(2)}) %slice-start) | async-done | bytes 2113560 | tf_op jit(solution)/shard_map/slice | solution.py:162
  50.3 4.2 %reshape.32 = f32[64,32,258]{2,1,0:T(8,128)} reshape(f32[64,8256]{1,0:T(8,128)S(1)} %slice-done) | data formatting | bytes 4227072 | tf_op jit(solution)/shard_map/reshape | solution.py:163
  54.5 3.7 %copy.21 = f32[64,32,258]{2,0,1:T(8,128)S(1)} copy(f32[64,32,258]{2,1,0:T(8,128)} %reshape.32) | data formatting | bytes 4227072 | tf_op jit(solution)/shard_map/reshape | solution.py:163
  58.2 2.4 %gather_fusion = f32[32,64,258]{2,1,0:T(8,128)} fusion(f32[32,64,258]{2,1,0:T(8,128)S(1)} %bitcast.13, s32[1024]{0:T(1024)S(1)} %pad_clamp_fusion), kind=kCustom, calls=%fused_computation | custom fusion | bytes 4227200 | tf_op jit(solution)/shard_map/jit(_take)/gather | solution.py:164
  60.6 3.8 %reshape_reshape.7 = f32[2,2,2,2,2,129,128]{6,5,4,3,2,1,0:T(8,128)S(1)} reshape(f32[32,64,258]{2,1,0:T(8,128)} %gather_fusion) | data formatting | bytes 4227072 | tf_op jit(solution)/shard_map/reshape;reshape | solution.py:76
  64.4 0.1 constant_dynamic-slice_fusion.12
  64.5 0.5 copy.17
  65.0 0.4 collective-permute-start.6
  65.4 2.5 %collective-permute-done.6 = f32[2,2,2,2,1,129,128]{6,3,5,4,2,1,0:T(2,128)} collective-permute-done((f32[2,2,2,2,1,129,128]{6,3,5,4,2,1,0:T(2,128)S(1)}, f32[2,2,2,2,1,129,128]{6,3,5,4,2,1,0:T(2,128)}, u32[]{:S(2)}, u32[]{:S(2)}) %collective-permute-start.6) | collective-permute-done | bytes 1056800 | tf_op jit(solution)/shard_map/ppermute | solution.py:67
  67.9 1.3 %copy_add_fusion = f32[2,2,2,2,1,129,128]{6,5,4,3,2,1,0:T(8,128)S(1)} fusion(f32[2,2,2,2,1,129,128]{6,3,5,4,2,1,0:T(2,128)} %collective-permute-done.6, f32[2,2,2,2,2,129,128]{6,5,4,3,2,1,0:T(8,128)S(1)} %reshape_reshape.7, s32[]{:T(128)S(6)} %select_n.135), kind=kLoop, calls=%fused_computation.2 | loop fusion | flops 264192 | bytes 3170308 | tf_op jit(solution)/shard_map/add | solution.py:67
  69.2 0.1 fusion.7
  69.4 1.8 %collective-permute-start.15 = (f32[2,2,1,2,1,43,128]{6,5,4,3,2,1,0:T(8,128)S(1)}, f32[2,2,1,2,1,43,128]{6,5,4,3,2,1,0:T(8,128)S(1)}, u32[]{:S(2)}, u32[]{:S(2)}) collective-permute-start(f32[2,2,1,2,1,43,128]{6,5,4,3,2,1,0:T(8,128)S(1)} %constant_dynamic-slice_fusion.3), channel_id=1, source_target_pairs={{0,4},{2,6},{4,0},{6,2},{1,5},{3,7},{5,1},{7,3},{8,12},{10,14},{12... | collective-permute-start | bytes 528392 | tf_op jit(solution)/shard_map/ppermute | solution.py:67
  71.2 0.1 collective-permute-start.11
  71.3 2.4 %collective-permute-start.7 = (f32[1,2,2,2,1,43,128]{6,5,4,3,2,1,0:T(8,128)S(1)}, f32[1,2,2,2,1,43,128]{6,5,4,3,2,1,0:T(8,128)S(1)}, u32[]{:S(2)}, u32[]{:S(2)}) collective-permute-start(f32[1,2,2,2,1,43,128]{6,5,4,3,2,1,0:T(8,128)S(1)} %constant_dynamic-slice_fusion.11), channel_id=1, source_target_pairs={{0,16},{8,24},{16,0},{24,8},{1,17},{9,25},{17,1},{25,9},{2,18},{10... | collective-permute-start | bytes 528392 | tf_op jit(solution)/shard_map/ppermute | solution.py:67
  73.7 3.0 %collective-permute-done.15 = f32[2,2,1,2,1,43,128]{6,5,4,3,2,1,0:T(8,128)S(1)} collective-permute-done((f32[2,2,1,2,1,43,128]{6,5,4,3,2,1,0:T(8,128)S(1)}, f32[2,2,1,2,1,43,128]{6,5,4,3,2,1,0:T(8,128)S(1)}, u32[]{:S(2)}, u32[]{:S(2)}) %collective-permute-start.15) | collective-permute-done | bytes 176160 | tf_op jit(solution)/shard_map/ppermute | solution.py:67
  76.7 0.8 collective-permute-start.16
  77.5 4.1 %collective-permute-done.11 = f32[2,1,2,2,1,43,128]{6,5,4,3,2,1,0:T(8,128)S(1)} collective-permute-done((f32[2,1,2,2,1,43,128]{6,5,4,3,2,1,0:T(8,128)S(1)}, f32[2,1,2,2,1,43,128]{6,5,4,3,2,1,0:T(8,128)S(1)}, u32[]{:S(2)}, u32[]{:S(2)}) %collective-permute-start.11) | collective-permute-done | bytes 176160 | tf_op jit(solution)/shard_map/ppermute | solution.py:67
  81.7 0.6 collective-permute-start.12
  82.2 1.2 %collective-permute-done.7 = f32[1,2,2,2,1,43,128]{6,5,4,3,2,1,0:T(8,128)S(1)} collective-permute-done((f32[1,2,2,2,1,43,128]{6,5,4,3,2,1,0:T(8,128)S(1)}, f32[1,2,2,2,1,43,128]{6,5,4,3,2,1,0:T(8,128)S(1)}, u32[]{:S(2)}, u32[]{:S(2)}) %collective-permute-start.7) | collective-permute-done | bytes 176160 | tf_op jit(solution)/shard_map/ppermute | solution.py:67
  83.4 0.1 collective-permute-start.8
  83.5 0.0 collective-permute-done.16
  83.6 2.5 %collective-permute-start.17 = (f32[1,2,1,1,1,43,128]{6,5,4,3,2,1,0:T(8,128)S(1)}, f32[1,2,1,1,1,43,128]{6,5,4,3,2,1,0:T(8,128)S(1)}, u32[]{:S(2)}, u32[]{:S(2)}) collective-permute-start(f32[1,2,1,1,1,43,128]{6,5,4,3,2,1,0:T(8,128)S(1)} %constant_dynamic-slice_fusion.1), channel_id=1, source_target_pairs={{0,16},{8,24},{16,0},{24,8},{1,17},{9,25},{17,1},{25,9},{2,18},{10... | collective-permute-start | bytes 132104 | tf_op jit(solution)/shard_map/ppermute | solution.py:67
  86.1 0.2 collective-permute-done.12
  86.4 0.7 collective-permute-start.13
  87.0 1.1 %collective-permute-done.8 = f32[1,1,2,2,1,43,128]{6,5,4,3,2,1,0:T(8,128)S(1)} collective-permute-done((f32[1,1,2,2,1,43,128]{6,5,4,3,2,1,0:T(8,128)S(1)}, f32[1,1,2,2,1,43,128]{6,5,4,3,2,1,0:T(8,128)S(1)}, u32[]{:S(2)}, u32[]{:S(2)}) %collective-permute-start.8) | collective-permute-done | bytes 88096 | tf_op jit(solution)/shard_map/ppermute | solution.py:67
  88.2 0.4 collective-permute-start.9
  88.6 0.0 collective-permute-done.17
  88.7 2.3 %collective-permute-start.18 = (f32[1,1,1,1,1,43,128]{6,5,4,3,2,1,0:T(8,128)S(1)}, f32[1,1,1,1,1,43,128]{6,5,4,3,2,1,0:T(8,128)S(1)}, u32[]{:S(2)}, u32[]{:S(2)}) collective-permute-start(f32[1,1,1,1,1,43,128]{6,5,4,3,2,1,0:T(8,128)S(1)} %constant_dynamic-slice_fusion), channel_id=1, source_target_pairs={{0,8},{8,0},{16,24},{24,16},{1,9},{9,1},{17,25},{25,17},{2,10},{10... | collective-permute-start | bytes 66056 | tf_op jit(solution)/shard_map/ppermute | solution.py:67
  91.0 0.0 collective-permute-done.13
  91.0 0.5 collective-permute-start.14
  91.6 0.8 collective-permute-done.9
  92.4 0.7 collective-permute-start.10
  93.0 0.0 collective-permute-done.18
  93.0 2.8 %collective-permute-done.14 = f32[1,1,1,1,1,43,128]{6,5,4,3,2,1,0:T(8,128)S(1)} collective-permute-done((f32[1,1,1,1,1,43,128]{6,5,4,3,2,1,0:T(8,128)S(1)}, f32[1,1,1,1,1,43,128]{6,5,4,3,2,1,0:T(8,128)S(1)}, u32[]{:S(2)}, u32[]{:S(2)}) %collective-permute-start.14) | collective-permute-done | bytes 22048 | tf_op jit(solution)/shard_map/ppermute | solution.py:67
  95.8 0.4 collective-permute-done.10
  96.3 0.8 reshape_reshape_reshape.3
  (29 shorter events, 0.5 us)
Async XLA Ops:
  0.0 16.1 %copy-start = (f32[3,4,8,4,128]{4,3,2,1,0:T(4,128)S(1)}, f32[3,4,8,4,128]{4,3,2,1,0:T(4,128)}, u32[]{:S(2)}) copy-start(f32[3,4,8,4,128]{4,3,2,1,0:T(4,128)} %param.3) | copy-start | bytes 589828
  0.9 15.2 %collective-permute-start.1 = (f32[3,1,8,4,128]{4,3,2,1,0:T(4,128)S(1)}, f32[3,1,8,4,128]{4,3,2,1,0:T(4,128)S(1)}, u32[]{:S(2)}, u32[]{:S(2)}) collective-permute-start(f32[3,1,8,4,128]{4,3,2,1,0:T(4,128)S(1)} %get-tuple-element.12), channel_id=1, source_target_pairs={{0,8},{8,16},{16,24},{24,0},{1,9},{9,17},{17,25},{25,1},{2,10},{10... | collective-permute-start | bytes 147464 | tf_op jit(solution)/shard_map/ppermute | solution.py:38
  4.0 12.1 %collective-permute-start = (f32[3,1,8,4,128]{4,3,2,1,0:T(4,128)S(1)}, f32[3,1,8,4,128]{4,3,2,1,0:T(4,128)S(1)}, u32[]{:S(2)}, u32[]{:S(2)}) collective-permute-start(f32[3,1,8,4,128]{4,3,2,1,0:T(4,128)S(1)} %get-tuple-element.11), channel_id=1, source_target_pairs={{8,0},{16,8},{24,16},{0,24},{9,1},{17,9},{25,17},{1,25},{10,2},{18... | collective-permute-start | bytes 147464 | tf_op jit(solution)/shard_map/ppermute | solution.py:39
  6.8 9.2 %collective-permute-start.3 = (f32[3,4,1,4,128]{4,3,2,1,0:T(4,128)S(1)}, f32[3,4,1,4,128]{4,3,2,1,0:T(4,128)S(1)}, u32[]{:S(2)}, u32[]{:S(2)}) collective-permute-start(f32[3,4,1,4,128]{4,3,2,1,0:T(4,128)S(1)} %get-tuple-element.14), channel_id=1, source_target_pairs={{0,2},{2,4},{4,6},{6,0},{1,3},{3,5},{5,7},{7,1},{8,10},{10,12},{12... | collective-permute-start | bytes 73736 | tf_op jit(solution)/shard_map/ppermute | solution.py:38
  8.5 7.6 %collective-permute-start.2 = (f32[3,4,1,4,128]{4,3,2,1,0:T(4,128)S(1)}, f32[3,4,1,4,128]{4,3,2,1,0:T(4,128)S(1)}, u32[]{:S(2)}, u32[]{:S(2)}) collective-permute-start(f32[3,4,1,4,128]{4,3,2,1,0:T(4,128)S(1)} %get-tuple-element.13), channel_id=1, source_target_pairs={{2,0},{4,2},{6,4},{0,6},{3,1},{5,3},{7,5},{1,7},{10,8},{12,10},{14... | collective-permute-start | bytes 73736 | tf_op jit(solution)/shard_map/ppermute | solution.py:39
  10.9 3.7 %collective-permute-start.5 = (f32[3,4,8,1,128]{4,3,2,1,0:T(1,128)S(1)}, f32[3,4,8,1,128]{4,3,2,1,0:T(1,128)S(1)}, u32[]{:S(2)}, u32[]{:S(2)}) collective-permute-start(f32[3,4,8,1,128]{4,3,2,1,0:T(1,128)S(1)} %get-tuple-element.16), channel_id=1, source_target_pairs={{0,1},{1,0},{2,3},{3,2},{4,5},{5,4},{6,7},{7,6},{8,9},{9,8},{10,11... | collective-permute-start | bytes 147464 | tf_op jit(solution)/shard_map/ppermute | solution.py:38
  14.6 1.4 %collective-permute-start.4 = (f32[3,4,8,1,128]{4,3,2,1,0:T(1,128)S(1)}, f32[3,4,8,1,128]{4,3,2,1,0:T(1,128)S(1)}, u32[]{:S(2)}, u32[]{:S(2)}) collective-permute-start(f32[3,4,8,1,128]{4,3,2,1,0:T(1,128)S(1)} %get-tuple-element.15), channel_id=1, source_target_pairs={{1,0},{0,1},{3,2},{2,3},{5,4},{4,5},{7,6},{6,7},{9,8},{8,9},{11,10... | collective-permute-start | bytes 147464 | tf_op jit(solution)/shard_map/ppermute | solution.py:39
  48.7 1.6 %slice-start = ((f32[64,8448]{1,0:T(8,128)}), f32[64,8256]{1,0:T(8,128)S(1)}, s32[]{:S(2)}) async-start(f32[64,8448]{1,0:T(8,128)} %shard_map.37), calls=%async_computation | async-start | bytes 4259840 | tf_op jit(solution)/shard_map/slice | solution.py:162
  65.0 2.9 %collective-permute-start.6 = (f32[2,2,2,2,1,129,128]{6,3,5,4,2,1,0:T(2,128)S(1)}, f32[2,2,2,2,1,129,128]{6,3,5,4,2,1,0:T(2,128)}, u32[]{:S(2)}, u32[]{:S(2)}) collective-permute-start(f32[2,2,2,2,1,129,128]{6,3,5,4,2,1,0:T(2,128)S(1)} %copy.17), channel_id=1, source_target_pairs={{0,1},{1,0},{2,3},{3,2},{4,5},{5,4},{6,7},{7,6},{8,9},{9,8},{10,11... | collective-permute-start | bytes 3170312 | tf_op jit(solution)/shard_map/ppermute | solution.py:67
  69.4 7.3 %collective-permute-start.15 = (f32[2,2,1,2,1,43,128]{6,5,4,3,2,1,0:T(8,128)S(1)}, f32[2,2,1,2,1,43,128]{6,5,4,3,2,1,0:T(8,128)S(1)}, u32[]{:S(2)}, u32[]{:S(2)}) collective-permute-start(f32[2,2,1,2,1,43,128]{6,5,4,3,2,1,0:T(8,128)S(1)} %constant_dynamic-slice_fusion.3), channel_id=1, source_target_pairs={{0,4},{2,6},{4,0},{6,2},{1,5},{3,7},{5,1},{7,3},{8,12},{10,14},{12... | collective-permute-start | bytes 528392 | tf_op jit(solution)/shard_map/ppermute | solution.py:67
  71.2 10.4 %collective-permute-start.11 = (f32[2,1,2,2,1,43,128]{6,5,4,3,2,1,0:T(8,128)S(1)}, f32[2,1,2,2,1,43,128]{6,5,4,3,2,1,0:T(8,128)S(1)}, u32[]{:S(2)}, u32[]{:S(2)}) collective-permute-start(f32[2,1,2,2,1,43,128]{6,5,4,3,2,1,0:T(8,128)S(1)} %constant_dynamic-slice_fusion.7), channel_id=1, source_target_pairs={{0,8},{8,0},{16,24},{24,16},{1,9},{9,1},{17,25},{25,17},{2,10},{10... | collective-permute-start | bytes 528392 | tf_op jit(solution)/shard_map/ppermute | solution.py:67
  71.3 12.1 %collective-permute-start.7 = (f32[1,2,2,2,1,43,128]{6,5,4,3,2,1,0:T(8,128)S(1)}, f32[1,2,2,2,1,43,128]{6,5,4,3,2,1,0:T(8,128)S(1)}, u32[]{:S(2)}, u32[]{:S(2)}) collective-permute-start(f32[1,2,2,2,1,43,128]{6,5,4,3,2,1,0:T(8,128)S(1)} %constant_dynamic-slice_fusion.11), channel_id=1, source_target_pairs={{0,16},{8,24},{16,0},{24,8},{1,17},{9,25},{17,1},{25,9},{2,18},{10... | collective-permute-start | bytes 528392 | tf_op jit(solution)/shard_map/ppermute | solution.py:67
  76.7 6.8 %collective-permute-start.16 = (f32[2,2,1,1,1,43,128]{6,5,4,3,2,1,0:T(8,128)S(1)}, f32[2,2,1,1,1,43,128]{6,5,4,3,2,1,0:T(8,128)S(1)}, u32[]{:S(2)}, u32[]{:S(2)}) collective-permute-start(f32[2,2,1,1,1,43,128]{6,5,4,3,2,1,0:T(8,128)S(1)} %constant_dynamic-slice_fusion.2), channel_id=1, source_target_pairs={{0,2},{2,0},{4,6},{6,4},{1,3},{3,1},{5,7},{7,5},{8,10},{10,8},{12,... | collective-permute-start | bytes 264200 | tf_op jit(solution)/shard_map/ppermute | solution.py:67
  81.7 4.7 %collective-permute-start.12 = (f32[2,1,1,2,1,43,128]{6,5,4,3,2,1,0:T(8,128)S(1)}, f32[2,1,1,2,1,43,128]{6,5,4,3,2,1,0:T(8,128)S(1)}, u32[]{:S(2)}, u32[]{:S(2)}) collective-permute-start(f32[2,1,1,2,1,43,128]{6,5,4,3,2,1,0:T(8,128)S(1)} %constant_dynamic-slice_fusion.6), channel_id=1, source_target_pairs={{0,4},{2,6},{4,0},{6,2},{1,5},{3,7},{5,1},{7,3},{8,12},{10,14},{12... | collective-permute-start | bytes 264200 | tf_op jit(solution)/shard_map/ppermute | solution.py:67
  83.4 4.7 %collective-permute-start.8 = (f32[1,1,2,2,1,43,128]{6,5,4,3,2,1,0:T(8,128)S(1)}, f32[1,1,2,2,1,43,128]{6,5,4,3,2,1,0:T(8,128)S(1)}, u32[]{:S(2)}, u32[]{:S(2)}) collective-permute-start(f32[1,1,2,2,1,43,128]{6,5,4,3,2,1,0:T(8,128)S(1)} %constant_dynamic-slice_fusion.10), channel_id=1, source_target_pairs={{0,8},{8,0},{16,24},{24,16},{1,9},{9,1},{17,25},{25,17},{2,10},{10... | collective-permute-start | bytes 264200 | tf_op jit(solution)/shard_map/ppermute | solution.py:67
  83.6 5.1 %collective-permute-start.17 = (f32[1,2,1,1,1,43,128]{6,5,4,3,2,1,0:T(8,128)S(1)}, f32[1,2,1,1,1,43,128]{6,5,4,3,2,1,0:T(8,128)S(1)}, u32[]{:S(2)}, u32[]{:S(2)}) collective-permute-start(f32[1,2,1,1,1,43,128]{6,5,4,3,2,1,0:T(8,128)S(1)} %constant_dynamic-slice_fusion.1), channel_id=1, source_target_pairs={{0,16},{8,24},{16,0},{24,8},{1,17},{9,25},{17,1},{25,9},{2,18},{10... | collective-permute-start | bytes 132104 | tf_op jit(solution)/shard_map/ppermute | solution.py:67
  86.4 4.6 %collective-permute-start.13 = (f32[2,1,1,1,1,43,128]{6,5,4,3,2,1,0:T(8,128)S(1)}, f32[2,1,1,1,1,43,128]{6,5,4,3,2,1,0:T(8,128)S(1)}, u32[]{:S(2)}, u32[]{:S(2)}) collective-permute-start(f32[2,1,1,1,1,43,128]{6,5,4,3,2,1,0:T(8,128)S(1)} %constant_dynamic-slice_fusion.5), channel_id=1, source_target_pairs={{0,2},{2,0},{4,6},{6,4},{1,3},{3,1},{5,7},{7,5},{8,10},{10,8},{12,... | collective-permute-start | bytes 132104 | tf_op jit(solution)/shard_map/ppermute | solution.py:67
  88.2 4.2 %collective-permute-start.9 = (f32[1,1,1,2,1,43,128]{6,5,4,3,2,1,0:T(8,128)S(1)}, f32[1,1,1,2,1,43,128]{6,5,4,3,2,1,0:T(8,128)S(1)}, u32[]{:S(2)}, u32[]{:S(2)}) collective-permute-start(f32[1,1,1,2,1,43,128]{6,5,4,3,2,1,0:T(8,128)S(1)} %constant_dynamic-slice_fusion.9), channel_id=1, source_target_pairs={{0,4},{2,6},{4,0},{6,2},{1,5},{3,7},{5,1},{7,3},{8,12},{10,14},{12... | collective-permute-start | bytes 132104 | tf_op jit(solution)/shard_map/ppermute | solution.py:67
  88.7 4.3 %collective-permute-start.18 = (f32[1,1,1,1,1,43,128]{6,5,4,3,2,1,0:T(8,128)S(1)}, f32[1,1,1,1,1,43,128]{6,5,4,3,2,1,0:T(8,128)S(1)}, u32[]{:S(2)}, u32[]{:S(2)}) collective-permute-start(f32[1,1,1,1,1,43,128]{6,5,4,3,2,1,0:T(8,128)S(1)} %constant_dynamic-slice_fusion), channel_id=1, source_target_pairs={{0,8},{8,0},{16,24},{24,16},{1,9},{9,1},{17,25},{25,17},{2,10},{10... | collective-permute-start | bytes 66056 | tf_op jit(solution)/shard_map/ppermute | solution.py:67
  91.0 4.8 %collective-permute-start.14 = (f32[1,1,1,1,1,43,128]{6,5,4,3,2,1,0:T(8,128)S(1)}, f32[1,1,1,1,1,43,128]{6,5,4,3,2,1,0:T(8,128)S(1)}, u32[]{:S(2)}, u32[]{:S(2)}) collective-permute-start(f32[1,1,1,1,1,43,128]{6,5,4,3,2,1,0:T(8,128)S(1)} %constant_dynamic-slice_fusion.4), channel_id=1, source_target_pairs={{0,16},{8,24},{16,0},{24,8},{1,17},{9,25},{17,1},{25,9},{2,18},{10... | collective-permute-start | bytes 66056 | tf_op jit(solution)/shard_map/ppermute | solution.py:67
  92.4 3.9 %collective-permute-start.10 = (f32[1,1,1,1,1,43,128]{6,5,4,3,2,1,0:T(8,128)S(1)}, f32[1,1,1,1,1,43,128]{6,5,4,3,2,1,0:T(8,128)S(1)}, u32[]{:S(2)}, u32[]{:S(2)}) collective-permute-start(f32[1,1,1,1,1,43,128]{6,5,4,3,2,1,0:T(8,128)S(1)} %constant_dynamic-slice_fusion.8), channel_id=1, source_target_pairs={{0,2},{2,0},{4,6},{6,4},{1,3},{3,1},{5,7},{7,5},{8,10},{10,8},{12,... | collective-permute-start | bytes 66056 | tf_op jit(solution)/shard_map/ppermute | solution.py:67

commit v6 on v5

--- a/solution.py
+++ b/solution.py
@@ -1,3 +1,5 @@
+import functools
+
 import jax
 import jax.numpy as jnp
 import numpy as np
@@ -90,7 +92,7 @@
     return value.reshape(1, rows, lanes)
 
 
-def triangle_kernel(w_ref, g_ref, m_ref, out_ref, sym_ref):
+def triangle_kernel(block_len, slot_ref, w_ref, g_ref, m_ref, out_ref, sym_ref):
     test, width = w_ref.shape[1], m_ref.shape[1]
     group = 4
     out_ref[...] = jnp.zeros(out_ref.shape, out_ref.dtype)
@@ -117,28 +119,41 @@
     def place(j, carry):
         slab = sym_ref[pl.ds(j, test, stride=width), :]
         offset = j * width - (j * (j - 1)) // 2
-        end = offset % 128 + width - j
-        rolled = pltpu.roll(slab, (offset - j) % 128, 1)
-        first = pl.multiple_of((offset // 128) * 128, 128)
-        second = pl.multiple_of(first + 128, 128)
-        low = lane >= offset % 128
-        out_ref[:, pl.ds(first, 128)] = jnp.where(low & (lane < end), rolled, out_ref[:, pl.ds(first, 128)])
-        out_ref[:, pl.ds(second, 128)] = jnp.where(lane < end - 128, rolled, out_ref[:, pl.ds(second, 128)])
-        return carry
+        stop = offset + width - j
+
+        def per_block(c, carry):
+            base_c = c * block_len
+            lo = jnp.maximum(offset, base_c) - base_c
+            hi = jnp.minimum(stop, base_c + block_len) - base_c
+            slot = slot_ref[c]
+
+            def per_tile(u, carry):
+                base = base_c + u * 128
+                rolled = pltpu.roll(slab, (offset - j - base) % 128, 1)
+                keep = (lane >= lo - u * 128) & (lane < hi - u * 128)
+                at = pl.multiple_of(u * 128, 128)
+                cur = out_ref[slot, :, pl.ds(at, 128)]
+                out_ref[slot, :, pl.ds(at, 128)] = jnp.where(keep, rolled, cur)
+                return carry
+
+            return lax.fori_loop(lo // 128, (hi - 1) // 128 + 1, per_tile, carry)
+
+        return lax.fori_loop(offset // block_len, (stop - 1) // block_len + 1, per_block, carry)
 
     lax.fori_loop(0, width, place, 0)
 
 
-def triangle(weighted, grads, modes_flat, pair_total, slots):
+def triangle(slots, weighted, grads, modes_flat, block_len):
+    owners = slots.shape[0]
     test, width = weighted.shape[1], modes_flat.shape[1]
-    tiles = max(pair_total // 128 + 2, -(-slots // 128))
+    tiles = -(-block_len // 128)
     return pl.pallas_call(
-        triangle_kernel,
-        out_shape=jax.ShapeDtypeStruct((test, tiles * 128), jnp.float32),
-        in_specs=[pl.BlockSpec(memory_space=pltpu.VMEM)] * 3,
+        functools.partial(triangle_kernel, block_len),
+        out_shape=jax.ShapeDtypeStruct((owners, test, tiles * 128), jnp.float32),
+        in_specs=[pl.BlockSpec(memory_space=pltpu.SMEM)] + [pl.BlockSpec(memory_space=pltpu.VMEM)] * 3,
         out_specs=pl.BlockSpec(memory_space=pltpu.VMEM),
         scratch_shapes=[pltpu.VMEM((test * width, width), jnp.float32)],
-    )(weighted, grads, modes_flat)
+    )(slots, weighted, grads, modes_flat)
 
 
 def shards(modes, cell_weight, pair_owner):
@@ -159,9 +174,11 @@
     grads_t = grad_flat.transpose(0, 3, 1, 2).reshape(3, width, 3 * cells)
     pair_total = width * (width + 1) // 2
     block_len = (pair_total + owners - 1) // owners
-    canon = triangle(weighted, grads_t, mode_flat.reshape(3 * cells, width), pair_total, owners * block_len)[:, : owners * block_len]
-    blocks = canon.reshape(TEST, owners, block_len).transpose(1, 0, 2)
-    partial_terms = jnp.take(blocks, pair_owner, axis=0, mode="clip").reshape(owners, TEST * block_len)
+    ranks = jnp.arange(owners, dtype=jnp.int32)
+    slots = jnp.sum(jnp.where(pair_owner[None, :] == ranks[:, None], ranks[None, :], 0), axis=1)
+    slots = jnp.clip(slots, 0, owners - 1).astype(jnp.int32)
+    placed = triangle(slots, weighted, grads_t, mode_flat.reshape(3 * cells, width), block_len)
+    partial_terms = placed[:, :, :block_len].reshape(owners, TEST * block_len)
     lanes = 128
     rows = -(-TEST * block_len // lanes)
     partial_terms = jnp.pad(partial_terms, ((0, 0), (0, rows * lanes - TEST * block_len)))

time: 97.6 us -> 96.8 us (level)
  local copies, waits for them, and re-layouts: 22.5 us -> 10.6 us
  Pallas kernels: 31.3 us -> 41.8 us
    pallas_call x1, Pallas kernels: 31.3 us -> 41.8 us  [triangle(): pl.pallas_call(functools.partial(triangle_kernel, block_len), out_shape=j...]
    reshape x2 -> x0, local copies, waits for them, and re-layouts: 7.88 us -> none  [shards(): blocks = canon.reshape(TEST, owners, block_len).transpose(1, 0, 2)]
    gather x1 -> x0, local copies, waits for them, and re-layouts: 2.37 us -> none  [shards(): jnp.take(blocks, pair_owner, axis=0, mode='clip')]
    slice x2 -> x0, local copies, waits for them, and re-layouts: 1.6 us -> none  [shards(): triangle(weighted, grads_t, mode_flat.reshape(3 * cells, width), pair_tot...]
  transfers between devices with their start and end apart: 19 -> 19, of which waited for: 10 -> 10; matrix products, arithmetic and copies ran while one was open for 6% -> 7% of each run, Pallas kernels for 0% -> 0%
where the time goes in v6:
time: 96.8 us; the launch traced here: 96.3 us
  Pallas kernels  41.8 us (43%)
  starting transfers between devices  21.9 us (23%)
  waiting for transfers between devices  16.8 us (17%)
  local copies, waits for them, and re-layouts  10.6 us (11%)
  other arithmetic  4.95 us (5%)
    pallas_call x1, Pallas kernels, triangle(): pl.pallas_call(functools.partial(triangle_kernel, block_len), out_shape=j...  41.8 us
    ppermute x13, waiting for transfers between devices, halve(): return keep + lax.ppermute(other, axis, pairs)  16 us
    ppermute x13, starting transfers between devices, halve(): return keep + lax.ppermute(other, axis, pairs)  13.3 us
    ppermute x3, starting transfers between devices, face_gradients(): lax.ppermute(lax.slice_in_dim(value, length - 1, length, axis=dim), axis,...  4.78 us
    ppermute x3, starting transfers between devices, face_gradients(): after = lax.ppermute(lax.slice_in_dim(value, 0, 1, axis=dim), axis, down)  3.83 us
    another operation x1, local copies, waits for them, and re-layouts, scatter_sum(): value = payload.reshape((2,) * len(stages) + (rows, lanes))  3.77 us
    slice x3, local copies, waits for them, and re-layouts, face_gradients(): after = lax.ppermute(lax.slice_in_dim(value, 0, 1, axis=dim), axis, down)  2.71 us
  transfers between devices with their start and end apart: 19, of which 10 were waited for; matrix products, arithmetic and copies ran while one was open for 7% of the time, Pallas kernels for 0%

profile of v6, /device:TPU:0, one launch (start us, length us, event | category | flops | bytes accessed | tf_op | source)
XLA Modules:
  0.0 96.3 jit_solution(12870264330673811872)
XLA Ops:
  0.0 0.8 fusion.8
  0.8 3.1 %collective-permute-start.1 = (f32[3,1,8,4,128]{4,3,2,1,0:T(4,128)S(1)}, f32[3,1,8,4,128]{4,3,2,1,0:T(4,128)S(1)}, u32[]{:S(2)}, u32[]{:S(2)}) collective-permute-start(f32[3,1,8,4,128]{4,3,2,1,0:T(4,128)S(1)} %get-tuple-element.12), channel_id=1, source_target_pairs={{0,8},{8,16},{16,24},{24,0},{1,9},{9,17},{17,25},{25,1},{2,10},{10... | collective-permute-start | bytes 147464 | tf_op jit(solution)/shard_map/ppermute | solution.py:40
  3.9 2.1 %collective-permute-start = (f32[3,1,8,4,128]{4,3,2,1,0:T(4,128)S(1)}, f32[3,1,8,4,128]{4,3,2,1,0:T(4,128)S(1)}, u32[]{:S(2)}, u32[]{:S(2)}) collective-permute-start(f32[3,1,8,4,128]{4,3,2,1,0:T(4,128)S(1)} %get-tuple-element.11), channel_id=1, source_target_pairs={{8,0},{16,8},{24,16},{0,24},{9,1},{17,9},{25,17},{1,25},{10,2},{18... | collective-permute-start | bytes 147464 | tf_op jit(solution)/shard_map/ppermute | solution.py:41
  6.0 0.8 fusion.9
  6.7 1.6 %collective-permute-start.3 = (f32[3,4,1,4,128]{4,3,2,1,0:T(4,128)S(1)}, f32[3,4,1,4,128]{4,3,2,1,0:T(4,128)S(1)}, u32[]{:S(2)}, u32[]{:S(2)}) collective-permute-start(f32[3,4,1,4,128]{4,3,2,1,0:T(4,128)S(1)} %get-tuple-element.14), channel_id=1, source_target_pairs={{0,2},{2,4},{4,6},{6,0},{1,3},{3,5},{5,7},{7,1},{8,10},{10,12},{12... | collective-permute-start | bytes 73736 | tf_op jit(solution)/shard_map/ppermute | solution.py:40
  8.4 1.3 %collective-permute-start.2 = (f32[3,4,1,4,128]{4,3,2,1,0:T(4,128)S(1)}, f32[3,4,1,4,128]{4,3,2,1,0:T(4,128)S(1)}, u32[]{:S(2)}, u32[]{:S(2)}) collective-permute-start(f32[3,4,1,4,128]{4,3,2,1,0:T(4,128)S(1)} %get-tuple-element.13), channel_id=1, source_target_pairs={{2,0},{4,2},{6,4},{0,6},{3,1},{5,3},{7,5},{1,7},{10,8},{12,10},{14... | collective-permute-start | bytes 73736 | tf_op jit(solution)/shard_map/ppermute | solution.py:41
  9.7 1.1 %fusion.10 = (f32[3,4,8,1,128]{4,3,2,1,0:T(1,128)S(1)}, f32[3,4,8,1,128]{4,3,2,1,0:T(1,128)S(1)}) fusion(f32[3,4,8,4,128]{4,3,2,1,0:T(4,128)} %param.3), kind=kLoop, calls=%fused_computation.51 | loop fusion | bytes 196608 | tf_op jit(solution)/shard_map/slice | solution.py:41
  10.8 0.0 copy-start
  10.8 0.1 collective-permute-start.5
  10.9 0.8 select_reduce_fusion
  11.7 0.7 broadcast_multiply_fusion
  12.4 0.1 copy.17
  12.5 0.1 mul.32
  12.6 1.0 %fusion.6 = f32[3,64,128]{1,2,0:T(8,128)S(1)} fusion(f32[3,128,128]{2,1,0:T(8,128)} %bitcast.12, f32[128]{0:T(128)S(1)} %mul.32), kind=kLoop, calls=%fused_computation.15 | loop fusion | flops 24576 | bytes 197120 | tf_op jit(solution)/shard_map/transpose | solution.py:173
  13.6 0.5 broadcast_clamp_fusion.slot_ref
  14.1 0.1 copy.18
  14.2 0.1 tile.4
  14.3 0.9 tile.10.w_ref
  15.2 0.0 collective-permute-done.5
  15.2 0.5 collective-permute-start.4
  15.7 0.8 collective-permute-done.4
  16.6 0.0 collective-permute-done.3
  16.6 0.0 collective-permute-done.2
  16.6 0.0 collective-permute-done.1
  16.6 0.0 collective-permute-done
  16.6 0.0 copy-done
  16.6 0.3 fusion.5
  17.0 1.1 %copy.19.g_ref = f32[3,128,384]{2,1,0:T(8,128)} copy(f32[3,128,384]{1,2,0:T(8,128)S(1)} %bitcast.14) | data formatting | bytes 1179648 | tf_op jit(solution)/shard_map/reshape | solution.py:174
  18.0 41.8 %shard_map.37 = f32[32,64,384]{2,1,0:T(8,128)} custom-call(s32[32]{0:T(128)} %broadcast_clamp_fusion.slot_ref, f32[3,64,384]{2,1,0:T(8,128)} %tile.10.w_ref, f32[3,128,384]{2,1,0:T(8,128)} %copy.19.g_ref, f32[384,128]{1,0:T(8,128)} %bitcast.13), custom_call_target="tpu_custom_call" | custom-call | tf_op jit(solution)/shard_map/pallas_call | solution.py:150
  59.8 3.8 %reshape_reshape.7 = f32[2,2,2,2,2,129,128]{6,5,4,3,2,1,0:T(8,128)S(1)} reshape(f32[32,64,258]{2,1,0:T(8,128)} %bitcast.11) | data formatting | bytes 4227072 | tf_op jit(solution)/shard_map/reshape;reshape | solution.py:78
  63.6 0.1 constant_dynamic-slice_fusion.11
  63.7 0.5 copy.20
  64.2 0.4 collective-permute-start.6
  64.6 2.5 %collective-permute-done.6 = f32[2,2,2,2,1,129,128]{6,3,5,4,2,1,0:T(2,128)} collective-permute-done((f32[2,2,2,2,1,129,128]{6,3,5,4,2,1,0:T(2,128)S(1)}, f32[2,2,2,2,1,129,128]{6,3,5,4,2,1,0:T(2,128)}, u32[]{:S(2)}, u32[]{:S(2)}) %collective-permute-start.6) | collective-permute-done | bytes 1056800 | tf_op jit(solution)/shard_map/ppermute | solution.py:69
  67.1 1.3 %copy_add_fusion = f32[2,2,2,2,1,129,128]{6,5,4,3,2,1,0:T(8,128)S(1)} fusion(f32[2,2,2,2,1,129,128]{6,3,5,4,2,1,0:T(2,128)} %collective-permute-done.6, f32[2,2,2,2,2,129,128]{6,5,4,3,2,1,0:T(8,128)S(1)} %reshape_reshape.7, s32[]{:T(128)S(6)} %select_n.140), kind=kLoop, calls=%fused_computation | loop fusion | flops 264192 | bytes 3170308 | tf_op jit(solution)/shard_map/add | solution.py:69
  68.4 0.1 fusion.7
  68.6 1.8 %collective-permute-start.15 = (f32[2,2,1,2,1,43,128]{6,5,4,3,2,1,0:T(8,128)S(1)}, f32[2,2,1,2,1,43,128]{6,5,4,3,2,1,0:T(8,128)S(1)}, u32[]{:S(2)}, u32[]{:S(2)}) collective-permute-start(f32[2,2,1,2,1,43,128]{6,5,4,3,2,1,0:T(8,128)S(1)} %constant_dynamic-slice_fusion.2), channel_id=1, source_target_pairs={{0,4},{2,6},{4,0},{6,2},{1,5},{3,7},{5,1},{7,3},{8,12},{10,14},{12... | collective-permute-start | bytes 528392 | tf_op jit(solution)/shard_map/ppermute | solution.py:69
  70.4 0.1 collective-permute-start.11
  70.5 2.4 %collective-permute-start.7 = (f32[1,2,2,2,1,43,128]{6,5,4,3,2,1,0:T(8,128)S(1)}, f32[1,2,2,2,1,43,128]{6,5,4,3,2,1,0:T(8,128)S(1)}, u32[]{:S(2)}, u32[]{:S(2)}) collective-permute-start(f32[1,2,2,2,1,43,128]{6,5,4,3,2,1,0:T(8,128)S(1)} %constant_dynamic-slice_fusion.10), channel_id=1, source_target_pairs={{0,16},{8,24},{16,0},{24,8},{1,17},{9,25},{17,1},{25,9},{2,18},{10... | collective-permute-start | bytes 528392 | tf_op jit(solution)/shard_map/ppermute | solution.py:69
  72.9 3.0 %collective-permute-done.15 = f32[2,2,1,2,1,43,128]{6,5,4,3,2,1,0:T(8,128)S(1)} collective-permute-done((f32[2,2,1,2,1,43,128]{6,5,4,3,2,1,0:T(8,128)S(1)}, f32[2,2,1,2,1,43,128]{6,5,4,3,2,1,0:T(8,128)S(1)}, u32[]{:S(2)}, u32[]{:S(2)}) %collective-permute-start.15) | collective-permute-done | bytes 176160 | tf_op jit(solution)/shard_map/ppermute | solution.py:69
  75.9 0.8 collective-permute-start.16
  76.7 4.1 %collective-permute-done.11 = f32[2,1,2,2,1,43,128]{6,5,4,3,2,1,0:T(8,128)S(1)} collective-permute-done((f32[2,1,2,2,1,43,128]{6,5,4,3,2,1,0:T(8,128)S(1)}, f32[2,1,2,2,1,43,128]{6,5,4,3,2,1,0:T(8,128)S(1)}, u32[]{:S(2)}, u32[]{:S(2)}) %collective-permute-start.11) | collective-permute-done | bytes 176160 | tf_op jit(solution)/shard_map/ppermute | solution.py:69
  80.9 0.6 collective-permute-start.12
  81.5 1.2 %collective-permute-done.7 = f32[1,2,2,2,1,43,128]{6,5,4,3,2,1,0:T(8,128)S(1)} collective-permute-done((f32[1,2,2,2,1,43,128]{6,5,4,3,2,1,0:T(8,128)S(1)}, f32[1,2,2,2,1,43,128]{6,5,4,3,2,1,0:T(8,128)S(1)}, u32[]{:S(2)}, u32[]{:S(2)}) %collective-permute-start.7) | collective-permute-done | bytes 176160 | tf_op jit(solution)/shard_map/ppermute | solution.py:69
  82.7 0.1 collective-permute-start.8
  82.7 0.0 collective-permute-done.16
  82.8 2.5 %collective-permute-start.17 = (f32[1,2,1,1,1,43,128]{6,5,4,3,2,1,0:T(8,128)S(1)}, f32[1,2,1,1,1,43,128]{6,5,4,3,2,1,0:T(8,128)S(1)}, u32[]{:S(2)}, u32[]{:S(2)}) collective-permute-start(f32[1,2,1,1,1,43,128]{6,5,4,3,2,1,0:T(8,128)S(1)} %constant_dynamic-slice_fusion), channel_id=1, source_target_pairs={{0,16},{8,24},{16,0},{24,8},{1,17},{9,25},{17,1},{25,9},{2,18},{10... | collective-permute-start | bytes 132104 | tf_op jit(solution)/shard_map/ppermute | solution.py:69
  85.3 0.2 collective-permute-done.12
  85.6 0.7 collective-permute-start.13
  86.3 1.1 %collective-permute-done.8 = f32[1,1,2,2,1,43,128]{6,5,4,3,2,1,0:T(8,128)S(1)} collective-permute-done((f32[1,1,2,2,1,43,128]{6,5,4,3,2,1,0:T(8,128)S(1)}, f32[1,1,2,2,1,43,128]{6,5,4,3,2,1,0:T(8,128)S(1)}, u32[]{:S(2)}, u32[]{:S(2)}) %collective-permute-start.8) | collective-permute-done | bytes 88096 | tf_op jit(solution)/shard_map/ppermute | solution.py:69
  87.4 0.4 collective-permute-start.9
  87.8 0.0 collective-permute-done.17
  87.9 2.3 %collective-permute-start.18 = (f32[1,1,1,1,1,43,128]{6,5,4,3,2,1,0:T(8,128)S(1)}, f32[1,1,1,1,1,43,128]{6,5,4,3,2,1,0:T(8,128)S(1)}, u32[]{:S(2)}, u32[]{:S(2)}) collective-permute-start(f32[1,1,1,1,1,43,128]{6,5,4,3,2,1,0:T(8,128)S(1)} %constant_dynamic-slice_fusion.12), channel_id=1, source_target_pairs={{0,8},{8,0},{16,24},{24,16},{1,9},{9,1},{17,25},{25,17},{2,10},{10... | collective-permute-start | bytes 66056 | tf_op jit(solution)/shard_map/ppermute | solution.py:69
  90.2 0.0 collective-permute-done.13
  90.2 0.5 collective-permute-start.14
  90.8 0.8 collective-permute-done.9
  91.6 0.7 collective-permute-start.10
  92.2 0.0 collective-permute-done.18
  92.2 2.8 %collective-permute-done.14 = f32[1,1,1,1,1,43,128]{6,5,4,3,2,1,0:T(8,128)S(1)} collective-permute-done((f32[1,1,1,1,1,43,128]{6,5,4,3,2,1,0:T(8,128)S(1)}, f32[1,1,1,1,1,43,128]{6,5,4,3,2,1,0:T(8,128)S(1)}, u32[]{:S(2)}, u32[]{:S(2)}) %collective-permute-start.14) | collective-permute-done | bytes 22048 | tf_op jit(solution)/shard_map/ppermute | solution.py:69
  95.0 0.4 collective-permute-done.10
  95.5 0.8 reshape_reshape_reshape.3
  (28 shorter events, 0.5 us)
Async XLA Ops:
  0.8 15.8 %collective-permute-start.1 = (f32[3,1,8,4,128]{4,3,2,1,0:T(4,128)S(1)}, f32[3,1,8,4,128]{4,3,2,1,0:T(4,128)S(1)}, u32[]{:S(2)}, u32[]{:S(2)}) collective-permute-start(f32[3,1,8,4,128]{4,3,2,1,0:T(4,128)S(1)} %get-tuple-element.12), channel_id=1, source_target_pairs={{0,8},{8,16},{16,24},{24,0},{1,9},{9,17},{17,25},{25,1},{2,10},{10... | collective-permute-start | bytes 147464 | tf_op jit(solution)/shard_map/ppermute | solution.py:40
  3.9 12.7 %collective-permute-start = (f32[3,1,8,4,128]{4,3,2,1,0:T(4,128)S(1)}, f32[3,1,8,4,128]{4,3,2,1,0:T(4,128)S(1)}, u32[]{:S(2)}, u32[]{:S(2)}) collective-permute-start(f32[3,1,8,4,128]{4,3,2,1,0:T(4,128)S(1)} %get-tuple-element.11), channel_id=1, source_target_pairs={{8,0},{16,8},{24,16},{0,24},{9,1},{17,9},{25,17},{1,25},{10,2},{18... | collective-permute-start | bytes 147464 | tf_op jit(solution)/shard_map/ppermute | solution.py:41
  6.7 9.8 %collective-permute-start.3 = (f32[3,4,1,4,128]{4,3,2,1,0:T(4,128)S(1)}, f32[3,4,1,4,128]{4,3,2,1,0:T(4,128)S(1)}, u32[]{:S(2)}, u32[]{:S(2)}) collective-permute-start(f32[3,4,1,4,128]{4,3,2,1,0:T(4,128)S(1)} %get-tuple-element.14), channel_id=1, source_target_pairs={{0,2},{2,4},{4,6},{6,0},{1,3},{3,5},{5,7},{7,1},{8,10},{10,12},{12... | collective-permute-start | bytes 73736 | tf_op jit(solution)/shard_map/ppermute | solution.py:40
  8.4 8.2 %collective-permute-start.2 = (f32[3,4,1,4,128]{4,3,2,1,0:T(4,128)S(1)}, f32[3,4,1,4,128]{4,3,2,1,0:T(4,128)S(1)}, u32[]{:S(2)}, u32[]{:S(2)}) collective-permute-start(f32[3,4,1,4,128]{4,3,2,1,0:T(4,128)S(1)} %get-tuple-element.13), channel_id=1, source_target_pairs={{2,0},{4,2},{6,4},{0,6},{3,1},{5,3},{7,5},{1,7},{10,8},{12,10},{14... | collective-permute-start | bytes 73736 | tf_op jit(solution)/shard_map/ppermute | solution.py:41
  10.8 5.8 %copy-start = (f32[3,4,8,4,128]{4,3,2,1,0:T(4,128)S(1)}, f32[3,4,8,4,128]{4,3,2,1,0:T(4,128)}, u32[]{:S(2)}) copy-start(f32[3,4,8,4,128]{4,3,2,1,0:T(4,128)} %param.3) | copy-start | bytes 589828
  10.8 4.4 %collective-permute-start.5 = (f32[3,4,8,1,128]{4,3,2,1,0:T(1,128)S(1)}, f32[3,4,8,1,128]{4,3,2,1,0:T(1,128)S(1)}, u32[]{:S(2)}, u32[]{:S(2)}) collective-permute-start(f32[3,4,8,1,128]{4,3,2,1,0:T(1,128)S(1)} %get-tuple-element.16), channel_id=1, source_target_pairs={{0,1},{1,0},{2,3},{3,2},{4,5},{5,4},{6,7},{7,6},{8,9},{9,8},{10,11... | collective-permute-start | bytes 147464 | tf_op jit(solution)/shard_map/ppermute | solution.py:40
  15.2 1.3 %collective-permute-start.4 = (f32[3,4,8,1,128]{4,3,2,1,0:T(1,128)S(1)}, f32[3,4,8,1,128]{4,3,2,1,0:T(1,128)S(1)}, u32[]{:S(2)}, u32[]{:S(2)}) collective-permute-start(f32[3,4,8,1,128]{4,3,2,1,0:T(1,128)S(1)} %get-tuple-element.15), channel_id=1, source_target_pairs={{1,0},{0,1},{3,2},{2,3},{5,4},{4,5},{7,6},{6,7},{9,8},{8,9},{11,10... | collective-permute-start | bytes 147464 | tf_op jit(solution)/shard_map/ppermute | solution.py:41
  64.2 2.9 %collective-permute-start.6 = (f32[2,2,2,2,1,129,128]{6,3,5,4,2,1,0:T(2,128)S(1)}, f32[2,2,2,2,1,129,128]{6,3,5,4,2,1,0:T(2,128)}, u32[]{:S(2)}, u32[]{:S(2)}) collective-permute-start(f32[2,2,2,2,1,129,128]{6,3,5,4,2,1,0:T(2,128)S(1)} %copy.20), channel_id=1, source_target_pairs={{0,1},{1,0},{2,3},{3,2},{4,5},{5,4},{6,7},{7,6},{8,9},{9,8},{10,11... | collective-permute-start | bytes 3170312 | tf_op jit(solution)/shard_map/ppermute | solution.py:69
  68.6 7.3 %collective-permute-start.15 = (f32[2,2,1,2,1,43,128]{6,5,4,3,2,1,0:T(8,128)S(1)}, f32[2,2,1,2,1,43,128]{6,5,4,3,2,1,0:T(8,128)S(1)}, u32[]{:S(2)}, u32[]{:S(2)}) collective-permute-start(f32[2,2,1,2,1,43,128]{6,5,4,3,2,1,0:T(8,128)S(1)} %constant_dynamic-slice_fusion.2), channel_id=1, source_target_pairs={{0,4},{2,6},{4,0},{6,2},{1,5},{3,7},{5,1},{7,3},{8,12},{10,14},{12... | collective-permute-start | bytes 528392 | tf_op jit(solution)/shard_map/ppermute | solution.py:69
  70.4 10.4 %collective-permute-start.11 = (f32[2,1,2,2,1,43,128]{6,5,4,3,2,1,0:T(8,128)S(1)}, f32[2,1,2,2,1,43,128]{6,5,4,3,2,1,0:T(8,128)S(1)}, u32[]{:S(2)}, u32[]{:S(2)}) collective-permute-start(f32[2,1,2,2,1,43,128]{6,5,4,3,2,1,0:T(8,128)S(1)} %constant_dynamic-slice_fusion.6), channel_id=1, source_target_pairs={{0,8},{8,0},{16,24},{24,16},{1,9},{9,1},{17,25},{25,17},{2,10},{10... | collective-permute-start | bytes 528392 | tf_op jit(solution)/shard_map/ppermute | solution.py:69
  70.5 12.1 %collective-permute-start.7 = (f32[1,2,2,2,1,43,128]{6,5,4,3,2,1,0:T(8,128)S(1)}, f32[1,2,2,2,1,43,128]{6,5,4,3,2,1,0:T(8,128)S(1)}, u32[]{:S(2)}, u32[]{:S(2)}) collective-permute-start(f32[1,2,2,2,1,43,128]{6,5,4,3,2,1,0:T(8,128)S(1)} %constant_dynamic-slice_fusion.10), channel_id=1, source_target_pairs={{0,16},{8,24},{16,0},{24,8},{1,17},{9,25},{17,1},{25,9},{2,18},{10... | collective-permute-start | bytes 528392 | tf_op jit(solution)/shard_map/ppermute | solution.py:69
  75.9 6.8 %collective-permute-start.16 = (f32[2,2,1,1,1,43,128]{6,5,4,3,2,1,0:T(8,128)S(1)}, f32[2,2,1,1,1,43,128]{6,5,4,3,2,1,0:T(8,128)S(1)}, u32[]{:S(2)}, u32[]{:S(2)}) collective-permute-start(f32[2,2,1,1,1,43,128]{6,5,4,3,2,1,0:T(8,128)S(1)} %constant_dynamic-slice_fusion.1), channel_id=1, source_target_pairs={{0,2},{2,0},{4,6},{6,4},{1,3},{3,1},{5,7},{7,5},{8,10},{10,8},{12,... | collective-permute-start | bytes 264200 | tf_op jit(solution)/shard_map/ppermute | solution.py:69
  80.9 4.7 %collective-permute-start.12 = (f32[2,1,1,2,1,43,128]{6,5,4,3,2,1,0:T(8,128)S(1)}, f32[2,1,1,2,1,43,128]{6,5,4,3,2,1,0:T(8,128)S(1)}, u32[]{:S(2)}, u32[]{:S(2)}) collective-permute-start(f32[2,1,1,2,1,43,128]{6,5,4,3,2,1,0:T(8,128)S(1)} %constant_dynamic-slice_fusion.5), channel_id=1, source_target_pairs={{0,4},{2,6},{4,0},{6,2},{1,5},{3,7},{5,1},{7,3},{8,12},{10,14},{12... | collective-permute-start | bytes 264200 | tf_op jit(solution)/shard_map/ppermute | solution.py:69
  82.7 4.7 %collective-permute-start.8 = (f32[1,1,2,2,1,43,128]{6,5,4,3,2,1,0:T(8,128)S(1)}, f32[1,1,2,2,1,43,128]{6,5,4,3,2,1,0:T(8,128)S(1)}, u32[]{:S(2)}, u32[]{:S(2)}) collective-permute-start(f32[1,1,2,2,1,43,128]{6,5,4,3,2,1,0:T(8,128)S(1)} %constant_dynamic-slice_fusion.9), channel_id=1, source_target_pairs={{0,8},{8,0},{16,24},{24,16},{1,9},{9,1},{17,25},{25,17},{2,10},{10... | collective-permute-start | bytes 264200 | tf_op jit(solution)/shard_map/ppermute | solution.py:69
  82.8 5.1 %collective-permute-start.17 = (f32[1,2,1,1,1,43,128]{6,5,4,3,2,1,0:T(8,128)S(1)}, f32[1,2,1,1,1,43,128]{6,5,4,3,2,1,0:T(8,128)S(1)}, u32[]{:S(2)}, u32[]{:S(2)}) collective-permute-start(f32[1,2,1,1,1,43,128]{6,5,4,3,2,1,0:T(8,128)S(1)} %constant_dynamic-slice_fusion), channel_id=1, source_target_pairs={{0,16},{8,24},{16,0},{24,8},{1,17},{9,25},{17,1},{25,9},{2,18},{10... | collective-permute-start | bytes 132104 | tf_op jit(solution)/shard_map/ppermute | solution.py:69
  85.6 4.6 %collective-permute-start.13 = (f32[2,1,1,1,1,43,128]{6,5,4,3,2,1,0:T(8,128)S(1)}, f32[2,1,1,1,1,43,128]{6,5,4,3,2,1,0:T(8,128)S(1)}, u32[]{:S(2)}, u32[]{:S(2)}) collective-permute-start(f32[2,1,1,1,1,43,128]{6,5,4,3,2,1,0:T(8,128)S(1)} %constant_dynamic-slice_fusion.4), channel_id=1, source_target_pairs={{0,2},{2,0},{4,6},{6,4},{1,3},{3,1},{5,7},{7,5},{8,10},{10,8},{12,... | collective-permute-start | bytes 132104 | tf_op jit(solution)/shard_map/ppermute | solution.py:69
  87.4 4.2 %collective-permute-start.9 = (f32[1,1,1,2,1,43,128]{6,5,4,3,2,1,0:T(8,128)S(1)}, f32[1,1,1,2,1,43,128]{6,5,4,3,2,1,0:T(8,128)S(1)}, u32[]{:S(2)}, u32[]{:S(2)}) collective-permute-start(f32[1,1,1,2,1,43,128]{6,5,4,3,2,1,0:T(8,128)S(1)} %constant_dynamic-slice_fusion.8), channel_id=1, source_target_pairs={{0,4},{2,6},{4,0},{6,2},{1,5},{3,7},{5,1},{7,3},{8,12},{10,14},{12... | collective-permute-start | bytes 132104 | tf_op jit(solution)/shard_map/ppermute | solution.py:69
  87.9 4.3 %collective-permute-start.18 = (f32[1,1,1,1,1,43,128]{6,5,4,3,2,1,0:T(8,128)S(1)}, f32[1,1,1,1,1,43,128]{6,5,4,3,2,1,0:T(8,128)S(1)}, u32[]{:S(2)}, u32[]{:S(2)}) collective-permute-start(f32[1,1,1,1,1,43,128]{6,5,4,3,2,1,0:T(8,128)S(1)} %constant_dynamic-slice_fusion.12), channel_id=1, source_target_pairs={{0,8},{8,0},{16,24},{24,16},{1,9},{9,1},{17,25},{25,17},{2,10},{10... | collective-permute-start | bytes 66056 | tf_op jit(solution)/shard_map/ppermute | solution.py:69
  90.2 4.8 %collective-permute-start.14 = (f32[1,1,1,1,1,43,128]{6,5,4,3,2,1,0:T(8,128)S(1)}, f32[1,1,1,1,1,43,128]{6,5,4,3,2,1,0:T(8,128)S(1)}, u32[]{:S(2)}, u32[]{:S(2)}) collective-permute-start(f32[1,1,1,1,1,43,128]{6,5,4,3,2,1,0:T(8,128)S(1)} %constant_dynamic-slice_fusion.3), channel_id=1, source_target_pairs={{0,16},{8,24},{16,0},{24,8},{1,17},{9,25},{17,1},{25,9},{2,18},{10... | collective-permute-start | bytes 66056 | tf_op jit(solution)/shard_map/ppermute | solution.py:69
  91.6 3.9 %collective-permute-start.10 = (f32[1,1,1,1,1,43,128]{6,5,4,3,2,1,0:T(8,128)S(1)}, f32[1,1,1,1,1,43,128]{6,5,4,3,2,1,0:T(8,128)S(1)}, u32[]{:S(2)}, u32[]{:S(2)}) collective-permute-start(f32[1,1,1,1,1,43,128]{6,5,4,3,2,1,0:T(8,128)S(1)} %constant_dynamic-slice_fusion.7), channel_id=1, source_target_pairs={{0,2},{2,0},{4,6},{6,4},{1,3},{3,1},{5,7},{7,5},{8,10},{10,8},{12,... | collective-permute-start | bytes 66056 | tf_op jit(solution)/shard_map/ppermute | solution.py:69

commit v7 on v6

--- a/solution.py
+++ b/solution.py
@@ -115,32 +115,20 @@
 
     lax.fori_loop(0, test // group, contract, 0)
     lane = lax.broadcasted_iota(jnp.int32, (test, 128), 1)
-
-    def place(j, carry):
+    for j in range(width):
         slab = sym_ref[pl.ds(j, test, stride=width), :]
         offset = j * width - (j * (j - 1)) // 2
         stop = offset + width - j
-
-        def per_block(c, carry):
-            base_c = c * block_len
-            lo = jnp.maximum(offset, base_c) - base_c
-            hi = jnp.minimum(stop, base_c + block_len) - base_c
+        for c in range(offset // block_len, (stop - 1) // block_len + 1):
+            lo = max(offset, c * block_len) - c * block_len
+            hi = min(stop, (c + 1) * block_len) - c * block_len
             slot = slot_ref[c]
-
-            def per_tile(u, carry):
-                base = base_c + u * 128
+            for u in range(lo // 128, (hi - 1) // 128 + 1):
+                base = c * block_len + u * 128
                 rolled = pltpu.roll(slab, (offset - j - base) % 128, 1)
                 keep = (lane >= lo - u * 128) & (lane < hi - u * 128)
-                at = pl.multiple_of(u * 128, 128)
-                cur = out_ref[slot, :, pl.ds(at, 128)]
-                out_ref[slot, :, pl.ds(at, 128)] = jnp.where(keep, rolled, cur)
-                return carry
-
-            return lax.fori_loop(lo // 128, (hi - 1) // 128 + 1, per_tile, carry)
-
-        return lax.fori_loop(offset // block_len, (stop - 1) // block_len + 1, per_block, carry)
-
-    lax.fori_loop(0, width, place, 0)
+                cur = out_ref[slot, :, pl.ds(u * 128, 128)]
+                out_ref[slot, :, pl.ds(u * 128, 128)] = jnp.where(keep, rolled, cur)
 
 
 def triangle(slots, weighted, grads, modes_flat, block_len):

time: 96.8 us -> 76 us (0.79)
  Pallas kernels: 41.8 us -> 21 us
    pallas_call x1, Pallas kernels: 41.8 us -> 21 us  [triangle(): pl.pallas_call(functools.partial(triangle_kernel, block_len), out_shape=j...]
  transfers between devices with their start and end apart: 19 -> 19, of which waited for: 10 -> 10; matrix products, arithmetic and copies ran while one was open for 7% -> 9% of each run, Pallas kernels for 0% -> 0%
where the time goes in v7:
time: 76 us; the launch traced here: 75.6 us
  starting transfers between devices  21.9 us (29%)
  Pallas kernels  21 us (28%)
  waiting for transfers between devices  16.8 us (22%)
  local copies, waits for them, and re-layouts  10.6 us (14%)
  other arithmetic  4.95 us (7%)
    pallas_call x1, Pallas kernels, triangle(): pl.pallas_call(functools.partial(triangle_kernel, block_len), out_shape=j...  21 us
    ppermute x13, waiting for transfers between devices, halve(): return keep + lax.ppermute(other, axis, pairs)  16 us
    ppermute x13, starting transfers between devices, halve(): return keep + lax.ppermute(other, axis, pairs)  13.3 us
    ppermute x3, starting transfers between devices, face_gradients(): lax.ppermute(lax.slice_in_dim(value, length - 1, length, axis=dim), axis,...  4.78 us
    ppermute x3, starting transfers between devices, face_gradients(): after = lax.ppermute(lax.slice_in_dim(value, 0, 1, axis=dim), axis, down)  3.83 us
    another operation x1, local copies, waits for them, and re-layouts, scatter_sum(): value = payload.reshape((2,) * len(stages) + (rows, lanes))  3.77 us
    slice x3, local copies, waits for them, and re-layouts, face_gradients(): after = lax.ppermute(lax.slice_in_dim(value, 0, 1, axis=dim), axis, down)  2.71 us
  transfers between devices with their start and end apart: 19, of which 10 were waited for; matrix products, arithmetic and copies ran while one was open for 9% of the time, Pallas kernels for 0%

profile of v7, /device:TPU:0, one launch (start us, length us, event | category | flops | bytes accessed | tf_op | source)
XLA Modules:
  0.0 75.6 jit_solution(15695302977362411729)
XLA Ops:
  0.0 0.8 %fusion.8 = (f32[3,1,8,4,128]{4,3,2,1,0:T(4,128)S(1)}, f32[3,1,8,4,128]{4,3,2,1,0:T(4,128)S(1)}) fusion(f32[3,4,8,4,128]{4,3,2,1,0:T(4,128)} %param.3), kind=kLoop, calls=%fused_computation.49 | loop fusion | bytes 196608 | tf_op jit(solution)/shard_map/slice | solution.py:41
  0.8 3.1 %collective-permute-start.1 = (f32[3,1,8,4,128]{4,3,2,1,0:T(4,128)S(1)}, f32[3,1,8,4,128]{4,3,2,1,0:T(4,128)S(1)}, u32[]{:S(2)}, u32[]{:S(2)}) collective-permute-start(f32[3,1,8,4,128]{4,3,2,1,0:T(4,128)S(1)} %get-tuple-element.12), channel_id=1, source_target_pairs={{0,8},{8,16},{16,24},{24,0},{1,9},{9,17},{17,25},{25,1},{2,10},{10... | collective-permute-start | bytes 147464 | tf_op jit(solution)/shard_map/ppermute | solution.py:40
  3.9 2.1 %collective-permute-start = (f32[3,1,8,4,128]{4,3,2,1,0:T(4,128)S(1)}, f32[3,1,8,4,128]{4,3,2,1,0:T(4,128)S(1)}, u32[]{:S(2)}, u32[]{:S(2)}) collective-permute-start(f32[3,1,8,4,128]{4,3,2,1,0:T(4,128)S(1)} %get-tuple-element.11), channel_id=1, source_target_pairs={{8,0},{16,8},{24,16},{0,24},{9,1},{17,9},{25,17},{1,25},{10,2},{18... | collective-permute-start | bytes 147464 | tf_op jit(solution)/shard_map/ppermute | solution.py:41
  6.0 0.8 %fusion.9 = (f32[3,4,1,4,128]{4,3,2,1,0:T(4,128)S(1)}, f32[3,4,1,4,128]{4,3,2,1,0:T(4,128)S(1)}) fusion(f32[3,4,8,4,128]{4,3,2,1,0:T(4,128)} %param.3), kind=kLoop, calls=%fused_computation.50 | loop fusion | bytes 98304 | tf_op jit(solution)/shard_map/slice | solution.py:41
  6.7 1.6 %collective-permute-start.3 = (f32[3,4,1,4,128]{4,3,2,1,0:T(4,128)S(1)}, f32[3,4,1,4,128]{4,3,2,1,0:T(4,128)S(1)}, u32[]{:S(2)}, u32[]{:S(2)}) collective-permute-start(f32[3,4,1,4,128]{4,3,2,1,0:T(4,128)S(1)} %get-tuple-element.14), channel_id=1, source_target_pairs={{0,2},{2,4},{4,6},{6,0},{1,3},{3,5},{5,7},{7,1},{8,10},{10,12},{12... | collective-permute-start | bytes 73736 | tf_op jit(solution)/shard_map/ppermute | solution.py:40
  8.4 1.3 %collective-permute-start.2 = (f32[3,4,1,4,128]{4,3,2,1,0:T(4,128)S(1)}, f32[3,4,1,4,128]{4,3,2,1,0:T(4,128)S(1)}, u32[]{:S(2)}, u32[]{:S(2)}) collective-permute-start(f32[3,4,1,4,128]{4,3,2,1,0:T(4,128)S(1)} %get-tuple-element.13), channel_id=1, source_target_pairs={{2,0},{4,2},{6,4},{0,6},{3,1},{5,3},{7,5},{1,7},{10,8},{12,10},{14... | collective-permute-start | bytes 73736 | tf_op jit(solution)/shard_map/ppermute | solution.py:41
  9.7 1.1 %fusion.10 = (f32[3,4,8,1,128]{4,3,2,1,0:T(1,128)S(1)}, f32[3,4,8,1,128]{4,3,2,1,0:T(1,128)S(1)}) fusion(f32[3,4,8,4,128]{4,3,2,1,0:T(4,128)} %param.3), kind=kLoop, calls=%fused_computation.51 | loop fusion | bytes 196608 | tf_op jit(solution)/shard_map/slice | solution.py:41
  10.8 0.0 copy-start
  10.8 0.1 collective-permute-start.5
  10.9 0.8 %select_reduce_fusion = s32[32]{0:T(128)S(1)} fusion(s32[32]{0:T(128)} %param.5), kind=kLoop, calls=%fused_computation.31 | loop fusion | flops 3040 | bytes 256 | tf_op jit(solution)/shard_map/reduce_sum | solution.py:166
  11.7 0.7 broadcast_multiply_fusion
  12.4 0.1 copy.17
  12.5 0.1 mul.32
  12.6 1.0 %fusion.6 = f32[3,64,128]{1,2,0:T(8,128)S(1)} fusion(f32[3,128,128]{2,1,0:T(8,128)} %bitcast.12, f32[128]{0:T(128)S(1)} %mul.32), kind=kLoop, calls=%fused_computation.15 | loop fusion | flops 24576 | bytes 197120 | tf_op jit(solution)/shard_map/transpose | solution.py:161
  13.6 0.5 broadcast_clamp_fusion.slot_ref
  14.1 0.1 copy.18
  14.2 0.1 tile.4
  14.3 0.9 %tile.10.w_ref = f32[3,64,384]{2,1,0:T(8,128)} reshape(f32[3,64,3,128]{3,2,1,0:T(4,128)S(1)} %tile.4) | data formatting | bytes 589824 | tf_op jit(solution)/shard_map/tile | solution.py:161
  15.2 0.0 collective-permute-done.5
  15.2 0.5 collective-permute-start.4
  15.7 0.8 %collective-permute-done.4 = f32[3,4,8,1,128]{4,3,2,1,0:T(1,128)S(1)} collective-permute-done((f32[3,4,8,1,128]{4,3,2,1,0:T(1,128)S(1)}, f32[3,4,8,1,128]{4,3,2,1,0:T(1,128)S(1)}, u32[]{:S(2)}, u32[]{:S(2)}) %collective-permute-start.4) | collective-permute-done | bytes 49184 | tf_op jit(solution)/shard_map/ppermute | solution.py:41
  16.6 0.0 collective-permute-done.3
  16.6 0.0 collective-permute-done.2
  16.6 0.0 collective-permute-done.1
  16.6 0.0 collective-permute-done
  16.6 0.0 copy-done
  16.6 0.3 fusion.5
  17.0 1.1 %copy.19.g_ref = f32[3,128,384]{2,1,0:T(8,128)} copy(f32[3,128,384]{1,2,0:T(8,128)S(1)} %bitcast.14) | data formatting | bytes 1179648 | tf_op jit(solution)/shard_map/reshape | solution.py:162
  18.0 21.0 %shard_map.37 = f32[32,64,384]{2,1,0:T(8,128)} custom-call(s32[32]{0:T(128)} %broadcast_clamp_fusion.slot_ref, f32[3,64,384]{2,1,0:T(8,128)} %tile.10.w_ref, f32[3,128,384]{2,1,0:T(8,128)} %copy.19.g_ref, f32[384,128]{1,0:T(8,128)} %bitcast.13), custom_call_target="tpu_custom_call" | custom-call | tf_op jit(solution)/shard_map/pallas_call | solution.py:138
  39.0 3.8 %reshape_reshape.7 = f32[2,2,2,2,2,129,128]{6,5,4,3,2,1,0:T(8,128)S(1)} reshape(f32[32,64,258]{2,1,0:T(8,128)} %bitcast.11) | data formatting | bytes 4227072 | tf_op jit(solution)/shard_map/reshape;reshape | solution.py:78
  42.8 0.1 constant_dynamic-slice_fusion.11
  42.9 0.5 copy.20
  43.5 0.4 collective-permute-start.6
  43.9 2.5 %collective-permute-done.6 = f32[2,2,2,2,1,129,128]{6,3,5,4,2,1,0:T(2,128)} collective-permute-done((f32[2,2,2,2,1,129,128]{6,3,5,4,2,1,0:T(2,128)S(1)}, f32[2,2,2,2,1,129,128]{6,3,5,4,2,1,0:T(2,128)}, u32[]{:S(2)}, u32[]{:S(2)}) %collective-permute-start.6) | collective-permute-done | bytes 1056800 | tf_op jit(solution)/shard_map/ppermute | solution.py:69
  46.3 1.3 %copy_add_fusion = f32[2,2,2,2,1,129,128]{6,5,4,3,2,1,0:T(8,128)S(1)} fusion(f32[2,2,2,2,1,129,128]{6,3,5,4,2,1,0:T(2,128)} %collective-permute-done.6, f32[2,2,2,2,2,129,128]{6,5,4,3,2,1,0:T(8,128)S(1)} %reshape_reshape.7, s32[]{:T(128)S(6)} %select_n.140), kind=kLoop, calls=%fused_computation | loop fusion | flops 264192 | bytes 3170308 | tf_op jit(solution)/shard_map/add | solution.py:69
  47.7 0.1 fusion.7
  47.8 1.8 %collective-permute-start.15 = (f32[2,2,1,2,1,43,128]{6,5,4,3,2,1,0:T(8,128)S(1)}, f32[2,2,1,2,1,43,128]{6,5,4,3,2,1,0:T(8,128)S(1)}, u32[]{:S(2)}, u32[]{:S(2)}) collective-permute-start(f32[2,2,1,2,1,43,128]{6,5,4,3,2,1,0:T(8,128)S(1)} %constant_dynamic-slice_fusion.2), channel_id=1, source_target_pairs={{0,4},{2,6},{4,0},{6,2},{1,5},{3,7},{5,1},{7,3},{8,12},{10,14},{12... | collective-permute-start | bytes 528392 | tf_op jit(solution)/shard_map/ppermute | solution.py:69
  49.6 0.1 collective-permute-start.11
  49.7 2.4 %collective-permute-start.7 = (f32[1,2,2,2,1,43,128]{6,5,4,3,2,1,0:T(8,128)S(1)}, f32[1,2,2,2,1,43,128]{6,5,4,3,2,1,0:T(8,128)S(1)}, u32[]{:S(2)}, u32[]{:S(2)}) collective-permute-start(f32[1,2,2,2,1,43,128]{6,5,4,3,2,1,0:T(8,128)S(1)} %constant_dynamic-slice_fusion.10), channel_id=1, source_target_pairs={{0,16},{8,24},{16,0},{24,8},{1,17},{9,25},{17,1},{25,9},{2,18},{10... | collective-permute-start | bytes 528392 | tf_op jit(solution)/shard_map/ppermute | solution.py:69
  52.1 3.0 %collective-permute-done.15 = f32[2,2,1,2,1,43,128]{6,5,4,3,2,1,0:T(8,128)S(1)} collective-permute-done((f32[2,2,1,2,1,43,128]{6,5,4,3,2,1,0:T(8,128)S(1)}, f32[2,2,1,2,1,43,128]{6,5,4,3,2,1,0:T(8,128)S(1)}, u32[]{:S(2)}, u32[]{:S(2)}) %collective-permute-start.15) | collective-permute-done | bytes 176160 | tf_op jit(solution)/shard_map/ppermute | solution.py:69
  55.2 0.8 %collective-permute-start.16 = (f32[2,2,1,1,1,43,128]{6,5,4,3,2,1,0:T(8,128)S(1)}, f32[2,2,1,1,1,43,128]{6,5,4,3,2,1,0:T(8,128)S(1)}, u32[]{:S(2)}, u32[]{:S(2)}) collective-permute-start(f32[2,2,1,1,1,43,128]{6,5,4,3,2,1,0:T(8,128)S(1)} %constant_dynamic-slice_fusion.1), channel_id=1, source_target_pairs={{0,2},{2,0},{4,6},{6,4},{1,3},{3,1},{5,7},{7,5},{8,10},{10,8},{12,... | collective-permute-start | bytes 264200 | tf_op jit(solution)/shard_map/ppermute | solution.py:69
  56.0 4.1 %collective-permute-done.11 = f32[2,1,2,2,1,43,128]{6,5,4,3,2,1,0:T(8,128)S(1)} collective-permute-done((f32[2,1,2,2,1,43,128]{6,5,4,3,2,1,0:T(8,128)S(1)}, f32[2,1,2,2,1,43,128]{6,5,4,3,2,1,0:T(8,128)S(1)}, u32[]{:S(2)}, u32[]{:S(2)}) %collective-permute-start.11) | collective-permute-done | bytes 176160 | tf_op jit(solution)/shard_map/ppermute | solution.py:69
  60.1 0.6 collective-permute-start.12
  60.7 1.2 %collective-permute-done.7 = f32[1,2,2,2,1,43,128]{6,5,4,3,2,1,0:T(8,128)S(1)} collective-permute-done((f32[1,2,2,2,1,43,128]{6,5,4,3,2,1,0:T(8,128)S(1)}, f32[1,2,2,2,1,43,128]{6,5,4,3,2,1,0:T(8,128)S(1)}, u32[]{:S(2)}, u32[]{:S(2)}) %collective-permute-start.7) | collective-permute-done | bytes 176160 | tf_op jit(solution)/shard_map/ppermute | solution.py:69
  61.9 0.1 collective-permute-start.8
  62.0 0.0 collective-permute-done.16
  62.0 2.5 %collective-permute-start.17 = (f32[1,2,1,1,1,43,128]{6,5,4,3,2,1,0:T(8,128)S(1)}, f32[1,2,1,1,1,43,128]{6,5,4,3,2,1,0:T(8,128)S(1)}, u32[]{:S(2)}, u32[]{:S(2)}) collective-permute-start(f32[1,2,1,1,1,43,128]{6,5,4,3,2,1,0:T(8,128)S(1)} %constant_dynamic-slice_fusion), channel_id=1, source_target_pairs={{0,16},{8,24},{16,0},{24,8},{1,17},{9,25},{17,1},{25,9},{2,18},{10... | collective-permute-start | bytes 132104 | tf_op jit(solution)/shard_map/ppermute | solution.py:69
  64.6 0.2 collective-permute-done.12
  64.8 0.7 collective-permute-start.13
  65.5 1.1 %collective-permute-done.8 = f32[1,1,2,2,1,43,128]{6,5,4,3,2,1,0:T(8,128)S(1)} collective-permute-done((f32[1,1,2,2,1,43,128]{6,5,4,3,2,1,0:T(8,128)S(1)}, f32[1,1,2,2,1,43,128]{6,5,4,3,2,1,0:T(8,128)S(1)}, u32[]{:S(2)}, u32[]{:S(2)}) %collective-permute-start.8) | collective-permute-done | bytes 88096 | tf_op jit(solution)/shard_map/ppermute | solution.py:69
  66.6 0.4 collective-permute-start.9
  67.1 0.0 collective-permute-done.17
  67.1 2.3 %collective-permute-start.18 = (f32[1,1,1,1,1,43,128]{6,5,4,3,2,1,0:T(8,128)S(1)}, f32[1,1,1,1,1,43,128]{6,5,4,3,2,1,0:T(8,128)S(1)}, u32[]{:S(2)}, u32[]{:S(2)}) collective-permute-start(f32[1,1,1,1,1,43,128]{6,5,4,3,2,1,0:T(8,128)S(1)} %constant_dynamic-slice_fusion.12), channel_id=1, source_target_pairs={{0,8},{8,0},{16,24},{24,16},{1,9},{9,1},{17,25},{25,17},{2,10},{10... | collective-permute-start | bytes 66056 | tf_op jit(solution)/shard_map/ppermute | solution.py:69
  69.4 0.0 collective-permute-done.13
  69.5 0.5 collective-permute-start.14
  70.0 0.8 %collective-permute-done.9 = f32[1,1,1,2,1,43,128]{6,5,4,3,2,1,0:T(8,128)S(1)} collective-permute-done((f32[1,1,1,2,1,43,128]{6,5,4,3,2,1,0:T(8,128)S(1)}, f32[1,1,1,2,1,43,128]{6,5,4,3,2,1,0:T(8,128)S(1)}, u32[]{:S(2)}, u32[]{:S(2)}) %collective-permute-start.9) | collective-permute-done | bytes 44064 | tf_op jit(solution)/shard_map/ppermute | solution.py:69
  70.8 0.7 collective-permute-start.10
  71.5 0.0 collective-permute-done.18
  71.5 2.8 %collective-permute-done.14 = f32[1,1,1,1,1,43,128]{6,5,4,3,2,1,0:T(8,128)S(1)} collective-permute-done((f32[1,1,1,1,1,43,128]{6,5,4,3,2,1,0:T(8,128)S(1)}, f32[1,1,1,1,1,43,128]{6,5,4,3,2,1,0:T(8,128)S(1)}, u32[]{:S(2)}, u32[]{:S(2)}) %collective-permute-start.14) | collective-permute-done | bytes 22048 | tf_op jit(solution)/shard_map/ppermute | solution.py:69
  74.3 0.4 collective-permute-done.10
  74.7 0.8 %reshape_reshape_reshape.3 = f32[64,258]{1,0:T(8,128)} reshape(f32[1,1,1,1,1,129,128]{6,5,4,3,2,1,0:T(8,128)S(1)} %pad_maximum_fusion.7) | data formatting | bytes 132096 | tf_op jit(solution)/shard_map/reshape;reshape;reshape | solution.py:174
  (28 shorter events, 0.5 us)
Async XLA Ops:
  0.8 15.8 %collective-permute-start.1 = (f32[3,1,8,4,128]{4,3,2,1,0:T(4,128)S(1)}, f32[3,1,8,4,128]{4,3,2,1,0:T(4,128)S(1)}, u32[]{:S(2)}, u32[]{:S(2)}) collective-permute-start(f32[3,1,8,4,128]{4,3,2,1,0:T(4,128)S(1)} %get-tuple-element.12), channel_id=1, source_target_pairs={{0,8},{8,16},{16,24},{24,0},{1,9},{9,17},{17,25},{25,1},{2,10},{10... | collective-permute-start | bytes 147464 | tf_op jit(solution)/shard_map/ppermute | solution.py:40
  3.9 12.7 %collective-permute-start = (f32[3,1,8,4,128]{4,3,2,1,0:T(4,128)S(1)}, f32[3,1,8,4,128]{4,3,2,1,0:T(4,128)S(1)}, u32[]{:S(2)}, u32[]{:S(2)}) collective-permute-start(f32[3,1,8,4,128]{4,3,2,1,0:T(4,128)S(1)} %get-tuple-element.11), channel_id=1, source_target_pairs={{8,0},{16,8},{24,16},{0,24},{9,1},{17,9},{25,17},{1,25},{10,2},{18... | collective-permute-start | bytes 147464 | tf_op jit(solution)/shard_map/ppermute | solution.py:41
  6.7 9.8 %collective-permute-start.3 = (f32[3,4,1,4,128]{4,3,2,1,0:T(4,128)S(1)}, f32[3,4,1,4,128]{4,3,2,1,0:T(4,128)S(1)}, u32[]{:S(2)}, u32[]{:S(2)}) collective-permute-start(f32[3,4,1,4,128]{4,3,2,1,0:T(4,128)S(1)} %get-tuple-element.14), channel_id=1, source_target_pairs={{0,2},{2,4},{4,6},{6,0},{1,3},{3,5},{5,7},{7,1},{8,10},{10,12},{12... | collective-permute-start | bytes 73736 | tf_op jit(solution)/shard_map/ppermute | solution.py:40
  8.4 8.2 %collective-permute-start.2 = (f32[3,4,1,4,128]{4,3,2,1,0:T(4,128)S(1)}, f32[3,4,1,4,128]{4,3,2,1,0:T(4,128)S(1)}, u32[]{:S(2)}, u32[]{:S(2)}) collective-permute-start(f32[3,4,1,4,128]{4,3,2,1,0:T(4,128)S(1)} %get-tuple-element.13), channel_id=1, source_target_pairs={{2,0},{4,2},{6,4},{0,6},{3,1},{5,3},{7,5},{1,7},{10,8},{12,10},{14... | collective-permute-start | bytes 73736 | tf_op jit(solution)/shard_map/ppermute | solution.py:41
  10.8 5.8 %copy-start = (f32[3,4,8,4,128]{4,3,2,1,0:T(4,128)S(1)}, f32[3,4,8,4,128]{4,3,2,1,0:T(4,128)}, u32[]{:S(2)}) copy-start(f32[3,4,8,4,128]{4,3,2,1,0:T(4,128)} %param.3) | copy-start | bytes 589828
  10.8 4.4 %collective-permute-start.5 = (f32[3,4,8,1,128]{4,3,2,1,0:T(1,128)S(1)}, f32[3,4,8,1,128]{4,3,2,1,0:T(1,128)S(1)}, u32[]{:S(2)}, u32[]{:S(2)}) collective-permute-start(f32[3,4,8,1,128]{4,3,2,1,0:T(1,128)S(1)} %get-tuple-element.16), channel_id=1, source_target_pairs={{0,1},{1,0},{2,3},{3,2},{4,5},{5,4},{6,7},{7,6},{8,9},{9,8},{10,11... | collective-permute-start | bytes 147464 | tf_op jit(solution)/shard_map/ppermute | solution.py:40
  15.2 1.3 %collective-permute-start.4 = (f32[3,4,8,1,128]{4,3,2,1,0:T(1,128)S(1)}, f32[3,4,8,1,128]{4,3,2,1,0:T(1,128)S(1)}, u32[]{:S(2)}, u32[]{:S(2)}) collective-permute-start(f32[3,4,8,1,128]{4,3,2,1,0:T(1,128)S(1)} %get-tuple-element.15), channel_id=1, source_target_pairs={{1,0},{0,1},{3,2},{2,3},{5,4},{4,5},{7,6},{6,7},{9,8},{8,9},{11,10... | collective-permute-start | bytes 147464 | tf_op jit(solution)/shard_map/ppermute | solution.py:41
  43.5 2.9 %collective-permute-start.6 = (f32[2,2,2,2,1,129,128]{6,3,5,4,2,1,0:T(2,128)S(1)}, f32[2,2,2,2,1,129,128]{6,3,5,4,2,1,0:T(2,128)}, u32[]{:S(2)}, u32[]{:S(2)}) collective-permute-start(f32[2,2,2,2,1,129,128]{6,3,5,4,2,1,0:T(2,128)S(1)} %copy.20), channel_id=1, source_target_pairs={{0,1},{1,0},{2,3},{3,2},{4,5},{5,4},{6,7},{7,6},{8,9},{9,8},{10,11... | collective-permute-start | bytes 3170312 | tf_op jit(solution)/shard_map/ppermute | solution.py:69
  47.8 7.3 %collective-permute-start.15 = (f32[2,2,1,2,1,43,128]{6,5,4,3,2,1,0:T(8,128)S(1)}, f32[2,2,1,2,1,43,128]{6,5,4,3,2,1,0:T(8,128)S(1)}, u32[]{:S(2)}, u32[]{:S(2)}) collective-permute-start(f32[2,2,1,2,1,43,128]{6,5,4,3,2,1,0:T(8,128)S(1)} %constant_dynamic-slice_fusion.2), channel_id=1, source_target_pairs={{0,4},{2,6},{4,0},{6,2},{1,5},{3,7},{5,1},{7,3},{8,12},{10,14},{12... | collective-permute-start | bytes 528392 | tf_op jit(solution)/shard_map/ppermute | solution.py:69
  49.6 10.4 %collective-permute-start.11 = (f32[2,1,2,2,1,43,128]{6,5,4,3,2,1,0:T(8,128)S(1)}, f32[2,1,2,2,1,43,128]{6,5,4,3,2,1,0:T(8,128)S(1)}, u32[]{:S(2)}, u32[]{:S(2)}) collective-permute-start(f32[2,1,2,2,1,43,128]{6,5,4,3,2,1,0:T(8,128)S(1)} %constant_dynamic-slice_fusion.6), channel_id=1, source_target_pairs={{0,8},{8,0},{16,24},{24,16},{1,9},{9,1},{17,25},{25,17},{2,10},{10... | collective-permute-start | bytes 528392 | tf_op jit(solution)/shard_map/ppermute | solution.py:69
  49.7 12.1 %collective-permute-start.7 = (f32[1,2,2,2,1,43,128]{6,5,4,3,2,1,0:T(8,128)S(1)}, f32[1,2,2,2,1,43,128]{6,5,4,3,2,1,0:T(8,128)S(1)}, u32[]{:S(2)}, u32[]{:S(2)}) collective-permute-start(f32[1,2,2,2,1,43,128]{6,5,4,3,2,1,0:T(8,128)S(1)} %constant_dynamic-slice_fusion.10), channel_id=1, source_target_pairs={{0,16},{8,24},{16,0},{24,8},{1,17},{9,25},{17,1},{25,9},{2,18},{10... | collective-permute-start | bytes 528392 | tf_op jit(solution)/shard_map/ppermute | solution.py:69
  55.2 6.8 %collective-permute-start.16 = (f32[2,2,1,1,1,43,128]{6,5,4,3,2,1,0:T(8,128)S(1)}, f32[2,2,1,1,1,43,128]{6,5,4,3,2,1,0:T(8,128)S(1)}, u32[]{:S(2)}, u32[]{:S(2)}) collective-permute-start(f32[2,2,1,1,1,43,128]{6,5,4,3,2,1,0:T(8,128)S(1)} %constant_dynamic-slice_fusion.1), channel_id=1, source_target_pairs={{0,2},{2,0},{4,6},{6,4},{1,3},{3,1},{5,7},{7,5},{8,10},{10,8},{12,... | collective-permute-start | bytes 264200 | tf_op jit(solution)/shard_map/ppermute | solution.py:69
  60.1 4.7 %collective-permute-start.12 = (f32[2,1,1,2,1,43,128]{6,5,4,3,2,1,0:T(8,128)S(1)}, f32[2,1,1,2,1,43,128]{6,5,4,3,2,1,0:T(8,128)S(1)}, u32[]{:S(2)}, u32[]{:S(2)}) collective-permute-start(f32[2,1,1,2,1,43,128]{6,5,4,3,2,1,0:T(8,128)S(1)} %constant_dynamic-slice_fusion.5), channel_id=1, source_target_pairs={{0,4},{2,6},{4,0},{6,2},{1,5},{3,7},{5,1},{7,3},{8,12},{10,14},{12... | collective-permute-start | bytes 264200 | tf_op jit(solution)/shard_map/ppermute | solution.py:69
  61.9 4.7 %collective-permute-start.8 = (f32[1,1,2,2,1,43,128]{6,5,4,3,2,1,0:T(8,128)S(1)}, f32[1,1,2,2,1,43,128]{6,5,4,3,2,1,0:T(8,128)S(1)}, u32[]{:S(2)}, u32[]{:S(2)}) collective-permute-start(f32[1,1,2,2,1,43,128]{6,5,4,3,2,1,0:T(8,128)S(1)} %constant_dynamic-slice_fusion.9), channel_id=1, source_target_pairs={{0,8},{8,0},{16,24},{24,16},{1,9},{9,1},{17,25},{25,17},{2,10},{10... | collective-permute-start | bytes 264200 | tf_op jit(solution)/shard_map/ppermute | solution.py:69
  62.0 5.1 %collective-permute-start.17 = (f32[1,2,1,1,1,43,128]{6,5,4,3,2,1,0:T(8,128)S(1)}, f32[1,2,1,1,1,43,128]{6,5,4,3,2,1,0:T(8,128)S(1)}, u32[]{:S(2)}, u32[]{:S(2)}) collective-permute-start(f32[1,2,1,1,1,43,128]{6,5,4,3,2,1,0:T(8,128)S(1)} %constant_dynamic-slice_fusion), channel_id=1, source_target_pairs={{0,16},{8,24},{16,0},{24,8},{1,17},{9,25},{17,1},{25,9},{2,18},{10... | collective-permute-start | bytes 132104 | tf_op jit(solution)/shard_map/ppermute | solution.py:69
  64.8 4.6 %collective-permute-start.13 = (f32[2,1,1,1,1,43,128]{6,5,4,3,2,1,0:T(8,128)S(1)}, f32[2,1,1,1,1,43,128]{6,5,4,3,2,1,0:T(8,128)S(1)}, u32[]{:S(2)}, u32[]{:S(2)}) collective-permute-start(f32[2,1,1,1,1,43,128]{6,5,4,3,2,1,0:T(8,128)S(1)} %constant_dynamic-slice_fusion.4), channel_id=1, source_target_pairs={{0,2},{2,0},{4,6},{6,4},{1,3},{3,1},{5,7},{7,5},{8,10},{10,8},{12,... | collective-permute-start | bytes 132104 | tf_op jit(solution)/shard_map/ppermute | solution.py:69
  66.6 4.2 %collective-permute-start.9 = (f32[1,1,1,2,1,43,128]{6,5,4,3,2,1,0:T(8,128)S(1)}, f32[1,1,1,2,1,43,128]{6,5,4,3,2,1,0:T(8,128)S(1)}, u32[]{:S(2)}, u32[]{:S(2)}) collective-permute-start(f32[1,1,1,2,1,43,128]{6,5,4,3,2,1,0:T(8,128)S(1)} %constant_dynamic-slice_fusion.8), channel_id=1, source_target_pairs={{0,4},{2,6},{4,0},{6,2},{1,5},{3,7},{5,1},{7,3},{8,12},{10,14},{12... | collective-permute-start | bytes 132104 | tf_op jit(solution)/shard_map/ppermute | solution.py:69
  67.1 4.3 %collective-permute-start.18 = (f32[1,1,1,1,1,43,128]{6,5,4,3,2,1,0:T(8,128)S(1)}, f32[1,1,1,1,1,43,128]{6,5,4,3,2,1,0:T(8,128)S(1)}, u32[]{:S(2)}, u32[]{:S(2)}) collective-permute-start(f32[1,1,1,1,1,43,128]{6,5,4,3,2,1,0:T(8,128)S(1)} %constant_dynamic-slice_fusion.12), channel_id=1, source_target_pairs={{0,8},{8,0},{16,24},{24,16},{1,9},{9,1},{17,25},{25,17},{2,10},{10... | collective-permute-start | bytes 66056 | tf_op jit(solution)/shard_map/ppermute | solution.py:69
  69.5 4.8 %collective-permute-start.14 = (f32[1,1,1,1,1,43,128]{6,5,4,3,2,1,0:T(8,128)S(1)}, f32[1,1,1,1,1,43,128]{6,5,4,3,2,1,0:T(8,128)S(1)}, u32[]{:S(2)}, u32[]{:S(2)}) collective-permute-start(f32[1,1,1,1,1,43,128]{6,5,4,3,2,1,0:T(8,128)S(1)} %constant_dynamic-slice_fusion.3), channel_id=1, source_target_pairs={{0,16},{8,24},{16,0},{24,8},{1,17},{9,25},{17,1},{25,9},{2,18},{10... | collective-permute-start | bytes 66056 | tf_op jit(solution)/shard_map/ppermute | solution.py:69
  70.8 3.9 %collective-permute-start.10 = (f32[1,1,1,1,1,43,128]{6,5,4,3,2,1,0:T(8,128)S(1)}, f32[1,1,1,1,1,43,128]{6,5,4,3,2,1,0:T(8,128)S(1)}, u32[]{:S(2)}, u32[]{:S(2)}) collective-permute-start(f32[1,1,1,1,1,43,128]{6,5,4,3,2,1,0:T(8,128)S(1)} %constant_dynamic-slice_fusion.7), channel_id=1, source_target_pairs={{0,2},{2,0},{4,6},{6,4},{1,3},{3,1},{5,7},{7,5},{8,10},{10,8},{12,... | collective-permute-start | bytes 66056 | tf_op jit(solution)/shard_map/ppermute | solution.py:69

commit v8 on v7

--- a/solution.py
+++ b/solution.py
@@ -80,12 +80,15 @@
     for k in first:
         value = halve(value, *stages[k], k)
     rest = [k for k in range(len(stages)) if k not in first]
+    tail = rest[:1] if rest and stages[rest[0]][1] > 1 else []
+    head = [k for k in rest if k not in tail][::-1]
     count = min(3, len(rest), rows)
     cuts = np.array_split(np.arange(rows), count) if count else [np.arange(rows)]
     parts = []
     for p, cut in enumerate(cuts):
         part = value[..., int(cut[0]) : int(cut[-1]) + 1, :]
-        for k in rest[p:] + rest[:p]:
+        turn = p % len(head) if head else 0
+        for k in head[turn:] + head[:turn] + tail:
             part = halve(part, *stages[k], k)
         parts.append(part)
     value = jnp.concatenate(parts, axis=-2) if len(parts) > 1 else parts[0]

time: 76 us -> 73.5 us (0.967)
  waiting for transfers between devices: 16.8 us -> 12.9 us
  starting transfers between devices: 21.9 us -> 23.3 us
    ppermute x13, waiting for transfers between devices: 16 us -> 12 us  [halve(): return keep + lax.ppermute(other, axis, pairs)]
    ppermute x13, starting transfers between devices: 13.3 us -> 14.7 us  [halve(): return keep + lax.ppermute(other, axis, pairs)]
  transfers between devices with their start and end apart: 19 -> 19, of which waited for: 10 -> 8; matrix products, arithmetic and copies ran while one was open for 9% -> 9% of each run, Pallas kernels for 0% -> 0%
where the time goes in v8:
time: 73.5 us; the launch traced here: 73 us
  starting transfers between devices  23.3 us (32%)
  Pallas kernels  21 us (29%)
  waiting for transfers between devices  12.9 us (18%)
  local copies, waits for them, and re-layouts  10.6 us (14%)
  other arithmetic  4.95 us (7%)
    pallas_call x1, Pallas kernels, triangle(): pl.pallas_call(functools.partial(triangle_kernel, block_len), out_shape=j...  21 us
    ppermute x13, starting transfers between devices, halve(): return keep + lax.ppermute(other, axis, pairs)  14.7 us
    ppermute x13, waiting for transfers between devices, halve(): return keep + lax.ppermute(other, axis, pairs)  12 us
    ppermute x3, starting transfers between devices, face_gradients(): lax.ppermute(lax.slice_in_dim(value, length - 1, length, axis=dim), axis,...  4.78 us
    ppermute x3, starting transfers between devices, face_gradients(): after = lax.ppermute(lax.slice_in_dim(value, 0, 1, axis=dim), axis, down)  3.83 us
    another operation x1, local copies, waits for them, and re-layouts, scatter_sum(): value = payload.reshape((2,) * len(stages) + (rows, lanes))  3.77 us
    slice x3, local copies, waits for them, and re-layouts, face_gradients(): after = lax.ppermute(lax.slice_in_dim(value, 0, 1, axis=dim), axis, down)  2.71 us
    add x13, other arithmetic, halve(): return keep + lax.ppermute(other, axis, pairs)  1.5 us
  transfers between devices with their start and end apart: 19, of which 8 were waited for; matrix products, arithmetic and copies ran while one was open for 9% of the time, Pallas kernels for 0%

profile of v8, /device:TPU:0, one launch (start us, length us, event | category | flops | bytes accessed | tf_op | source)
XLA Modules:
  0.0 73.0 jit_solution(11602238574675061812)
XLA Ops:
  0.0 0.8 %fusion.8 = (f32[3,1,8,4,128]{4,3,2,1,0:T(4,128)S(1)}, f32[3,1,8,4,128]{4,3,2,1,0:T(4,128)S(1)}) fusion(f32[3,4,8,4,128]{4,3,2,1,0:T(4,128)} %param.3), kind=kLoop, calls=%fused_computation.49 | loop fusion | bytes 196608 | tf_op jit(solution)/shard_map/slice | solution.py:41
  0.8 3.1 %collective-permute-start.1 = (f32[3,1,8,4,128]{4,3,2,1,0:T(4,128)S(1)}, f32[3,1,8,4,128]{4,3,2,1,0:T(4,128)S(1)}, u32[]{:S(2)}, u32[]{:S(2)}) collective-permute-start(f32[3,1,8,4,128]{4,3,2,1,0:T(4,128)S(1)} %get-tuple-element.12), channel_id=1, source_target_pairs={{0,8},{8,16},{16,24},{24,0},{1,9},{9,17},{17,25},{25,1},{2,10},{10... | collective-permute-start | bytes 147464 | tf_op jit(solution)/shard_map/ppermute | solution.py:40
  3.9 2.1 %collective-permute-start = (f32[3,1,8,4,128]{4,3,2,1,0:T(4,128)S(1)}, f32[3,1,8,4,128]{4,3,2,1,0:T(4,128)S(1)}, u32[]{:S(2)}, u32[]{:S(2)}) collective-permute-start(f32[3,1,8,4,128]{4,3,2,1,0:T(4,128)S(1)} %get-tuple-element.11), channel_id=1, source_target_pairs={{8,0},{16,8},{24,16},{0,24},{9,1},{17,9},{25,17},{1,25},{10,2},{18... | collective-permute-start | bytes 147464 | tf_op jit(solution)/shard_map/ppermute | solution.py:41
  6.0 0.8 %fusion.9 = (f32[3,4,1,4,128]{4,3,2,1,0:T(4,128)S(1)}, f32[3,4,1,4,128]{4,3,2,1,0:T(4,128)S(1)}) fusion(f32[3,4,8,4,128]{4,3,2,1,0:T(4,128)} %param.3), kind=kLoop, calls=%fused_computation.50 | loop fusion | bytes 98304 | tf_op jit(solution)/shard_map/slice | solution.py:41
  6.7 1.6 %collective-permute-start.3 = (f32[3,4,1,4,128]{4,3,2,1,0:T(4,128)S(1)}, f32[3,4,1,4,128]{4,3,2,1,0:T(4,128)S(1)}, u32[]{:S(2)}, u32[]{:S(2)}) collective-permute-start(f32[3,4,1,4,128]{4,3,2,1,0:T(4,128)S(1)} %get-tuple-element.14), channel_id=1, source_target_pairs={{0,2},{2,4},{4,6},{6,0},{1,3},{3,5},{5,7},{7,1},{8,10},{10,12},{12... | collective-permute-start | bytes 73736 | tf_op jit(solution)/shard_map/ppermute | solution.py:40
  8.4 1.3 %collective-permute-start.2 = (f32[3,4,1,4,128]{4,3,2,1,0:T(4,128)S(1)}, f32[3,4,1,4,128]{4,3,2,1,0:T(4,128)S(1)}, u32[]{:S(2)}, u32[]{:S(2)}) collective-permute-start(f32[3,4,1,4,128]{4,3,2,1,0:T(4,128)S(1)} %get-tuple-element.13), channel_id=1, source_target_pairs={{2,0},{4,2},{6,4},{0,6},{3,1},{5,3},{7,5},{1,7},{10,8},{12,10},{14... | collective-permute-start | bytes 73736 | tf_op jit(solution)/shard_map/ppermute | solution.py:41
  9.7 1.1 %fusion.10 = (f32[3,4,8,1,128]{4,3,2,1,0:T(1,128)S(1)}, f32[3,4,8,1,128]{4,3,2,1,0:T(1,128)S(1)}) fusion(f32[3,4,8,4,128]{4,3,2,1,0:T(4,128)} %param.3), kind=kLoop, calls=%fused_computation.51 | loop fusion | bytes 196608 | tf_op jit(solution)/shard_map/slice | solution.py:41
  10.8 0.0 copy-start
  10.8 0.1 collective-permute-start.5
  10.9 0.8 %select_reduce_fusion = s32[32]{0:T(128)S(1)} fusion(s32[32]{0:T(128)} %param.5), kind=kLoop, calls=%fused_computation.31 | loop fusion | flops 3040 | bytes 256 | tf_op jit(solution)/shard_map/reduce_sum | solution.py:169
  11.7 0.7 broadcast_multiply_fusion
  12.4 0.1 copy.17
  12.5 0.1 mul.32
  12.6 1.0 %fusion.6 = f32[3,64,128]{1,2,0:T(8,128)S(1)} fusion(f32[3,128,128]{2,1,0:T(8,128)} %bitcast.12, f32[128]{0:T(128)S(1)} %mul.32), kind=kLoop, calls=%fused_computation.15 | loop fusion | flops 24576 | bytes 197120 | tf_op jit(solution)/shard_map/transpose | solution.py:164
  13.6 0.5 broadcast_clamp_fusion.slot_ref
  14.1 0.1 copy.18
  14.2 0.1 tile.4
  14.3 0.9 %tile.10.w_ref = f32[3,64,384]{2,1,0:T(8,128)} reshape(f32[3,64,3,128]{3,2,1,0:T(4,128)S(1)} %tile.4) | data formatting | bytes 589824 | tf_op jit(solution)/shard_map/tile | solution.py:164
  15.2 0.0 collective-permute-done.5
  15.2 0.5 collective-permute-start.4
  15.7 0.8 %collective-permute-done.4 = f32[3,4,8,1,128]{4,3,2,1,0:T(1,128)S(1)} collective-permute-done((f32[3,4,8,1,128]{4,3,2,1,0:T(1,128)S(1)}, f32[3,4,8,1,128]{4,3,2,1,0:T(1,128)S(1)}, u32[]{:S(2)}, u32[]{:S(2)}) %collective-permute-start.4) | collective-permute-done | bytes 49184 | tf_op jit(solution)/shard_map/ppermute | solution.py:41
  16.6 0.0 collective-permute-done.3
  16.6 0.0 collective-permute-done.2
  16.6 0.0 collective-permute-done.1
  16.6 0.0 collective-permute-done
  16.6 0.0 copy-done
  16.6 0.3 fusion.5
  17.0 1.1 %copy.19.g_ref = f32[3,128,384]{2,1,0:T(8,128)} copy(f32[3,128,384]{1,2,0:T(8,128)S(1)} %bitcast.14) | data formatting | bytes 1179648 | tf_op jit(solution)/shard_map/reshape | solution.py:165
  18.0 21.0 %shard_map.37 = f32[32,64,384]{2,1,0:T(8,128)} custom-call(s32[32]{0:T(128)} %broadcast_clamp_fusion.slot_ref, f32[3,64,384]{2,1,0:T(8,128)} %tile.10.w_ref, f32[3,128,384]{2,1,0:T(8,128)} %copy.19.g_ref, f32[384,128]{1,0:T(8,128)} %bitcast.13), custom_call_target="tpu_custom_call" | custom-call | tf_op jit(solution)/shard_map/pallas_call | solution.py:141
  39.0 3.8 %reshape_reshape.7 = f32[2,2,2,2,2,129,128]{6,5,4,3,2,1,0:T(8,128)S(1)} reshape(f32[32,64,258]{2,1,0:T(8,128)} %bitcast.11) | data formatting | bytes 4227072 | tf_op jit(solution)/shard_map/reshape;reshape | solution.py:78
  42.8 0.1 constant_dynamic-slice_fusion.11
  42.9 0.5 copy.20
  43.5 0.4 collective-permute-start.6
  43.9 2.5 %collective-permute-done.6 = f32[2,2,2,2,1,129,128]{6,3,5,4,2,1,0:T(2,128)} collective-permute-done((f32[2,2,2,2,1,129,128]{6,3,5,4,2,1,0:T(2,128)S(1)}, f32[2,2,2,2,1,129,128]{6,3,5,4,2,1,0:T(2,128)}, u32[]{:S(2)}, u32[]{:S(2)}) %collective-permute-start.6) | collective-permute-done | bytes 1056800 | tf_op jit(solution)/shard_map/ppermute | solution.py:69
  46.3 1.3 %copy_add_fusion = f32[2,2,2,2,1,129,128]{6,5,4,3,2,1,0:T(8,128)S(1)} fusion(f32[2,2,2,2,1,129,128]{6,3,5,4,2,1,0:T(2,128)} %collective-permute-done.6, f32[2,2,2,2,2,129,128]{6,5,4,3,2,1,0:T(8,128)S(1)} %reshape_reshape.7, s32[]{:T(128)S(6)} %select_n.138), kind=kLoop, calls=%fused_computation | loop fusion | flops 264192 | bytes 3170308 | tf_op jit(solution)/shard_map/add | solution.py:69
  47.7 0.1 fusion.7
  47.8 0.1 collective-permute-start.15
  47.9 1.8 %collective-permute-start.11 = (f32[2,2,1,2,1,43,128]{6,5,4,3,2,1,0:T(8,128)S(1)}, f32[2,2,1,2,1,43,128]{6,5,4,3,2,1,0:T(8,128)S(1)}, u32[]{:S(2)}, u32[]{:S(2)}) collective-permute-start(f32[2,2,1,2,1,43,128]{6,5,4,3,2,1,0:T(8,128)S(1)} %constant_dynamic-slice_fusion.6), channel_id=1, source_target_pairs={{0,4},{2,6},{4,0},{6,2},{1,5},{3,7},{5,1},{7,3},{8,12},{10,14},{12... | collective-permute-start | bytes 528392 | tf_op jit(solution)/shard_map/ppermute | solution.py:69
  49.7 0.7 collective-permute-start.7
  50.4 4.7 %collective-permute-done.15 = f32[2,1,2,2,1,43,128]{6,5,4,3,2,1,0:T(8,128)S(1)} collective-permute-done((f32[2,1,2,2,1,43,128]{6,5,4,3,2,1,0:T(8,128)S(1)}, f32[2,1,2,2,1,43,128]{6,5,4,3,2,1,0:T(8,128)S(1)}, u32[]{:S(2)}, u32[]{:S(2)}) %collective-permute-start.15) | collective-permute-done | bytes 176160 | tf_op jit(solution)/shard_map/ppermute | solution.py:69
  55.2 0.8 %collective-permute-start.16 = (f32[2,1,2,1,1,43,128]{6,5,4,3,2,1,0:T(8,128)S(1)}, f32[2,1,2,1,1,43,128]{6,5,4,3,2,1,0:T(8,128)S(1)}, u32[]{:S(2)}, u32[]{:S(2)}) collective-permute-start(f32[2,1,2,1,1,43,128]{6,5,4,3,2,1,0:T(8,128)S(1)} %constant_dynamic-slice_fusion.1), channel_id=1, source_target_pairs={{0,2},{2,0},{4,6},{6,4},{1,3},{3,1},{5,7},{7,5},{8,10},{10,8},{12,... | collective-permute-start | bytes 264200 | tf_op jit(solution)/shard_map/ppermute | solution.py:69
  56.0 0.0 collective-permute-done.11
  56.0 1.0 %collective-permute-start.12 = (f32[2,1,1,2,1,43,128]{6,5,4,3,2,1,0:T(8,128)S(1)}, f32[2,1,1,2,1,43,128]{6,5,4,3,2,1,0:T(8,128)S(1)}, u32[]{:S(2)}, u32[]{:S(2)}) collective-permute-start(f32[2,1,1,2,1,43,128]{6,5,4,3,2,1,0:T(8,128)S(1)} %constant_dynamic-slice_fusion.5), channel_id=1, source_target_pairs={{0,8},{8,0},{16,24},{24,16},{1,9},{9,1},{17,25},{25,17},{2,10},{10... | collective-permute-start | bytes 264200 | tf_op jit(solution)/shard_map/ppermute | solution.py:69
  57.0 0.0 collective-permute-done.7
  57.1 1.7 %collective-permute-start.8 = (f32[2,2,1,1,1,43,128]{6,5,4,3,2,1,0:T(8,128)S(1)}, f32[2,2,1,1,1,43,128]{6,5,4,3,2,1,0:T(8,128)S(1)}, u32[]{:S(2)}, u32[]{:S(2)}) collective-permute-start(f32[2,2,1,1,1,43,128]{6,5,4,3,2,1,0:T(8,128)S(1)} %constant_dynamic-slice_fusion.9), channel_id=1, source_target_pairs={{0,4},{2,6},{4,0},{6,2},{1,5},{3,7},{5,1},{7,3},{8,12},{10,14},{12... | collective-permute-start | bytes 264200 | tf_op jit(solution)/shard_map/ppermute | solution.py:69
  58.8 1.0 %collective-permute-done.16 = f32[2,1,2,1,1,43,128]{6,5,4,3,2,1,0:T(8,128)S(1)} collective-permute-done((f32[2,1,2,1,1,43,128]{6,5,4,3,2,1,0:T(8,128)S(1)}, f32[2,1,2,1,1,43,128]{6,5,4,3,2,1,0:T(8,128)S(1)}, u32[]{:S(2)}, u32[]{:S(2)}) %collective-permute-start.16) | collective-permute-done | bytes 88096 | tf_op jit(solution)/shard_map/ppermute | solution.py:69
  59.9 1.7 %collective-permute-start.17 = (f32[2,1,1,1,1,43,128]{6,5,4,3,2,1,0:T(8,128)S(1)}, f32[2,1,1,1,1,43,128]{6,5,4,3,2,1,0:T(8,128)S(1)}, u32[]{:S(2)}, u32[]{:S(2)}) collective-permute-start(f32[2,1,1,1,1,43,128]{6,5,4,3,2,1,0:T(8,128)S(1)} %constant_dynamic-slice_fusion), channel_id=1, source_target_pairs={{0,4},{2,6},{4,0},{6,2},{1,5},{3,7},{5,1},{7,3},{8,12},{10,14},{12... | collective-permute-start | bytes 132104 | tf_op jit(solution)/shard_map/ppermute | solution.py:69
  61.6 0.0 collective-permute-done.12
  61.7 0.7 collective-permute-start.13
  62.3 0.0 collective-permute-done.8
  62.4 1.9 %collective-permute-start.9 = (f32[2,1,1,1,1,43,128]{6,5,4,3,2,1,0:T(8,128)S(1)}, f32[2,1,1,1,1,43,128]{6,5,4,3,2,1,0:T(8,128)S(1)}, u32[]{:S(2)}, u32[]{:S(2)}) collective-permute-start(f32[2,1,1,1,1,43,128]{6,5,4,3,2,1,0:T(8,128)S(1)} %constant_dynamic-slice_fusion.8), channel_id=1, source_target_pairs={{0,8},{8,0},{16,24},{24,16},{1,9},{9,1},{17,25},{25,17},{2,10},{10... | collective-permute-start | bytes 132104 | tf_op jit(solution)/shard_map/ppermute | solution.py:69
  64.2 0.0 collective-permute-done.17
  64.2 0.9 %collective-permute-start.18 = (f32[1,1,1,1,1,43,128]{6,5,4,3,2,1,0:T(8,128)S(1)}, f32[1,1,1,1,1,43,128]{6,5,4,3,2,1,0:T(8,128)S(1)}, u32[]{:S(2)}, u32[]{:S(2)}) collective-permute-start(f32[1,1,1,1,1,43,128]{6,5,4,3,2,1,0:T(8,128)S(1)} %constant_dynamic-slice_fusion.12), channel_id=1, source_target_pairs={{0,16},{8,24},{16,0},{24,8},{1,17},{9,25},{17,1},{25,9},{2,18},{10... | collective-permute-start | bytes 66056 | tf_op jit(solution)/shard_map/ppermute | solution.py:69
  65.1 0.7 collective-permute-done.13
  65.8 1.5 %collective-permute-start.14 = (f32[1,1,1,1,1,43,128]{6,5,4,3,2,1,0:T(8,128)S(1)}, f32[1,1,1,1,1,43,128]{6,5,4,3,2,1,0:T(8,128)S(1)}, u32[]{:S(2)}, u32[]{:S(2)}) collective-permute-start(f32[1,1,1,1,1,43,128]{6,5,4,3,2,1,0:T(8,128)S(1)} %constant_dynamic-slice_fusion.3), channel_id=1, source_target_pairs={{0,16},{8,24},{16,0},{24,8},{1,17},{9,25},{17,1},{25,9},{2,18},{10... | collective-permute-start | bytes 66056 | tf_op jit(solution)/shard_map/ppermute | solution.py:69
  67.3 0.0 collective-permute-done.9
  67.4 1.6 %collective-permute-start.10 = (f32[1,1,1,1,1,43,128]{6,5,4,3,2,1,0:T(8,128)S(1)}, f32[1,1,1,1,1,43,128]{6,5,4,3,2,1,0:T(8,128)S(1)}, u32[]{:S(2)}, u32[]{:S(2)}) collective-permute-start(f32[1,1,1,1,1,43,128]{6,5,4,3,2,1,0:T(8,128)S(1)} %constant_dynamic-slice_fusion.7), channel_id=1, source_target_pairs={{0,16},{8,24},{16,0},{24,8},{1,17},{9,25},{17,1},{25,9},{2,18},{10... | collective-permute-start | bytes 66056 | tf_op jit(solution)/shard_map/ppermute | solution.py:69
  68.9 0.3 collective-permute-done.18
  69.2 1.4 %collective-permute-done.14 = f32[1,1,1,1,1,43,128]{6,5,4,3,2,1,0:T(8,128)S(1)} collective-permute-done((f32[1,1,1,1,1,43,128]{6,5,4,3,2,1,0:T(8,128)S(1)}, f32[1,1,1,1,1,43,128]{6,5,4,3,2,1,0:T(8,128)S(1)}, u32[]{:S(2)}, u32[]{:S(2)}) %collective-permute-start.14) | collective-permute-done | bytes 22048 | tf_op jit(solution)/shard_map/ppermute | solution.py:69
  70.6 1.5 %collective-permute-done.10 = f32[1,1,1,1,1,43,128]{6,5,4,3,2,1,0:T(8,128)S(1)} collective-permute-done((f32[1,1,1,1,1,43,128]{6,5,4,3,2,1,0:T(8,128)S(1)}, f32[1,1,1,1,1,43,128]{6,5,4,3,2,1,0:T(8,128)S(1)}, u32[]{:S(2)}, u32[]{:S(2)}) %collective-permute-start.10) | collective-permute-done | bytes 22048 | tf_op jit(solution)/shard_map/ppermute | solution.py:69
  72.2 0.8 %reshape_reshape_reshape.3 = f32[64,258]{1,0:T(8,128)} reshape(f32[1,1,1,1,1,129,128]{6,5,4,3,2,1,0:T(8,128)S(1)} %pad_maximum_fusion.7) | data formatting | bytes 132096 | tf_op jit(solution)/shard_map/reshape;reshape;reshape | solution.py:177
  (28 shorter events, 0.5 us)
Async XLA Ops:
  0.8 15.8 %collective-permute-start.1 = (f32[3,1,8,4,128]{4,3,2,1,0:T(4,128)S(1)}, f32[3,1,8,4,128]{4,3,2,1,0:T(4,128)S(1)}, u32[]{:S(2)}, u32[]{:S(2)}) collective-permute-start(f32[3,1,8,4,128]{4,3,2,1,0:T(4,128)S(1)} %get-tuple-element.12), channel_id=1, source_target_pairs={{0,8},{8,16},{16,24},{24,0},{1,9},{9,17},{17,25},{25,1},{2,10},{10... | collective-permute-start | bytes 147464 | tf_op jit(solution)/shard_map/ppermute | solution.py:40
  3.9 12.7 %collective-permute-start = (f32[3,1,8,4,128]{4,3,2,1,0:T(4,128)S(1)}, f32[3,1,8,4,128]{4,3,2,1,0:T(4,128)S(1)}, u32[]{:S(2)}, u32[]{:S(2)}) collective-permute-start(f32[3,1,8,4,128]{4,3,2,1,0:T(4,128)S(1)} %get-tuple-element.11), channel_id=1, source_target_pairs={{8,0},{16,8},{24,16},{0,24},{9,1},{17,9},{25,17},{1,25},{10,2},{18... | collective-permute-start | bytes 147464 | tf_op jit(solution)/shard_map/ppermute | solution.py:41
  6.7 9.8 %collective-permute-start.3 = (f32[3,4,1,4,128]{4,3,2,1,0:T(4,128)S(1)}, f32[3,4,1,4,128]{4,3,2,1,0:T(4,128)S(1)}, u32[]{:S(2)}, u32[]{:S(2)}) collective-permute-start(f32[3,4,1,4,128]{4,3,2,1,0:T(4,128)S(1)} %get-tuple-element.14), channel_id=1, source_target_pairs={{0,2},{2,4},{4,6},{6,0},{1,3},{3,5},{5,7},{7,1},{8,10},{10,12},{12... | collective-permute-start | bytes 73736 | tf_op jit(solution)/shard_map/ppermute | solution.py:40
  8.4 8.2 %collective-permute-start.2 = (f32[3,4,1,4,128]{4,3,2,1,0:T(4,128)S(1)}, f32[3,4,1,4,128]{4,3,2,1,0:T(4,128)S(1)}, u32[]{:S(2)}, u32[]{:S(2)}) collective-permute-start(f32[3,4,1,4,128]{4,3,2,1,0:T(4,128)S(1)} %get-tuple-element.13), channel_id=1, source_target_pairs={{2,0},{4,2},{6,4},{0,6},{3,1},{5,3},{7,5},{1,7},{10,8},{12,10},{14... | collective-permute-start | bytes 73736 | tf_op jit(solution)/shard_map/ppermute | solution.py:41
  10.8 5.8 %copy-start = (f32[3,4,8,4,128]{4,3,2,1,0:T(4,128)S(1)}, f32[3,4,8,4,128]{4,3,2,1,0:T(4,128)}, u32[]{:S(2)}) copy-start(f32[3,4,8,4,128]{4,3,2,1,0:T(4,128)} %param.3) | copy-start | bytes 589828
  10.8 4.4 %collective-permute-start.5 = (f32[3,4,8,1,128]{4,3,2,1,0:T(1,128)S(1)}, f32[3,4,8,1,128]{4,3,2,1,0:T(1,128)S(1)}, u32[]{:S(2)}, u32[]{:S(2)}) collective-permute-start(f32[3,4,8,1,128]{4,3,2,1,0:T(1,128)S(1)} %get-tuple-element.16), channel_id=1, source_target_pairs={{0,1},{1,0},{2,3},{3,2},{4,5},{5,4},{6,7},{7,6},{8,9},{9,8},{10,11... | collective-permute-start | bytes 147464 | tf_op jit(solution)/shard_map/ppermute | solution.py:40
  15.2 1.3 %collective-permute-start.4 = (f32[3,4,8,1,128]{4,3,2,1,0:T(1,128)S(1)}, f32[3,4,8,1,128]{4,3,2,1,0:T(1,128)S(1)}, u32[]{:S(2)}, u32[]{:S(2)}) collective-permute-start(f32[3,4,8,1,128]{4,3,2,1,0:T(1,128)S(1)} %get-tuple-element.15), channel_id=1, source_target_pairs={{1,0},{0,1},{3,2},{2,3},{5,4},{4,5},{7,6},{6,7},{9,8},{8,9},{11,10... | collective-permute-start | bytes 147464 | tf_op jit(solution)/shard_map/ppermute | solution.py:41
  43.5 2.9 %collective-permute-start.6 = (f32[2,2,2,2,1,129,128]{6,3,5,4,2,1,0:T(2,128)S(1)}, f32[2,2,2,2,1,129,128]{6,3,5,4,2,1,0:T(2,128)}, u32[]{:S(2)}, u32[]{:S(2)}) collective-permute-start(f32[2,2,2,2,1,129,128]{6,3,5,4,2,1,0:T(2,128)S(1)} %copy.20), channel_id=1, source_target_pairs={{0,1},{1,0},{2,3},{3,2},{4,5},{5,4},{6,7},{7,6},{8,9},{9,8},{10,11... | collective-permute-start | bytes 3170312 | tf_op jit(solution)/shard_map/ppermute | solution.py:69
  47.8 7.3 %collective-permute-start.15 = (f32[2,1,2,2,1,43,128]{6,5,4,3,2,1,0:T(8,128)S(1)}, f32[2,1,2,2,1,43,128]{6,5,4,3,2,1,0:T(8,128)S(1)}, u32[]{:S(2)}, u32[]{:S(2)}) collective-permute-start(f32[2,1,2,2,1,43,128]{6,5,4,3,2,1,0:T(8,128)S(1)} %constant_dynamic-slice_fusion.2), channel_id=1, source_target_pairs={{0,8},{8,0},{16,24},{24,16},{1,9},{9,1},{17,25},{25,17},{2,10},{10... | collective-permute-start | bytes 528392 | tf_op jit(solution)/shard_map/ppermute | solution.py:69
  47.9 8.0 %collective-permute-start.11 = (f32[2,2,1,2,1,43,128]{6,5,4,3,2,1,0:T(8,128)S(1)}, f32[2,2,1,2,1,43,128]{6,5,4,3,2,1,0:T(8,128)S(1)}, u32[]{:S(2)}, u32[]{:S(2)}) collective-permute-start(f32[2,2,1,2,1,43,128]{6,5,4,3,2,1,0:T(8,128)S(1)} %constant_dynamic-slice_fusion.6), channel_id=1, source_target_pairs={{0,4},{2,6},{4,0},{6,2},{1,5},{3,7},{5,1},{7,3},{8,12},{10,14},{12... | collective-permute-start | bytes 528392 | tf_op jit(solution)/shard_map/ppermute | solution.py:69
  49.7 7.3 %collective-permute-start.7 = (f32[2,2,2,1,1,43,128]{6,5,4,3,2,1,0:T(8,128)S(1)}, f32[2,2,2,1,1,43,128]{6,5,4,3,2,1,0:T(8,128)S(1)}, u32[]{:S(2)}, u32[]{:S(2)}) collective-permute-start(f32[2,2,2,1,1,43,128]{6,5,4,3,2,1,0:T(8,128)S(1)} %constant_dynamic-slice_fusion.10), channel_id=1, source_target_pairs={{0,2},{2,0},{4,6},{6,4},{1,3},{3,1},{5,7},{7,5},{8,10},{10,8},{12,... | collective-permute-start | bytes 528392 | tf_op jit(solution)/shard_map/ppermute | solution.py:69
  55.2 4.7 %collective-permute-start.16 = (f32[2,1,2,1,1,43,128]{6,5,4,3,2,1,0:T(8,128)S(1)}, f32[2,1,2,1,1,43,128]{6,5,4,3,2,1,0:T(8,128)S(1)}, u32[]{:S(2)}, u32[]{:S(2)}) collective-permute-start(f32[2,1,2,1,1,43,128]{6,5,4,3,2,1,0:T(8,128)S(1)} %constant_dynamic-slice_fusion.1), channel_id=1, source_target_pairs={{0,2},{2,0},{4,6},{6,4},{1,3},{3,1},{5,7},{7,5},{8,10},{10,8},{12,... | collective-permute-start | bytes 264200 | tf_op jit(solution)/shard_map/ppermute | solution.py:69
  56.0 5.6 %collective-permute-start.12 = (f32[2,1,1,2,1,43,128]{6,5,4,3,2,1,0:T(8,128)S(1)}, f32[2,1,1,2,1,43,128]{6,5,4,3,2,1,0:T(8,128)S(1)}, u32[]{:S(2)}, u32[]{:S(2)}) collective-permute-start(f32[2,1,1,2,1,43,128]{6,5,4,3,2,1,0:T(8,128)S(1)} %constant_dynamic-slice_fusion.5), channel_id=1, source_target_pairs={{0,8},{8,0},{16,24},{24,16},{1,9},{9,1},{17,25},{25,17},{2,10},{10... | collective-permute-start | bytes 264200 | tf_op jit(solution)/shard_map/ppermute | solution.py:69
  57.1 5.2 %collective-permute-start.8 = (f32[2,2,1,1,1,43,128]{6,5,4,3,2,1,0:T(8,128)S(1)}, f32[2,2,1,1,1,43,128]{6,5,4,3,2,1,0:T(8,128)S(1)}, u32[]{:S(2)}, u32[]{:S(2)}) collective-permute-start(f32[2,2,1,1,1,43,128]{6,5,4,3,2,1,0:T(8,128)S(1)} %constant_dynamic-slice_fusion.9), channel_id=1, source_target_pairs={{0,4},{2,6},{4,0},{6,2},{1,5},{3,7},{5,1},{7,3},{8,12},{10,14},{12... | collective-permute-start | bytes 264200 | tf_op jit(solution)/shard_map/ppermute | solution.py:69
  59.9 4.3 %collective-permute-start.17 = (f32[2,1,1,1,1,43,128]{6,5,4,3,2,1,0:T(8,128)S(1)}, f32[2,1,1,1,1,43,128]{6,5,4,3,2,1,0:T(8,128)S(1)}, u32[]{:S(2)}, u32[]{:S(2)}) collective-permute-start(f32[2,1,1,1,1,43,128]{6,5,4,3,2,1,0:T(8,128)S(1)} %constant_dynamic-slice_fusion), channel_id=1, source_target_pairs={{0,4},{2,6},{4,0},{6,2},{1,5},{3,7},{5,1},{7,3},{8,12},{10,14},{12... | collective-permute-start | bytes 132104 | tf_op jit(solution)/shard_map/ppermute | solution.py:69
  61.7 4.2 %collective-permute-start.13 = (f32[2,1,1,1,1,43,128]{6,5,4,3,2,1,0:T(8,128)S(1)}, f32[2,1,1,1,1,43,128]{6,5,4,3,2,1,0:T(8,128)S(1)}, u32[]{:S(2)}, u32[]{:S(2)}) collective-permute-start(f32[2,1,1,1,1,43,128]{6,5,4,3,2,1,0:T(8,128)S(1)} %constant_dynamic-slice_fusion.4), channel_id=1, source_target_pairs={{0,2},{2,0},{4,6},{6,4},{1,3},{3,1},{5,7},{7,5},{8,10},{10,8},{12,... | collective-permute-start | bytes 132104 | tf_op jit(solution)/shard_map/ppermute | solution.py:69
  62.4 5.0 %collective-permute-start.9 = (f32[2,1,1,1,1,43,128]{6,5,4,3,2,1,0:T(8,128)S(1)}, f32[2,1,1,1,1,43,128]{6,5,4,3,2,1,0:T(8,128)S(1)}, u32[]{:S(2)}, u32[]{:S(2)}) collective-permute-start(f32[2,1,1,1,1,43,128]{6,5,4,3,2,1,0:T(8,128)S(1)} %constant_dynamic-slice_fusion.8), channel_id=1, source_target_pairs={{0,8},{8,0},{16,24},{24,16},{1,9},{9,1},{17,25},{25,17},{2,10},{10... | collective-permute-start | bytes 132104 | tf_op jit(solution)/shard_map/ppermute | solution.py:69
  64.2 5.0 %collective-permute-start.18 = (f32[1,1,1,1,1,43,128]{6,5,4,3,2,1,0:T(8,128)S(1)}, f32[1,1,1,1,1,43,128]{6,5,4,3,2,1,0:T(8,128)S(1)}, u32[]{:S(2)}, u32[]{:S(2)}) collective-permute-start(f32[1,1,1,1,1,43,128]{6,5,4,3,2,1,0:T(8,128)S(1)} %constant_dynamic-slice_fusion.12), channel_id=1, source_target_pairs={{0,16},{8,24},{16,0},{24,8},{1,17},{9,25},{17,1},{25,9},{2,18},{10... | collective-permute-start | bytes 66056 | tf_op jit(solution)/shard_map/ppermute | solution.py:69
  65.8 4.8 %collective-permute-start.14 = (f32[1,1,1,1,1,43,128]{6,5,4,3,2,1,0:T(8,128)S(1)}, f32[1,1,1,1,1,43,128]{6,5,4,3,2,1,0:T(8,128)S(1)}, u32[]{:S(2)}, u32[]{:S(2)}) collective-permute-start(f32[1,1,1,1,1,43,128]{6,5,4,3,2,1,0:T(8,128)S(1)} %constant_dynamic-slice_fusion.3), channel_id=1, source_target_pairs={{0,16},{8,24},{16,0},{24,8},{1,17},{9,25},{17,1},{25,9},{2,18},{10... | collective-permute-start | bytes 66056 | tf_op jit(solution)/shard_map/ppermute | solution.py:69
  67.4 4.8 %collective-permute-start.10 = (f32[1,1,1,1,1,43,128]{6,5,4,3,2,1,0:T(8,128)S(1)}, f32[1,1,1,1,1,43,128]{6,5,4,3,2,1,0:T(8,128)S(1)}, u32[]{:S(2)}, u32[]{:S(2)}) collective-permute-start(f32[1,1,1,1,1,43,128]{6,5,4,3,2,1,0:T(8,128)S(1)} %constant_dynamic-slice_fusion.7), channel_id=1, source_target_pairs={{0,16},{8,24},{16,0},{24,8},{1,17},{9,25},{17,1},{25,9},{2,18},{10... | collective-permute-start | bytes 66056 | tf_op jit(solution)/shard_map/ppermute | solution.py:69

commit v9 on v8

--- a/solution.py
+++ b/solution.py
@@ -109,7 +109,7 @@
             zt = zt + w_ref[2, pl.ds(i, 1), :] * g_ref[2]
             slabs.append(zt)
         zt = jnp.concatenate(slabs, axis=0)
-        part = jnp.dot(zt, m_ref[...], precision=lax.Precision.HIGHEST, preferred_element_type=jnp.float32)
+        part = jnp.dot(zt, m_ref[...], precision=lax.Precision.HIGH, preferred_element_type=jnp.float32)
         for u in range(group):
             piece = part[u * width : (u + 1) * width, :]
             start = pl.multiple_of((step * group + u) * width, width)

time: 73.5 us -> 68 us (0.925)
  Pallas kernels: 21 us -> 15.6 us
    pallas_call x1, Pallas kernels: 21 us -> 15.6 us  [triangle(): pl.pallas_call(functools.partial(triangle_kernel, block_len), out_shape=j...]
  transfers between devices with their start and end apart: 19 -> 19, of which waited for: 8 -> 8; matrix products, arithmetic and copies ran while one was open for 9% -> 10% of each run, Pallas kernels for 0% -> 0%
where the time goes in v9:
time: 68 us; the launch traced here: 67.5 us
  starting transfers between devices  23.3 us (34%)
  Pallas kernels  15.6 us (23%)
  waiting for transfers between devices  12.9 us (19%)
  local copies, waits for them, and re-layouts  10.6 us (16%)
  other arithmetic  4.95 us (7%)
    pallas_call x1, Pallas kernels, triangle(): pl.pallas_call(functools.partial(triangle_kernel, block_len), out_shape=j...  15.6 us
    ppermute x13, starting transfers between devices, halve(): return keep + lax.ppermute(other, axis, pairs)  14.7 us
    ppermute x13, waiting for transfers between devices, halve(): return keep + lax.ppermute(other, axis, pairs)  12 us
    ppermute x3, starting transfers between devices, face_gradients(): lax.ppermute(lax.slice_in_dim(value, length - 1, length, axis=dim), axis,...  4.78 us
    ppermute x3, starting transfers between devices, face_gradients(): after = lax.ppermute(lax.slice_in_dim(value, 0, 1, axis=dim), axis, down)  3.83 us
    another operation x1, local copies, waits for them, and re-layouts, scatter_sum(): value = payload.reshape((2,) * len(stages) + (rows, lanes))  3.77 us
    slice x3, local copies, waits for them, and re-layouts, face_gradients(): after = lax.ppermute(lax.slice_in_dim(value, 0, 1, axis=dim), axis, down)  2.71 us
    add x13, other arithmetic, halve(): return keep + lax.ppermute(other, axis, pairs)  1.5 us
  transfers between devices with their start and end apart: 19, of which 8 were waited for; matrix products, arithmetic and copies ran while one was open for 10% of the time, Pallas kernels for 0%

profile of v9, /device:TPU:0, one launch (start us, length us, event | category | flops | bytes accessed | tf_op | source)
XLA Modules:
  0.0 67.5 jit_solution(5984736779315764965)
XLA Ops:
  0.0 0.8 %fusion.8 = (f32[3,1,8,4,128]{4,3,2,1,0:T(4,128)S(1)}, f32[3,1,8,4,128]{4,3,2,1,0:T(4,128)S(1)}) fusion(f32[3,4,8,4,128]{4,3,2,1,0:T(4,128)} %param.3), kind=kLoop, calls=%fused_computation.49 | loop fusion | bytes 196608 | tf_op jit(solution)/shard_map/slice | solution.py:41
  0.8 3.1 %collective-permute-start.1 = (f32[3,1,8,4,128]{4,3,2,1,0:T(4,128)S(1)}, f32[3,1,8,4,128]{4,3,2,1,0:T(4,128)S(1)}, u32[]{:S(2)}, u32[]{:S(2)}) collective-permute-start(f32[3,1,8,4,128]{4,3,2,1,0:T(4,128)S(1)} %get-tuple-element.12), channel_id=1, source_target_pairs={{0,8},{8,16},{16,24},{24,0},{1,9},{9,17},{17,25},{25,1},{2,10},{10... | collective-permute-start | bytes 147464 | tf_op jit(solution)/shard_map/ppermute | solution.py:40
  3.9 2.1 %collective-permute-start = (f32[3,1,8,4,128]{4,3,2,1,0:T(4,128)S(1)}, f32[3,1,8,4,128]{4,3,2,1,0:T(4,128)S(1)}, u32[]{:S(2)}, u32[]{:S(2)}) collective-permute-start(f32[3,1,8,4,128]{4,3,2,1,0:T(4,128)S(1)} %get-tuple-element.11), channel_id=1, source_target_pairs={{8,0},{16,8},{24,16},{0,24},{9,1},{17,9},{25,17},{1,25},{10,2},{18... | collective-permute-start | bytes 147464 | tf_op jit(solution)/shard_map/ppermute | solution.py:41
  6.0 0.8 %fusion.9 = (f32[3,4,1,4,128]{4,3,2,1,0:T(4,128)S(1)}, f32[3,4,1,4,128]{4,3,2,1,0:T(4,128)S(1)}) fusion(f32[3,4,8,4,128]{4,3,2,1,0:T(4,128)} %param.3), kind=kLoop, calls=%fused_computation.50 | loop fusion | bytes 98304 | tf_op jit(solution)/shard_map/slice | solution.py:41
  6.7 1.6 %collective-permute-start.3 = (f32[3,4,1,4,128]{4,3,2,1,0:T(4,128)S(1)}, f32[3,4,1,4,128]{4,3,2,1,0:T(4,128)S(1)}, u32[]{:S(2)}, u32[]{:S(2)}) collective-permute-start(f32[3,4,1,4,128]{4,3,2,1,0:T(4,128)S(1)} %get-tuple-element.14), channel_id=1, source_target_pairs={{0,2},{2,4},{4,6},{6,0},{1,3},{3,5},{5,7},{7,1},{8,10},{10,12},{12... | collective-permute-start | bytes 73736 | tf_op jit(solution)/shard_map/ppermute | solution.py:40
  8.4 1.3 %collective-permute-start.2 = (f32[3,4,1,4,128]{4,3,2,1,0:T(4,128)S(1)}, f32[3,4,1,4,128]{4,3,2,1,0:T(4,128)S(1)}, u32[]{:S(2)}, u32[]{:S(2)}) collective-permute-start(f32[3,4,1,4,128]{4,3,2,1,0:T(4,128)S(1)} %get-tuple-element.13), channel_id=1, source_target_pairs={{2,0},{4,2},{6,4},{0,6},{3,1},{5,3},{7,5},{1,7},{10,8},{12,10},{14... | collective-permute-start | bytes 73736 | tf_op jit(solution)/shard_map/ppermute | solution.py:41
  9.7 1.1 %fusion.10 = (f32[3,4,8,1,128]{4,3,2,1,0:T(1,128)S(1)}, f32[3,4,8,1,128]{4,3,2,1,0:T(1,128)S(1)}) fusion(f32[3,4,8,4,128]{4,3,2,1,0:T(4,128)} %param.3), kind=kLoop, calls=%fused_computation.51 | loop fusion | bytes 196608 | tf_op jit(solution)/shard_map/slice | solution.py:41
  10.8 0.0 copy-start
  10.8 0.1 collective-permute-start.5
  10.9 0.8 %select_reduce_fusion = s32[32]{0:T(128)S(1)} fusion(s32[32]{0:T(128)} %param.5), kind=kLoop, calls=%fused_computation.31 | loop fusion | flops 3040 | bytes 256 | tf_op jit(solution)/shard_map/reduce_sum | solution.py:169
  11.7 0.7 %broadcast_multiply_fusion = f32[4,8,4]{1,2,0:T(4,128)S(1)} fusion(f32[4,8,4]{1,2,0:T(4,128)} %param.4), kind=kLoop, calls=%fused_computation.46 | loop fusion | flops 128 | bytes 1024 | tf_op jit(solution)/shard_map/mul | solution.py:163
  12.4 0.1 copy.17
  12.5 0.1 mul.32
  12.6 1.0 %fusion.6 = f32[3,64,128]{1,2,0:T(8,128)S(1)} fusion(f32[3,128,128]{2,1,0:T(8,128)} %bitcast.12, f32[128]{0:T(128)S(1)} %mul.32), kind=kLoop, calls=%fused_computation.15 | loop fusion | flops 24576 | bytes 197120 | tf_op jit(solution)/shard_map/transpose | solution.py:164
  13.6 0.5 broadcast_clamp_fusion.slot_ref
  14.1 0.1 copy.18
  14.2 0.1 tile.4
  14.3 0.9 %tile.10.w_ref = f32[3,64,384]{2,1,0:T(8,128)} reshape(f32[3,64,3,128]{3,2,1,0:T(4,128)S(1)} %tile.4) | data formatting | bytes 589824 | tf_op jit(solution)/shard_map/tile | solution.py:164
  15.2 0.0 collective-permute-done.5
  15.2 0.5 collective-permute-start.4
  15.7 0.8 %collective-permute-done.4 = f32[3,4,8,1,128]{4,3,2,1,0:T(1,128)S(1)} collective-permute-done((f32[3,4,8,1,128]{4,3,2,1,0:T(1,128)S(1)}, f32[3,4,8,1,128]{4,3,2,1,0:T(1,128)S(1)}, u32[]{:S(2)}, u32[]{:S(2)}) %collective-permute-start.4) | collective-permute-done | bytes 49184 | tf_op jit(solution)/shard_map/ppermute | solution.py:41
  16.6 0.0 collective-permute-done.3
  16.6 0.0 collective-permute-done.2
  16.6 0.0 collective-permute-done.1
  16.6 0.0 collective-permute-done
  16.6 0.0 copy-done
  16.6 0.3 fusion.5
  17.0 1.1 %copy.19.g_ref = f32[3,128,384]{2,1,0:T(8,128)} copy(f32[3,128,384]{1,2,0:T(8,128)S(1)} %bitcast.14) | data formatting | bytes 1179648 | tf_op jit(solution)/shard_map/reshape | solution.py:165
  18.0 15.6 %shard_map.37 = f32[32,64,384]{2,1,0:T(8,128)} custom-call(s32[32]{0:T(128)} %broadcast_clamp_fusion.slot_ref, f32[3,64,384]{2,1,0:T(8,128)} %tile.10.w_ref, f32[3,128,384]{2,1,0:T(8,128)} %copy.19.g_ref, f32[384,128]{1,0:T(8,128)} %bitcast.13), custom_call_target="tpu_custom_call" | custom-call | tf_op jit(solution)/shard_map/pallas_call | solution.py:141
  33.6 3.8 %reshape_reshape.7 = f32[2,2,2,2,2,129,128]{6,5,4,3,2,1,0:T(8,128)S(1)} reshape(f32[32,64,258]{2,1,0:T(8,128)} %bitcast.11) | data formatting | bytes 4227072 | tf_op jit(solution)/shard_map/reshape;reshape | solution.py:78
  37.3 0.1 constant_dynamic-slice_fusion.11
  37.4 0.5 copy.20
  38.0 0.4 collective-permute-start.6
  38.4 2.5 %collective-permute-done.6 = f32[2,2,2,2,1,129,128]{6,3,5,4,2,1,0:T(2,128)} collective-permute-done((f32[2,2,2,2,1,129,128]{6,3,5,4,2,1,0:T(2,128)S(1)}, f32[2,2,2,2,1,129,128]{6,3,5,4,2,1,0:T(2,128)}, u32[]{:S(2)}, u32[]{:S(2)}) %collective-permute-start.6) | collective-permute-done | bytes 1056800 | tf_op jit(solution)/shard_map/ppermute | solution.py:69
  40.8 1.3 %copy_add_fusion = f32[2,2,2,2,1,129,128]{6,5,4,3,2,1,0:T(8,128)S(1)} fusion(f32[2,2,2,2,1,129,128]{6,3,5,4,2,1,0:T(2,128)} %collective-permute-done.6, f32[2,2,2,2,2,129,128]{6,5,4,3,2,1,0:T(8,128)S(1)} %reshape_reshape.7, s32[]{:T(128)S(6)} %select_n.138), kind=kLoop, calls=%fused_computation | loop fusion | flops 264192 | bytes 3170308 | tf_op jit(solution)/shard_map/add | solution.py:69
  42.2 0.1 fusion.7
  42.4 0.1 collective-permute-start.15
  42.5 1.8 %collective-permute-start.11 = (f32[2,2,1,2,1,43,128]{6,5,4,3,2,1,0:T(8,128)S(1)}, f32[2,2,1,2,1,43,128]{6,5,4,3,2,1,0:T(8,128)S(1)}, u32[]{:S(2)}, u32[]{:S(2)}) collective-permute-start(f32[2,2,1,2,1,43,128]{6,5,4,3,2,1,0:T(8,128)S(1)} %constant_dynamic-slice_fusion.6), channel_id=1, source_target_pairs={{0,4},{2,6},{4,0},{6,2},{1,5},{3,7},{5,1},{7,3},{8,12},{10,14},{12... | collective-permute-start | bytes 528392 | tf_op jit(solution)/shard_map/ppermute | solution.py:69
  44.3 0.7 collective-permute-start.7
  44.9 4.7 %collective-permute-done.15 = f32[2,1,2,2,1,43,128]{6,5,4,3,2,1,0:T(8,128)S(1)} collective-permute-done((f32[2,1,2,2,1,43,128]{6,5,4,3,2,1,0:T(8,128)S(1)}, f32[2,1,2,2,1,43,128]{6,5,4,3,2,1,0:T(8,128)S(1)}, u32[]{:S(2)}, u32[]{:S(2)}) %collective-permute-start.15) | collective-permute-done | bytes 176160 | tf_op jit(solution)/shard_map/ppermute | solution.py:69
  49.7 0.8 %collective-permute-start.16 = (f32[2,1,2,1,1,43,128]{6,5,4,3,2,1,0:T(8,128)S(1)}, f32[2,1,2,1,1,43,128]{6,5,4,3,2,1,0:T(8,128)S(1)}, u32[]{:S(2)}, u32[]{:S(2)}) collective-permute-start(f32[2,1,2,1,1,43,128]{6,5,4,3,2,1,0:T(8,128)S(1)} %constant_dynamic-slice_fusion.1), channel_id=1, source_target_pairs={{0,2},{2,0},{4,6},{6,4},{1,3},{3,1},{5,7},{7,5},{8,10},{10,8},{12,... | collective-permute-start | bytes 264200 | tf_op jit(solution)/shard_map/ppermute | solution.py:69
  50.5 0.0 collective-permute-done.11
  50.5 1.0 %collective-permute-start.12 = (f32[2,1,1,2,1,43,128]{6,5,4,3,2,1,0:T(8,128)S(1)}, f32[2,1,1,2,1,43,128]{6,5,4,3,2,1,0:T(8,128)S(1)}, u32[]{:S(2)}, u32[]{:S(2)}) collective-permute-start(f32[2,1,1,2,1,43,128]{6,5,4,3,2,1,0:T(8,128)S(1)} %constant_dynamic-slice_fusion.5), channel_id=1, source_target_pairs={{0,8},{8,0},{16,24},{24,16},{1,9},{9,1},{17,25},{25,17},{2,10},{10... | collective-permute-start | bytes 264200 | tf_op jit(solution)/shard_map/ppermute | solution.py:69
  51.6 0.0 collective-permute-done.7
  51.6 1.7 %collective-permute-start.8 = (f32[2,2,1,1,1,43,128]{6,5,4,3,2,1,0:T(8,128)S(1)}, f32[2,2,1,1,1,43,128]{6,5,4,3,2,1,0:T(8,128)S(1)}, u32[]{:S(2)}, u32[]{:S(2)}) collective-permute-start(f32[2,2,1,1,1,43,128]{6,5,4,3,2,1,0:T(8,128)S(1)} %constant_dynamic-slice_fusion.9), channel_id=1, source_target_pairs={{0,4},{2,6},{4,0},{6,2},{1,5},{3,7},{5,1},{7,3},{8,12},{10,14},{12... | collective-permute-start | bytes 264200 | tf_op jit(solution)/shard_map/ppermute | solution.py:69
  53.4 1.0 %collective-permute-done.16 = f32[2,1,2,1,1,43,128]{6,5,4,3,2,1,0:T(8,128)S(1)} collective-permute-done((f32[2,1,2,1,1,43,128]{6,5,4,3,2,1,0:T(8,128)S(1)}, f32[2,1,2,1,1,43,128]{6,5,4,3,2,1,0:T(8,128)S(1)}, u32[]{:S(2)}, u32[]{:S(2)}) %collective-permute-start.16) | collective-permute-done | bytes 88096 | tf_op jit(solution)/shard_map/ppermute | solution.py:69
  54.4 1.7 %collective-permute-start.17 = (f32[2,1,1,1,1,43,128]{6,5,4,3,2,1,0:T(8,128)S(1)}, f32[2,1,1,1,1,43,128]{6,5,4,3,2,1,0:T(8,128)S(1)}, u32[]{:S(2)}, u32[]{:S(2)}) collective-permute-start(f32[2,1,1,1,1,43,128]{6,5,4,3,2,1,0:T(8,128)S(1)} %constant_dynamic-slice_fusion), channel_id=1, source_target_pairs={{0,4},{2,6},{4,0},{6,2},{1,5},{3,7},{5,1},{7,3},{8,12},{10,14},{12... | collective-permute-start | bytes 132104 | tf_op jit(solution)/shard_map/ppermute | solution.py:69
  56.1 0.0 collective-permute-done.12
  56.2 0.7 collective-permute-start.13
  56.8 0.0 collective-permute-done.8
  56.9 1.8 %collective-permute-start.9 = (f32[2,1,1,1,1,43,128]{6,5,4,3,2,1,0:T(8,128)S(1)}, f32[2,1,1,1,1,43,128]{6,5,4,3,2,1,0:T(8,128)S(1)}, u32[]{:S(2)}, u32[]{:S(2)}) collective-permute-start(f32[2,1,1,1,1,43,128]{6,5,4,3,2,1,0:T(8,128)S(1)} %constant_dynamic-slice_fusion.8), channel_id=1, source_target_pairs={{0,8},{8,0},{16,24},{24,16},{1,9},{9,1},{17,25},{25,17},{2,10},{10... | collective-permute-start | bytes 132104 | tf_op jit(solution)/shard_map/ppermute | solution.py:69
  58.7 0.0 collective-permute-done.17
  58.8 0.9 %collective-permute-start.18 = (f32[1,1,1,1,1,43,128]{6,5,4,3,2,1,0:T(8,128)S(1)}, f32[1,1,1,1,1,43,128]{6,5,4,3,2,1,0:T(8,128)S(1)}, u32[]{:S(2)}, u32[]{:S(2)}) collective-permute-start(f32[1,1,1,1,1,43,128]{6,5,4,3,2,1,0:T(8,128)S(1)} %constant_dynamic-slice_fusion.12), channel_id=1, source_target_pairs={{0,16},{8,24},{16,0},{24,8},{1,17},{9,25},{17,1},{25,9},{2,18},{10... | collective-permute-start | bytes 66056 | tf_op jit(solution)/shard_map/ppermute | solution.py:69
  59.7 0.7 collective-permute-done.13
  60.4 1.5 %collective-permute-start.14 = (f32[1,1,1,1,1,43,128]{6,5,4,3,2,1,0:T(8,128)S(1)}, f32[1,1,1,1,1,43,128]{6,5,4,3,2,1,0:T(8,128)S(1)}, u32[]{:S(2)}, u32[]{:S(2)}) collective-permute-start(f32[1,1,1,1,1,43,128]{6,5,4,3,2,1,0:T(8,128)S(1)} %constant_dynamic-slice_fusion.3), channel_id=1, source_target_pairs={{0,16},{8,24},{16,0},{24,8},{1,17},{9,25},{17,1},{25,9},{2,18},{10... | collective-permute-start | bytes 66056 | tf_op jit(solution)/shard_map/ppermute | solution.py:69
  61.9 0.0 collective-permute-done.9
  61.9 1.6 %collective-permute-start.10 = (f32[1,1,1,1,1,43,128]{6,5,4,3,2,1,0:T(8,128)S(1)}, f32[1,1,1,1,1,43,128]{6,5,4,3,2,1,0:T(8,128)S(1)}, u32[]{:S(2)}, u32[]{:S(2)}) collective-permute-start(f32[1,1,1,1,1,43,128]{6,5,4,3,2,1,0:T(8,128)S(1)} %constant_dynamic-slice_fusion.7), channel_id=1, source_target_pairs={{0,16},{8,24},{16,0},{24,8},{1,17},{9,25},{17,1},{25,9},{2,18},{10... | collective-permute-start | bytes 66056 | tf_op jit(solution)/shard_map/ppermute | solution.py:69
  63.5 0.3 collective-permute-done.18
  63.8 1.4 %collective-permute-done.14 = f32[1,1,1,1,1,43,128]{6,5,4,3,2,1,0:T(8,128)S(1)} collective-permute-done((f32[1,1,1,1,1,43,128]{6,5,4,3,2,1,0:T(8,128)S(1)}, f32[1,1,1,1,1,43,128]{6,5,4,3,2,1,0:T(8,128)S(1)}, u32[]{:S(2)}, u32[]{:S(2)}) %collective-permute-start.14) | collective-permute-done | bytes 22048 | tf_op jit(solution)/shard_map/ppermute | solution.py:69
  65.2 1.5 %collective-permute-done.10 = f32[1,1,1,1,1,43,128]{6,5,4,3,2,1,0:T(8,128)S(1)} collective-permute-done((f32[1,1,1,1,1,43,128]{6,5,4,3,2,1,0:T(8,128)S(1)}, f32[1,1,1,1,1,43,128]{6,5,4,3,2,1,0:T(8,128)S(1)}, u32[]{:S(2)}, u32[]{:S(2)}) %collective-permute-start.10) | collective-permute-done | bytes 22048 | tf_op jit(solution)/shard_map/ppermute | solution.py:69
  66.7 0.8 %reshape_reshape_reshape.3 = f32[64,258]{1,0:T(8,128)} reshape(f32[1,1,1,1,1,129,128]{6,5,4,3,2,1,0:T(8,128)S(1)} %pad_maximum_fusion.7) | data formatting | bytes 132096 | tf_op jit(solution)/shard_map/reshape;reshape;reshape | solution.py:177
  (28 shorter events, 0.5 us)
Async XLA Ops:
  0.8 15.8 %collective-permute-start.1 = (f32[3,1,8,4,128]{4,3,2,1,0:T(4,128)S(1)}, f32[3,1,8,4,128]{4,3,2,1,0:T(4,128)S(1)}, u32[]{:S(2)}, u32[]{:S(2)}) collective-permute-start(f32[3,1,8,4,128]{4,3,2,1,0:T(4,128)S(1)} %get-tuple-element.12), channel_id=1, source_target_pairs={{0,8},{8,16},{16,24},{24,0},{1,9},{9,17},{17,25},{25,1},{2,10},{10... | collective-permute-start | bytes 147464 | tf_op jit(solution)/shard_map/ppermute | solution.py:40
  3.9 12.7 %collective-permute-start = (f32[3,1,8,4,128]{4,3,2,1,0:T(4,128)S(1)}, f32[3,1,8,4,128]{4,3,2,1,0:T(4,128)S(1)}, u32[]{:S(2)}, u32[]{:S(2)}) collective-permute-start(f32[3,1,8,4,128]{4,3,2,1,0:T(4,128)S(1)} %get-tuple-element.11), channel_id=1, source_target_pairs={{8,0},{16,8},{24,16},{0,24},{9,1},{17,9},{25,17},{1,25},{10,2},{18... | collective-permute-start | bytes 147464 | tf_op jit(solution)/shard_map/ppermute | solution.py:41
  6.7 9.8 %collective-permute-start.3 = (f32[3,4,1,4,128]{4,3,2,1,0:T(4,128)S(1)}, f32[3,4,1,4,128]{4,3,2,1,0:T(4,128)S(1)}, u32[]{:S(2)}, u32[]{:S(2)}) collective-permute-start(f32[3,4,1,4,128]{4,3,2,1,0:T(4,128)S(1)} %get-tuple-element.14), channel_id=1, source_target_pairs={{0,2},{2,4},{4,6},{6,0},{1,3},{3,5},{5,7},{7,1},{8,10},{10,12},{12... | collective-permute-start | bytes 73736 | tf_op jit(solution)/shard_map/ppermute | solution.py:40
  8.4 8.2 %collective-permute-start.2 = (f32[3,4,1,4,128]{4,3,2,1,0:T(4,128)S(1)}, f32[3,4,1,4,128]{4,3,2,1,0:T(4,128)S(1)}, u32[]{:S(2)}, u32[]{:S(2)}) collective-permute-start(f32[3,4,1,4,128]{4,3,2,1,0:T(4,128)S(1)} %get-tuple-element.13), channel_id=1, source_target_pairs={{2,0},{4,2},{6,4},{0,6},{3,1},{5,3},{7,5},{1,7},{10,8},{12,10},{14... | collective-permute-start | bytes 73736 | tf_op jit(solution)/shard_map/ppermute | solution.py:41
  10.8 5.8 %copy-start = (f32[3,4,8,4,128]{4,3,2,1,0:T(4,128)S(1)}, f32[3,4,8,4,128]{4,3,2,1,0:T(4,128)}, u32[]{:S(2)}) copy-start(f32[3,4,8,4,128]{4,3,2,1,0:T(4,128)} %param.3) | copy-start | bytes 589828
  10.8 4.4 %collective-permute-start.5 = (f32[3,4,8,1,128]{4,3,2,1,0:T(1,128)S(1)}, f32[3,4,8,1,128]{4,3,2,1,0:T(1,128)S(1)}, u32[]{:S(2)}, u32[]{:S(2)}) collective-permute-start(f32[3,4,8,1,128]{4,3,2,1,0:T(1,128)S(1)} %get-tuple-element.16), channel_id=1, source_target_pairs={{0,1},{1,0},{2,3},{3,2},{4,5},{5,4},{6,7},{7,6},{8,9},{9,8},{10,11... | collective-permute-start | bytes 147464 | tf_op jit(solution)/shard_map/ppermute | solution.py:40
  15.2 1.3 %collective-permute-start.4 = (f32[3,4,8,1,128]{4,3,2,1,0:T(1,128)S(1)}, f32[3,4,8,1,128]{4,3,2,1,0:T(1,128)S(1)}, u32[]{:S(2)}, u32[]{:S(2)}) collective-permute-start(f32[3,4,8,1,128]{4,3,2,1,0:T(1,128)S(1)} %get-tuple-element.15), channel_id=1, source_target_pairs={{1,0},{0,1},{3,2},{2,3},{5,4},{4,5},{7,6},{6,7},{9,8},{8,9},{11,10... | collective-permute-start | bytes 147464 | tf_op jit(solution)/shard_map/ppermute | solution.py:41
  38.0 2.9 %collective-permute-start.6 = (f32[2,2,2,2,1,129,128]{6,3,5,4,2,1,0:T(2,128)S(1)}, f32[2,2,2,2,1,129,128]{6,3,5,4,2,1,0:T(2,128)}, u32[]{:S(2)}, u32[]{:S(2)}) collective-permute-start(f32[2,2,2,2,1,129,128]{6,3,5,4,2,1,0:T(2,128)S(1)} %copy.20), channel_id=1, source_target_pairs={{0,1},{1,0},{2,3},{3,2},{4,5},{5,4},{6,7},{7,6},{8,9},{9,8},{10,11... | collective-permute-start | bytes 3170312 | tf_op jit(solution)/shard_map/ppermute | solution.py:69
  42.4 7.3 %collective-permute-start.15 = (f32[2,1,2,2,1,43,128]{6,5,4,3,2,1,0:T(8,128)S(1)}, f32[2,1,2,2,1,43,128]{6,5,4,3,2,1,0:T(8,128)S(1)}, u32[]{:S(2)}, u32[]{:S(2)}) collective-permute-start(f32[2,1,2,2,1,43,128]{6,5,4,3,2,1,0:T(8,128)S(1)} %constant_dynamic-slice_fusion.2), channel_id=1, source_target_pairs={{0,8},{8,0},{16,24},{24,16},{1,9},{9,1},{17,25},{25,17},{2,10},{10... | collective-permute-start | bytes 528392 | tf_op jit(solution)/shard_map/ppermute | solution.py:69
  42.5 8.0 %collective-permute-start.11 = (f32[2,2,1,2,1,43,128]{6,5,4,3,2,1,0:T(8,128)S(1)}, f32[2,2,1,2,1,43,128]{6,5,4,3,2,1,0:T(8,128)S(1)}, u32[]{:S(2)}, u32[]{:S(2)}) collective-permute-start(f32[2,2,1,2,1,43,128]{6,5,4,3,2,1,0:T(8,128)S(1)} %constant_dynamic-slice_fusion.6), channel_id=1, source_target_pairs={{0,4},{2,6},{4,0},{6,2},{1,5},{3,7},{5,1},{7,3},{8,12},{10,14},{12... | collective-permute-start | bytes 528392 | tf_op jit(solution)/shard_map/ppermute | solution.py:69
  44.3 7.3 %collective-permute-start.7 = (f32[2,2,2,1,1,43,128]{6,5,4,3,2,1,0:T(8,128)S(1)}, f32[2,2,2,1,1,43,128]{6,5,4,3,2,1,0:T(8,128)S(1)}, u32[]{:S(2)}, u32[]{:S(2)}) collective-permute-start(f32[2,2,2,1,1,43,128]{6,5,4,3,2,1,0:T(8,128)S(1)} %constant_dynamic-slice_fusion.10), channel_id=1, source_target_pairs={{0,2},{2,0},{4,6},{6,4},{1,3},{3,1},{5,7},{7,5},{8,10},{10,8},{12,... | collective-permute-start | bytes 528392 | tf_op jit(solution)/shard_map/ppermute | solution.py:69
  49.7 4.7 %collective-permute-start.16 = (f32[2,1,2,1,1,43,128]{6,5,4,3,2,1,0:T(8,128)S(1)}, f32[2,1,2,1,1,43,128]{6,5,4,3,2,1,0:T(8,128)S(1)}, u32[]{:S(2)}, u32[]{:S(2)}) collective-permute-start(f32[2,1,2,1,1,43,128]{6,5,4,3,2,1,0:T(8,128)S(1)} %constant_dynamic-slice_fusion.1), channel_id=1, source_target_pairs={{0,2},{2,0},{4,6},{6,4},{1,3},{3,1},{5,7},{7,5},{8,10},{10,8},{12,... | collective-permute-start | bytes 264200 | tf_op jit(solution)/shard_map/ppermute | solution.py:69
  50.5 5.6 %collective-permute-start.12 = (f32[2,1,1,2,1,43,128]{6,5,4,3,2,1,0:T(8,128)S(1)}, f32[2,1,1,2,1,43,128]{6,5,4,3,2,1,0:T(8,128)S(1)}, u32[]{:S(2)}, u32[]{:S(2)}) collective-permute-start(f32[2,1,1,2,1,43,128]{6,5,4,3,2,1,0:T(8,128)S(1)} %constant_dynamic-slice_fusion.5), channel_id=1, source_target_pairs={{0,8},{8,0},{16,24},{24,16},{1,9},{9,1},{17,25},{25,17},{2,10},{10... | collective-permute-start | bytes 264200 | tf_op jit(solution)/shard_map/ppermute | solution.py:69
  51.6 5.2 %collective-permute-start.8 = (f32[2,2,1,1,1,43,128]{6,5,4,3,2,1,0:T(8,128)S(1)}, f32[2,2,1,1,1,43,128]{6,5,4,3,2,1,0:T(8,128)S(1)}, u32[]{:S(2)}, u32[]{:S(2)}) collective-permute-start(f32[2,2,1,1,1,43,128]{6,5,4,3,2,1,0:T(8,128)S(1)} %constant_dynamic-slice_fusion.9), channel_id=1, source_target_pairs={{0,4},{2,6},{4,0},{6,2},{1,5},{3,7},{5,1},{7,3},{8,12},{10,14},{12... | collective-permute-start | bytes 264200 | tf_op jit(solution)/shard_map/ppermute | solution.py:69
  54.4 4.3 %collective-permute-start.17 = (f32[2,1,1,1,1,43,128]{6,5,4,3,2,1,0:T(8,128)S(1)}, f32[2,1,1,1,1,43,128]{6,5,4,3,2,1,0:T(8,128)S(1)}, u32[]{:S(2)}, u32[]{:S(2)}) collective-permute-start(f32[2,1,1,1,1,43,128]{6,5,4,3,2,1,0:T(8,128)S(1)} %constant_dynamic-slice_fusion), channel_id=1, source_target_pairs={{0,4},{2,6},{4,0},{6,2},{1,5},{3,7},{5,1},{7,3},{8,12},{10,14},{12... | collective-permute-start | bytes 132104 | tf_op jit(solution)/shard_map/ppermute | solution.py:69
  56.2 4.2 %collective-permute-start.13 = (f32[2,1,1,1,1,43,128]{6,5,4,3,2,1,0:T(8,128)S(1)}, f32[2,1,1,1,1,43,128]{6,5,4,3,2,1,0:T(8,128)S(1)}, u32[]{:S(2)}, u32[]{:S(2)}) collective-permute-start(f32[2,1,1,1,1,43,128]{6,5,4,3,2,1,0:T(8,128)S(1)} %constant_dynamic-slice_fusion.4), channel_id=1, source_target_pairs={{0,2},{2,0},{4,6},{6,4},{1,3},{3,1},{5,7},{7,5},{8,10},{10,8},{12,... | collective-permute-start | bytes 132104 | tf_op jit(solution)/shard_map/ppermute | solution.py:69
  56.9 5.0 %collective-permute-start.9 = (f32[2,1,1,1,1,43,128]{6,5,4,3,2,1,0:T(8,128)S(1)}, f32[2,1,1,1,1,43,128]{6,5,4,3,2,1,0:T(8,128)S(1)}, u32[]{:S(2)}, u32[]{:S(2)}) collective-permute-start(f32[2,1,1,1,1,43,128]{6,5,4,3,2,1,0:T(8,128)S(1)} %constant_dynamic-slice_fusion.8), channel_id=1, source_target_pairs={{0,8},{8,0},{16,24},{24,16},{1,9},{9,1},{17,25},{25,17},{2,10},{10... | collective-permute-start | bytes 132104 | tf_op jit(solution)/shard_map/ppermute | solution.py:69
  58.8 5.0 %collective-permute-start.18 = (f32[1,1,1,1,1,43,128]{6,5,4,3,2,1,0:T(8,128)S(1)}, f32[1,1,1,1,1,43,128]{6,5,4,3,2,1,0:T(8,128)S(1)}, u32[]{:S(2)}, u32[]{:S(2)}) collective-permute-start(f32[1,1,1,1,1,43,128]{6,5,4,3,2,1,0:T(8,128)S(1)} %constant_dynamic-slice_fusion.12), channel_id=1, source_target_pairs={{0,16},{8,24},{16,0},{24,8},{1,17},{9,25},{17,1},{25,9},{2,18},{10... | collective-permute-start | bytes 66056 | tf_op jit(solution)/shard_map/ppermute | solution.py:69
  60.4 4.8 %collective-permute-start.14 = (f32[1,1,1,1,1,43,128]{6,5,4,3,2,1,0:T(8,128)S(1)}, f32[1,1,1,1,1,43,128]{6,5,4,3,2,1,0:T(8,128)S(1)}, u32[]{:S(2)}, u32[]{:S(2)}) collective-permute-start(f32[1,1,1,1,1,43,128]{6,5,4,3,2,1,0:T(8,128)S(1)} %constant_dynamic-slice_fusion.3), channel_id=1, source_target_pairs={{0,16},{8,24},{16,0},{24,8},{1,17},{9,25},{17,1},{25,9},{2,18},{10... | collective-permute-start | bytes 66056 | tf_op jit(solution)/shard_map/ppermute | solution.py:69
  61.9 4.8 %collective-permute-start.10 = (f32[1,1,1,1,1,43,128]{6,5,4,3,2,1,0:T(8,128)S(1)}, f32[1,1,1,1,1,43,128]{6,5,4,3,2,1,0:T(8,128)S(1)}, u32[]{:S(2)}, u32[]{:S(2)}) collective-permute-start(f32[1,1,1,1,1,43,128]{6,5,4,3,2,1,0:T(8,128)S(1)} %constant_dynamic-slice_fusion.7), channel_id=1, source_target_pairs={{0,16},{8,24},{16,0},{24,8},{1,17},{9,25},{17,1},{25,9},{2,18},{10... | collective-permute-start | bytes 66056 | tf_op jit(solution)/shard_map/ppermute | solution.py:69

commit v10 on v9

--- a/solution.py
+++ b/solution.py
@@ -37,12 +37,20 @@
         peers, length = lax.axis_size(axis), value.shape[dim]
         up = [(i, (i + 1) % peers) for i in range(peers)]
         down = [(j, i) for i, j in up]
-        before = lax.ppermute(lax.slice_in_dim(value, length - 1, length, axis=dim), axis, up)
-        after = lax.ppermute(lax.slice_in_dim(value, 0, 1, axis=dim), axis, down)
-        if axis == "gz":
+        last = lax.slice_in_dim(value, length - 1, length, axis=dim)
+        leading = lax.slice_in_dim(value, 0, 1, axis=dim)
+        if axis == "gz" and peers == 2:
             level = lax.axis_index(axis)
-            before = jnp.where(level == 0, jnp.float32(0.0), before)
-            after = jnp.where(level == peers - 1, jnp.float32(0.0), after)
+            got = lax.ppermute(jnp.where(level == 0, last, leading), axis, [(0, 1), (1, 0)])
+            before = jnp.where(level == 1, got, jnp.float32(0.0))
+            after = jnp.where(level == 0, got, jnp.float32(0.0))
+        else:
+            before = lax.ppermute(last, axis, up)
+            after = lax.ppermute(leading, axis, down)
+            if axis == "gz":
+                level = lax.axis_index(axis)
+                before = jnp.where(level == 0, jnp.float32(0.0), before)
+                after = jnp.where(level == peers - 1, jnp.float32(0.0), after)
         ext = jnp.concatenate([before, value, after], axis=dim)
         high = lax.slice_in_dim(ext, 2, length + 2, axis=dim)
         low = lax.slice_in_dim(ext, 0, length, axis=dim)

time: 68 us -> 66.8 us (0.982)
  local copies, waits for them, and re-layouts: 10.6 us -> 9.43 us
  other arithmetic: 4.95 us -> 6.05 us
  waiting for transfers between devices: 12.9 us -> 12.1 us
    select_n x2, other arithmetic: 0.09 us -> 1.22 us  [the longest x1 1.15 us: face_gradients(): jnp.where(level == 0, last, leading)]
    slice x3 -> x2, local copies, waits for them, and re-layouts: 2.71 us -> 1.59 us  [face_gradients(): leading = lax.slice_in_dim(value, 0, 1, axis=dim)]
    ppermute x6 -> x5, waiting for transfers between devices: 0.84 us -> 0.01 us  [the longest x2 0.01 us: face_gradients(): before = lax.ppermute(last, axis, up)]
    ppermute x6 -> x5, starting transfers between devices: 8.61 us -> 8.14 us  [the longest x2 4.71 us: face_gradients(): before = lax.ppermute(last, axis, up)]
  transfers between devices with their start and end apart: 19 -> 18, of which waited for: 8 -> 7; matrix products, arithmetic and copies ran while one was open for 10% -> 10% of each run, Pallas kernels for 0% -> 0%
where the time goes in v10:
time: 66.8 us; the launch traced here: 66.4 us
  starting transfers between devices  23 us (34%)
  Pallas kernels  15.6 us (23%)
  waiting for transfers between devices  12.1 us (18%)
  local copies, waits for them, and re-layouts  9.43 us (14%)
  other arithmetic  6.05 us (9%)
    pallas_call x1, Pallas kernels, triangle(): pl.pallas_call(functools.partial(triangle_kernel, block_len), out_shape=j...  15.6 us
    ppermute x13, starting transfers between devices, halve(): return keep + lax.ppermute(other, axis, pairs)  14.8 us
    ppermute x13, waiting for transfers between devices, halve(): return keep + lax.ppermute(other, axis, pairs)  12.1 us
    ppermute x2, starting transfers between devices, face_gradients(): before = lax.ppermute(last, axis, up)  4.71 us
    another operation x1, local copies, waits for them, and re-layouts, scatter_sum(): value = payload.reshape((2,) * len(stages) + (rows, lanes))  3.77 us
    ppermute x2, starting transfers between devices, face_gradients(): after = lax.ppermute(leading, axis, down)  3.37 us
    slice x2, local copies, waits for them, and re-layouts, face_gradients(): leading = lax.slice_in_dim(value, 0, 1, axis=dim)  1.59 us
    add x13, other arithmetic, halve(): return keep + lax.ppermute(other, axis, pairs)  1.5 us
  transfers between devices with their start and end apart: 18, of which 7 were waited for; matrix products, arithmetic and copies ran while one was open for 10% of the time, Pallas kernels for 0%

profile of v10, /device:TPU:0, one launch (start us, length us, event | category | flops | bytes accessed | tf_op | source)
XLA Modules:
  0.0 66.4 jit_solution(9266998076979534118)
XLA Ops:
  0.0 0.8 %fusion.8 = (f32[3,1,8,4,128]{4,3,2,1,0:T(4,128)S(1)}, f32[3,1,8,4,128]{4,3,2,1,0:T(4,128)S(1)}) fusion(f32[3,4,8,4,128]{4,3,2,1,0:T(4,128)} %param.3), kind=kLoop, calls=%fused_computation.50 | loop fusion | bytes 196608 | tf_op jit(solution)/shard_map/slice | solution.py:41
  0.8 3.1 %collective-permute-start.1 = (f32[3,1,8,4,128]{4,3,2,1,0:T(4,128)S(1)}, f32[3,1,8,4,128]{4,3,2,1,0:T(4,128)S(1)}, u32[]{:S(2)}, u32[]{:S(2)}) collective-permute-start(f32[3,1,8,4,128]{4,3,2,1,0:T(4,128)S(1)} %get-tuple-element.12), channel_id=1, source_target_pairs={{0,8},{8,16},{16,24},{24,0},{1,9},{9,17},{17,25},{25,1},{2,10},{10... | collective-permute-start | bytes 147464 | tf_op jit(solution)/shard_map/ppermute | solution.py:48
  3.9 2.1 %collective-permute-start = (f32[3,1,8,4,128]{4,3,2,1,0:T(4,128)S(1)}, f32[3,1,8,4,128]{4,3,2,1,0:T(4,128)S(1)}, u32[]{:S(2)}, u32[]{:S(2)}) collective-permute-start(f32[3,1,8,4,128]{4,3,2,1,0:T(4,128)S(1)} %get-tuple-element.11), channel_id=1, source_target_pairs={{8,0},{16,8},{24,16},{0,24},{9,1},{17,9},{25,17},{1,25},{10,2},{18... | collective-permute-start | bytes 147464 | tf_op jit(solution)/shard_map/ppermute | solution.py:49
  6.0 0.8 %fusion.9 = (f32[3,4,1,4,128]{4,3,2,1,0:T(4,128)S(1)}, f32[3,4,1,4,128]{4,3,2,1,0:T(4,128)S(1)}) fusion(f32[3,4,8,4,128]{4,3,2,1,0:T(4,128)} %param.3), kind=kLoop, calls=%fused_computation.51 | loop fusion | bytes 98304 | tf_op jit(solution)/shard_map/slice | solution.py:41
  6.7 1.6 %collective-permute-start.3 = (f32[3,4,1,4,128]{4,3,2,1,0:T(4,128)S(1)}, f32[3,4,1,4,128]{4,3,2,1,0:T(4,128)S(1)}, u32[]{:S(2)}, u32[]{:S(2)}) collective-permute-start(f32[3,4,1,4,128]{4,3,2,1,0:T(4,128)S(1)} %get-tuple-element.14), channel_id=1, source_target_pairs={{0,2},{2,4},{4,6},{6,0},{1,3},{3,5},{5,7},{7,1},{8,10},{10,12},{12... | collective-permute-start | bytes 73736 | tf_op jit(solution)/shard_map/ppermute | solution.py:48
  8.4 1.3 %collective-permute-start.2 = (f32[3,4,1,4,128]{4,3,2,1,0:T(4,128)S(1)}, f32[3,4,1,4,128]{4,3,2,1,0:T(4,128)S(1)}, u32[]{:S(2)}, u32[]{:S(2)}) collective-permute-start(f32[3,4,1,4,128]{4,3,2,1,0:T(4,128)S(1)} %get-tuple-element.13), channel_id=1, source_target_pairs={{2,0},{4,2},{6,4},{0,6},{3,1},{5,3},{7,5},{1,7},{10,8},{12,10},{14... | collective-permute-start | bytes 73736 | tf_op jit(solution)/shard_map/ppermute | solution.py:49
  9.7 0.0 copy-start
  9.7 1.2 %broadcast_select_fusion.2 = f32[3,4,8,1,128]{4,3,2,1,0:T(1,128)S(1)} fusion(pred[]{:T(512)S(6)} %eq.37, f32[3,4,8,4,128]{4,3,2,1,0:T(4,128)} %param.3), kind=kLoop, calls=%fused_computation.24 | loop fusion | flops 12288 | bytes 147457 | tf_op jit(solution)/shard_map/jit(_where)/select_n | solution.py:44
  10.8 0.1 collective-permute-start.4
  10.9 0.8 %select_reduce_fusion = s32[32]{0:T(128)S(1)} fusion(s32[32]{0:T(128)} %param.5), kind=kLoop, calls=%fused_computation.32 | loop fusion | flops 3040 | bytes 256 | tf_op jit(solution)/shard_map/reduce_sum | solution.py:177
  11.7 0.7 %broadcast_multiply_fusion = f32[4,8,4]{1,2,0:T(4,128)S(1)} fusion(f32[4,8,4]{1,2,0:T(4,128)} %param.4), kind=kLoop, calls=%fused_computation.47 | loop fusion | flops 128 | bytes 1024 | tf_op jit(solution)/shard_map/mul | solution.py:171
  12.4 0.1 copy.17
  12.5 0.1 mul.32
  12.6 1.0 %fusion.6 = f32[3,64,128]{1,2,0:T(8,128)S(1)} fusion(f32[3,128,128]{2,1,0:T(8,128)} %bitcast.12, f32[128]{0:T(128)S(1)} %mul.32), kind=kLoop, calls=%fused_computation.15 | loop fusion | flops 24576 | bytes 197120 | tf_op jit(solution)/shard_map/transpose | solution.py:172
  13.6 0.5 broadcast_clamp_fusion.slot_ref
  14.1 0.1 copy.18
  14.2 0.1 tile.4
  14.3 0.9 %tile.10.w_ref = f32[3,64,384]{2,1,0:T(8,128)} reshape(f32[3,64,3,128]{3,2,1,0:T(4,128)S(1)} %tile.4) | data formatting | bytes 589824 | tf_op jit(solution)/shard_map/tile | solution.py:172
  15.2 0.0 collective-permute-done.4
  15.2 0.1 broadcast_select_fusion.1
  15.2 0.0 collective-permute-done.3
  15.3 0.0 collective-permute-done.2
  15.3 0.0 collective-permute-done.1
  15.3 0.0 collective-permute-done
  15.3 0.0 copy-done
  15.3 0.3 fusion.5
  15.6 1.0 %copy.19.g_ref = f32[3,128,384]{2,1,0:T(8,128)} copy(f32[3,128,384]{1,2,0:T(8,128)S(1)} %bitcast.14) | data formatting | bytes 1179648 | tf_op jit(solution)/shard_map/reshape | solution.py:173
  16.7 15.6 %shard_map.37 = f32[32,64,384]{2,1,0:T(8,128)} custom-call(s32[32]{0:T(128)} %broadcast_clamp_fusion.slot_ref, f32[3,64,384]{2,1,0:T(8,128)} %tile.10.w_ref, f32[3,128,384]{2,1,0:T(8,128)} %copy.19.g_ref, f32[384,128]{1,0:T(8,128)} %bitcast.13), custom_call_target="tpu_custom_call" | custom-call | tf_op jit(solution)/shard_map/pallas_call | solution.py:149
  32.2 3.8 %reshape_reshape.7 = f32[2,2,2,2,2,129,128]{6,5,4,3,2,1,0:T(8,128)S(1)} reshape(f32[32,64,258]{2,1,0:T(8,128)} %bitcast.11) | data formatting | bytes 4227072 | tf_op jit(solution)/shard_map/reshape;reshape | solution.py:86
  36.0 0.1 constant_dynamic-slice_fusion.11
  36.1 0.5 copy.20
  36.7 0.6 collective-permute-start.5
  37.2 2.4 %collective-permute-done.5 = f32[2,2,2,2,1,129,128]{6,3,5,4,2,1,0:T(2,128)} collective-permute-done((f32[2,2,2,2,1,129,128]{6,3,5,4,2,1,0:T(2,128)S(1)}, f32[2,2,2,2,1,129,128]{6,3,5,4,2,1,0:T(2,128)}, u32[]{:S(2)}, u32[]{:S(2)}) %collective-permute-start.5) | collective-permute-done | bytes 1056800 | tf_op jit(solution)/shard_map/ppermute | solution.py:77
  39.6 1.3 %copy_add_fusion = f32[2,2,2,2,1,129,128]{6,5,4,3,2,1,0:T(8,128)S(1)} fusion(f32[2,2,2,2,1,129,128]{6,3,5,4,2,1,0:T(2,128)} %collective-permute-done.5, f32[2,2,2,2,2,129,128]{6,5,4,3,2,1,0:T(8,128)S(1)} %reshape_reshape.7, s32[]{:T(128)S(6)} %select_n.145), kind=kLoop, calls=%fused_computation | loop fusion | flops 264192 | bytes 3170308 | tf_op jit(solution)/shard_map/add | solution.py:77
  41.0 0.1 fusion.7
  41.2 0.1 collective-permute-start.14
  41.3 1.7 %collective-permute-start.10 = (f32[2,2,1,2,1,43,128]{6,5,4,3,2,1,0:T(8,128)S(1)}, f32[2,2,1,2,1,43,128]{6,5,4,3,2,1,0:T(8,128)S(1)}, u32[]{:S(2)}, u32[]{:S(2)}) collective-permute-start(f32[2,2,1,2,1,43,128]{6,5,4,3,2,1,0:T(8,128)S(1)} %constant_dynamic-slice_fusion.6), channel_id=1, source_target_pairs={{0,4},{2,6},{4,0},{6,2},{1,5},{3,7},{5,1},{7,3},{8,12},{10,14},{12... | collective-permute-start | bytes 528392 | tf_op jit(solution)/shard_map/ppermute | solution.py:77
  43.0 0.7 collective-permute-start.6
  43.7 4.8 %collective-permute-done.14 = f32[2,1,2,2,1,43,128]{6,5,4,3,2,1,0:T(8,128)S(1)} collective-permute-done((f32[2,1,2,2,1,43,128]{6,5,4,3,2,1,0:T(8,128)S(1)}, f32[2,1,2,2,1,43,128]{6,5,4,3,2,1,0:T(8,128)S(1)}, u32[]{:S(2)}, u32[]{:S(2)}) %collective-permute-start.14) | collective-permute-done | bytes 176160 | tf_op jit(solution)/shard_map/ppermute | solution.py:77
  48.5 0.8 %collective-permute-start.15 = (f32[2,1,2,1,1,43,128]{6,5,4,3,2,1,0:T(8,128)S(1)}, f32[2,1,2,1,1,43,128]{6,5,4,3,2,1,0:T(8,128)S(1)}, u32[]{:S(2)}, u32[]{:S(2)}) collective-permute-start(f32[2,1,2,1,1,43,128]{6,5,4,3,2,1,0:T(8,128)S(1)} %constant_dynamic-slice_fusion.1), channel_id=1, source_target_pairs={{0,2},{2,0},{4,6},{6,4},{1,3},{3,1},{5,7},{7,5},{8,10},{10,8},{12,... | collective-permute-start | bytes 264200 | tf_op jit(solution)/shard_map/ppermute | solution.py:77
  49.3 0.0 collective-permute-done.10
  49.4 1.0 %collective-permute-start.11 = (f32[2,1,1,2,1,43,128]{6,5,4,3,2,1,0:T(8,128)S(1)}, f32[2,1,1,2,1,43,128]{6,5,4,3,2,1,0:T(8,128)S(1)}, u32[]{:S(2)}, u32[]{:S(2)}) collective-permute-start(f32[2,1,1,2,1,43,128]{6,5,4,3,2,1,0:T(8,128)S(1)} %constant_dynamic-slice_fusion.5), channel_id=1, source_target_pairs={{0,8},{8,0},{16,24},{24,16},{1,9},{9,1},{17,25},{25,17},{2,10},{10... | collective-permute-start | bytes 264200 | tf_op jit(solution)/shard_map/ppermute | solution.py:77
  50.4 0.0 collective-permute-done.6
  50.5 1.7 %collective-permute-start.7 = (f32[2,2,1,1,1,43,128]{6,5,4,3,2,1,0:T(8,128)S(1)}, f32[2,2,1,1,1,43,128]{6,5,4,3,2,1,0:T(8,128)S(1)}, u32[]{:S(2)}, u32[]{:S(2)}) collective-permute-start(f32[2,2,1,1,1,43,128]{6,5,4,3,2,1,0:T(8,128)S(1)} %constant_dynamic-slice_fusion.9), channel_id=1, source_target_pairs={{0,4},{2,6},{4,0},{6,2},{1,5},{3,7},{5,1},{7,3},{8,12},{10,14},{12... | collective-permute-start | bytes 264200 | tf_op jit(solution)/shard_map/ppermute | solution.py:77
  52.2 1.0 %collective-permute-done.15 = f32[2,1,2,1,1,43,128]{6,5,4,3,2,1,0:T(8,128)S(1)} collective-permute-done((f32[2,1,2,1,1,43,128]{6,5,4,3,2,1,0:T(8,128)S(1)}, f32[2,1,2,1,1,43,128]{6,5,4,3,2,1,0:T(8,128)S(1)}, u32[]{:S(2)}, u32[]{:S(2)}) %collective-permute-start.15) | collective-permute-done | bytes 88096 | tf_op jit(solution)/shard_map/ppermute | solution.py:77
  53.2 1.7 %collective-permute-start.16 = (f32[2,1,1,1,1,43,128]{6,5,4,3,2,1,0:T(8,128)S(1)}, f32[2,1,1,1,1,43,128]{6,5,4,3,2,1,0:T(8,128)S(1)}, u32[]{:S(2)}, u32[]{:S(2)}) collective-permute-start(f32[2,1,1,1,1,43,128]{6,5,4,3,2,1,0:T(8,128)S(1)} %constant_dynamic-slice_fusion), channel_id=1, source_target_pairs={{0,4},{2,6},{4,0},{6,2},{1,5},{3,7},{5,1},{7,3},{8,12},{10,14},{12... | collective-permute-start | bytes 132104 | tf_op jit(solution)/shard_map/ppermute | solution.py:77
  55.0 0.0 collective-permute-done.11
  55.0 0.7 collective-permute-start.12
  55.7 0.0 collective-permute-done.7
  55.7 1.9 %collective-permute-start.8 = (f32[2,1,1,1,1,43,128]{6,5,4,3,2,1,0:T(8,128)S(1)}, f32[2,1,1,1,1,43,128]{6,5,4,3,2,1,0:T(8,128)S(1)}, u32[]{:S(2)}, u32[]{:S(2)}) collective-permute-start(f32[2,1,1,1,1,43,128]{6,5,4,3,2,1,0:T(8,128)S(1)} %constant_dynamic-slice_fusion.8), channel_id=1, source_target_pairs={{0,8},{8,0},{16,24},{24,16},{1,9},{9,1},{17,25},{25,17},{2,10},{10... | collective-permute-start | bytes 132104 | tf_op jit(solution)/shard_map/ppermute | solution.py:77
  57.6 0.0 collective-permute-done.16
  57.6 0.9 %collective-permute-start.17 = (f32[1,1,1,1,1,43,128]{6,5,4,3,2,1,0:T(8,128)S(1)}, f32[1,1,1,1,1,43,128]{6,5,4,3,2,1,0:T(8,128)S(1)}, u32[]{:S(2)}, u32[]{:S(2)}) collective-permute-start(f32[1,1,1,1,1,43,128]{6,5,4,3,2,1,0:T(8,128)S(1)} %constant_dynamic-slice_fusion.12), channel_id=1, source_target_pairs={{0,16},{8,24},{16,0},{24,8},{1,17},{9,25},{17,1},{25,9},{2,18},{10... | collective-permute-start | bytes 66056 | tf_op jit(solution)/shard_map/ppermute | solution.py:77
  58.5 0.7 %collective-permute-done.12 = f32[2,1,1,1,1,43,128]{6,5,4,3,2,1,0:T(8,128)S(1)} collective-permute-done((f32[2,1,1,1,1,43,128]{6,5,4,3,2,1,0:T(8,128)S(1)}, f32[2,1,1,1,1,43,128]{6,5,4,3,2,1,0:T(8,128)S(1)}, u32[]{:S(2)}, u32[]{:S(2)}) %collective-permute-start.12) | collective-permute-done | bytes 44064 | tf_op jit(solution)/shard_map/ppermute | solution.py:77
  59.2 1.5 %collective-permute-start.13 = (f32[1,1,1,1,1,43,128]{6,5,4,3,2,1,0:T(8,128)S(1)}, f32[1,1,1,1,1,43,128]{6,5,4,3,2,1,0:T(8,128)S(1)}, u32[]{:S(2)}, u32[]{:S(2)}) collective-permute-start(f32[1,1,1,1,1,43,128]{6,5,4,3,2,1,0:T(8,128)S(1)} %constant_dynamic-slice_fusion.3), channel_id=1, source_target_pairs={{0,16},{8,24},{16,0},{24,8},{1,17},{9,25},{17,1},{25,9},{2,18},{10... | collective-permute-start | bytes 66056 | tf_op jit(solution)/shard_map/ppermute | solution.py:77
  60.7 0.0 collective-permute-done.8
  60.7 1.6 %collective-permute-start.9 = (f32[1,1,1,1,1,43,128]{6,5,4,3,2,1,0:T(8,128)S(1)}, f32[1,1,1,1,1,43,128]{6,5,4,3,2,1,0:T(8,128)S(1)}, u32[]{:S(2)}, u32[]{:S(2)}) collective-permute-start(f32[1,1,1,1,1,43,128]{6,5,4,3,2,1,0:T(8,128)S(1)} %constant_dynamic-slice_fusion.7), channel_id=1, source_target_pairs={{0,16},{8,24},{16,0},{24,8},{1,17},{9,25},{17,1},{25,9},{2,18},{10... | collective-permute-start | bytes 66056 | tf_op jit(solution)/shard_map/ppermute | solution.py:77
  62.3 0.3 collective-permute-done.17
  62.6 1.4 %collective-permute-done.13 = f32[1,1,1,1,1,43,128]{6,5,4,3,2,1,0:T(8,128)S(1)} collective-permute-done((f32[1,1,1,1,1,43,128]{6,5,4,3,2,1,0:T(8,128)S(1)}, f32[1,1,1,1,1,43,128]{6,5,4,3,2,1,0:T(8,128)S(1)}, u32[]{:S(2)}, u32[]{:S(2)}) %collective-permute-start.13) | collective-permute-done | bytes 22048 | tf_op jit(solution)/shard_map/ppermute | solution.py:77
  64.0 1.5 %collective-permute-done.9 = f32[1,1,1,1,1,43,128]{6,5,4,3,2,1,0:T(8,128)S(1)} collective-permute-done((f32[1,1,1,1,1,43,128]{6,5,4,3,2,1,0:T(8,128)S(1)}, f32[1,1,1,1,1,43,128]{6,5,4,3,2,1,0:T(8,128)S(1)}, u32[]{:S(2)}, u32[]{:S(2)}) %collective-permute-start.9) | collective-permute-done | bytes 22048 | tf_op jit(solution)/shard_map/ppermute | solution.py:77
  65.5 0.8 %reshape_reshape_reshape.3 = f32[64,258]{1,0:T(8,128)} reshape(f32[1,1,1,1,1,129,128]{6,5,4,3,2,1,0:T(8,128)S(1)} %pad_maximum_fusion.7) | data formatting | bytes 132096 | tf_op jit(solution)/shard_map/reshape;reshape;reshape | solution.py:185
  (26 shorter events, 0.4 us)
Async XLA Ops:
  0.8 14.4 %collective-permute-start.1 = (f32[3,1,8,4,128]{4,3,2,1,0:T(4,128)S(1)}, f32[3,1,8,4,128]{4,3,2,1,0:T(4,128)S(1)}, u32[]{:S(2)}, u32[]{:S(2)}) collective-permute-start(f32[3,1,8,4,128]{4,3,2,1,0:T(4,128)S(1)} %get-tuple-element.12), channel_id=1, source_target_pairs={{0,8},{8,16},{16,24},{24,0},{1,9},{9,17},{17,25},{25,1},{2,10},{10... | collective-permute-start | bytes 147464 | tf_op jit(solution)/shard_map/ppermute | solution.py:48
  3.9 11.4 %collective-permute-start = (f32[3,1,8,4,128]{4,3,2,1,0:T(4,128)S(1)}, f32[3,1,8,4,128]{4,3,2,1,0:T(4,128)S(1)}, u32[]{:S(2)}, u32[]{:S(2)}) collective-permute-start(f32[3,1,8,4,128]{4,3,2,1,0:T(4,128)S(1)} %get-tuple-element.11), channel_id=1, source_target_pairs={{8,0},{16,8},{24,16},{0,24},{9,1},{17,9},{25,17},{1,25},{10,2},{18... | collective-permute-start | bytes 147464 | tf_op jit(solution)/shard_map/ppermute | solution.py:49
  6.7 8.5 %collective-permute-start.3 = (f32[3,4,1,4,128]{4,3,2,1,0:T(4,128)S(1)}, f32[3,4,1,4,128]{4,3,2,1,0:T(4,128)S(1)}, u32[]{:S(2)}, u32[]{:S(2)}) collective-permute-start(f32[3,4,1,4,128]{4,3,2,1,0:T(4,128)S(1)} %get-tuple-element.14), channel_id=1, source_target_pairs={{0,2},{2,4},{4,6},{6,0},{1,3},{3,5},{5,7},{7,1},{8,10},{10,12},{12... | collective-permute-start | bytes 73736 | tf_op jit(solution)/shard_map/ppermute | solution.py:48
  8.4 6.9 %collective-permute-start.2 = (f32[3,4,1,4,128]{4,3,2,1,0:T(4,128)S(1)}, f32[3,4,1,4,128]{4,3,2,1,0:T(4,128)S(1)}, u32[]{:S(2)}, u32[]{:S(2)}) collective-permute-start(f32[3,4,1,4,128]{4,3,2,1,0:T(4,128)S(1)} %get-tuple-element.13), channel_id=1, source_target_pairs={{2,0},{4,2},{6,4},{0,6},{3,1},{5,3},{7,5},{1,7},{10,8},{12,10},{14... | collective-permute-start | bytes 73736 | tf_op jit(solution)/shard_map/ppermute | solution.py:49
  9.7 5.6 %copy-start = (f32[3,4,8,4,128]{4,3,2,1,0:T(4,128)S(1)}, f32[3,4,8,4,128]{4,3,2,1,0:T(4,128)}, u32[]{:S(2)}) copy-start(f32[3,4,8,4,128]{4,3,2,1,0:T(4,128)} %param.3) | copy-start | bytes 589828
  10.8 4.3 %collective-permute-start.4 = (f32[3,4,8,1,128]{4,3,2,1,0:T(1,128)S(1)}, f32[3,4,8,1,128]{4,3,2,1,0:T(1,128)S(1)}, u32[]{:S(2)}, u32[]{:S(2)}) collective-permute-start(f32[3,4,8,1,128]{4,3,2,1,0:T(1,128)S(1)} %broadcast_select_fusion.2), channel_id=1, source_target_pairs={{0,1},{1,0},{2,3},{3,2},{4,5},{5,4},{6,7},{7,6},{8,9},{9,8},{10,11... | collective-permute-start | bytes 147464 | tf_op jit(solution)/shard_map/ppermute | solution.py:44
  36.7 3.0 %collective-permute-start.5 = (f32[2,2,2,2,1,129,128]{6,3,5,4,2,1,0:T(2,128)S(1)}, f32[2,2,2,2,1,129,128]{6,3,5,4,2,1,0:T(2,128)}, u32[]{:S(2)}, u32[]{:S(2)}) collective-permute-start(f32[2,2,2,2,1,129,128]{6,3,5,4,2,1,0:T(2,128)S(1)} %copy.20), channel_id=1, source_target_pairs={{0,1},{1,0},{2,3},{3,2},{4,5},{5,4},{6,7},{7,6},{8,9},{9,8},{10,11... | collective-permute-start | bytes 3170312 | tf_op jit(solution)/shard_map/ppermute | solution.py:77
  41.2 7.3 %collective-permute-start.14 = (f32[2,1,2,2,1,43,128]{6,5,4,3,2,1,0:T(8,128)S(1)}, f32[2,1,2,2,1,43,128]{6,5,4,3,2,1,0:T(8,128)S(1)}, u32[]{:S(2)}, u32[]{:S(2)}) collective-permute-start(f32[2,1,2,2,1,43,128]{6,5,4,3,2,1,0:T(8,128)S(1)} %constant_dynamic-slice_fusion.2), channel_id=1, source_target_pairs={{0,8},{8,0},{16,24},{24,16},{1,9},{9,1},{17,25},{25,17},{2,10},{10... | collective-permute-start | bytes 528392 | tf_op jit(solution)/shard_map/ppermute | solution.py:77
  41.3 8.1 %collective-permute-start.10 = (f32[2,2,1,2,1,43,128]{6,5,4,3,2,1,0:T(8,128)S(1)}, f32[2,2,1,2,1,43,128]{6,5,4,3,2,1,0:T(8,128)S(1)}, u32[]{:S(2)}, u32[]{:S(2)}) collective-permute-start(f32[2,2,1,2,1,43,128]{6,5,4,3,2,1,0:T(8,128)S(1)} %constant_dynamic-slice_fusion.6), channel_id=1, source_target_pairs={{0,4},{2,6},{4,0},{6,2},{1,5},{3,7},{5,1},{7,3},{8,12},{10,14},{12... | collective-permute-start | bytes 528392 | tf_op jit(solution)/shard_map/ppermute | solution.py:77
  43.0 7.4 %collective-permute-start.6 = (f32[2,2,2,1,1,43,128]{6,5,4,3,2,1,0:T(8,128)S(1)}, f32[2,2,2,1,1,43,128]{6,5,4,3,2,1,0:T(8,128)S(1)}, u32[]{:S(2)}, u32[]{:S(2)}) collective-permute-start(f32[2,2,2,1,1,43,128]{6,5,4,3,2,1,0:T(8,128)S(1)} %constant_dynamic-slice_fusion.10), channel_id=1, source_target_pairs={{0,2},{2,0},{4,6},{6,4},{1,3},{3,1},{5,7},{7,5},{8,10},{10,8},{12,... | collective-permute-start | bytes 528392 | tf_op jit(solution)/shard_map/ppermute | solution.py:77
  48.5 4.7 %collective-permute-start.15 = (f32[2,1,2,1,1,43,128]{6,5,4,3,2,1,0:T(8,128)S(1)}, f32[2,1,2,1,1,43,128]{6,5,4,3,2,1,0:T(8,128)S(1)}, u32[]{:S(2)}, u32[]{:S(2)}) collective-permute-start(f32[2,1,2,1,1,43,128]{6,5,4,3,2,1,0:T(8,128)S(1)} %constant_dynamic-slice_fusion.1), channel_id=1, source_target_pairs={{0,2},{2,0},{4,6},{6,4},{1,3},{3,1},{5,7},{7,5},{8,10},{10,8},{12,... | collective-permute-start | bytes 264200 | tf_op jit(solution)/shard_map/ppermute | solution.py:77
  49.4 5.6 %collective-permute-start.11 = (f32[2,1,1,2,1,43,128]{6,5,4,3,2,1,0:T(8,128)S(1)}, f32[2,1,1,2,1,43,128]{6,5,4,3,2,1,0:T(8,128)S(1)}, u32[]{:S(2)}, u32[]{:S(2)}) collective-permute-start(f32[2,1,1,2,1,43,128]{6,5,4,3,2,1,0:T(8,128)S(1)} %constant_dynamic-slice_fusion.5), channel_id=1, source_target_pairs={{0,8},{8,0},{16,24},{24,16},{1,9},{9,1},{17,25},{25,17},{2,10},{10... | collective-permute-start | bytes 264200 | tf_op jit(solution)/shard_map/ppermute | solution.py:77
  50.5 5.2 %collective-permute-start.7 = (f32[2,2,1,1,1,43,128]{6,5,4,3,2,1,0:T(8,128)S(1)}, f32[2,2,1,1,1,43,128]{6,5,4,3,2,1,0:T(8,128)S(1)}, u32[]{:S(2)}, u32[]{:S(2)}) collective-permute-start(f32[2,2,1,1,1,43,128]{6,5,4,3,2,1,0:T(8,128)S(1)} %constant_dynamic-slice_fusion.9), channel_id=1, source_target_pairs={{0,4},{2,6},{4,0},{6,2},{1,5},{3,7},{5,1},{7,3},{8,12},{10,14},{12... | collective-permute-start | bytes 264200 | tf_op jit(solution)/shard_map/ppermute | solution.py:77
  53.2 4.3 %collective-permute-start.16 = (f32[2,1,1,1,1,43,128]{6,5,4,3,2,1,0:T(8,128)S(1)}, f32[2,1,1,1,1,43,128]{6,5,4,3,2,1,0:T(8,128)S(1)}, u32[]{:S(2)}, u32[]{:S(2)}) collective-permute-start(f32[2,1,1,1,1,43,128]{6,5,4,3,2,1,0:T(8,128)S(1)} %constant_dynamic-slice_fusion), channel_id=1, source_target_pairs={{0,4},{2,6},{4,0},{6,2},{1,5},{3,7},{5,1},{7,3},{8,12},{10,14},{12... | collective-permute-start | bytes 132104 | tf_op jit(solution)/shard_map/ppermute | solution.py:77
  55.0 4.2 %collective-permute-start.12 = (f32[2,1,1,1,1,43,128]{6,5,4,3,2,1,0:T(8,128)S(1)}, f32[2,1,1,1,1,43,128]{6,5,4,3,2,1,0:T(8,128)S(1)}, u32[]{:S(2)}, u32[]{:S(2)}) collective-permute-start(f32[2,1,1,1,1,43,128]{6,5,4,3,2,1,0:T(8,128)S(1)} %constant_dynamic-slice_fusion.4), channel_id=1, source_target_pairs={{0,2},{2,0},{4,6},{6,4},{1,3},{3,1},{5,7},{7,5},{8,10},{10,8},{12,... | collective-permute-start | bytes 132104 | tf_op jit(solution)/shard_map/ppermute | solution.py:77
  55.7 5.0 %collective-permute-start.8 = (f32[2,1,1,1,1,43,128]{6,5,4,3,2,1,0:T(8,128)S(1)}, f32[2,1,1,1,1,43,128]{6,5,4,3,2,1,0:T(8,128)S(1)}, u32[]{:S(2)}, u32[]{:S(2)}) collective-permute-start(f32[2,1,1,1,1,43,128]{6,5,4,3,2,1,0:T(8,128)S(1)} %constant_dynamic-slice_fusion.8), channel_id=1, source_target_pairs={{0,8},{8,0},{16,24},{24,16},{1,9},{9,1},{17,25},{25,17},{2,10},{10... | collective-permute-start | bytes 132104 | tf_op jit(solution)/shard_map/ppermute | solution.py:77
  57.6 5.0 %collective-permute-start.17 = (f32[1,1,1,1,1,43,128]{6,5,4,3,2,1,0:T(8,128)S(1)}, f32[1,1,1,1,1,43,128]{6,5,4,3,2,1,0:T(8,128)S(1)}, u32[]{:S(2)}, u32[]{:S(2)}) collective-permute-start(f32[1,1,1,1,1,43,128]{6,5,4,3,2,1,0:T(8,128)S(1)} %constant_dynamic-slice_fusion.12), channel_id=1, source_target_pairs={{0,16},{8,24},{16,0},{24,8},{1,17},{9,25},{17,1},{25,9},{2,18},{10... | collective-permute-start | bytes 66056 | tf_op jit(solution)/shard_map/ppermute | solution.py:77
  59.2 4.8 %collective-permute-start.13 = (f32[1,1,1,1,1,43,128]{6,5,4,3,2,1,0:T(8,128)S(1)}, f32[1,1,1,1,1,43,128]{6,5,4,3,2,1,0:T(8,128)S(1)}, u32[]{:S(2)}, u32[]{:S(2)}) collective-permute-start(f32[1,1,1,1,1,43,128]{6,5,4,3,2,1,0:T(8,128)S(1)} %constant_dynamic-slice_fusion.3), channel_id=1, source_target_pairs={{0,16},{8,24},{16,0},{24,8},{1,17},{9,25},{17,1},{25,9},{2,18},{10... | collective-permute-start | bytes 66056 | tf_op jit(solution)/shard_map/ppermute | solution.py:77
  60.7 4.8 %collective-permute-start.9 = (f32[1,1,1,1,1,43,128]{6,5,4,3,2,1,0:T(8,128)S(1)}, f32[1,1,1,1,1,43,128]{6,5,4,3,2,1,0:T(8,128)S(1)}, u32[]{:S(2)}, u32[]{:S(2)}) collective-permute-start(f32[1,1,1,1,1,43,128]{6,5,4,3,2,1,0:T(8,128)S(1)} %constant_dynamic-slice_fusion.7), channel_id=1, source_target_pairs={{0,16},{8,24},{16,0},{24,8},{1,17},{9,25},{17,1},{25,9},{2,18},{10... | collective-permute-start | bytes 66056 | tf_op jit(solution)/shard_map/ppermute | solution.py:77

commit v11 on v10

--- a/solution.py
+++ b/solution.py
@@ -103,10 +103,12 @@
     return value.reshape(1, rows, lanes)
 
 
-def triangle_kernel(block_len, slot_ref, w_ref, g_ref, m_ref, out_ref, sym_ref):
+def triangle_kernel(block_len, dense, slot_ref, w_ref, g_ref, m_ref, out_ref, sym_ref, rest_ref):
     test, width = w_ref.shape[1], m_ref.shape[1]
     group = 4
+    full = block_len // 128 if dense else out_ref.shape[2] // 128
     out_ref[...] = jnp.zeros(out_ref.shape, out_ref.dtype)
+    rest_ref[...] = jnp.zeros(rest_ref.shape, rest_ref.dtype)
 
     def contract(step, carry):
         slabs = []
@@ -138,20 +140,42 @@
                 base = c * block_len + u * 128
                 rolled = pltpu.roll(slab, (offset - j - base) % 128, 1)
                 keep = (lane >= lo - u * 128) & (lane < hi - u * 128)
-                cur = out_ref[slot, :, pl.ds(u * 128, 128)]
-                out_ref[slot, :, pl.ds(u * 128, 128)] = jnp.where(keep, rolled, cur)
-
-
-def triangle(slots, weighted, grads, modes_flat, block_len):
+                if u < full and dense:
+                    target = out_ref.at[slot, pl.ds(u * test, test), :]
+                elif u < full:
+                    target = out_ref.at[slot, :, pl.ds(u * 128, 128)]
+                else:
+                    target = rest_ref.at[slot]
+                target[...] = jnp.where(keep, rolled, target[...])
+    if dense:
+        spare = block_len - full * 128
+        row = lax.broadcasted_iota(jnp.int32, (test, 128), 0)
+        for s in range(out_ref.shape[0]):
+            tail = rest_ref[s]
+            picked = jnp.zeros((test, 128), jnp.float32)
+            for r in range(spare):
+                hit = (lane >= r * test) & (lane < (r + 1) * test) & (lane - r * test == row)
+                picked = jnp.where(hit, jnp.broadcast_to(tail[:, r : r + 1], (test, 128)), picked)
+            out_ref[s, pl.ds(full * test, 1), :] = jnp.sum(picked, axis=0, keepdims=True)
+
+
+def triangle(slots, weighted, grads, modes_flat, block_len, dense):
     owners = slots.shape[0]
     test, width = weighted.shape[1], modes_flat.shape[1]
     tiles = -(-block_len // 128)
+    if dense:
+        shape = (owners, (block_len // 128) * test + 1, 128)
+    else:
+        shape = (owners, test, tiles * 128)
     return pl.pallas_call(
-        functools.partial(triangle_kernel, block_len),
-        out_shape=jax.ShapeDtypeStruct((owners, test, tiles * 128), jnp.float32),
+        functools.partial(triangle_kernel, block_len, dense),
+        out_shape=jax.ShapeDtypeStruct(shape, jnp.float32),
         in_specs=[pl.BlockSpec(memory_space=pltpu.SMEM)] + [pl.BlockSpec(memory_space=pltpu.VMEM)] * 3,
         out_specs=pl.BlockSpec(memory_space=pltpu.VMEM),
-        scratch_shapes=[pltpu.VMEM((test * width, width), jnp.float32)],
+        scratch_shapes=[
+            pltpu.VMEM((test * width, width), jnp.float32),
+            pltpu.VMEM((owners if dense else 1, test, 128), jnp.float32),
+        ],
     )(slots, weighted, grads, modes_flat)
 
 
@@ -176,14 +200,20 @@
     ranks = jnp.arange(owners, dtype=jnp.int32)
     slots = jnp.sum(jnp.where(pair_owner[None, :] == ranks[:, None], ranks[None, :], 0), axis=1)
     slots = jnp.clip(slots, 0, owners - 1).astype(jnp.int32)
-    placed = triangle(slots, weighted, grads_t, mode_flat.reshape(3 * cells, width), block_len)
+    full, spare = block_len // 128, block_len % 128
+    dense = 0 < spare and spare * TEST <= 128
+    placed = triangle(slots, weighted, grads_t, mode_flat.reshape(3 * cells, width), block_len, dense)
+    if dense:
+        owned = scatter_sum(placed, ("gx", "gy", "gz"))[0]
+        main = owned[: full * TEST].reshape(full, TEST, 128).transpose(1, 0, 2).reshape(TEST, full * 128)
+        tail = owned[full * TEST, : spare * TEST].reshape(spare, TEST).T
+        return jnp.concatenate([main, tail], axis=1)
     partial_terms = placed[:, :, :block_len].reshape(owners, TEST * block_len)
     lanes = 128
     rows = -(-TEST * block_len // lanes)
     partial_terms = jnp.pad(partial_terms, ((0, 0), (0, rows * lanes - TEST * block_len)))
     owned = scatter_sum(partial_terms.reshape(owners, rows, lanes), ("gx", "gy", "gz"))
     return owned.reshape(-1)[: TEST * block_len].reshape(TEST, block_len)
-
 
 def solution(mesh):
     placed = (P("groups", "gx", "gy", "gz", None), P("gx", "gy", "gz"), P())

time: 66.8 us -> 65.3 us (0.978)
  local copies, waits for them, and re-layouts: 9.43 us -> 6.9 us
  waiting for transfers between devices: 12.1 us -> 10.8 us
  starting transfers between devices: 23 us -> 23.8 us
  other arithmetic: 6.05 us -> 6.83 us
    ppermute x2, starting transfers between devices: 4.71 us -> 0.01 us  [face_gradients(): before = lax.ppermute(last, axis, up)]
    another operation x2 -> x1, local copies, waits for them, and re-layouts: 4.61 us -> 0.08 us  [shards(): tail = owned[full * TEST, :spare * TEST].reshape(spare, TEST).T]
    ppermute x2, starting transfers between devices: 3.37 us -> 7.12 us  [face_gradients(): after = lax.ppermute(leading, axis, down)]
    dynamic_slice x0 -> x1, local copies, waits for them, and re-layouts: none -> 1.73 us  [halve(): keep = lax.dynamic_index_in_dim(value, mine, dim, keepdims=True)]
    ppermute x13, waiting for transfers between devices: 12.1 us -> 10.4 us  [halve(): return keep + lax.ppermute(other, axis, pairs)]
    ppermute x13, starting transfers between devices: 14.8 us -> 16.1 us  [halve(): return keep + lax.ppermute(other, axis, pairs)]
    pallas_call x1, Pallas kernels: 15.6 us -> 16.2 us  [triangle(): pl.pallas_call(functools.partial(triangle_kernel, block_len, dense), out_...]
  transfers between devices with their start and end apart: 18 -> 18, of which waited for: 7 -> 7; matrix products, arithmetic and copies ran while one was open for 10% -> 11% of each run, Pallas kernels for 0% -> 0%
where the time goes in v11:
time: 65.3 us; the launch traced here: 64.9 us
  starting transfers between devices  23.8 us (36%)
  Pallas kernels  16.2 us (25%)
  waiting for transfers between devices  10.8 us (17%)
  local copies, waits for them, and re-layouts  6.9 us (11%)
  other arithmetic  6.83 us (10%)
    pallas_call x1, Pallas kernels, triangle(): pl.pallas_call(functools.partial(triangle_kernel, block_len, dense), out_...  16.2 us
    ppermute x13, starting transfers between devices, halve(): return keep + lax.ppermute(other, axis, pairs)  16.1 us
    ppermute x13, waiting for transfers between devices, halve(): return keep + lax.ppermute(other, axis, pairs)  10.4 us
    ppermute x2, starting transfers between devices, face_gradients(): after = lax.ppermute(leading, axis, down)  7.12 us
    dynamic_slice x1, local copies, waits for them, and re-layouts, halve(): keep = lax.dynamic_index_in_dim(value, mine, dim, keepdims=True)  1.73 us
    add x13, other arithmetic, halve(): return keep + lax.ppermute(other, axis, pairs)  1.64 us
    slice x2, local copies, waits for them, and re-layouts, face_gradients(): leading = lax.slice_in_dim(value, 0, 1, axis=dim)  1.59 us
  transfers between devices with their start and end apart: 18, of which 7 were waited for; matrix products, arithmetic and copies ran while one was open for 11% of the time, Pallas kernels for 0%

profile of v11, /device:TPU:0, one launch (start us, length us, event | category | flops | bytes accessed | tf_op | source)
XLA Modules:
  0.0 64.9 jit_solution(9279107745209117770)
XLA Ops:
  0.0 1.1 %broadcast_select_fusion.2 = f32[3,4,8,1,128]{4,3,2,1,0:T(1,128)S(1)} fusion(pred[]{:T(512)S(6)} %eq.37, f32[3,4,8,4,128]{4,3,2,1,0:T(4,128)} %param.3), kind=kLoop, calls=%fused_computation.22 | loop fusion | flops 12288 | bytes 147457 | tf_op jit(solution)/shard_map/jit(_where)/select_n | solution.py:44
  1.1 0.5 collective-permute-start.4
  1.6 0.8 %fusion.8 = (f32[3,1,8,4,128]{4,3,2,1,0:T(4,128)S(1)}, f32[3,1,8,4,128]{4,3,2,1,0:T(4,128)S(1)}) fusion(f32[3,4,8,4,128]{4,3,2,1,0:T(4,128)} %param.3), kind=kLoop, calls=%fused_computation.55 | loop fusion | bytes 196608 | tf_op jit(solution)/shard_map/slice | solution.py:41
  2.5 4.7 %collective-permute-start = (f32[3,1,8,4,128]{4,3,2,1,0:T(4,128)S(1)}, f32[3,1,8,4,128]{4,3,2,1,0:T(4,128)S(1)}, u32[]{:S(2)}, u32[]{:S(2)}) collective-permute-start(f32[3,1,8,4,128]{4,3,2,1,0:T(4,128)S(1)} %get-tuple-element.13), channel_id=1, source_target_pairs={{8,0},{16,8},{24,16},{0,24},{9,1},{17,9},{25,17},{1,25},{10,2},{18... | collective-permute-start | bytes 147464 | tf_op jit(solution)/shard_map/ppermute | solution.py:49
  7.1 0.0 collective-permute-start.1
  7.1 0.8 %fusion.9 = (f32[3,4,1,4,128]{4,3,2,1,0:T(4,128)S(1)}, f32[3,4,1,4,128]{4,3,2,1,0:T(4,128)S(1)}) fusion(f32[3,4,8,4,128]{4,3,2,1,0:T(4,128)} %param.3), kind=kLoop, calls=%fused_computation.56 | loop fusion | bytes 98304 | tf_op jit(solution)/shard_map/slice | solution.py:41
  7.9 2.4 %collective-permute-start.2 = (f32[3,4,1,4,128]{4,3,2,1,0:T(4,128)S(1)}, f32[3,4,1,4,128]{4,3,2,1,0:T(4,128)S(1)}, u32[]{:S(2)}, u32[]{:S(2)}) collective-permute-start(f32[3,4,1,4,128]{4,3,2,1,0:T(4,128)S(1)} %get-tuple-element.15), channel_id=1, source_target_pairs={{2,0},{4,2},{6,4},{0,6},{3,1},{5,3},{7,5},{1,7},{10,8},{12,10},{14... | collective-permute-start | bytes 73736 | tf_op jit(solution)/shard_map/ppermute | solution.py:49
  10.3 0.7 %broadcast_multiply_fusion = f32[4,8,4]{1,2,0:T(4,128)S(1)} fusion(f32[4,8,4]{1,2,0:T(4,128)} %param.4), kind=kLoop, calls=%fused_computation.51 | loop fusion | flops 128 | bytes 1024 | tf_op jit(solution)/shard_map/mul | solution.py:195
  11.0 0.1 copy.23
  11.1 0.1 mul.32
  11.2 0.8 %select_reduce_fusion = s32[32]{0:T(128)S(1)} fusion(s32[32]{0:T(128)} %param.5), kind=kLoop, calls=%fused_computation.35 | loop fusion | flops 3040 | bytes 256 | tf_op jit(solution)/shard_map/reduce_sum | solution.py:201
  12.0 1.0 %fusion.6 = f32[3,64,128]{1,2,0:T(8,128)S(1)} fusion(f32[3,128,128]{2,1,0:T(8,128)} %bitcast.20, f32[128]{0:T(128)S(1)} %mul.32), kind=kLoop, calls=%fused_computation.15 | loop fusion | flops 24576 | bytes 197120 | tf_op jit(solution)/shard_map/transpose | solution.py:196
  13.0 0.5 broadcast_clamp_fusion.slot_ref
  13.6 0.1 copy.24
  13.7 0.1 tile.4
  13.7 0.9 %tile.10.w_ref = f32[3,64,384]{2,1,0:T(8,128)} reshape(f32[3,64,3,128]{3,2,1,0:T(4,128)S(1)} %tile.4) | data formatting | bytes 589824 | tf_op jit(solution)/shard_map/tile | solution.py:196
  14.6 0.1 broadcast_select_fusion.1
  14.7 0.0 collective-permute-done.2
  14.7 0.4 collective-permute-done.3
  15.1 0.0 collective-permute-done
  15.1 0.0 collective-permute-done.1
  15.1 0.3 fusion.5
  15.4 1.1 %copy.25.g_ref = f32[3,128,384]{2,1,0:T(8,128)} copy(f32[3,128,384]{1,2,0:T(8,128)S(1)} %bitcast.22) | data formatting | bytes 1179648 | tf_op jit(solution)/shard_map/reshape | solution.py:197
  16.5 16.2 %shard_map.37 = f32[32,129,128]{2,1,0:T(8,128)} custom-call(s32[32]{0:T(128)} %broadcast_clamp_fusion.slot_ref, f32[3,64,384]{2,1,0:T(8,128)} %tile.10.w_ref, f32[3,128,384]{2,1,0:T(8,128)} %copy.25.g_ref, f32[384,128]{1,0:T(8,128)} %bitcast.21), custom_call_target="tpu_custom_call" | custom-call | tf_op jit(solution)/shard_map/pallas_call | solution.py:170
  32.7 1.7 %constant_dynamic-slice_fusion.12 = (f32[2,2,2,2,1,129,128]{6,5,4,3,2,1,0:T(8,128)S(1)}, f32[2,2,2,2,1,129,128]{6,5,4,3,2,1,0:T(8,128)S(1)}) fusion(f32[2,2,2,2,2,129,128]{6,5,4,3,2,1,0:T(8,128)} %bitcast.19, s32[]{:T(128)S(6)} %select_n.145, s32[]{:T(128)S(6)} %select_n.146), kind=kLoop, calls=%fused_computation.49 | loop fusion | bytes 4227080 | tf_op jit(solution)/shard_map/jit(dynamic_index_in_dim)/dynamic_slice | solution.py:75
  34.5 0.5 copy.31
  35.0 0.1 collective-permute-start.5
  35.2 2.6 %collective-permute-done.5 = f32[2,2,2,2,1,129,128]{6,3,5,4,2,1,0:T(2,128)S(1)} collective-permute-done((f32[2,2,2,2,1,129,128]{6,3,5,4,2,1,0:T(2,128)S(1)}, f32[2,2,2,2,1,129,128]{6,3,5,4,2,1,0:T(2,128)S(1)}, u32[]{:S(2)}, u32[]{:S(2)}) %collective-permute-start.5) | collective-permute-done | bytes 1056800 | tf_op jit(solution)/shard_map/ppermute | solution.py:77
  37.7 0.7 %copy_add_fusion = f32[2,2,2,2,1,129,128]{6,3,5,4,2,1,0:T(2,128)S(1)} fusion(f32[2,2,2,2,1,129,128]{6,3,5,4,2,1,0:T(2,128)S(1)} %collective-permute-done.5, f32[2,2,2,2,1,129,128]{6,5,4,3,2,1,0:T(8,128)S(1)} %get-tuple-element.5), kind=kLoop, calls=%fused_computation | loop fusion | flops 264192 | bytes 3170304 | tf_op jit(solution)/shard_map/add | solution.py:77
  38.5 0.1 fusion.7
  38.6 0.2 constant_dynamic-slice_fusion.10
  38.7 1.7 %collective-permute-start.6 = (f32[2,2,2,1,1,43,128]{6,3,5,4,2,1,0:T(1,128)S(1)}, f32[2,2,2,1,1,43,128]{6,3,5,4,2,1,0:T(1,128)S(1)}, u32[]{:S(2)}, u32[]{:S(2)}) collective-permute-start(f32[2,2,2,1,1,43,128]{6,3,5,4,2,1,0:T(1,128)S(1)} %constant_dynamic-slice_fusion.10), channel_id=1, source_target_pairs={{0,2},{2,0},{4,6},{6,4},{1,3},{3,1},{5,7},{7,5},{8,10},{10,8},{12,... | collective-permute-start | bytes 528392 | tf_op jit(solution)/shard_map/ppermute | solution.py:77
  40.4 1.6 %collective-permute-start.10 = (f32[2,2,1,2,1,43,128]{6,3,5,4,2,1,0:T(2,128)S(1)}, f32[2,2,1,2,1,43,128]{6,3,5,4,2,1,0:T(2,128)S(1)}, u32[]{:S(2)}, u32[]{:S(2)}) collective-permute-start(f32[2,2,1,2,1,43,128]{6,3,5,4,2,1,0:T(2,128)S(1)} %constant_dynamic-slice_fusion.6), channel_id=1, source_target_pairs={{0,4},{2,6},{4,0},{6,2},{1,5},{3,7},{5,1},{7,3},{8,12},{10,14},{12... | collective-permute-start | bytes 528392 | tf_op jit(solution)/shard_map/ppermute | solution.py:77
  42.1 0.1 collective-permute-start.14
  42.1 3.2 %collective-permute-done.6 = f32[2,2,2,1,1,43,128]{6,3,5,4,2,1,0:T(1,128)S(1)} collective-permute-done((f32[2,2,2,1,1,43,128]{6,3,5,4,2,1,0:T(1,128)S(1)}, f32[2,2,2,1,1,43,128]{6,3,5,4,2,1,0:T(1,128)S(1)}, u32[]{:S(2)}, u32[]{:S(2)}) %collective-permute-start.6) | collective-permute-done | bytes 176160 | tf_op jit(solution)/shard_map/ppermute | solution.py:77
  45.3 0.2 dynamic-slice_add_fusion.2
  45.6 1.5 %collective-permute-start.7 = (f32[2,2,1,1,1,43,128]{6,3,5,4,2,1,0:T(1,128)S(1)}, f32[2,2,1,1,1,43,128]{6,3,5,4,2,1,0:T(1,128)S(1)}, u32[]{:S(2)}, u32[]{:S(2)}) collective-permute-start(f32[2,2,1,1,1,43,128]{6,3,5,4,2,1,0:T(1,128)S(1)} %constant_dynamic-slice_fusion.9), channel_id=1, source_target_pairs={{0,4},{2,6},{4,0},{6,2},{1,5},{3,7},{5,1},{7,3},{8,12},{10,14},{12... | collective-permute-start | bytes 264200 | tf_op jit(solution)/shard_map/ppermute | solution.py:77
  47.0 0.1 dynamic-slice_add_fusion.1
  47.2 0.1 collective-permute-start.11
  47.3 0.8 %collective-permute-done.14 = f32[2,1,2,2,1,43,128]{6,3,5,4,2,1,0:T(2,128)S(1)} collective-permute-done((f32[2,1,2,2,1,43,128]{6,3,5,4,2,1,0:T(2,128)S(1)}, f32[2,1,2,2,1,43,128]{6,3,5,4,2,1,0:T(2,128)S(1)}, u32[]{:S(2)}, u32[]{:S(2)}) %collective-permute-start.14) | collective-permute-done | bytes 176160 | tf_op jit(solution)/shard_map/ppermute | solution.py:77
  48.1 0.1 dynamic-slice_add_fusion
  48.2 0.1 constant_dynamic-slice_fusion.1
  48.3 1.0 %collective-permute-start.15 = (f32[2,1,2,1,1,43,128]{6,3,5,4,2,1,0:T(1,128)S(1)}, f32[2,1,2,1,1,43,128]{6,3,5,4,2,1,0:T(1,128)S(1)}, u32[]{:S(2)}, u32[]{:S(2)}) collective-permute-start(f32[2,1,2,1,1,43,128]{6,3,5,4,2,1,0:T(1,128)S(1)} %constant_dynamic-slice_fusion.1), channel_id=1, source_target_pairs={{0,2},{2,0},{4,6},{6,4},{1,3},{3,1},{5,7},{7,5},{8,10},{10,8},{12,... | collective-permute-start | bytes 264200 | tf_op jit(solution)/shard_map/ppermute | solution.py:77
  49.3 0.9 %collective-permute-done.7 = f32[2,2,1,1,1,43,128]{6,3,5,4,2,1,0:T(1,128)S(1)} collective-permute-done((f32[2,2,1,1,1,43,128]{6,3,5,4,2,1,0:T(1,128)S(1)}, f32[2,2,1,1,1,43,128]{6,3,5,4,2,1,0:T(1,128)S(1)}, u32[]{:S(2)}, u32[]{:S(2)}) %collective-permute-start.7) | collective-permute-done | bytes 88096 | tf_op jit(solution)/shard_map/ppermute | solution.py:77
  50.1 0.1 dynamic-slice_add_fusion.5
  50.2 1.2 %collective-permute-start.8 = (f32[2,1,1,1,1,43,128]{6,3,5,4,2,1,0:T(1,128)S(1)}, f32[2,1,1,1,1,43,128]{6,3,5,4,2,1,0:T(1,128)S(1)}, u32[]{:S(2)}, u32[]{:S(2)}) collective-permute-start(f32[2,1,1,1,1,43,128]{6,3,5,4,2,1,0:T(1,128)S(1)} %constant_dynamic-slice_fusion.8), channel_id=1, source_target_pairs={{0,8},{8,0},{16,24},{24,16},{1,9},{9,1},{17,25},{25,17},{2,10},{10... | collective-permute-start | bytes 132104 | tf_op jit(solution)/shard_map/ppermute | solution.py:77
  51.5 0.8 %collective-permute-done.11 = f32[2,1,1,2,1,43,128]{6,3,5,4,2,1,0:T(2,128)S(1)} collective-permute-done((f32[2,1,1,2,1,43,128]{6,3,5,4,2,1,0:T(2,128)S(1)}, f32[2,1,1,2,1,43,128]{6,3,5,4,2,1,0:T(2,128)S(1)}, u32[]{:S(2)}, u32[]{:S(2)}) %collective-permute-start.11) | collective-permute-done | bytes 88096 | tf_op jit(solution)/shard_map/ppermute | solution.py:77
  52.3 1.8 %collective-permute-start.12 = (f32[2,1,1,1,1,43,128]{6,3,5,4,2,1,0:T(1,128)S(1)}, f32[2,1,1,1,1,43,128]{6,3,5,4,2,1,0:T(1,128)S(1)}, u32[]{:S(2)}, u32[]{:S(2)}) collective-permute-start(f32[2,1,1,1,1,43,128]{6,3,5,4,2,1,0:T(1,128)S(1)} %constant_dynamic-slice_fusion.4), channel_id=1, source_target_pairs={{0,2},{2,0},{4,6},{6,4},{1,3},{3,1},{5,7},{7,5},{8,10},{10,8},{12,... | collective-permute-start | bytes 132104 | tf_op jit(solution)/shard_map/ppermute | solution.py:77
  54.1 0.0 collective-permute-done.15
  54.1 0.1 dynamic-slice_add_fusion.3
  54.3 0.1 collective-permute-start.16
  54.4 0.0 collective-permute-done.8
  54.4 4.0 %collective-permute-start.9 = (f32[1,1,1,1,1,43,128]{6,3,5,4,2,1,0:T(1,128)S(1)}, f32[1,1,1,1,1,43,128]{6,3,5,4,2,1,0:T(1,128)S(1)}, u32[]{:S(2)}, u32[]{:S(2)}) collective-permute-start(f32[1,1,1,1,1,43,128]{6,3,5,4,2,1,0:T(1,128)S(1)} %constant_dynamic-slice_fusion.7), channel_id=1, source_target_pairs={{0,16},{8,24},{16,0},{24,8},{1,17},{9,25},{17,1},{25,9},{2,18},{10... | collective-permute-start | bytes 66056 | tf_op jit(solution)/shard_map/ppermute | solution.py:77
  58.4 0.0 collective-permute-done.12
  58.4 0.1 dynamic-slice_add_fusion.7
  58.5 0.5 collective-permute-start.13
  59.1 2.5 %collective-permute-start.17 = (f32[1,1,1,1,1,43,128]{6,3,5,4,2,1,0:T(1,128)S(1)}, f32[1,1,1,1,1,43,128]{6,3,5,4,2,1,0:T(1,128)S(1)}, u32[]{:S(2)}, u32[]{:S(2)}) collective-permute-start(f32[1,1,1,1,1,43,128]{6,3,5,4,2,1,0:T(1,128)S(1)} %constant_dynamic-slice_fusion.13), channel_id=1, source_target_pairs={{0,16},{8,24},{16,0},{24,8},{1,17},{9,25},{17,1},{25,9},{2,18},{10... | collective-permute-start | bytes 66056 | tf_op jit(solution)/shard_map/ppermute | solution.py:77
  61.6 0.0 collective-permute-done.9
  61.7 2.2 %collective-permute-done.17 = f32[1,1,1,1,1,43,128]{6,3,5,4,2,1,0:T(1,128)S(1)} collective-permute-done((f32[1,1,1,1,1,43,128]{6,3,5,4,2,1,0:T(1,128)S(1)}, f32[1,1,1,1,1,43,128]{6,3,5,4,2,1,0:T(1,128)S(1)}, u32[]{:S(2)}, u32[]{:S(2)}) %collective-permute-start.17) | collective-permute-done | bytes 22048 | tf_op jit(solution)/shard_map/ppermute | solution.py:77
  63.9 0.0 collective-permute-done.13
  64.0 0.1 pad_maximum_fusion.8
  64.1 0.1 reshape_squeeze.3
  64.1 0.1 copy.29
  64.2 0.6 %pad_maximum_fusion.7 = f32[64,258]{1,0:T(8,128)} fusion(f32[64,2]{1,0:T(8,128)S(1)} %copy.29, f32[64,256]{1,0:T(8,128)S(1)} %bitcast.26), kind=kLoop, calls=%fused_computation.19 | loop fusion | flops 16512 | bytes 132096 | tf_op jit(solution)/shard_map/concatenate | solution.py:210
  (25 shorter events, 0.5 us)
Async XLA Ops:
  1.1 13.5 %collective-permute-start.4 = (f32[3,4,8,1,128]{4,3,2,1,0:T(1,128)S(1)}, f32[3,4,8,1,128]{4,3,2,1,0:T(1,128)S(1)}, u32[]{:S(2)}, u32[]{:S(2)}) collective-permute-start(f32[3,4,8,1,128]{4,3,2,1,0:T(1,128)S(1)} %broadcast_select_fusion.2), channel_id=1, source_target_pairs={{0,1},{1,0},{2,3},{3,2},{4,5},{5,4},{6,7},{7,6},{8,9},{9,8},{10,11... | collective-permute-start | bytes 147464 | tf_op jit(solution)/shard_map/ppermute | solution.py:44
  2.5 12.6 %copy-start = (f32[3,4,8,4,128]{4,3,2,1,0:T(4,128)S(1)}, f32[3,4,8,4,128]{4,3,2,1,0:T(4,128)}, u32[]{:S(2)}) copy-start(f32[3,4,8,4,128]{4,3,2,1,0:T(4,128)} %param.3) | copy-start | bytes 589828
  2.5 12.6 %collective-permute-start = (f32[3,1,8,4,128]{4,3,2,1,0:T(4,128)S(1)}, f32[3,1,8,4,128]{4,3,2,1,0:T(4,128)S(1)}, u32[]{:S(2)}, u32[]{:S(2)}) collective-permute-start(f32[3,1,8,4,128]{4,3,2,1,0:T(4,128)S(1)} %get-tuple-element.13), channel_id=1, source_target_pairs={{8,0},{16,8},{24,16},{0,24},{9,1},{17,9},{25,17},{1,25},{10,2},{18... | collective-permute-start | bytes 147464 | tf_op jit(solution)/shard_map/ppermute | solution.py:49
  7.1 7.9 %collective-permute-start.1 = (f32[3,1,8,4,128]{4,3,2,1,0:T(4,128)S(1)}, f32[3,1,8,4,128]{4,3,2,1,0:T(4,128)S(1)}, u32[]{:S(2)}, u32[]{:S(2)}) collective-permute-start(f32[3,1,8,4,128]{4,3,2,1,0:T(4,128)S(1)} %get-tuple-element.14), channel_id=1, source_target_pairs={{0,8},{8,16},{16,24},{24,0},{1,9},{9,17},{17,25},{25,1},{2,10},{10... | collective-permute-start | bytes 147464 | tf_op jit(solution)/shard_map/ppermute | solution.py:48
  7.9 6.8 %collective-permute-start.2 = (f32[3,4,1,4,128]{4,3,2,1,0:T(4,128)S(1)}, f32[3,4,1,4,128]{4,3,2,1,0:T(4,128)S(1)}, u32[]{:S(2)}, u32[]{:S(2)}) collective-permute-start(f32[3,4,1,4,128]{4,3,2,1,0:T(4,128)S(1)} %get-tuple-element.15), channel_id=1, source_target_pairs={{2,0},{4,2},{6,4},{0,6},{3,1},{5,3},{7,5},{1,7},{10,8},{12,10},{14... | collective-permute-start | bytes 73736 | tf_op jit(solution)/shard_map/ppermute | solution.py:49
  10.3 4.7 %collective-permute-start.3 = (f32[3,4,1,4,128]{4,3,2,1,0:T(4,128)S(1)}, f32[3,4,1,4,128]{4,3,2,1,0:T(4,128)S(1)}, u32[]{:S(2)}, u32[]{:S(2)}) collective-permute-start(f32[3,4,1,4,128]{4,3,2,1,0:T(4,128)S(1)} %get-tuple-element.16), channel_id=1, source_target_pairs={{0,2},{2,4},{4,6},{6,0},{1,3},{3,5},{5,7},{7,1},{8,10},{10,12},{12... | collective-permute-start | bytes 73736 | tf_op jit(solution)/shard_map/ppermute | solution.py:48
  35.0 2.7 %collective-permute-start.5 = (f32[2,2,2,2,1,129,128]{6,3,5,4,2,1,0:T(2,128)S(1)}, f32[2,2,2,2,1,129,128]{6,3,5,4,2,1,0:T(2,128)S(1)}, u32[]{:S(2)}, u32[]{:S(2)}) collective-permute-start(f32[2,2,2,2,1,129,128]{6,3,5,4,2,1,0:T(2,128)S(1)} %copy.31), channel_id=1, source_target_pairs={{0,1},{1,0},{2,3},{3,2},{4,5},{5,4},{6,7},{7,6},{8,9},{9,8},{10,11... | collective-permute-start | bytes 3170312 | tf_op jit(solution)/shard_map/ppermute | solution.py:77
  38.7 6.6 %collective-permute-start.6 = (f32[2,2,2,1,1,43,128]{6,3,5,4,2,1,0:T(1,128)S(1)}, f32[2,2,2,1,1,43,128]{6,3,5,4,2,1,0:T(1,128)S(1)}, u32[]{:S(2)}, u32[]{:S(2)}) collective-permute-start(f32[2,2,2,1,1,43,128]{6,3,5,4,2,1,0:T(1,128)S(1)} %constant_dynamic-slice_fusion.10), channel_id=1, source_target_pairs={{0,2},{2,0},{4,6},{6,4},{1,3},{3,1},{5,7},{7,5},{8,10},{10,8},{12,... | collective-permute-start | bytes 528392 | tf_op jit(solution)/shard_map/ppermute | solution.py:77
  40.4 6.6 %collective-permute-start.10 = (f32[2,2,1,2,1,43,128]{6,3,5,4,2,1,0:T(2,128)S(1)}, f32[2,2,1,2,1,43,128]{6,3,5,4,2,1,0:T(2,128)S(1)}, u32[]{:S(2)}, u32[]{:S(2)}) collective-permute-start(f32[2,2,1,2,1,43,128]{6,3,5,4,2,1,0:T(2,128)S(1)} %constant_dynamic-slice_fusion.6), channel_id=1, source_target_pairs={{0,4},{2,6},{4,0},{6,2},{1,5},{3,7},{5,1},{7,3},{8,12},{10,14},{12... | collective-permute-start | bytes 528392 | tf_op jit(solution)/shard_map/ppermute | solution.py:77
  42.1 6.0 %collective-permute-start.14 = (f32[2,1,2,2,1,43,128]{6,3,5,4,2,1,0:T(2,128)S(1)}, f32[2,1,2,2,1,43,128]{6,3,5,4,2,1,0:T(2,128)S(1)}, u32[]{:S(2)}, u32[]{:S(2)}) collective-permute-start(f32[2,1,2,2,1,43,128]{6,3,5,4,2,1,0:T(2,128)S(1)} %constant_dynamic-slice_fusion.2), channel_id=1, source_target_pairs={{0,8},{8,0},{16,24},{24,16},{1,9},{9,1},{17,25},{25,17},{2,10},{10... | collective-permute-start | bytes 528392 | tf_op jit(solution)/shard_map/ppermute | solution.py:77
  45.6 4.6 %collective-permute-start.7 = (f32[2,2,1,1,1,43,128]{6,3,5,4,2,1,0:T(1,128)S(1)}, f32[2,2,1,1,1,43,128]{6,3,5,4,2,1,0:T(1,128)S(1)}, u32[]{:S(2)}, u32[]{:S(2)}) collective-permute-start(f32[2,2,1,1,1,43,128]{6,3,5,4,2,1,0:T(1,128)S(1)} %constant_dynamic-slice_fusion.9), channel_id=1, source_target_pairs={{0,4},{2,6},{4,0},{6,2},{1,5},{3,7},{5,1},{7,3},{8,12},{10,14},{12... | collective-permute-start | bytes 264200 | tf_op jit(solution)/shard_map/ppermute | solution.py:77
  47.2 5.0 %collective-permute-start.11 = (f32[2,1,1,2,1,43,128]{6,3,5,4,2,1,0:T(2,128)S(1)}, f32[2,1,1,2,1,43,128]{6,3,5,4,2,1,0:T(2,128)S(1)}, u32[]{:S(2)}, u32[]{:S(2)}) collective-permute-start(f32[2,1,1,2,1,43,128]{6,3,5,4,2,1,0:T(2,128)S(1)} %constant_dynamic-slice_fusion.5), channel_id=1, source_target_pairs={{0,8},{8,0},{16,24},{24,16},{1,9},{9,1},{17,25},{25,17},{2,10},{10... | collective-permute-start | bytes 264200 | tf_op jit(solution)/shard_map/ppermute | solution.py:77
  48.3 5.9 %collective-permute-start.15 = (f32[2,1,2,1,1,43,128]{6,3,5,4,2,1,0:T(1,128)S(1)}, f32[2,1,2,1,1,43,128]{6,3,5,4,2,1,0:T(1,128)S(1)}, u32[]{:S(2)}, u32[]{:S(2)}) collective-permute-start(f32[2,1,2,1,1,43,128]{6,3,5,4,2,1,0:T(1,128)S(1)} %constant_dynamic-slice_fusion.1), channel_id=1, source_target_pairs={{0,2},{2,0},{4,6},{6,4},{1,3},{3,1},{5,7},{7,5},{8,10},{10,8},{12,... | collective-permute-start | bytes 264200 | tf_op jit(solution)/shard_map/ppermute | solution.py:77
  50.2 4.1 %collective-permute-start.8 = (f32[2,1,1,1,1,43,128]{6,3,5,4,2,1,0:T(1,128)S(1)}, f32[2,1,1,1,1,43,128]{6,3,5,4,2,1,0:T(1,128)S(1)}, u32[]{:S(2)}, u32[]{:S(2)}) collective-permute-start(f32[2,1,1,1,1,43,128]{6,3,5,4,2,1,0:T(1,128)S(1)} %constant_dynamic-slice_fusion.8), channel_id=1, source_target_pairs={{0,8},{8,0},{16,24},{24,16},{1,9},{9,1},{17,25},{25,17},{2,10},{10... | collective-permute-start | bytes 132104 | tf_op jit(solution)/shard_map/ppermute | solution.py:77
  52.3 6.1 %collective-permute-start.12 = (f32[2,1,1,1,1,43,128]{6,3,5,4,2,1,0:T(1,128)S(1)}, f32[2,1,1,1,1,43,128]{6,3,5,4,2,1,0:T(1,128)S(1)}, u32[]{:S(2)}, u32[]{:S(2)}) collective-permute-start(f32[2,1,1,1,1,43,128]{6,3,5,4,2,1,0:T(1,128)S(1)} %constant_dynamic-slice_fusion.4), channel_id=1, source_target_pairs={{0,2},{2,0},{4,6},{6,4},{1,3},{3,1},{5,7},{7,5},{8,10},{10,8},{12,... | collective-permute-start | bytes 132104 | tf_op jit(solution)/shard_map/ppermute | solution.py:77
  54.3 4.8 %collective-permute-start.16 = (f32[2,1,1,1,1,43,128]{6,3,5,4,2,1,0:T(1,128)S(1)}, f32[2,1,1,1,1,43,128]{6,3,5,4,2,1,0:T(1,128)S(1)}, u32[]{:S(2)}, u32[]{:S(2)}) collective-permute-start(f32[2,1,1,1,1,43,128]{6,3,5,4,2,1,0:T(1,128)S(1)} %constant_dynamic-slice_fusion), channel_id=1, source_target_pairs={{0,4},{2,6},{4,0},{6,2},{1,5},{3,7},{5,1},{7,3},{8,12},{10,14},{12... | collective-permute-start | bytes 132104 | tf_op jit(solution)/shard_map/ppermute | solution.py:77
  54.4 7.2 %collective-permute-start.9 = (f32[1,1,1,1,1,43,128]{6,3,5,4,2,1,0:T(1,128)S(1)}, f32[1,1,1,1,1,43,128]{6,3,5,4,2,1,0:T(1,128)S(1)}, u32[]{:S(2)}, u32[]{:S(2)}) collective-permute-start(f32[1,1,1,1,1,43,128]{6,3,5,4,2,1,0:T(1,128)S(1)} %constant_dynamic-slice_fusion.7), channel_id=1, source_target_pairs={{0,16},{8,24},{16,0},{24,8},{1,17},{9,25},{17,1},{25,9},{2,18},{10... | collective-permute-start | bytes 66056 | tf_op jit(solution)/shard_map/ppermute | solution.py:77
  58.5 5.4 %collective-permute-start.13 = (f32[1,1,1,1,1,43,128]{6,3,5,4,2,1,0:T(1,128)S(1)}, f32[1,1,1,1,1,43,128]{6,3,5,4,2,1,0:T(1,128)S(1)}, u32[]{:S(2)}, u32[]{:S(2)}) collective-permute-start(f32[1,1,1,1,1,43,128]{6,3,5,4,2,1,0:T(1,128)S(1)} %constant_dynamic-slice_fusion.3), channel_id=1, source_target_pairs={{0,16},{8,24},{16,0},{24,8},{1,17},{9,25},{17,1},{25,9},{2,18},{10... | collective-permute-start | bytes 66056 | tf_op jit(solution)/shard_map/ppermute | solution.py:77
  59.1 4.8 %collective-permute-start.17 = (f32[1,1,1,1,1,43,128]{6,3,5,4,2,1,0:T(1,128)S(1)}, f32[1,1,1,1,1,43,128]{6,3,5,4,2,1,0:T(1,128)S(1)}, u32[]{:S(2)}, u32[]{:S(2)}) collective-permute-start(f32[1,1,1,1,1,43,128]{6,3,5,4,2,1,0:T(1,128)S(1)} %constant_dynamic-slice_fusion.13), channel_id=1, source_target_pairs={{0,16},{8,24},{16,0},{24,8},{1,17},{9,25},{17,1},{25,9},{2,18},{10... | collective-permute-start | bytes 66056 | tf_op jit(solution)/shard_map/ppermute | solution.py:77

commit v12 on v11

--- a/solution.py
+++ b/solution.py
@@ -77,14 +77,14 @@
     return keep + lax.ppermute(other, axis, pairs)
 
 
-def scatter_sum(payload, axes):
+def scatter_sum(payload, axes, local=True):
     sizes = [lax.axis_size(a) for a in axes]
     if any(s & (s - 1) for s in sizes):
         return lax.psum_scatter(payload, tuple(axes), scatter_dimension=0, tiled=True)
     stages = halving_stages(axes)
     rows, lanes = payload.shape[1], payload.shape[2]
     value = payload.reshape((2,) * len(stages) + (rows, lanes))
-    first = [k for k, s in enumerate(stages) if s[0] == axes[-1]]
+    first = [k for k, s in enumerate(stages) if local and s[0] == axes[-1]]
     for k in first:
         value = halve(value, *stages[k], k)
     rest = [k for k in range(len(stages)) if k not in first]
@@ -103,7 +103,7 @@
     return value.reshape(1, rows, lanes)
 
 
-def triangle_kernel(block_len, dense, slot_ref, w_ref, g_ref, m_ref, out_ref, sym_ref, rest_ref):
+def triangle_kernel(block_len, dense, slot_ref, side_ref, w_ref, g_ref, m_ref, out_ref, sym_ref, rest_ref):
     test, width = w_ref.shape[1], m_ref.shape[1]
     group = 4
     full = block_len // 128 if dense else out_ref.shape[2] // 128
@@ -141,7 +141,7 @@
                 rolled = pltpu.roll(slab, (offset - j - base) % 128, 1)
                 keep = (lane >= lo - u * 128) & (lane < hi - u * 128)
                 if u < full and dense:
-                    target = out_ref.at[slot, pl.ds(u * test, test), :]
+                    target = out_ref.at[(slot + side_ref[0]) % 2, slot // 2, pl.ds(u * test, test), :]
                 elif u < full:
                     target = out_ref.at[slot, :, pl.ds(u * 128, 128)]
                 else:
@@ -150,33 +150,33 @@
     if dense:
         spare = block_len - full * 128
         row = lax.broadcasted_iota(jnp.int32, (test, 128), 0)
-        for s in range(out_ref.shape[0]):
+        for s in range(rest_ref.shape[0]):
             tail = rest_ref[s]
             picked = jnp.zeros((test, 128), jnp.float32)
             for r in range(spare):
                 hit = (lane >= r * test) & (lane < (r + 1) * test) & (lane - r * test == row)
                 picked = jnp.where(hit, jnp.broadcast_to(tail[:, r : r + 1], (test, 128)), picked)
-            out_ref[s, pl.ds(full * test, 1), :] = jnp.sum(picked, axis=0, keepdims=True)
-
-
-def triangle(slots, weighted, grads, modes_flat, block_len, dense):
+            out_ref[(s + side_ref[0]) % 2, s // 2, pl.ds(full * test, 1), :] = jnp.sum(picked, axis=0, keepdims=True)
+
+
+def triangle(slots, side, weighted, grads, modes_flat, block_len, dense):
     owners = slots.shape[0]
     test, width = weighted.shape[1], modes_flat.shape[1]
     tiles = -(-block_len // 128)
     if dense:
-        shape = (owners, (block_len // 128) * test + 1, 128)
+        shape = (2, owners // 2, (block_len // 128) * test + 1, 128)
     else:
         shape = (owners, test, tiles * 128)
     return pl.pallas_call(
         functools.partial(triangle_kernel, block_len, dense),
         out_shape=jax.ShapeDtypeStruct(shape, jnp.float32),
-        in_specs=[pl.BlockSpec(memory_space=pltpu.SMEM)] + [pl.BlockSpec(memory_space=pltpu.VMEM)] * 3,
+        in_specs=[pl.BlockSpec(memory_space=pltpu.SMEM)] * 2 + [pl.BlockSpec(memory_space=pltpu.VMEM)] * 3,
         out_specs=pl.BlockSpec(memory_space=pltpu.VMEM),
         scratch_shapes=[
             pltpu.VMEM((test * width, width), jnp.float32),
             pltpu.VMEM((owners if dense else 1, test, 128), jnp.float32),
         ],
-    )(slots, weighted, grads, modes_flat)
+    )(slots, side, weighted, grads, modes_flat)
 
 
 def shards(modes, cell_weight, pair_owner):
@@ -201,10 +201,12 @@
     slots = jnp.sum(jnp.where(pair_owner[None, :] == ranks[:, None], ranks[None, :], 0), axis=1)
     slots = jnp.clip(slots, 0, owners - 1).astype(jnp.int32)
     full, spare = block_len // 128, block_len % 128
-    dense = 0 < spare and spare * TEST <= 128
-    placed = triangle(slots, weighted, grads_t, mode_flat.reshape(3 * cells, width), block_len, dense)
+    dense = 0 < spare and spare * TEST <= 128 and size_z == 2
+    side = lax.axis_index("gz").astype(jnp.int32).reshape(1)
+    placed = triangle(slots, side, weighted, grads_t, mode_flat.reshape(3 * cells, width), block_len, dense)
     if dense:
-        owned = scatter_sum(placed, ("gx", "gy", "gz"))[0]
+        merged = placed[0] + lax.ppermute(placed[1], "gz", [(0, 1), (1, 0)])
+        owned = scatter_sum(merged, ("gx", "gy"), local=False)[0]
         main = owned[: full * TEST].reshape(full, TEST, 128).transpose(1, 0, 2).reshape(TEST, full * 128)
         tail = owned[full * TEST, : spare * TEST].reshape(spare, TEST).T
         return jnp.concatenate([main, tail], axis=1)

time: 65.3 us -> 65.4 us (level)
  waiting for transfers between devices: 10.8 us -> 12.7 us
  other arithmetic: 6.83 us -> 5.65 us
  starting transfers between devices: 23.8 us -> 23.1 us
    ppermute x0 -> x1, waiting for transfers between devices: none -> 2.88 us  [shards(): merged = placed[0] + lax.ppermute(placed[1], 'gz', [(0, 1), (1, 0)])]
    squeeze x0 -> x2, local copies, waits for them, and re-layouts: none -> 2.51 us  [shards(): merged = placed[0] + lax.ppermute(placed[1], 'gz', [(0, 1), (1, 0)])]
    dynamic_slice x1 -> x0, local copies, waits for them, and re-layouts: 1.73 us -> none  [halve(): keep = lax.dynamic_index_in_dim(value, mine, dim, keepdims=True)]
    add x13 -> x12, other arithmetic: 1.64 us -> 0.16 us  [halve(): return keep + lax.ppermute(other, axis, pairs)]
    ppermute x13 -> x12, waiting for transfers between devices: 10.4 us -> 9.49 us  [halve(): return keep + lax.ppermute(other, axis, pairs)]
    ppermute x13 -> x12, starting transfers between devices: 16.1 us -> 15.4 us  [halve(): return keep + lax.ppermute(other, axis, pairs)]
  transfers between devices with their start and end apart: 18 -> 18, of which waited for: 7 -> 8; matrix products, arithmetic and copies ran while one was open for 11% -> 10% of each run, Pallas kernels for 0% -> 0%
where the time goes in v12:
time: 65.4 us; the launch traced here: 65 us
  starting transfers between devices  23.1 us (35%)
  Pallas kernels  16.3 us (25%)
  waiting for transfers between devices  12.7 us (19%)
  local copies, waits for them, and re-layouts  7 us (11%)
  other arithmetic  5.65 us (9%)
    pallas_call x1, Pallas kernels, triangle(): pl.pallas_call(functools.partial(triangle_kernel, block_len, dense), out_...  16.3 us
    ppermute x12, starting transfers between devices, halve(): return keep + lax.ppermute(other, axis, pairs)  15.4 us
    ppermute x12, waiting for transfers between devices, halve(): return keep + lax.ppermute(other, axis, pairs)  9.49 us
    ppermute x2, starting transfers between devices, face_gradients(): after = lax.ppermute(leading, axis, down)  7.12 us
    ppermute x1, waiting for transfers between devices, shards(): merged = placed[0] + lax.ppermute(placed[1], 'gz', [(0, 1), (1, 0)])  2.88 us
    squeeze x2, local copies, waits for them, and re-layouts, shards(): merged = placed[0] + lax.ppermute(placed[1], 'gz', [(0, 1), (1, 0)])  2.51 us
    slice x2, local copies, waits for them, and re-layouts, face_gradients(): leading = lax.slice_in_dim(value, 0, 1, axis=dim)  1.59 us
  transfers between devices with their start and end apart: 18, of which 8 were waited for; matrix products, arithmetic and copies ran while one was open for 10% of the time, Pallas kernels for 0%

profile of v12, /device:TPU:0, one launch (start us, length us, event | category | flops | bytes accessed | tf_op | source)
XLA Modules:
  0.0 65.0 jit_solution(13896241689778806508)
XLA Ops:
  0.0 1.1 %broadcast_select_fusion.2 = f32[3,4,8,1,128]{4,3,2,1,0:T(1,128)S(1)} fusion(pred[]{:T(512)S(6)} %eq.36, f32[3,4,8,4,128]{4,3,2,1,0:T(4,128)} %param.3), kind=kLoop, calls=%fused_computation.27 | loop fusion | flops 12288 | bytes 147457 | tf_op jit(solution)/shard_map/jit(_where)/select_n | solution.py:44
  1.1 0.5 collective-permute-start.4
  1.6 0.8 %fusion.9 = (f32[3,1,8,4,128]{4,3,2,1,0:T(4,128)S(1)}, f32[3,1,8,4,128]{4,3,2,1,0:T(4,128)S(1)}) fusion(f32[3,4,8,4,128]{4,3,2,1,0:T(4,128)} %param.3), kind=kLoop, calls=%fused_computation.55 | loop fusion | bytes 196608 | tf_op jit(solution)/shard_map/slice | solution.py:41
  2.5 0.0 copy-start.1
  2.5 4.7 %collective-permute-start = (f32[3,1,8,4,128]{4,3,2,1,0:T(4,128)S(1)}, f32[3,1,8,4,128]{4,3,2,1,0:T(4,128)S(1)}, u32[]{:S(2)}, u32[]{:S(2)}) collective-permute-start(f32[3,1,8,4,128]{4,3,2,1,0:T(4,128)S(1)} %get-tuple-element.11), channel_id=1, source_target_pairs={{8,0},{16,8},{24,16},{0,24},{9,1},{17,9},{25,17},{1,25},{10,2},{18... | collective-permute-start | bytes 147464 | tf_op jit(solution)/shard_map/ppermute | solution.py:49
  7.1 0.0 collective-permute-start.1
  7.1 0.8 %fusion.10 = (f32[3,4,1,4,128]{4,3,2,1,0:T(4,128)S(1)}, f32[3,4,1,4,128]{4,3,2,1,0:T(4,128)S(1)}) fusion(f32[3,4,8,4,128]{4,3,2,1,0:T(4,128)} %param.3), kind=kLoop, calls=%fused_computation.56 | loop fusion | bytes 98304 | tf_op jit(solution)/shard_map/slice | solution.py:41
  7.9 2.4 %collective-permute-start.2 = (f32[3,4,1,4,128]{4,3,2,1,0:T(4,128)S(1)}, f32[3,4,1,4,128]{4,3,2,1,0:T(4,128)S(1)}, u32[]{:S(2)}, u32[]{:S(2)}) collective-permute-start(f32[3,4,1,4,128]{4,3,2,1,0:T(4,128)S(1)} %get-tuple-element.13), channel_id=1, source_target_pairs={{2,0},{4,2},{6,4},{0,6},{3,1},{5,3},{7,5},{1,7},{10,8},{12,10},{14... | collective-permute-start | bytes 73736 | tf_op jit(solution)/shard_map/ppermute | solution.py:49
  10.3 0.0 collective-permute-start.3
  10.3 0.7 %broadcast_multiply_fusion = f32[4,8,4]{1,2,0:T(4,128)S(1)} fusion(f32[4,8,4]{1,2,0:T(4,128)} %param.4), kind=kLoop, calls=%fused_computation.51 | loop fusion | flops 128 | bytes 1024 | tf_op jit(solution)/shard_map/mul | solution.py:195
  11.0 0.1 copy.23
  11.1 0.1 mul.32
  11.2 0.8 %select_reduce_fusion = s32[32]{0:T(128)S(1)} fusion(s32[32]{0:T(128)} %param.5), kind=kLoop, calls=%fused_computation.37 | loop fusion | flops 3040 | bytes 256 | tf_op jit(solution)/shard_map/reduce_sum | solution.py:201
  12.0 1.0 %fusion.7 = f32[3,64,128]{1,2,0:T(8,128)S(1)} fusion(f32[3,128,128]{2,1,0:T(8,128)} %bitcast.26, f32[128]{0:T(128)S(1)} %mul.32), kind=kLoop, calls=%fused_computation.17 | loop fusion | flops 24576 | bytes 197120 | tf_op jit(solution)/shard_map/transpose | solution.py:196
  13.0 0.5 broadcast_clamp_fusion.slot_ref
  13.6 0.1 copy.24
  13.7 0.1 tile.4
  13.7 0.9 %tile.10.w_ref = f32[3,64,384]{2,1,0:T(8,128)} reshape(f32[3,64,3,128]{3,2,1,0:T(4,128)S(1)} %tile.4) | data formatting | bytes 589824 | tf_op jit(solution)/shard_map/tile | solution.py:196
  14.6 0.0 collective-permute-done.4
  14.6 0.1 broadcast_select_fusion.1
  14.7 0.0 collective-permute-done.2
  14.7 0.4 collective-permute-done.3
  15.1 0.0 collective-permute-done
  15.1 0.0 collective-permute-done.1
  15.1 0.0 copy-done.1
  15.1 0.3 fusion.6
  15.4 1.1 %copy.25.g_ref = f32[3,128,384]{2,1,0:T(8,128)} copy(f32[3,128,384]{1,2,0:T(8,128)S(1)} %bitcast.28) | data formatting | bytes 1179648 | tf_op jit(solution)/shard_map/reshape | solution.py:197
  16.5 16.3 %shard_map.37 = f32[2,16,129,128]{3,2,1,0:T(8,128)} custom-call(s32[32]{0:T(128)} %broadcast_clamp_fusion.slot_ref, s32[1]{0:T(128)} %bitcast.side_ref, f32[3,64,384]{2,1,0:T(8,128)} %tile.10.w_ref, f32[3,128,384]{2,1,0:T(8,128)} %copy.25.g_ref, f32[384,128]{1,0:T(8,128)} %bitcast.27), custom_call_target="tpu_custom_call" | custom-call | tf_op jit(solution)/shard_map/pallas_call | solution.py:170
  32.8 1.3 %slice_bitcast_fusion = f32[16,129,128]{2,1,0:T(8,128)S(1)} fusion(f32[2,16,129,128]{3,2,1,0:T(8,128)} %shard_map.37), kind=kLoop, calls=%fused_computation | loop fusion | bytes 2113536 | tf_op jit(solution)/shard_map/squeeze | solution.py:208
  34.1 0.0 copy-start
  34.1 1.2 %copy.26 = f32[16,129,128]{2,0,1:T(8,128)} copy(f32[16,129,128]{2,1,0:T(8,128)S(1)} %slice_bitcast_fusion) | data formatting | bytes 2113536 | tf_op jit(solution)/shard_map/squeeze | solution.py:208
  35.3 0.0 collective-permute-start.5
  35.3 2.9 %collective-permute-done.5 = f32[16,129,128]{2,0,1:T(8,128)S(1)} collective-permute-done((f32[16,129,128]{2,0,1:T(8,128)}, f32[16,129,128]{2,0,1:T(8,128)S(1)}, u32[]{:S(2)}, u32[]{:S(2)}) %collective-permute-start.5) | collective-permute-done | bytes 1056800 | tf_op jit(solution)/shard_map/ppermute | solution.py:208
  38.2 0.0 copy-done
  38.2 0.3 fusion
  38.5 0.1 fusion.8
  38.7 1.7 %collective-permute-start.6 = (f32[2,2,2,1,43,128]{5,4,3,2,1,0:T(8,128)S(1)}, f32[2,2,2,1,43,128]{5,4,3,2,1,0:T(8,128)S(1)}, u32[]{:S(2)}, u32[]{:S(2)}) collective-permute-start(f32[2,2,2,1,43,128]{5,4,3,2,1,0:T(8,128)S(1)} %constant_dynamic-slice_fusion.10), channel_id=1, source_target_pairs={{0,2},{2,0},{4,6},{6,4},{1,3},{3,1},{5,7},{7,5},{8,10},{10,8},{12,... | collective-permute-start | bytes 528392 | tf_op jit(solution)/shard_map/ppermute | solution.py:77
  40.4 1.6 %collective-permute-start.10 = (f32[2,2,1,2,43,128]{5,4,3,2,1,0:T(8,128)S(1)}, f32[2,2,1,2,43,128]{5,4,3,2,1,0:T(8,128)S(1)}, u32[]{:S(2)}, u32[]{:S(2)}) collective-permute-start(f32[2,2,1,2,43,128]{5,4,3,2,1,0:T(8,128)S(1)} %constant_dynamic-slice_fusion.6), channel_id=1, source_target_pairs={{0,4},{2,6},{4,0},{6,2},{1,5},{3,7},{5,1},{7,3},{8,12},{10,14},{12... | collective-permute-start | bytes 528392 | tf_op jit(solution)/shard_map/ppermute | solution.py:77
  42.0 0.1 collective-permute-start.14
  42.1 3.6 %collective-permute-done.6 = f32[2,2,2,1,43,128]{5,4,3,2,1,0:T(8,128)S(1)} collective-permute-done((f32[2,2,2,1,43,128]{5,4,3,2,1,0:T(8,128)S(1)}, f32[2,2,2,1,43,128]{5,4,3,2,1,0:T(8,128)S(1)}, u32[]{:S(2)}, u32[]{:S(2)}) %collective-permute-start.6) | collective-permute-done | bytes 176160 | tf_op jit(solution)/shard_map/ppermute | solution.py:77
  45.8 1.5 %collective-permute-start.7 = (f32[2,2,1,1,43,128]{5,4,3,2,1,0:T(8,128)S(1)}, f32[2,2,1,1,43,128]{5,4,3,2,1,0:T(8,128)S(1)}, u32[]{:S(2)}, u32[]{:S(2)}) collective-permute-start(f32[2,2,1,1,43,128]{5,4,3,2,1,0:T(8,128)S(1)} %constant_dynamic-slice_fusion.9), channel_id=1, source_target_pairs={{0,4},{2,6},{4,0},{6,2},{1,5},{3,7},{5,1},{7,3},{8,12},{10,14},{12... | collective-permute-start | bytes 264200 | tf_op jit(solution)/shard_map/ppermute | solution.py:77
  47.3 0.0 collective-permute-done.10
  47.3 0.1 collective-permute-start.11
  47.4 1.1 %collective-permute-done.14 = f32[2,1,2,2,43,128]{5,4,3,2,1,0:T(8,128)S(1)} collective-permute-done((f32[2,1,2,2,43,128]{5,4,3,2,1,0:T(8,128)S(1)}, f32[2,1,2,2,43,128]{5,4,3,2,1,0:T(8,128)S(1)}, u32[]{:S(2)}, u32[]{:S(2)}) %collective-permute-start.14) | collective-permute-done | bytes 176160 | tf_op jit(solution)/shard_map/ppermute | solution.py:77
  48.5 0.7 %collective-permute-start.15 = (f32[2,1,2,1,43,128]{5,4,3,2,1,0:T(8,128)S(1)}, f32[2,1,2,1,43,128]{5,4,3,2,1,0:T(8,128)S(1)}, u32[]{:S(2)}, u32[]{:S(2)}) collective-permute-start(f32[2,1,2,1,43,128]{5,4,3,2,1,0:T(8,128)S(1)} %constant_dynamic-slice_fusion.1), channel_id=1, source_target_pairs={{0,2},{2,0},{4,6},{6,4},{1,3},{3,1},{5,7},{7,5},{8,10},{10,8},{12,... | collective-permute-start | bytes 264200 | tf_op jit(solution)/shard_map/ppermute | solution.py:77
  49.3 1.2 %collective-permute-done.7 = f32[2,2,1,1,43,128]{5,4,3,2,1,0:T(8,128)S(1)} collective-permute-done((f32[2,2,1,1,43,128]{5,4,3,2,1,0:T(8,128)S(1)}, f32[2,2,1,1,43,128]{5,4,3,2,1,0:T(8,128)S(1)}, u32[]{:S(2)}, u32[]{:S(2)}) %collective-permute-start.7) | collective-permute-done | bytes 88096 | tf_op jit(solution)/shard_map/ppermute | solution.py:77
  50.5 0.9 %collective-permute-start.8 = (f32[2,1,1,1,43,128]{5,4,3,2,1,0:T(8,128)S(1)}, f32[2,1,1,1,43,128]{5,4,3,2,1,0:T(8,128)S(1)}, u32[]{:S(2)}, u32[]{:S(2)}) collective-permute-start(f32[2,1,1,1,43,128]{5,4,3,2,1,0:T(8,128)S(1)} %constant_dynamic-slice_fusion.8), channel_id=1, source_target_pairs={{0,8},{8,0},{16,24},{24,16},{1,9},{9,1},{17,25},{25,17},{2,10},{10... | collective-permute-start | bytes 132104 | tf_op jit(solution)/shard_map/ppermute | solution.py:77
  51.4 1.2 %collective-permute-done.11 = f32[2,1,1,2,43,128]{5,4,3,2,1,0:T(8,128)S(1)} collective-permute-done((f32[2,1,1,2,43,128]{5,4,3,2,1,0:T(8,128)S(1)}, f32[2,1,1,2,43,128]{5,4,3,2,1,0:T(8,128)S(1)}, u32[]{:S(2)}, u32[]{:S(2)}) %collective-permute-start.11) | collective-permute-done | bytes 88096 | tf_op jit(solution)/shard_map/ppermute | solution.py:77
  52.6 1.8 %collective-permute-start.12 = (f32[2,1,1,1,43,128]{5,4,3,2,1,0:T(8,128)S(1)}, f32[2,1,1,1,43,128]{5,4,3,2,1,0:T(8,128)S(1)}, u32[]{:S(2)}, u32[]{:S(2)}) collective-permute-start(f32[2,1,1,1,43,128]{5,4,3,2,1,0:T(8,128)S(1)} %constant_dynamic-slice_fusion.4), channel_id=1, source_target_pairs={{0,2},{2,0},{4,6},{6,4},{1,3},{3,1},{5,7},{7,5},{8,10},{10,8},{12,... | collective-permute-start | bytes 132104 | tf_op jit(solution)/shard_map/ppermute | solution.py:77
  54.4 0.0 collective-permute-done.15
  54.4 0.1 collective-permute-start.16
  54.5 0.2 collective-permute-done.8
  54.7 4.0 %collective-permute-start.9 = (f32[1,1,1,1,43,128]{5,4,3,2,1,0:T(8,128)S(1)}, f32[1,1,1,1,43,128]{5,4,3,2,1,0:T(8,128)S(1)}, u32[]{:S(2)}, u32[]{:S(2)}) collective-permute-start(f32[1,1,1,1,43,128]{5,4,3,2,1,0:T(8,128)S(1)} %constant_dynamic-slice_fusion.7), channel_id=1, source_target_pairs={{0,16},{8,24},{16,0},{24,8},{1,17},{9,25},{17,1},{25,9},{2,18},{10... | collective-permute-start | bytes 66056 | tf_op jit(solution)/shard_map/ppermute | solution.py:77
  58.6 0.0 collective-permute-done.12
  58.7 0.6 collective-permute-start.13
  59.2 0.0 collective-permute-done.16
  59.3 2.5 %collective-permute-start.17 = (f32[1,1,1,1,43,128]{5,4,3,2,1,0:T(8,128)S(1)}, f32[1,1,1,1,43,128]{5,4,3,2,1,0:T(8,128)S(1)}, u32[]{:S(2)}, u32[]{:S(2)}) collective-permute-start(f32[1,1,1,1,43,128]{5,4,3,2,1,0:T(8,128)S(1)} %constant_dynamic-slice_fusion.11), channel_id=1, source_target_pairs={{0,16},{8,24},{16,0},{24,8},{1,17},{9,25},{17,1},{25,9},{2,18},{10... | collective-permute-start | bytes 66056 | tf_op jit(solution)/shard_map/ppermute | solution.py:77
  61.8 0.0 collective-permute-done.9
  61.8 2.3 %collective-permute-done.17 = f32[1,1,1,1,43,128]{5,4,3,2,1,0:T(8,128)S(1)} collective-permute-done((f32[1,1,1,1,43,128]{5,4,3,2,1,0:T(8,128)S(1)}, f32[1,1,1,1,43,128]{5,4,3,2,1,0:T(8,128)S(1)}, u32[]{:S(2)}, u32[]{:S(2)}) %collective-permute-start.17) | collective-permute-done | bytes 22048 | tf_op jit(solution)/shard_map/ppermute | solution.py:77
  64.1 0.0 collective-permute-done.13
  64.1 0.1 copy.28
  64.2 0.1 reshape_squeeze.3
  64.3 0.1 copy.29
  64.4 0.6 pad_maximum_fusion.7
  (28 shorter events, 0.4 us)
Async XLA Ops:
  1.1 13.5 %collective-permute-start.4 = (f32[3,4,8,1,128]{4,3,2,1,0:T(1,128)S(1)}, f32[3,4,8,1,128]{4,3,2,1,0:T(1,128)S(1)}, u32[]{:S(2)}, u32[]{:S(2)}) collective-permute-start(f32[3,4,8,1,128]{4,3,2,1,0:T(1,128)S(1)} %broadcast_select_fusion.2), channel_id=1, source_target_pairs={{0,1},{1,0},{2,3},{3,2},{4,5},{5,4},{6,7},{7,6},{8,9},{9,8},{10,11... | collective-permute-start | bytes 147464 | tf_op jit(solution)/shard_map/ppermute | solution.py:44
  2.5 12.6 %copy-start.1 = (f32[3,4,8,4,128]{4,3,2,1,0:T(4,128)S(1)}, f32[3,4,8,4,128]{4,3,2,1,0:T(4,128)}, u32[]{:S(2)}) copy-start(f32[3,4,8,4,128]{4,3,2,1,0:T(4,128)} %param.3) | copy-start | bytes 589828
  2.5 12.6 %collective-permute-start = (f32[3,1,8,4,128]{4,3,2,1,0:T(4,128)S(1)}, f32[3,1,8,4,128]{4,3,2,1,0:T(4,128)S(1)}, u32[]{:S(2)}, u32[]{:S(2)}) collective-permute-start(f32[3,1,8,4,128]{4,3,2,1,0:T(4,128)S(1)} %get-tuple-element.11), channel_id=1, source_target_pairs={{8,0},{16,8},{24,16},{0,24},{9,1},{17,9},{25,17},{1,25},{10,2},{18... | collective-permute-start | bytes 147464 | tf_op jit(solution)/shard_map/ppermute | solution.py:49
  7.1 7.9 %collective-permute-start.1 = (f32[3,1,8,4,128]{4,3,2,1,0:T(4,128)S(1)}, f32[3,1,8,4,128]{4,3,2,1,0:T(4,128)S(1)}, u32[]{:S(2)}, u32[]{:S(2)}) collective-permute-start(f32[3,1,8,4,128]{4,3,2,1,0:T(4,128)S(1)} %get-tuple-element.12), channel_id=1, source_target_pairs={{0,8},{8,16},{16,24},{24,0},{1,9},{9,17},{17,25},{25,1},{2,10},{10... | collective-permute-start | bytes 147464 | tf_op jit(solution)/shard_map/ppermute | solution.py:48
  7.9 6.8 %collective-permute-start.2 = (f32[3,4,1,4,128]{4,3,2,1,0:T(4,128)S(1)}, f32[3,4,1,4,128]{4,3,2,1,0:T(4,128)S(1)}, u32[]{:S(2)}, u32[]{:S(2)}) collective-permute-start(f32[3,4,1,4,128]{4,3,2,1,0:T(4,128)S(1)} %get-tuple-element.13), channel_id=1, source_target_pairs={{2,0},{4,2},{6,4},{0,6},{3,1},{5,3},{7,5},{1,7},{10,8},{12,10},{14... | collective-permute-start | bytes 73736 | tf_op jit(solution)/shard_map/ppermute | solution.py:49
  10.3 4.7 %collective-permute-start.3 = (f32[3,4,1,4,128]{4,3,2,1,0:T(4,128)S(1)}, f32[3,4,1,4,128]{4,3,2,1,0:T(4,128)S(1)}, u32[]{:S(2)}, u32[]{:S(2)}) collective-permute-start(f32[3,4,1,4,128]{4,3,2,1,0:T(4,128)S(1)} %get-tuple-element.14), channel_id=1, source_target_pairs={{0,2},{2,4},{4,6},{6,0},{1,3},{3,5},{5,7},{7,1},{8,10},{10,12},{12... | collective-permute-start | bytes 73736 | tf_op jit(solution)/shard_map/ppermute | solution.py:48
  34.1 4.1 %copy-start = (f32[2,16,129,128]{3,2,1,0:T(8,128)S(1)}, f32[2,16,129,128]{3,2,1,0:T(8,128)}, u32[]{:S(2)}) copy-start(f32[2,16,129,128]{3,2,1,0:T(8,128)} %shard_map.37) | copy-start | bytes 6340612
  35.3 2.9 %collective-permute-start.5 = (f32[16,129,128]{2,0,1:T(8,128)}, f32[16,129,128]{2,0,1:T(8,128)S(1)}, u32[]{:S(2)}, u32[]{:S(2)}) collective-permute-start(f32[16,129,128]{2,0,1:T(8,128)} %copy.26), channel_id=1, source_target_pairs={{0,1},{1,0},{2,3},{3,2},{4,5},{5,4},{6,7},{7,6},{8,9},{9,8},{10,11... | collective-permute-start | bytes 3170312 | tf_op jit(solution)/shard_map/ppermute | solution.py:208
  38.7 7.0 %collective-permute-start.6 = (f32[2,2,2,1,43,128]{5,4,3,2,1,0:T(8,128)S(1)}, f32[2,2,2,1,43,128]{5,4,3,2,1,0:T(8,128)S(1)}, u32[]{:S(2)}, u32[]{:S(2)}) collective-permute-start(f32[2,2,2,1,43,128]{5,4,3,2,1,0:T(8,128)S(1)} %constant_dynamic-slice_fusion.10), channel_id=1, source_target_pairs={{0,2},{2,0},{4,6},{6,4},{1,3},{3,1},{5,7},{7,5},{8,10},{10,8},{12,... | collective-permute-start | bytes 528392 | tf_op jit(solution)/shard_map/ppermute | solution.py:77
  40.4 6.8 %collective-permute-start.10 = (f32[2,2,1,2,43,128]{5,4,3,2,1,0:T(8,128)S(1)}, f32[2,2,1,2,43,128]{5,4,3,2,1,0:T(8,128)S(1)}, u32[]{:S(2)}, u32[]{:S(2)}) collective-permute-start(f32[2,2,1,2,43,128]{5,4,3,2,1,0:T(8,128)S(1)} %constant_dynamic-slice_fusion.6), channel_id=1, source_target_pairs={{0,4},{2,6},{4,0},{6,2},{1,5},{3,7},{5,1},{7,3},{8,12},{10,14},{12... | collective-permute-start | bytes 528392 | tf_op jit(solution)/shard_map/ppermute | solution.py:77
  42.0 6.4 %collective-permute-start.14 = (f32[2,1,2,2,43,128]{5,4,3,2,1,0:T(8,128)S(1)}, f32[2,1,2,2,43,128]{5,4,3,2,1,0:T(8,128)S(1)}, u32[]{:S(2)}, u32[]{:S(2)}) collective-permute-start(f32[2,1,2,2,43,128]{5,4,3,2,1,0:T(8,128)S(1)} %constant_dynamic-slice_fusion.2), channel_id=1, source_target_pairs={{0,8},{8,0},{16,24},{24,16},{1,9},{9,1},{17,25},{25,17},{2,10},{10... | collective-permute-start | bytes 528392 | tf_op jit(solution)/shard_map/ppermute | solution.py:77
  45.8 4.7 %collective-permute-start.7 = (f32[2,2,1,1,43,128]{5,4,3,2,1,0:T(8,128)S(1)}, f32[2,2,1,1,43,128]{5,4,3,2,1,0:T(8,128)S(1)}, u32[]{:S(2)}, u32[]{:S(2)}) collective-permute-start(f32[2,2,1,1,43,128]{5,4,3,2,1,0:T(8,128)S(1)} %constant_dynamic-slice_fusion.9), channel_id=1, source_target_pairs={{0,4},{2,6},{4,0},{6,2},{1,5},{3,7},{5,1},{7,3},{8,12},{10,14},{12... | collective-permute-start | bytes 264200 | tf_op jit(solution)/shard_map/ppermute | solution.py:77
  47.3 5.2 %collective-permute-start.11 = (f32[2,1,1,2,43,128]{5,4,3,2,1,0:T(8,128)S(1)}, f32[2,1,1,2,43,128]{5,4,3,2,1,0:T(8,128)S(1)}, u32[]{:S(2)}, u32[]{:S(2)}) collective-permute-start(f32[2,1,1,2,43,128]{5,4,3,2,1,0:T(8,128)S(1)} %constant_dynamic-slice_fusion.5), channel_id=1, source_target_pairs={{0,8},{8,0},{16,24},{24,16},{1,9},{9,1},{17,25},{25,17},{2,10},{10... | collective-permute-start | bytes 264200 | tf_op jit(solution)/shard_map/ppermute | solution.py:77
  48.5 5.8 %collective-permute-start.15 = (f32[2,1,2,1,43,128]{5,4,3,2,1,0:T(8,128)S(1)}, f32[2,1,2,1,43,128]{5,4,3,2,1,0:T(8,128)S(1)}, u32[]{:S(2)}, u32[]{:S(2)}) collective-permute-start(f32[2,1,2,1,43,128]{5,4,3,2,1,0:T(8,128)S(1)} %constant_dynamic-slice_fusion.1), channel_id=1, source_target_pairs={{0,2},{2,0},{4,6},{6,4},{1,3},{3,1},{5,7},{7,5},{8,10},{10,8},{12,... | collective-permute-start | bytes 264200 | tf_op jit(solution)/shard_map/ppermute | solution.py:77
  50.5 4.2 %collective-permute-start.8 = (f32[2,1,1,1,43,128]{5,4,3,2,1,0:T(8,128)S(1)}, f32[2,1,1,1,43,128]{5,4,3,2,1,0:T(8,128)S(1)}, u32[]{:S(2)}, u32[]{:S(2)}) collective-permute-start(f32[2,1,1,1,43,128]{5,4,3,2,1,0:T(8,128)S(1)} %constant_dynamic-slice_fusion.8), channel_id=1, source_target_pairs={{0,8},{8,0},{16,24},{24,16},{1,9},{9,1},{17,25},{25,17},{2,10},{10... | collective-permute-start | bytes 132104 | tf_op jit(solution)/shard_map/ppermute | solution.py:77
  52.6 6.1 %collective-permute-start.12 = (f32[2,1,1,1,43,128]{5,4,3,2,1,0:T(8,128)S(1)}, f32[2,1,1,1,43,128]{5,4,3,2,1,0:T(8,128)S(1)}, u32[]{:S(2)}, u32[]{:S(2)}) collective-permute-start(f32[2,1,1,1,43,128]{5,4,3,2,1,0:T(8,128)S(1)} %constant_dynamic-slice_fusion.4), channel_id=1, source_target_pairs={{0,2},{2,0},{4,6},{6,4},{1,3},{3,1},{5,7},{7,5},{8,10},{10,8},{12,... | collective-permute-start | bytes 132104 | tf_op jit(solution)/shard_map/ppermute | solution.py:77
  54.4 4.8 %collective-permute-start.16 = (f32[2,1,1,1,43,128]{5,4,3,2,1,0:T(8,128)S(1)}, f32[2,1,1,1,43,128]{5,4,3,2,1,0:T(8,128)S(1)}, u32[]{:S(2)}, u32[]{:S(2)}) collective-permute-start(f32[2,1,1,1,43,128]{5,4,3,2,1,0:T(8,128)S(1)} %constant_dynamic-slice_fusion), channel_id=1, source_target_pairs={{0,4},{2,6},{4,0},{6,2},{1,5},{3,7},{5,1},{7,3},{8,12},{10,14},{12... | collective-permute-start | bytes 132104 | tf_op jit(solution)/shard_map/ppermute | solution.py:77
  54.7 7.1 %collective-permute-start.9 = (f32[1,1,1,1,43,128]{5,4,3,2,1,0:T(8,128)S(1)}, f32[1,1,1,1,43,128]{5,4,3,2,1,0:T(8,128)S(1)}, u32[]{:S(2)}, u32[]{:S(2)}) collective-permute-start(f32[1,1,1,1,43,128]{5,4,3,2,1,0:T(8,128)S(1)} %constant_dynamic-slice_fusion.7), channel_id=1, source_target_pairs={{0,16},{8,24},{16,0},{24,8},{1,17},{9,25},{17,1},{25,9},{2,18},{10... | collective-permute-start | bytes 66056 | tf_op jit(solution)/shard_map/ppermute | solution.py:77
  58.7 5.4 %collective-permute-start.13 = (f32[1,1,1,1,43,128]{5,4,3,2,1,0:T(8,128)S(1)}, f32[1,1,1,1,43,128]{5,4,3,2,1,0:T(8,128)S(1)}, u32[]{:S(2)}, u32[]{:S(2)}) collective-permute-start(f32[1,1,1,1,43,128]{5,4,3,2,1,0:T(8,128)S(1)} %constant_dynamic-slice_fusion.3), channel_id=1, source_target_pairs={{0,16},{8,24},{16,0},{24,8},{1,17},{9,25},{17,1},{25,9},{2,18},{10... | collective-permute-start | bytes 66056 | tf_op jit(solution)/shard_map/ppermute | solution.py:77
  59.3 4.8 %collective-permute-start.17 = (f32[1,1,1,1,43,128]{5,4,3,2,1,0:T(8,128)S(1)}, f32[1,1,1,1,43,128]{5,4,3,2,1,0:T(8,128)S(1)}, u32[]{:S(2)}, u32[]{:S(2)}) collective-permute-start(f32[1,1,1,1,43,128]{5,4,3,2,1,0:T(8,128)S(1)} %constant_dynamic-slice_fusion.11), channel_id=1, source_target_pairs={{0,16},{8,24},{16,0},{24,8},{1,17},{9,25},{17,1},{25,9},{2,18},{10... | collective-permute-start | bytes 66056 | tf_op jit(solution)/shard_map/ppermute | solution.py:77

commit v13 on v11

--- a/solution.py
+++ b/solution.py
@@ -105,7 +105,7 @@
 
 def triangle_kernel(block_len, dense, slot_ref, w_ref, g_ref, m_ref, out_ref, sym_ref, rest_ref):
     test, width = w_ref.shape[1], m_ref.shape[1]
-    group = 4
+    group = 8
     full = block_len // 128 if dense else out_ref.shape[2] // 128
     out_ref[...] = jnp.zeros(out_ref.shape, out_ref.dtype)
     rest_ref[...] = jnp.zeros(rest_ref.shape, rest_ref.dtype)

time: 65.3 us -> 63.4 us (0.971)
  Pallas kernels: 16.2 us -> 14.3 us
    pallas_call x1, Pallas kernels: 16.2 us -> 14.3 us  [triangle(): pl.pallas_call(functools.partial(triangle_kernel, block_len, dense), out_...]
where the time goes in v13:
time: 63.4 us; the launch traced here: 63 us
  starting transfers between devices  23.8 us (38%)
  Pallas kernels  14.3 us (23%)
  waiting for transfers between devices  10.8 us (17%)
  local copies, waits for them, and re-layouts  6.9 us (11%)
  other arithmetic  6.83 us (11%)
    ppermute x13, starting transfers between devices, halve(): return keep + lax.ppermute(other, axis, pairs)  16.1 us
    pallas_call x1, Pallas kernels, triangle(): pl.pallas_call(functools.partial(triangle_kernel, block_len, dense), out_...  14.3 us
    ppermute x13, waiting for transfers between devices, halve(): return keep + lax.ppermute(other, axis, pairs)  10.4 us
    ppermute x2, starting transfers between devices, face_gradients(): after = lax.ppermute(leading, axis, down)  7.12 us
    dynamic_slice x1, local copies, waits for them, and re-layouts, halve(): keep = lax.dynamic_index_in_dim(value, mine, dim, keepdims=True)  1.73 us
    add x13, other arithmetic, halve(): return keep + lax.ppermute(other, axis, pairs)  1.64 us
    slice x2, local copies, waits for them, and re-layouts, face_gradients(): leading = lax.slice_in_dim(value, 0, 1, axis=dim)  1.59 us
  transfers between devices with their start and end apart: 18, of which 7 were waited for; matrix products, arithmetic and copies ran while one was open for 11% of the time, Pallas kernels for 0%

profile of v13, /device:TPU:0, one launch (start us, length us, event | category | flops | bytes accessed | tf_op | source)
XLA Modules:
  0.0 63.0 jit_solution(1534619935014504893)
XLA Ops:
  0.0 1.1 %broadcast_select_fusion.2 = f32[3,4,8,1,128]{4,3,2,1,0:T(1,128)S(1)} fusion(pred[]{:T(512)S(6)} %eq.37, f32[3,4,8,4,128]{4,3,2,1,0:T(4,128)} %param.3), kind=kLoop, calls=%fused_computation.22 | loop fusion | flops 12288 | bytes 147457 | tf_op jit(solution)/shard_map/jit(_where)/select_n | solution.py:44
  1.1 0.5 collective-permute-start.4
  1.6 0.8 %fusion.8 = (f32[3,1,8,4,128]{4,3,2,1,0:T(4,128)S(1)}, f32[3,1,8,4,128]{4,3,2,1,0:T(4,128)S(1)}) fusion(f32[3,4,8,4,128]{4,3,2,1,0:T(4,128)} %param.3), kind=kLoop, calls=%fused_computation.55 | loop fusion | bytes 196608 | tf_op jit(solution)/shard_map/slice | solution.py:41
  2.5 4.7 %collective-permute-start = (f32[3,1,8,4,128]{4,3,2,1,0:T(4,128)S(1)}, f32[3,1,8,4,128]{4,3,2,1,0:T(4,128)S(1)}, u32[]{:S(2)}, u32[]{:S(2)}) collective-permute-start(f32[3,1,8,4,128]{4,3,2,1,0:T(4,128)S(1)} %get-tuple-element.13), channel_id=1, source_target_pairs={{8,0},{16,8},{24,16},{0,24},{9,1},{17,9},{25,17},{1,25},{10,2},{18... | collective-permute-start | bytes 147464 | tf_op jit(solution)/shard_map/ppermute | solution.py:49
  7.1 0.0 collective-permute-start.1
  7.1 0.8 %fusion.9 = (f32[3,4,1,4,128]{4,3,2,1,0:T(4,128)S(1)}, f32[3,4,1,4,128]{4,3,2,1,0:T(4,128)S(1)}) fusion(f32[3,4,8,4,128]{4,3,2,1,0:T(4,128)} %param.3), kind=kLoop, calls=%fused_computation.56 | loop fusion | bytes 98304 | tf_op jit(solution)/shard_map/slice | solution.py:41
  7.9 2.4 %collective-permute-start.2 = (f32[3,4,1,4,128]{4,3,2,1,0:T(4,128)S(1)}, f32[3,4,1,4,128]{4,3,2,1,0:T(4,128)S(1)}, u32[]{:S(2)}, u32[]{:S(2)}) collective-permute-start(f32[3,4,1,4,128]{4,3,2,1,0:T(4,128)S(1)} %get-tuple-element.15), channel_id=1, source_target_pairs={{2,0},{4,2},{6,4},{0,6},{3,1},{5,3},{7,5},{1,7},{10,8},{12,10},{14... | collective-permute-start | bytes 73736 | tf_op jit(solution)/shard_map/ppermute | solution.py:49
  10.3 0.0 collective-permute-start.3
  10.3 0.7 %broadcast_multiply_fusion = f32[4,8,4]{1,2,0:T(4,128)S(1)} fusion(f32[4,8,4]{1,2,0:T(4,128)} %param.4), kind=kLoop, calls=%fused_computation.51 | loop fusion | flops 128 | bytes 1024 | tf_op jit(solution)/shard_map/mul | solution.py:195
  11.0 0.1 copy.23
  11.1 0.1 mul.32
  11.2 0.8 %select_reduce_fusion = s32[32]{0:T(128)S(1)} fusion(s32[32]{0:T(128)} %param.5), kind=kLoop, calls=%fused_computation.35 | loop fusion | flops 3040 | bytes 256 | tf_op jit(solution)/shard_map/reduce_sum | solution.py:201
  12.0 1.0 %fusion.6 = f32[3,64,128]{1,2,0:T(8,128)S(1)} fusion(f32[3,128,128]{2,1,0:T(8,128)} %bitcast.20, f32[128]{0:T(128)S(1)} %mul.32), kind=kLoop, calls=%fused_computation.15 | loop fusion | flops 24576 | bytes 197120 | tf_op jit(solution)/shard_map/transpose | solution.py:196
  13.0 0.5 broadcast_clamp_fusion.slot_ref
  13.6 0.1 copy.24
  13.7 0.1 tile.4
  13.7 0.9 %tile.10.w_ref = f32[3,64,384]{2,1,0:T(8,128)} reshape(f32[3,64,3,128]{3,2,1,0:T(4,128)S(1)} %tile.4) | data formatting | bytes 589824 | tf_op jit(solution)/shard_map/tile | solution.py:196
  14.6 0.0 collective-permute-done.4
  14.6 0.1 broadcast_select_fusion.1
  14.7 0.4 collective-permute-done.3
  15.1 0.0 collective-permute-done
  15.1 0.0 collective-permute-done.1
  15.1 0.3 fusion.5
  15.4 1.1 %copy.25.g_ref = f32[3,128,384]{2,1,0:T(8,128)} copy(f32[3,128,384]{1,2,0:T(8,128)S(1)} %bitcast.22) | data formatting | bytes 1179648 | tf_op jit(solution)/shard_map/reshape | solution.py:197
  16.5 14.3 %shard_map.37 = f32[32,129,128]{2,1,0:T(8,128)} custom-call(s32[32]{0:T(128)} %broadcast_clamp_fusion.slot_ref, f32[3,64,384]{2,1,0:T(8,128)} %tile.10.w_ref, f32[3,128,384]{2,1,0:T(8,128)} %copy.25.g_ref, f32[384,128]{1,0:T(8,128)} %bitcast.21), custom_call_target="tpu_custom_call" | custom-call | tf_op jit(solution)/shard_map/pallas_call | solution.py:170
  30.8 1.7 %constant_dynamic-slice_fusion.12 = (f32[2,2,2,2,1,129,128]{6,5,4,3,2,1,0:T(8,128)S(1)}, f32[2,2,2,2,1,129,128]{6,5,4,3,2,1,0:T(8,128)S(1)}) fusion(f32[2,2,2,2,2,129,128]{6,5,4,3,2,1,0:T(8,128)} %bitcast.19, s32[]{:T(128)S(6)} %select_n.145, s32[]{:T(128)S(6)} %select_n.146), kind=kLoop, calls=%fused_computation.49 | loop fusion | bytes 4227080 | tf_op jit(solution)/shard_map/jit(dynamic_index_in_dim)/dynamic_slice | solution.py:75
  32.6 0.5 copy.31
  33.1 0.1 collective-permute-start.5
  33.3 2.6 %collective-permute-done.5 = f32[2,2,2,2,1,129,128]{6,3,5,4,2,1,0:T(2,128)S(1)} collective-permute-done((f32[2,2,2,2,1,129,128]{6,3,5,4,2,1,0:T(2,128)S(1)}, f32[2,2,2,2,1,129,128]{6,3,5,4,2,1,0:T(2,128)S(1)}, u32[]{:S(2)}, u32[]{:S(2)}) %collective-permute-start.5) | collective-permute-done | bytes 1056800 | tf_op jit(solution)/shard_map/ppermute | solution.py:77
  35.8 0.7 %copy_add_fusion = f32[2,2,2,2,1,129,128]{6,3,5,4,2,1,0:T(2,128)S(1)} fusion(f32[2,2,2,2,1,129,128]{6,3,5,4,2,1,0:T(2,128)S(1)} %collective-permute-done.5, f32[2,2,2,2,1,129,128]{6,5,4,3,2,1,0:T(8,128)S(1)} %get-tuple-element.5), kind=kLoop, calls=%fused_computation | loop fusion | flops 264192 | bytes 3170304 | tf_op jit(solution)/shard_map/add | solution.py:77
  36.6 0.1 fusion.7
  36.7 0.2 constant_dynamic-slice_fusion.10
  36.8 1.7 %collective-permute-start.6 = (f32[2,2,2,1,1,43,128]{6,3,5,4,2,1,0:T(1,128)S(1)}, f32[2,2,2,1,1,43,128]{6,3,5,4,2,1,0:T(1,128)S(1)}, u32[]{:S(2)}, u32[]{:S(2)}) collective-permute-start(f32[2,2,2,1,1,43,128]{6,3,5,4,2,1,0:T(1,128)S(1)} %constant_dynamic-slice_fusion.10), channel_id=1, source_target_pairs={{0,2},{2,0},{4,6},{6,4},{1,3},{3,1},{5,7},{7,5},{8,10},{10,8},{12,... | collective-permute-start | bytes 528392 | tf_op jit(solution)/shard_map/ppermute | solution.py:77
  38.5 1.6 %collective-permute-start.10 = (f32[2,2,1,2,1,43,128]{6,3,5,4,2,1,0:T(2,128)S(1)}, f32[2,2,1,2,1,43,128]{6,3,5,4,2,1,0:T(2,128)S(1)}, u32[]{:S(2)}, u32[]{:S(2)}) collective-permute-start(f32[2,2,1,2,1,43,128]{6,3,5,4,2,1,0:T(2,128)S(1)} %constant_dynamic-slice_fusion.6), channel_id=1, source_target_pairs={{0,4},{2,6},{4,0},{6,2},{1,5},{3,7},{5,1},{7,3},{8,12},{10,14},{12... | collective-permute-start | bytes 528392 | tf_op jit(solution)/shard_map/ppermute | solution.py:77
  40.1 0.1 collective-permute-start.14
  40.2 3.2 %collective-permute-done.6 = f32[2,2,2,1,1,43,128]{6,3,5,4,2,1,0:T(1,128)S(1)} collective-permute-done((f32[2,2,2,1,1,43,128]{6,3,5,4,2,1,0:T(1,128)S(1)}, f32[2,2,2,1,1,43,128]{6,3,5,4,2,1,0:T(1,128)S(1)}, u32[]{:S(2)}, u32[]{:S(2)}) %collective-permute-start.6) | collective-permute-done | bytes 176160 | tf_op jit(solution)/shard_map/ppermute | solution.py:77
  43.4 0.2 dynamic-slice_add_fusion.2
  43.7 1.5 %collective-permute-start.7 = (f32[2,2,1,1,1,43,128]{6,3,5,4,2,1,0:T(1,128)S(1)}, f32[2,2,1,1,1,43,128]{6,3,5,4,2,1,0:T(1,128)S(1)}, u32[]{:S(2)}, u32[]{:S(2)}) collective-permute-start(f32[2,2,1,1,1,43,128]{6,3,5,4,2,1,0:T(1,128)S(1)} %constant_dynamic-slice_fusion.9), channel_id=1, source_target_pairs={{0,4},{2,6},{4,0},{6,2},{1,5},{3,7},{5,1},{7,3},{8,12},{10,14},{12... | collective-permute-start | bytes 264200 | tf_op jit(solution)/shard_map/ppermute | solution.py:77
  45.1 0.0 collective-permute-done.10
  45.1 0.1 dynamic-slice_add_fusion.1
  45.3 0.1 collective-permute-start.11
  45.4 0.8 %collective-permute-done.14 = f32[2,1,2,2,1,43,128]{6,3,5,4,2,1,0:T(2,128)S(1)} collective-permute-done((f32[2,1,2,2,1,43,128]{6,3,5,4,2,1,0:T(2,128)S(1)}, f32[2,1,2,2,1,43,128]{6,3,5,4,2,1,0:T(2,128)S(1)}, u32[]{:S(2)}, u32[]{:S(2)}) %collective-permute-start.14) | collective-permute-done | bytes 176160 | tf_op jit(solution)/shard_map/ppermute | solution.py:77
  46.2 0.1 dynamic-slice_add_fusion
  46.3 0.1 constant_dynamic-slice_fusion.1
  46.3 1.0 %collective-permute-start.15 = (f32[2,1,2,1,1,43,128]{6,3,5,4,2,1,0:T(1,128)S(1)}, f32[2,1,2,1,1,43,128]{6,3,5,4,2,1,0:T(1,128)S(1)}, u32[]{:S(2)}, u32[]{:S(2)}) collective-permute-start(f32[2,1,2,1,1,43,128]{6,3,5,4,2,1,0:T(1,128)S(1)} %constant_dynamic-slice_fusion.1), channel_id=1, source_target_pairs={{0,2},{2,0},{4,6},{6,4},{1,3},{3,1},{5,7},{7,5},{8,10},{10,8},{12,... | collective-permute-start | bytes 264200 | tf_op jit(solution)/shard_map/ppermute | solution.py:77
  47.4 0.9 %collective-permute-done.7 = f32[2,2,1,1,1,43,128]{6,3,5,4,2,1,0:T(1,128)S(1)} collective-permute-done((f32[2,2,1,1,1,43,128]{6,3,5,4,2,1,0:T(1,128)S(1)}, f32[2,2,1,1,1,43,128]{6,3,5,4,2,1,0:T(1,128)S(1)}, u32[]{:S(2)}, u32[]{:S(2)}) %collective-permute-start.7) | collective-permute-done | bytes 88096 | tf_op jit(solution)/shard_map/ppermute | solution.py:77
  48.2 0.1 dynamic-slice_add_fusion.5
  48.3 1.2 %collective-permute-start.8 = (f32[2,1,1,1,1,43,128]{6,3,5,4,2,1,0:T(1,128)S(1)}, f32[2,1,1,1,1,43,128]{6,3,5,4,2,1,0:T(1,128)S(1)}, u32[]{:S(2)}, u32[]{:S(2)}) collective-permute-start(f32[2,1,1,1,1,43,128]{6,3,5,4,2,1,0:T(1,128)S(1)} %constant_dynamic-slice_fusion.8), channel_id=1, source_target_pairs={{0,8},{8,0},{16,24},{24,16},{1,9},{9,1},{17,25},{25,17},{2,10},{10... | collective-permute-start | bytes 132104 | tf_op jit(solution)/shard_map/ppermute | solution.py:77
  49.5 0.8 %collective-permute-done.11 = f32[2,1,1,2,1,43,128]{6,3,5,4,2,1,0:T(2,128)S(1)} collective-permute-done((f32[2,1,1,2,1,43,128]{6,3,5,4,2,1,0:T(2,128)S(1)}, f32[2,1,1,2,1,43,128]{6,3,5,4,2,1,0:T(2,128)S(1)}, u32[]{:S(2)}, u32[]{:S(2)}) %collective-permute-start.11) | collective-permute-done | bytes 88096 | tf_op jit(solution)/shard_map/ppermute | solution.py:77
  50.4 1.8 %collective-permute-start.12 = (f32[2,1,1,1,1,43,128]{6,3,5,4,2,1,0:T(1,128)S(1)}, f32[2,1,1,1,1,43,128]{6,3,5,4,2,1,0:T(1,128)S(1)}, u32[]{:S(2)}, u32[]{:S(2)}) collective-permute-start(f32[2,1,1,1,1,43,128]{6,3,5,4,2,1,0:T(1,128)S(1)} %constant_dynamic-slice_fusion.4), channel_id=1, source_target_pairs={{0,2},{2,0},{4,6},{6,4},{1,3},{3,1},{5,7},{7,5},{8,10},{10,8},{12,... | collective-permute-start | bytes 132104 | tf_op jit(solution)/shard_map/ppermute | solution.py:77
  52.2 0.1 dynamic-slice_add_fusion.3
  52.4 0.1 collective-permute-start.16
  52.5 0.0 collective-permute-done.8
  52.5 4.0 %collective-permute-start.9 = (f32[1,1,1,1,1,43,128]{6,3,5,4,2,1,0:T(1,128)S(1)}, f32[1,1,1,1,1,43,128]{6,3,5,4,2,1,0:T(1,128)S(1)}, u32[]{:S(2)}, u32[]{:S(2)}) collective-permute-start(f32[1,1,1,1,1,43,128]{6,3,5,4,2,1,0:T(1,128)S(1)} %constant_dynamic-slice_fusion.7), channel_id=1, source_target_pairs={{0,16},{8,24},{16,0},{24,8},{1,17},{9,25},{17,1},{25,9},{2,18},{10... | collective-permute-start | bytes 66056 | tf_op jit(solution)/shard_map/ppermute | solution.py:77
  56.5 0.1 dynamic-slice_add_fusion.7
  56.6 0.5 collective-permute-start.13
  57.1 0.0 collective-permute-done.16
  57.2 2.5 %collective-permute-start.17 = (f32[1,1,1,1,1,43,128]{6,3,5,4,2,1,0:T(1,128)S(1)}, f32[1,1,1,1,1,43,128]{6,3,5,4,2,1,0:T(1,128)S(1)}, u32[]{:S(2)}, u32[]{:S(2)}) collective-permute-start(f32[1,1,1,1,1,43,128]{6,3,5,4,2,1,0:T(1,128)S(1)} %constant_dynamic-slice_fusion.13), channel_id=1, source_target_pairs={{0,16},{8,24},{16,0},{24,8},{1,17},{9,25},{17,1},{25,9},{2,18},{10... | collective-permute-start | bytes 66056 | tf_op jit(solution)/shard_map/ppermute | solution.py:77
  59.8 2.2 %collective-permute-done.17 = f32[1,1,1,1,1,43,128]{6,3,5,4,2,1,0:T(1,128)S(1)} collective-permute-done((f32[1,1,1,1,1,43,128]{6,3,5,4,2,1,0:T(1,128)S(1)}, f32[1,1,1,1,1,43,128]{6,3,5,4,2,1,0:T(1,128)S(1)}, u32[]{:S(2)}, u32[]{:S(2)}) %collective-permute-start.17) | collective-permute-done | bytes 22048 | tf_op jit(solution)/shard_map/ppermute | solution.py:77
  62.0 0.0 collective-permute-done.13
  62.1 0.1 pad_maximum_fusion.8
  62.2 0.1 reshape_squeeze.3
  62.2 0.1 copy.29
  62.3 0.6 %pad_maximum_fusion.7 = f32[64,258]{1,0:T(8,128)} fusion(f32[64,2]{1,0:T(8,128)S(1)} %copy.29, f32[64,256]{1,0:T(8,128)S(1)} %bitcast.26), kind=kLoop, calls=%fused_computation.19 | loop fusion | flops 16512 | bytes 132096 | tf_op jit(solution)/shard_map/concatenate | solution.py:210
  (25 shorter events, 0.5 us)
Async XLA Ops:
  1.1 13.5 %collective-permute-start.4 = (f32[3,4,8,1,128]{4,3,2,1,0:T(1,128)S(1)}, f32[3,4,8,1,128]{4,3,2,1,0:T(1,128)S(1)}, u32[]{:S(2)}, u32[]{:S(2)}) collective-permute-start(f32[3,4,8,1,128]{4,3,2,1,0:T(1,128)S(1)} %broadcast_select_fusion.2), channel_id=1, source_target_pairs={{0,1},{1,0},{2,3},{3,2},{4,5},{5,4},{6,7},{7,6},{8,9},{9,8},{10,11... | collective-permute-start | bytes 147464 | tf_op jit(solution)/shard_map/ppermute | solution.py:44
  2.5 12.6 %copy-start = (f32[3,4,8,4,128]{4,3,2,1,0:T(4,128)S(1)}, f32[3,4,8,4,128]{4,3,2,1,0:T(4,128)}, u32[]{:S(2)}) copy-start(f32[3,4,8,4,128]{4,3,2,1,0:T(4,128)} %param.3) | copy-start | bytes 589828
  2.5 12.6 %collective-permute-start = (f32[3,1,8,4,128]{4,3,2,1,0:T(4,128)S(1)}, f32[3,1,8,4,128]{4,3,2,1,0:T(4,128)S(1)}, u32[]{:S(2)}, u32[]{:S(2)}) collective-permute-start(f32[3,1,8,4,128]{4,3,2,1,0:T(4,128)S(1)} %get-tuple-element.13), channel_id=1, source_target_pairs={{8,0},{16,8},{24,16},{0,24},{9,1},{17,9},{25,17},{1,25},{10,2},{18... | collective-permute-start | bytes 147464 | tf_op jit(solution)/shard_map/ppermute | solution.py:49
  7.1 7.9 %collective-permute-start.1 = (f32[3,1,8,4,128]{4,3,2,1,0:T(4,128)S(1)}, f32[3,1,8,4,128]{4,3,2,1,0:T(4,128)S(1)}, u32[]{:S(2)}, u32[]{:S(2)}) collective-permute-start(f32[3,1,8,4,128]{4,3,2,1,0:T(4,128)S(1)} %get-tuple-element.14), channel_id=1, source_target_pairs={{0,8},{8,16},{16,24},{24,0},{1,9},{9,17},{17,25},{25,1},{2,10},{10... | collective-permute-start | bytes 147464 | tf_op jit(solution)/shard_map/ppermute | solution.py:48
  7.9 6.8 %collective-permute-start.2 = (f32[3,4,1,4,128]{4,3,2,1,0:T(4,128)S(1)}, f32[3,4,1,4,128]{4,3,2,1,0:T(4,128)S(1)}, u32[]{:S(2)}, u32[]{:S(2)}) collective-permute-start(f32[3,4,1,4,128]{4,3,2,1,0:T(4,128)S(1)} %get-tuple-element.15), channel_id=1, source_target_pairs={{2,0},{4,2},{6,4},{0,6},{3,1},{5,3},{7,5},{1,7},{10,8},{12,10},{14... | collective-permute-start | bytes 73736 | tf_op jit(solution)/shard_map/ppermute | solution.py:49
  10.3 4.7 %collective-permute-start.3 = (f32[3,4,1,4,128]{4,3,2,1,0:T(4,128)S(1)}, f32[3,4,1,4,128]{4,3,2,1,0:T(4,128)S(1)}, u32[]{:S(2)}, u32[]{:S(2)}) collective-permute-start(f32[3,4,1,4,128]{4,3,2,1,0:T(4,128)S(1)} %get-tuple-element.16), channel_id=1, source_target_pairs={{0,2},{2,4},{4,6},{6,0},{1,3},{3,5},{5,7},{7,1},{8,10},{10,12},{12... | collective-permute-start | bytes 73736 | tf_op jit(solution)/shard_map/ppermute | solution.py:48
  33.1 2.7 %collective-permute-start.5 = (f32[2,2,2,2,1,129,128]{6,3,5,4,2,1,0:T(2,128)S(1)}, f32[2,2,2,2,1,129,128]{6,3,5,4,2,1,0:T(2,128)S(1)}, u32[]{:S(2)}, u32[]{:S(2)}) collective-permute-start(f32[2,2,2,2,1,129,128]{6,3,5,4,2,1,0:T(2,128)S(1)} %copy.31), channel_id=1, source_target_pairs={{0,1},{1,0},{2,3},{3,2},{4,5},{5,4},{6,7},{7,6},{8,9},{9,8},{10,11... | collective-permute-start | bytes 3170312 | tf_op jit(solution)/shard_map/ppermute | solution.py:77
  36.8 6.6 %collective-permute-start.6 = (f32[2,2,2,1,1,43,128]{6,3,5,4,2,1,0:T(1,128)S(1)}, f32[2,2,2,1,1,43,128]{6,3,5,4,2,1,0:T(1,128)S(1)}, u32[]{:S(2)}, u32[]{:S(2)}) collective-permute-start(f32[2,2,2,1,1,43,128]{6,3,5,4,2,1,0:T(1,128)S(1)} %constant_dynamic-slice_fusion.10), channel_id=1, source_target_pairs={{0,2},{2,0},{4,6},{6,4},{1,3},{3,1},{5,7},{7,5},{8,10},{10,8},{12,... | collective-permute-start | bytes 528392 | tf_op jit(solution)/shard_map/ppermute | solution.py:77
  38.5 6.6 %collective-permute-start.10 = (f32[2,2,1,2,1,43,128]{6,3,5,4,2,1,0:T(2,128)S(1)}, f32[2,2,1,2,1,43,128]{6,3,5,4,2,1,0:T(2,128)S(1)}, u32[]{:S(2)}, u32[]{:S(2)}) collective-permute-start(f32[2,2,1,2,1,43,128]{6,3,5,4,2,1,0:T(2,128)S(1)} %constant_dynamic-slice_fusion.6), channel_id=1, source_target_pairs={{0,4},{2,6},{4,0},{6,2},{1,5},{3,7},{5,1},{7,3},{8,12},{10,14},{12... | collective-permute-start | bytes 528392 | tf_op jit(solution)/shard_map/ppermute | solution.py:77
  40.1 6.0 %collective-permute-start.14 = (f32[2,1,2,2,1,43,128]{6,3,5,4,2,1,0:T(2,128)S(1)}, f32[2,1,2,2,1,43,128]{6,3,5,4,2,1,0:T(2,128)S(1)}, u32[]{:S(2)}, u32[]{:S(2)}) collective-permute-start(f32[2,1,2,2,1,43,128]{6,3,5,4,2,1,0:T(2,128)S(1)} %constant_dynamic-slice_fusion.2), channel_id=1, source_target_pairs={{0,8},{8,0},{16,24},{24,16},{1,9},{9,1},{17,25},{25,17},{2,10},{10... | collective-permute-start | bytes 528392 | tf_op jit(solution)/shard_map/ppermute | solution.py:77
  43.7 4.6 %collective-permute-start.7 = (f32[2,2,1,1,1,43,128]{6,3,5,4,2,1,0:T(1,128)S(1)}, f32[2,2,1,1,1,43,128]{6,3,5,4,2,1,0:T(1,128)S(1)}, u32[]{:S(2)}, u32[]{:S(2)}) collective-permute-start(f32[2,2,1,1,1,43,128]{6,3,5,4,2,1,0:T(1,128)S(1)} %constant_dynamic-slice_fusion.9), channel_id=1, source_target_pairs={{0,4},{2,6},{4,0},{6,2},{1,5},{3,7},{5,1},{7,3},{8,12},{10,14},{12... | collective-permute-start | bytes 264200 | tf_op jit(solution)/shard_map/ppermute | solution.py:77
  45.3 5.0 %collective-permute-start.11 = (f32[2,1,1,2,1,43,128]{6,3,5,4,2,1,0:T(2,128)S(1)}, f32[2,1,1,2,1,43,128]{6,3,5,4,2,1,0:T(2,128)S(1)}, u32[]{:S(2)}, u32[]{:S(2)}) collective-permute-start(f32[2,1,1,2,1,43,128]{6,3,5,4,2,1,0:T(2,128)S(1)} %constant_dynamic-slice_fusion.5), channel_id=1, source_target_pairs={{0,8},{8,0},{16,24},{24,16},{1,9},{9,1},{17,25},{25,17},{2,10},{10... | collective-permute-start | bytes 264200 | tf_op jit(solution)/shard_map/ppermute | solution.py:77
  46.3 5.9 %collective-permute-start.15 = (f32[2,1,2,1,1,43,128]{6,3,5,4,2,1,0:T(1,128)S(1)}, f32[2,1,2,1,1,43,128]{6,3,5,4,2,1,0:T(1,128)S(1)}, u32[]{:S(2)}, u32[]{:S(2)}) collective-permute-start(f32[2,1,2,1,1,43,128]{6,3,5,4,2,1,0:T(1,128)S(1)} %constant_dynamic-slice_fusion.1), channel_id=1, source_target_pairs={{0,2},{2,0},{4,6},{6,4},{1,3},{3,1},{5,7},{7,5},{8,10},{10,8},{12,... | collective-permute-start | bytes 264200 | tf_op jit(solution)/shard_map/ppermute | solution.py:77
  48.3 4.1 %collective-permute-start.8 = (f32[2,1,1,1,1,43,128]{6,3,5,4,2,1,0:T(1,128)S(1)}, f32[2,1,1,1,1,43,128]{6,3,5,4,2,1,0:T(1,128)S(1)}, u32[]{:S(2)}, u32[]{:S(2)}) collective-permute-start(f32[2,1,1,1,1,43,128]{6,3,5,4,2,1,0:T(1,128)S(1)} %constant_dynamic-slice_fusion.8), channel_id=1, source_target_pairs={{0,8},{8,0},{16,24},{24,16},{1,9},{9,1},{17,25},{25,17},{2,10},{10... | collective-permute-start | bytes 132104 | tf_op jit(solution)/shard_map/ppermute | solution.py:77
  50.4 6.1 %collective-permute-start.12 = (f32[2,1,1,1,1,43,128]{6,3,5,4,2,1,0:T(1,128)S(1)}, f32[2,1,1,1,1,43,128]{6,3,5,4,2,1,0:T(1,128)S(1)}, u32[]{:S(2)}, u32[]{:S(2)}) collective-permute-start(f32[2,1,1,1,1,43,128]{6,3,5,4,2,1,0:T(1,128)S(1)} %constant_dynamic-slice_fusion.4), channel_id=1, source_target_pairs={{0,2},{2,0},{4,6},{6,4},{1,3},{3,1},{5,7},{7,5},{8,10},{10,8},{12,... | collective-permute-start | bytes 132104 | tf_op jit(solution)/shard_map/ppermute | solution.py:77
  52.4 4.8 %collective-permute-start.16 = (f32[2,1,1,1,1,43,128]{6,3,5,4,2,1,0:T(1,128)S(1)}, f32[2,1,1,1,1,43,128]{6,3,5,4,2,1,0:T(1,128)S(1)}, u32[]{:S(2)}, u32[]{:S(2)}) collective-permute-start(f32[2,1,1,1,1,43,128]{6,3,5,4,2,1,0:T(1,128)S(1)} %constant_dynamic-slice_fusion), channel_id=1, source_target_pairs={{0,4},{2,6},{4,0},{6,2},{1,5},{3,7},{5,1},{7,3},{8,12},{10,14},{12... | collective-permute-start | bytes 132104 | tf_op jit(solution)/shard_map/ppermute | solution.py:77
  52.5 7.2 %collective-permute-start.9 = (f32[1,1,1,1,1,43,128]{6,3,5,4,2,1,0:T(1,128)S(1)}, f32[1,1,1,1,1,43,128]{6,3,5,4,2,1,0:T(1,128)S(1)}, u32[]{:S(2)}, u32[]{:S(2)}) collective-permute-start(f32[1,1,1,1,1,43,128]{6,3,5,4,2,1,0:T(1,128)S(1)} %constant_dynamic-slice_fusion.7), channel_id=1, source_target_pairs={{0,16},{8,24},{16,0},{24,8},{1,17},{9,25},{17,1},{25,9},{2,18},{10... | collective-permute-start | bytes 66056 | tf_op jit(solution)/shard_map/ppermute | solution.py:77
  56.6 5.4 %collective-permute-start.13 = (f32[1,1,1,1,1,43,128]{6,3,5,4,2,1,0:T(1,128)S(1)}, f32[1,1,1,1,1,43,128]{6,3,5,4,2,1,0:T(1,128)S(1)}, u32[]{:S(2)}, u32[]{:S(2)}) collective-permute-start(f32[1,1,1,1,1,43,128]{6,3,5,4,2,1,0:T(1,128)S(1)} %constant_dynamic-slice_fusion.3), channel_id=1, source_target_pairs={{0,16},{8,24},{16,0},{24,8},{1,17},{9,25},{17,1},{25,9},{2,18},{10... | collective-permute-start | bytes 66056 | tf_op jit(solution)/shard_map/ppermute | solution.py:77
  57.2 4.8 %collective-permute-start.17 = (f32[1,1,1,1,1,43,128]{6,3,5,4,2,1,0:T(1,128)S(1)}, f32[1,1,1,1,1,43,128]{6,3,5,4,2,1,0:T(1,128)S(1)}, u32[]{:S(2)}, u32[]{:S(2)}) collective-permute-start(f32[1,1,1,1,1,43,128]{6,3,5,4,2,1,0:T(1,128)S(1)} %constant_dynamic-slice_fusion.13), channel_id=1, source_target_pairs={{0,16},{8,24},{16,0},{24,8},{1,17},{9,25},{17,1},{25,9},{2,18},{10... | collective-permute-start | bytes 66056 | tf_op jit(solution)/shard_map/ppermute | solution.py:77

commit v14 on v13

--- a/solution.py
+++ b/solution.py
@@ -105,7 +105,7 @@
 
 def triangle_kernel(block_len, dense, slot_ref, w_ref, g_ref, m_ref, out_ref, sym_ref, rest_ref):
     test, width = w_ref.shape[1], m_ref.shape[1]
-    group = 8
+    group = 16
     full = block_len // 128 if dense else out_ref.shape[2] // 128
     out_ref[...] = jnp.zeros(out_ref.shape, out_ref.dtype)
     rest_ref[...] = jnp.zeros(rest_ref.shape, rest_ref.dtype)

time: 63.4 us -> 62.5 us (0.986)
  Pallas kernels: 14.3 us -> 13.5 us
    pallas_call x1, Pallas kernels: 14.3 us -> 13.5 us  [triangle(): pl.pallas_call(functools.partial(triangle_kernel, block_len, dense), out_...]
where the time goes in v14:
time: 62.5 us; the launch traced here: 62.2 us
  starting transfers between devices  23.8 us (38%)
  Pallas kernels  13.5 us (22%)
  waiting for transfers between devices  10.8 us (17%)
  local copies, waits for them, and re-layouts  6.9 us (11%)
  other arithmetic  6.83 us (11%)
    ppermute x13, starting transfers between devices, halve(): return keep + lax.ppermute(other, axis, pairs)  16.1 us
    pallas_call x1, Pallas kernels, triangle(): pl.pallas_call(functools.partial(triangle_kernel, block_len, dense), out_...  13.5 us
    ppermute x13, waiting for transfers between devices, halve(): return keep + lax.ppermute(other, axis, pairs)  10.4 us
    ppermute x2, starting transfers between devices, face_gradients(): after = lax.ppermute(leading, axis, down)  7.12 us
    dynamic_slice x1, local copies, waits for them, and re-layouts, halve(): keep = lax.dynamic_index_in_dim(value, mine, dim, keepdims=True)  1.73 us
    add x13, other arithmetic, halve(): return keep + lax.ppermute(other, axis, pairs)  1.64 us
    slice x2, local copies, waits for them, and re-layouts, face_gradients(): leading = lax.slice_in_dim(value, 0, 1, axis=dim)  1.59 us
  transfers between devices with their start and end apart: 18, of which 7 were waited for; matrix products, arithmetic and copies ran while one was open for 11% of the time, Pallas kernels for 0%

profile of v14, /device:TPU:0, one launch (start us, length us, event | category | flops | bytes accessed | tf_op | source)
XLA Modules:
  0.0 62.2 jit_solution(11232005583643347917)
XLA Ops:
  0.0 1.1 %broadcast_select_fusion.2 = f32[3,4,8,1,128]{4,3,2,1,0:T(1,128)S(1)} fusion(pred[]{:T(512)S(6)} %eq.37, f32[3,4,8,4,128]{4,3,2,1,0:T(4,128)} %param.3), kind=kLoop, calls=%fused_computation.22 | loop fusion | flops 12288 | bytes 147457 | tf_op jit(solution)/shard_map/jit(_where)/select_n | solution.py:44
  1.1 0.5 collective-permute-start.4
  1.6 0.8 %fusion.8 = (f32[3,1,8,4,128]{4,3,2,1,0:T(4,128)S(1)}, f32[3,1,8,4,128]{4,3,2,1,0:T(4,128)S(1)}) fusion(f32[3,4,8,4,128]{4,3,2,1,0:T(4,128)} %param.3), kind=kLoop, calls=%fused_computation.55 | loop fusion | bytes 196608 | tf_op jit(solution)/shard_map/slice | solution.py:41
  2.5 4.7 %collective-permute-start = (f32[3,1,8,4,128]{4,3,2,1,0:T(4,128)S(1)}, f32[3,1,8,4,128]{4,3,2,1,0:T(4,128)S(1)}, u32[]{:S(2)}, u32[]{:S(2)}) collective-permute-start(f32[3,1,8,4,128]{4,3,2,1,0:T(4,128)S(1)} %get-tuple-element.13), channel_id=1, source_target_pairs={{8,0},{16,8},{24,16},{0,24},{9,1},{17,9},{25,17},{1,25},{10,2},{18... | collective-permute-start | bytes 147464 | tf_op jit(solution)/shard_map/ppermute | solution.py:49
  7.1 0.0 collective-permute-start.1
  7.1 0.8 %fusion.9 = (f32[3,4,1,4,128]{4,3,2,1,0:T(4,128)S(1)}, f32[3,4,1,4,128]{4,3,2,1,0:T(4,128)S(1)}) fusion(f32[3,4,8,4,128]{4,3,2,1,0:T(4,128)} %param.3), kind=kLoop, calls=%fused_computation.56 | loop fusion | bytes 98304 | tf_op jit(solution)/shard_map/slice | solution.py:41
  7.9 2.4 %collective-permute-start.2 = (f32[3,4,1,4,128]{4,3,2,1,0:T(4,128)S(1)}, f32[3,4,1,4,128]{4,3,2,1,0:T(4,128)S(1)}, u32[]{:S(2)}, u32[]{:S(2)}) collective-permute-start(f32[3,4,1,4,128]{4,3,2,1,0:T(4,128)S(1)} %get-tuple-element.15), channel_id=1, source_target_pairs={{2,0},{4,2},{6,4},{0,6},{3,1},{5,3},{7,5},{1,7},{10,8},{12,10},{14... | collective-permute-start | bytes 73736 | tf_op jit(solution)/shard_map/ppermute | solution.py:49
  10.3 0.0 collective-permute-start.3
  10.3 0.7 %broadcast_multiply_fusion = f32[4,8,4]{1,2,0:T(4,128)S(1)} fusion(f32[4,8,4]{1,2,0:T(4,128)} %param.4), kind=kLoop, calls=%fused_computation.51 | loop fusion | flops 128 | bytes 1024 | tf_op jit(solution)/shard_map/mul | solution.py:195
  11.0 0.1 copy.23
  11.1 0.1 mul.32
  11.2 0.8 %select_reduce_fusion = s32[32]{0:T(128)S(1)} fusion(s32[32]{0:T(128)} %param.5), kind=kLoop, calls=%fused_computation.35 | loop fusion | flops 3040 | bytes 256 | tf_op jit(solution)/shard_map/reduce_sum | solution.py:201
  12.0 1.0 %fusion.6 = f32[3,64,128]{1,2,0:T(8,128)S(1)} fusion(f32[3,128,128]{2,1,0:T(8,128)} %bitcast.20, f32[128]{0:T(128)S(1)} %mul.32), kind=kLoop, calls=%fused_computation.15 | loop fusion | flops 24576 | bytes 197120 | tf_op jit(solution)/shard_map/transpose | solution.py:196
  13.0 0.5 broadcast_clamp_fusion.slot_ref
  13.6 0.1 copy.24
  13.7 0.1 tile.4
  13.7 0.9 %tile.10.w_ref = f32[3,64,384]{2,1,0:T(8,128)} reshape(f32[3,64,3,128]{3,2,1,0:T(4,128)S(1)} %tile.4) | data formatting | bytes 589824 | tf_op jit(solution)/shard_map/tile | solution.py:196
  14.6 0.0 collective-permute-done.4
  14.6 0.1 broadcast_select_fusion.1
  14.7 0.0 collective-permute-done.2
  14.7 0.4 collective-permute-done.3
  15.1 0.0 collective-permute-done
  15.1 0.0 collective-permute-done.1
  15.1 0.3 fusion.5
  15.4 1.1 %copy.25.g_ref = f32[3,128,384]{2,1,0:T(8,128)} copy(f32[3,128,384]{1,2,0:T(8,128)S(1)} %bitcast.22) | data formatting | bytes 1179648 | tf_op jit(solution)/shard_map/reshape | solution.py:197
  16.5 13.5 %shard_map.37 = f32[32,129,128]{2,1,0:T(8,128)} custom-call(s32[32]{0:T(128)} %broadcast_clamp_fusion.slot_ref, f32[3,64,384]{2,1,0:T(8,128)} %tile.10.w_ref, f32[3,128,384]{2,1,0:T(8,128)} %copy.25.g_ref, f32[384,128]{1,0:T(8,128)} %bitcast.21), custom_call_target="tpu_custom_call" | custom-call | tf_op jit(solution)/shard_map/pallas_call | solution.py:170
  30.0 1.7 %constant_dynamic-slice_fusion.12 = (f32[2,2,2,2,1,129,128]{6,5,4,3,2,1,0:T(8,128)S(1)}, f32[2,2,2,2,1,129,128]{6,5,4,3,2,1,0:T(8,128)S(1)}) fusion(f32[2,2,2,2,2,129,128]{6,5,4,3,2,1,0:T(8,128)} %bitcast.19, s32[]{:T(128)S(6)} %select_n.145, s32[]{:T(128)S(6)} %select_n.146), kind=kLoop, calls=%fused_computation.49 | loop fusion | bytes 4227080 | tf_op jit(solution)/shard_map/jit(dynamic_index_in_dim)/dynamic_slice | solution.py:75
  31.7 0.5 copy.31
  32.3 0.1 collective-permute-start.5
  32.5 2.6 %collective-permute-done.5 = f32[2,2,2,2,1,129,128]{6,3,5,4,2,1,0:T(2,128)S(1)} collective-permute-done((f32[2,2,2,2,1,129,128]{6,3,5,4,2,1,0:T(2,128)S(1)}, f32[2,2,2,2,1,129,128]{6,3,5,4,2,1,0:T(2,128)S(1)}, u32[]{:S(2)}, u32[]{:S(2)}) %collective-permute-start.5) | collective-permute-done | bytes 1056800 | tf_op jit(solution)/shard_map/ppermute | solution.py:77
  35.0 0.7 %copy_add_fusion = f32[2,2,2,2,1,129,128]{6,3,5,4,2,1,0:T(2,128)S(1)} fusion(f32[2,2,2,2,1,129,128]{6,3,5,4,2,1,0:T(2,128)S(1)} %collective-permute-done.5, f32[2,2,2,2,1,129,128]{6,5,4,3,2,1,0:T(8,128)S(1)} %get-tuple-element.5), kind=kLoop, calls=%fused_computation | loop fusion | flops 264192 | bytes 3170304 | tf_op jit(solution)/shard_map/add | solution.py:77
  35.7 0.1 fusion.7
  35.8 0.2 constant_dynamic-slice_fusion.10
  36.0 1.7 %collective-permute-start.6 = (f32[2,2,2,1,1,43,128]{6,3,5,4,2,1,0:T(1,128)S(1)}, f32[2,2,2,1,1,43,128]{6,3,5,4,2,1,0:T(1,128)S(1)}, u32[]{:S(2)}, u32[]{:S(2)}) collective-permute-start(f32[2,2,2,1,1,43,128]{6,3,5,4,2,1,0:T(1,128)S(1)} %constant_dynamic-slice_fusion.10), channel_id=1, source_target_pairs={{0,2},{2,0},{4,6},{6,4},{1,3},{3,1},{5,7},{7,5},{8,10},{10,8},{12,... | collective-permute-start | bytes 528392 | tf_op jit(solution)/shard_map/ppermute | solution.py:77
  37.7 1.6 %collective-permute-start.10 = (f32[2,2,1,2,1,43,128]{6,3,5,4,2,1,0:T(2,128)S(1)}, f32[2,2,1,2,1,43,128]{6,3,5,4,2,1,0:T(2,128)S(1)}, u32[]{:S(2)}, u32[]{:S(2)}) collective-permute-start(f32[2,2,1,2,1,43,128]{6,3,5,4,2,1,0:T(2,128)S(1)} %constant_dynamic-slice_fusion.6), channel_id=1, source_target_pairs={{0,4},{2,6},{4,0},{6,2},{1,5},{3,7},{5,1},{7,3},{8,12},{10,14},{12... | collective-permute-start | bytes 528392 | tf_op jit(solution)/shard_map/ppermute | solution.py:77
  39.3 0.1 collective-permute-start.14
  39.4 3.2 %collective-permute-done.6 = f32[2,2,2,1,1,43,128]{6,3,5,4,2,1,0:T(1,128)S(1)} collective-permute-done((f32[2,2,2,1,1,43,128]{6,3,5,4,2,1,0:T(1,128)S(1)}, f32[2,2,2,1,1,43,128]{6,3,5,4,2,1,0:T(1,128)S(1)}, u32[]{:S(2)}, u32[]{:S(2)}) %collective-permute-start.6) | collective-permute-done | bytes 176160 | tf_op jit(solution)/shard_map/ppermute | solution.py:77
  42.6 0.2 dynamic-slice_add_fusion.2
  42.8 1.5 %collective-permute-start.7 = (f32[2,2,1,1,1,43,128]{6,3,5,4,2,1,0:T(1,128)S(1)}, f32[2,2,1,1,1,43,128]{6,3,5,4,2,1,0:T(1,128)S(1)}, u32[]{:S(2)}, u32[]{:S(2)}) collective-permute-start(f32[2,2,1,1,1,43,128]{6,3,5,4,2,1,0:T(1,128)S(1)} %constant_dynamic-slice_fusion.9), channel_id=1, source_target_pairs={{0,4},{2,6},{4,0},{6,2},{1,5},{3,7},{5,1},{7,3},{8,12},{10,14},{12... | collective-permute-start | bytes 264200 | tf_op jit(solution)/shard_map/ppermute | solution.py:77
  44.3 0.1 dynamic-slice_add_fusion.1
  44.4 0.1 collective-permute-start.11
  44.5 0.8 %collective-permute-done.14 = f32[2,1,2,2,1,43,128]{6,3,5,4,2,1,0:T(2,128)S(1)} collective-permute-done((f32[2,1,2,2,1,43,128]{6,3,5,4,2,1,0:T(2,128)S(1)}, f32[2,1,2,2,1,43,128]{6,3,5,4,2,1,0:T(2,128)S(1)}, u32[]{:S(2)}, u32[]{:S(2)}) %collective-permute-start.14) | collective-permute-done | bytes 176160 | tf_op jit(solution)/shard_map/ppermute | solution.py:77
  45.3 0.1 dynamic-slice_add_fusion
  45.4 0.1 constant_dynamic-slice_fusion.1
  45.5 1.0 %collective-permute-start.15 = (f32[2,1,2,1,1,43,128]{6,3,5,4,2,1,0:T(1,128)S(1)}, f32[2,1,2,1,1,43,128]{6,3,5,4,2,1,0:T(1,128)S(1)}, u32[]{:S(2)}, u32[]{:S(2)}) collective-permute-start(f32[2,1,2,1,1,43,128]{6,3,5,4,2,1,0:T(1,128)S(1)} %constant_dynamic-slice_fusion.1), channel_id=1, source_target_pairs={{0,2},{2,0},{4,6},{6,4},{1,3},{3,1},{5,7},{7,5},{8,10},{10,8},{12,... | collective-permute-start | bytes 264200 | tf_op jit(solution)/shard_map/ppermute | solution.py:77
  46.5 0.9 %collective-permute-done.7 = f32[2,2,1,1,1,43,128]{6,3,5,4,2,1,0:T(1,128)S(1)} collective-permute-done((f32[2,2,1,1,1,43,128]{6,3,5,4,2,1,0:T(1,128)S(1)}, f32[2,2,1,1,1,43,128]{6,3,5,4,2,1,0:T(1,128)S(1)}, u32[]{:S(2)}, u32[]{:S(2)}) %collective-permute-start.7) | collective-permute-done | bytes 88096 | tf_op jit(solution)/shard_map/ppermute | solution.py:77
  47.4 0.1 dynamic-slice_add_fusion.5
  47.5 1.2 %collective-permute-start.8 = (f32[2,1,1,1,1,43,128]{6,3,5,4,2,1,0:T(1,128)S(1)}, f32[2,1,1,1,1,43,128]{6,3,5,4,2,1,0:T(1,128)S(1)}, u32[]{:S(2)}, u32[]{:S(2)}) collective-permute-start(f32[2,1,1,1,1,43,128]{6,3,5,4,2,1,0:T(1,128)S(1)} %constant_dynamic-slice_fusion.8), channel_id=1, source_target_pairs={{0,8},{8,0},{16,24},{24,16},{1,9},{9,1},{17,25},{25,17},{2,10},{10... | collective-permute-start | bytes 132104 | tf_op jit(solution)/shard_map/ppermute | solution.py:77
  48.7 0.8 %collective-permute-done.11 = f32[2,1,1,2,1,43,128]{6,3,5,4,2,1,0:T(2,128)S(1)} collective-permute-done((f32[2,1,1,2,1,43,128]{6,3,5,4,2,1,0:T(2,128)S(1)}, f32[2,1,1,2,1,43,128]{6,3,5,4,2,1,0:T(2,128)S(1)}, u32[]{:S(2)}, u32[]{:S(2)}) %collective-permute-start.11) | collective-permute-done | bytes 88096 | tf_op jit(solution)/shard_map/ppermute | solution.py:77
  49.6 1.8 %collective-permute-start.12 = (f32[2,1,1,1,1,43,128]{6,3,5,4,2,1,0:T(1,128)S(1)}, f32[2,1,1,1,1,43,128]{6,3,5,4,2,1,0:T(1,128)S(1)}, u32[]{:S(2)}, u32[]{:S(2)}) collective-permute-start(f32[2,1,1,1,1,43,128]{6,3,5,4,2,1,0:T(1,128)S(1)} %constant_dynamic-slice_fusion.4), channel_id=1, source_target_pairs={{0,2},{2,0},{4,6},{6,4},{1,3},{3,1},{5,7},{7,5},{8,10},{10,8},{12,... | collective-permute-start | bytes 132104 | tf_op jit(solution)/shard_map/ppermute | solution.py:77
  51.4 0.0 collective-permute-done.15
  51.4 0.1 dynamic-slice_add_fusion.3
  51.5 0.1 collective-permute-start.16
  51.6 0.0 collective-permute-done.8
  51.7 4.0 %collective-permute-start.9 = (f32[1,1,1,1,1,43,128]{6,3,5,4,2,1,0:T(1,128)S(1)}, f32[1,1,1,1,1,43,128]{6,3,5,4,2,1,0:T(1,128)S(1)}, u32[]{:S(2)}, u32[]{:S(2)}) collective-permute-start(f32[1,1,1,1,1,43,128]{6,3,5,4,2,1,0:T(1,128)S(1)} %constant_dynamic-slice_fusion.7), channel_id=1, source_target_pairs={{0,16},{8,24},{16,0},{24,8},{1,17},{9,25},{17,1},{25,9},{2,18},{10... | collective-permute-start | bytes 66056 | tf_op jit(solution)/shard_map/ppermute | solution.py:77
  55.7 0.0 collective-permute-done.12
  55.7 0.1 dynamic-slice_add_fusion.7
  55.8 0.5 collective-permute-start.13
  56.4 2.5 %collective-permute-start.17 = (f32[1,1,1,1,1,43,128]{6,3,5,4,2,1,0:T(1,128)S(1)}, f32[1,1,1,1,1,43,128]{6,3,5,4,2,1,0:T(1,128)S(1)}, u32[]{:S(2)}, u32[]{:S(2)}) collective-permute-start(f32[1,1,1,1,1,43,128]{6,3,5,4,2,1,0:T(1,128)S(1)} %constant_dynamic-slice_fusion.13), channel_id=1, source_target_pairs={{0,16},{8,24},{16,0},{24,8},{1,17},{9,25},{17,1},{25,9},{2,18},{10... | collective-permute-start | bytes 66056 | tf_op jit(solution)/shard_map/ppermute | solution.py:77
  58.9 2.2 %collective-permute-done.17 = f32[1,1,1,1,1,43,128]{6,3,5,4,2,1,0:T(1,128)S(1)} collective-permute-done((f32[1,1,1,1,1,43,128]{6,3,5,4,2,1,0:T(1,128)S(1)}, f32[1,1,1,1,1,43,128]{6,3,5,4,2,1,0:T(1,128)S(1)}, u32[]{:S(2)}, u32[]{:S(2)}) %collective-permute-start.17) | collective-permute-done | bytes 22048 | tf_op jit(solution)/shard_map/ppermute | solution.py:77
  61.3 0.1 pad_maximum_fusion.8
  61.3 0.1 reshape_squeeze.3
  61.4 0.1 copy.29
  61.5 0.6 %pad_maximum_fusion.7 = f32[64,258]{1,0:T(8,128)} fusion(f32[64,2]{1,0:T(8,128)S(1)} %copy.29, f32[64,256]{1,0:T(8,128)S(1)} %bitcast.26), kind=kLoop, calls=%fused_computation.19 | loop fusion | flops 16512 | bytes 132096 | tf_op jit(solution)/shard_map/concatenate | solution.py:210
  (25 shorter events, 0.5 us)
Async XLA Ops:
  1.1 13.5 %collective-permute-start.4 = (f32[3,4,8,1,128]{4,3,2,1,0:T(1,128)S(1)}, f32[3,4,8,1,128]{4,3,2,1,0:T(1,128)S(1)}, u32[]{:S(2)}, u32[]{:S(2)}) collective-permute-start(f32[3,4,8,1,128]{4,3,2,1,0:T(1,128)S(1)} %broadcast_select_fusion.2), channel_id=1, source_target_pairs={{0,1},{1,0},{2,3},{3,2},{4,5},{5,4},{6,7},{7,6},{8,9},{9,8},{10,11... | collective-permute-start | bytes 147464 | tf_op jit(solution)/shard_map/ppermute | solution.py:44
  2.5 12.6 %copy-start = (f32[3,4,8,4,128]{4,3,2,1,0:T(4,128)S(1)}, f32[3,4,8,4,128]{4,3,2,1,0:T(4,128)}, u32[]{:S(2)}) copy-start(f32[3,4,8,4,128]{4,3,2,1,0:T(4,128)} %param.3) | copy-start | bytes 589828
  2.5 12.6 %collective-permute-start = (f32[3,1,8,4,128]{4,3,2,1,0:T(4,128)S(1)}, f32[3,1,8,4,128]{4,3,2,1,0:T(4,128)S(1)}, u32[]{:S(2)}, u32[]{:S(2)}) collective-permute-start(f32[3,1,8,4,128]{4,3,2,1,0:T(4,128)S(1)} %get-tuple-element.13), channel_id=1, source_target_pairs={{8,0},{16,8},{24,16},{0,24},{9,1},{17,9},{25,17},{1,25},{10,2},{18... | collective-permute-start | bytes 147464 | tf_op jit(solution)/shard_map/ppermute | solution.py:49
  7.1 7.9 %collective-permute-start.1 = (f32[3,1,8,4,128]{4,3,2,1,0:T(4,128)S(1)}, f32[3,1,8,4,128]{4,3,2,1,0:T(4,128)S(1)}, u32[]{:S(2)}, u32[]{:S(2)}) collective-permute-start(f32[3,1,8,4,128]{4,3,2,1,0:T(4,128)S(1)} %get-tuple-element.14), channel_id=1, source_target_pairs={{0,8},{8,16},{16,24},{24,0},{1,9},{9,17},{17,25},{25,1},{2,10},{10... | collective-permute-start | bytes 147464 | tf_op jit(solution)/shard_map/ppermute | solution.py:48
  7.9 6.8 %collective-permute-start.2 = (f32[3,4,1,4,128]{4,3,2,1,0:T(4,128)S(1)}, f32[3,4,1,4,128]{4,3,2,1,0:T(4,128)S(1)}, u32[]{:S(2)}, u32[]{:S(2)}) collective-permute-start(f32[3,4,1,4,128]{4,3,2,1,0:T(4,128)S(1)} %get-tuple-element.15), channel_id=1, source_target_pairs={{2,0},{4,2},{6,4},{0,6},{3,1},{5,3},{7,5},{1,7},{10,8},{12,10},{14... | collective-permute-start | bytes 73736 | tf_op jit(solution)/shard_map/ppermute | solution.py:49
  10.3 4.7 %collective-permute-start.3 = (f32[3,4,1,4,128]{4,3,2,1,0:T(4,128)S(1)}, f32[3,4,1,4,128]{4,3,2,1,0:T(4,128)S(1)}, u32[]{:S(2)}, u32[]{:S(2)}) collective-permute-start(f32[3,4,1,4,128]{4,3,2,1,0:T(4,128)S(1)} %get-tuple-element.16), channel_id=1, source_target_pairs={{0,2},{2,4},{4,6},{6,0},{1,3},{3,5},{5,7},{7,1},{8,10},{10,12},{12... | collective-permute-start | bytes 73736 | tf_op jit(solution)/shard_map/ppermute | solution.py:48
  32.3 2.7 %collective-permute-start.5 = (f32[2,2,2,2,1,129,128]{6,3,5,4,2,1,0:T(2,128)S(1)}, f32[2,2,2,2,1,129,128]{6,3,5,4,2,1,0:T(2,128)S(1)}, u32[]{:S(2)}, u32[]{:S(2)}) collective-permute-start(f32[2,2,2,2,1,129,128]{6,3,5,4,2,1,0:T(2,128)S(1)} %copy.31), channel_id=1, source_target_pairs={{0,1},{1,0},{2,3},{3,2},{4,5},{5,4},{6,7},{7,6},{8,9},{9,8},{10,11... | collective-permute-start | bytes 3170312 | tf_op jit(solution)/shard_map/ppermute | solution.py:77
  36.0 6.6 %collective-permute-start.6 = (f32[2,2,2,1,1,43,128]{6,3,5,4,2,1,0:T(1,128)S(1)}, f32[2,2,2,1,1,43,128]{6,3,5,4,2,1,0:T(1,128)S(1)}, u32[]{:S(2)}, u32[]{:S(2)}) collective-permute-start(f32[2,2,2,1,1,43,128]{6,3,5,4,2,1,0:T(1,128)S(1)} %constant_dynamic-slice_fusion.10), channel_id=1, source_target_pairs={{0,2},{2,0},{4,6},{6,4},{1,3},{3,1},{5,7},{7,5},{8,10},{10,8},{12,... | collective-permute-start | bytes 528392 | tf_op jit(solution)/shard_map/ppermute | solution.py:77
  37.7 6.6 %collective-permute-start.10 = (f32[2,2,1,2,1,43,128]{6,3,5,4,2,1,0:T(2,128)S(1)}, f32[2,2,1,2,1,43,128]{6,3,5,4,2,1,0:T(2,128)S(1)}, u32[]{:S(2)}, u32[]{:S(2)}) collective-permute-start(f32[2,2,1,2,1,43,128]{6,3,5,4,2,1,0:T(2,128)S(1)} %constant_dynamic-slice_fusion.6), channel_id=1, source_target_pairs={{0,4},{2,6},{4,0},{6,2},{1,5},{3,7},{5,1},{7,3},{8,12},{10,14},{12... | collective-permute-start | bytes 528392 | tf_op jit(solution)/shard_map/ppermute | solution.py:77
  39.3 6.0 %collective-permute-start.14 = (f32[2,1,2,2,1,43,128]{6,3,5,4,2,1,0:T(2,128)S(1)}, f32[2,1,2,2,1,43,128]{6,3,5,4,2,1,0:T(2,128)S(1)}, u32[]{:S(2)}, u32[]{:S(2)}) collective-permute-start(f32[2,1,2,2,1,43,128]{6,3,5,4,2,1,0:T(2,128)S(1)} %constant_dynamic-slice_fusion.2), channel_id=1, source_target_pairs={{0,8},{8,0},{16,24},{24,16},{1,9},{9,1},{17,25},{25,17},{2,10},{10... | collective-permute-start | bytes 528392 | tf_op jit(solution)/shard_map/ppermute | solution.py:77
  42.8 4.6 %collective-permute-start.7 = (f32[2,2,1,1,1,43,128]{6,3,5,4,2,1,0:T(1,128)S(1)}, f32[2,2,1,1,1,43,128]{6,3,5,4,2,1,0:T(1,128)S(1)}, u32[]{:S(2)}, u32[]{:S(2)}) collective-permute-start(f32[2,2,1,1,1,43,128]{6,3,5,4,2,1,0:T(1,128)S(1)} %constant_dynamic-slice_fusion.9), channel_id=1, source_target_pairs={{0,4},{2,6},{4,0},{6,2},{1,5},{3,7},{5,1},{7,3},{8,12},{10,14},{12... | collective-permute-start | bytes 264200 | tf_op jit(solution)/shard_map/ppermute | solution.py:77
  44.4 5.0 %collective-permute-start.11 = (f32[2,1,1,2,1,43,128]{6,3,5,4,2,1,0:T(2,128)S(1)}, f32[2,1,1,2,1,43,128]{6,3,5,4,2,1,0:T(2,128)S(1)}, u32[]{:S(2)}, u32[]{:S(2)}) collective-permute-start(f32[2,1,1,2,1,43,128]{6,3,5,4,2,1,0:T(2,128)S(1)} %constant_dynamic-slice_fusion.5), channel_id=1, source_target_pairs={{0,8},{8,0},{16,24},{24,16},{1,9},{9,1},{17,25},{25,17},{2,10},{10... | collective-permute-start | bytes 264200 | tf_op jit(solution)/shard_map/ppermute | solution.py:77
  45.5 5.9 %collective-permute-start.15 = (f32[2,1,2,1,1,43,128]{6,3,5,4,2,1,0:T(1,128)S(1)}, f32[2,1,2,1,1,43,128]{6,3,5,4,2,1,0:T(1,128)S(1)}, u32[]{:S(2)}, u32[]{:S(2)}) collective-permute-start(f32[2,1,2,1,1,43,128]{6,3,5,4,2,1,0:T(1,128)S(1)} %constant_dynamic-slice_fusion.1), channel_id=1, source_target_pairs={{0,2},{2,0},{4,6},{6,4},{1,3},{3,1},{5,7},{7,5},{8,10},{10,8},{12,... | collective-permute-start | bytes 264200 | tf_op jit(solution)/shard_map/ppermute | solution.py:77
  47.5 4.1 %collective-permute-start.8 = (f32[2,1,1,1,1,43,128]{6,3,5,4,2,1,0:T(1,128)S(1)}, f32[2,1,1,1,1,43,128]{6,3,5,4,2,1,0:T(1,128)S(1)}, u32[]{:S(2)}, u32[]{:S(2)}) collective-permute-start(f32[2,1,1,1,1,43,128]{6,3,5,4,2,1,0:T(1,128)S(1)} %constant_dynamic-slice_fusion.8), channel_id=1, source_target_pairs={{0,8},{8,0},{16,24},{24,16},{1,9},{9,1},{17,25},{25,17},{2,10},{10... | collective-permute-start | bytes 132104 | tf_op jit(solution)/shard_map/ppermute | solution.py:77
  49.6 6.1 %collective-permute-start.12 = (f32[2,1,1,1,1,43,128]{6,3,5,4,2,1,0:T(1,128)S(1)}, f32[2,1,1,1,1,43,128]{6,3,5,4,2,1,0:T(1,128)S(1)}, u32[]{:S(2)}, u32[]{:S(2)}) collective-permute-start(f32[2,1,1,1,1,43,128]{6,3,5,4,2,1,0:T(1,128)S(1)} %constant_dynamic-slice_fusion.4), channel_id=1, source_target_pairs={{0,2},{2,0},{4,6},{6,4},{1,3},{3,1},{5,7},{7,5},{8,10},{10,8},{12,... | collective-permute-start | bytes 132104 | tf_op jit(solution)/shard_map/ppermute | solution.py:77
  51.5 4.8 %collective-permute-start.16 = (f32[2,1,1,1,1,43,128]{6,3,5,4,2,1,0:T(1,128)S(1)}, f32[2,1,1,1,1,43,128]{6,3,5,4,2,1,0:T(1,128)S(1)}, u32[]{:S(2)}, u32[]{:S(2)}) collective-permute-start(f32[2,1,1,1,1,43,128]{6,3,5,4,2,1,0:T(1,128)S(1)} %constant_dynamic-slice_fusion), channel_id=1, source_target_pairs={{0,4},{2,6},{4,0},{6,2},{1,5},{3,7},{5,1},{7,3},{8,12},{10,14},{12... | collective-permute-start | bytes 132104 | tf_op jit(solution)/shard_map/ppermute | solution.py:77
  51.7 7.2 %collective-permute-start.9 = (f32[1,1,1,1,1,43,128]{6,3,5,4,2,1,0:T(1,128)S(1)}, f32[1,1,1,1,1,43,128]{6,3,5,4,2,1,0:T(1,128)S(1)}, u32[]{:S(2)}, u32[]{:S(2)}) collective-permute-start(f32[1,1,1,1,1,43,128]{6,3,5,4,2,1,0:T(1,128)S(1)} %constant_dynamic-slice_fusion.7), channel_id=1, source_target_pairs={{0,16},{8,24},{16,0},{24,8},{1,17},{9,25},{17,1},{25,9},{2,18},{10... | collective-permute-start | bytes 66056 | tf_op jit(solution)/shard_map/ppermute | solution.py:77
  55.8 5.4 %collective-permute-start.13 = (f32[1,1,1,1,1,43,128]{6,3,5,4,2,1,0:T(1,128)S(1)}, f32[1,1,1,1,1,43,128]{6,3,5,4,2,1,0:T(1,128)S(1)}, u32[]{:S(2)}, u32[]{:S(2)}) collective-permute-start(f32[1,1,1,1,1,43,128]{6,3,5,4,2,1,0:T(1,128)S(1)} %constant_dynamic-slice_fusion.3), channel_id=1, source_target_pairs={{0,16},{8,24},{16,0},{24,8},{1,17},{9,25},{17,1},{25,9},{2,18},{10... | collective-permute-start | bytes 66056 | tf_op jit(solution)/shard_map/ppermute | solution.py:77
  56.4 4.8 %collective-permute-start.17 = (f32[1,1,1,1,1,43,128]{6,3,5,4,2,1,0:T(1,128)S(1)}, f32[1,1,1,1,1,43,128]{6,3,5,4,2,1,0:T(1,128)S(1)}, u32[]{:S(2)}, u32[]{:S(2)}) collective-permute-start(f32[1,1,1,1,1,43,128]{6,3,5,4,2,1,0:T(1,128)S(1)} %constant_dynamic-slice_fusion.13), channel_id=1, source_target_pairs={{0,16},{8,24},{16,0},{24,8},{1,17},{9,25},{17,1},{25,9},{2,18},{10... | collective-permute-start | bytes 66056 | tf_op jit(solution)/shard_map/ppermute | solution.py:77

commit v15 on v14

--- a/solution.py
+++ b/solution.py
@@ -105,7 +105,7 @@
 
 def triangle_kernel(block_len, dense, slot_ref, w_ref, g_ref, m_ref, out_ref, sym_ref, rest_ref):
     test, width = w_ref.shape[1], m_ref.shape[1]
-    group = 16
+    group = 32
     full = block_len // 128 if dense else out_ref.shape[2] // 128
     out_ref[...] = jnp.zeros(out_ref.shape, out_ref.dtype)
     rest_ref[...] = jnp.zeros(rest_ref.shape, rest_ref.dtype)

time: 62.5 us -> 62 us (level)
  no operation moved by 1% of the time
where the time goes in v15:
time: 62 us; the launch traced here: 61.7 us
  starting transfers between devices  23.8 us (38%)
  Pallas kernels  13 us (21%)
  waiting for transfers between devices  10.8 us (17%)
  local copies, waits for them, and re-layouts  6.9 us (11%)
  other arithmetic  6.83 us (11%)
    ppermute x13, starting transfers between devices, halve(): return keep + lax.ppermute(other, axis, pairs)  16.1 us
    pallas_call x1, Pallas kernels, triangle(): pl.pallas_call(functools.partial(triangle_kernel, block_len, dense), out_...  13 us
    ppermute x13, waiting for transfers between devices, halve(): return keep + lax.ppermute(other, axis, pairs)  10.4 us
    ppermute x2, starting transfers between devices, face_gradients(): after = lax.ppermute(leading, axis, down)  7.12 us
    dynamic_slice x1, local copies, waits for them, and re-layouts, halve(): keep = lax.dynamic_index_in_dim(value, mine, dim, keepdims=True)  1.73 us
    add x13, other arithmetic, halve(): return keep + lax.ppermute(other, axis, pairs)  1.64 us
    slice x2, local copies, waits for them, and re-layouts, face_gradients(): leading = lax.slice_in_dim(value, 0, 1, axis=dim)  1.59 us
  transfers between devices with their start and end apart: 18, of which 7 were waited for; matrix products, arithmetic and copies ran while one was open for 11% of the time, Pallas kernels for 0%

profile of v15, /device:TPU:0, one launch (start us, length us, event | category | flops | bytes accessed | tf_op | source)
XLA Modules:
  0.0 61.7 jit_solution(15704240007141554869)
XLA Ops:
  0.0 1.1 %broadcast_select_fusion.2 = f32[3,4,8,1,128]{4,3,2,1,0:T(1,128)S(1)} fusion(pred[]{:T(512)S(6)} %eq.37, f32[3,4,8,4,128]{4,3,2,1,0:T(4,128)} %param.3), kind=kLoop, calls=%fused_computation.22 | loop fusion | flops 12288 | bytes 147457 | tf_op jit(solution)/shard_map/jit(_where)/select_n | solution.py:44
  1.1 0.5 collective-permute-start.4
  1.6 0.8 %fusion.8 = (f32[3,1,8,4,128]{4,3,2,1,0:T(4,128)S(1)}, f32[3,1,8,4,128]{4,3,2,1,0:T(4,128)S(1)}) fusion(f32[3,4,8,4,128]{4,3,2,1,0:T(4,128)} %param.3), kind=kLoop, calls=%fused_computation.55 | loop fusion | bytes 196608 | tf_op jit(solution)/shard_map/slice | solution.py:41
  2.5 4.7 %collective-permute-start = (f32[3,1,8,4,128]{4,3,2,1,0:T(4,128)S(1)}, f32[3,1,8,4,128]{4,3,2,1,0:T(4,128)S(1)}, u32[]{:S(2)}, u32[]{:S(2)}) collective-permute-start(f32[3,1,8,4,128]{4,3,2,1,0:T(4,128)S(1)} %get-tuple-element.13), channel_id=1, source_target_pairs={{8,0},{16,8},{24,16},{0,24},{9,1},{17,9},{25,17},{1,25},{10,2},{18... | collective-permute-start | bytes 147464 | tf_op jit(solution)/shard_map/ppermute | solution.py:49
  7.1 0.0 collective-permute-start.1
  7.1 0.8 %fusion.9 = (f32[3,4,1,4,128]{4,3,2,1,0:T(4,128)S(1)}, f32[3,4,1,4,128]{4,3,2,1,0:T(4,128)S(1)}) fusion(f32[3,4,8,4,128]{4,3,2,1,0:T(4,128)} %param.3), kind=kLoop, calls=%fused_computation.56 | loop fusion | bytes 98304 | tf_op jit(solution)/shard_map/slice | solution.py:41
  7.9 2.4 %collective-permute-start.2 = (f32[3,4,1,4,128]{4,3,2,1,0:T(4,128)S(1)}, f32[3,4,1,4,128]{4,3,2,1,0:T(4,128)S(1)}, u32[]{:S(2)}, u32[]{:S(2)}) collective-permute-start(f32[3,4,1,4,128]{4,3,2,1,0:T(4,128)S(1)} %get-tuple-element.15), channel_id=1, source_target_pairs={{2,0},{4,2},{6,4},{0,6},{3,1},{5,3},{7,5},{1,7},{10,8},{12,10},{14... | collective-permute-start | bytes 73736 | tf_op jit(solution)/shard_map/ppermute | solution.py:49
  10.3 0.0 collective-permute-start.3
  10.3 0.7 %broadcast_multiply_fusion = f32[4,8,4]{1,2,0:T(4,128)S(1)} fusion(f32[4,8,4]{1,2,0:T(4,128)} %param.4), kind=kLoop, calls=%fused_computation.51 | loop fusion | flops 128 | bytes 1024 | tf_op jit(solution)/shard_map/mul | solution.py:195
  11.0 0.1 copy.23
  11.1 0.1 mul.32
  11.2 0.8 %select_reduce_fusion = s32[32]{0:T(128)S(1)} fusion(s32[32]{0:T(128)} %param.5), kind=kLoop, calls=%fused_computation.35 | loop fusion | flops 3040 | bytes 256 | tf_op jit(solution)/shard_map/reduce_sum | solution.py:201
  12.0 1.0 %fusion.6 = f32[3,64,128]{1,2,0:T(8,128)S(1)} fusion(f32[3,128,128]{2,1,0:T(8,128)} %bitcast.20, f32[128]{0:T(128)S(1)} %mul.32), kind=kLoop, calls=%fused_computation.15 | loop fusion | flops 24576 | bytes 197120 | tf_op jit(solution)/shard_map/transpose | solution.py:196
  13.0 0.5 broadcast_clamp_fusion.slot_ref
  13.6 0.1 copy.24
  13.7 0.1 tile.4
  13.7 0.9 %tile.10.w_ref = f32[3,64,384]{2,1,0:T(8,128)} reshape(f32[3,64,3,128]{3,2,1,0:T(4,128)S(1)} %tile.4) | data formatting | bytes 589824 | tf_op jit(solution)/shard_map/tile | solution.py:196
  14.6 0.0 collective-permute-done.4
  14.6 0.1 broadcast_select_fusion.1
  14.7 0.0 collective-permute-done.2
  14.7 0.4 collective-permute-done.3
  15.1 0.0 collective-permute-done
  15.1 0.0 collective-permute-done.1
  15.1 0.3 fusion.5
  15.4 1.1 %copy.25.g_ref = f32[3,128,384]{2,1,0:T(8,128)} copy(f32[3,128,384]{1,2,0:T(8,128)S(1)} %bitcast.22) | data formatting | bytes 1179648 | tf_op jit(solution)/shard_map/reshape | solution.py:197
  16.5 13.0 %shard_map.37 = f32[32,129,128]{2,1,0:T(8,128)} custom-call(s32[32]{0:T(128)} %broadcast_clamp_fusion.slot_ref, f32[3,64,384]{2,1,0:T(8,128)} %tile.10.w_ref, f32[3,128,384]{2,1,0:T(8,128)} %copy.25.g_ref, f32[384,128]{1,0:T(8,128)} %bitcast.21), custom_call_target="tpu_custom_call" | custom-call | tf_op jit(solution)/shard_map/pallas_call | solution.py:170
  29.5 1.7 %constant_dynamic-slice_fusion.12 = (f32[2,2,2,2,1,129,128]{6,5,4,3,2,1,0:T(8,128)S(1)}, f32[2,2,2,2,1,129,128]{6,5,4,3,2,1,0:T(8,128)S(1)}) fusion(f32[2,2,2,2,2,129,128]{6,5,4,3,2,1,0:T(8,128)} %bitcast.19, s32[]{:T(128)S(6)} %select_n.145, s32[]{:T(128)S(6)} %select_n.146), kind=kLoop, calls=%fused_computation.49 | loop fusion | bytes 4227080 | tf_op jit(solution)/shard_map/jit(dynamic_index_in_dim)/dynamic_slice | solution.py:75
  31.2 0.5 copy.31
  31.8 0.1 collective-permute-start.5
  32.0 2.6 %collective-permute-done.5 = f32[2,2,2,2,1,129,128]{6,3,5,4,2,1,0:T(2,128)S(1)} collective-permute-done((f32[2,2,2,2,1,129,128]{6,3,5,4,2,1,0:T(2,128)S(1)}, f32[2,2,2,2,1,129,128]{6,3,5,4,2,1,0:T(2,128)S(1)}, u32[]{:S(2)}, u32[]{:S(2)}) %collective-permute-start.5) | collective-permute-done | bytes 1056800 | tf_op jit(solution)/shard_map/ppermute | solution.py:77
  34.5 0.7 %copy_add_fusion = f32[2,2,2,2,1,129,128]{6,3,5,4,2,1,0:T(2,128)S(1)} fusion(f32[2,2,2,2,1,129,128]{6,3,5,4,2,1,0:T(2,128)S(1)} %collective-permute-done.5, f32[2,2,2,2,1,129,128]{6,5,4,3,2,1,0:T(8,128)S(1)} %get-tuple-element.5), kind=kLoop, calls=%fused_computation | loop fusion | flops 264192 | bytes 3170304 | tf_op jit(solution)/shard_map/add | solution.py:77
  35.2 0.1 fusion.7
  35.3 0.2 constant_dynamic-slice_fusion.10
  35.5 1.7 %collective-permute-start.6 = (f32[2,2,2,1,1,43,128]{6,3,5,4,2,1,0:T(1,128)S(1)}, f32[2,2,2,1,1,43,128]{6,3,5,4,2,1,0:T(1,128)S(1)}, u32[]{:S(2)}, u32[]{:S(2)}) collective-permute-start(f32[2,2,2,1,1,43,128]{6,3,5,4,2,1,0:T(1,128)S(1)} %constant_dynamic-slice_fusion.10), channel_id=1, source_target_pairs={{0,2},{2,0},{4,6},{6,4},{1,3},{3,1},{5,7},{7,5},{8,10},{10,8},{12,... | collective-permute-start | bytes 528392 | tf_op jit(solution)/shard_map/ppermute | solution.py:77
  37.2 1.6 %collective-permute-start.10 = (f32[2,2,1,2,1,43,128]{6,3,5,4,2,1,0:T(2,128)S(1)}, f32[2,2,1,2,1,43,128]{6,3,5,4,2,1,0:T(2,128)S(1)}, u32[]{:S(2)}, u32[]{:S(2)}) collective-permute-start(f32[2,2,1,2,1,43,128]{6,3,5,4,2,1,0:T(2,128)S(1)} %constant_dynamic-slice_fusion.6), channel_id=1, source_target_pairs={{0,4},{2,6},{4,0},{6,2},{1,5},{3,7},{5,1},{7,3},{8,12},{10,14},{12... | collective-permute-start | bytes 528392 | tf_op jit(solution)/shard_map/ppermute | solution.py:77
  38.8 0.1 collective-permute-start.14
  38.9 3.2 %collective-permute-done.6 = f32[2,2,2,1,1,43,128]{6,3,5,4,2,1,0:T(1,128)S(1)} collective-permute-done((f32[2,2,2,1,1,43,128]{6,3,5,4,2,1,0:T(1,128)S(1)}, f32[2,2,2,1,1,43,128]{6,3,5,4,2,1,0:T(1,128)S(1)}, u32[]{:S(2)}, u32[]{:S(2)}) %collective-permute-start.6) | collective-permute-done | bytes 176160 | tf_op jit(solution)/shard_map/ppermute | solution.py:77
  42.1 0.2 dynamic-slice_add_fusion.2
  42.3 1.5 %collective-permute-start.7 = (f32[2,2,1,1,1,43,128]{6,3,5,4,2,1,0:T(1,128)S(1)}, f32[2,2,1,1,1,43,128]{6,3,5,4,2,1,0:T(1,128)S(1)}, u32[]{:S(2)}, u32[]{:S(2)}) collective-permute-start(f32[2,2,1,1,1,43,128]{6,3,5,4,2,1,0:T(1,128)S(1)} %constant_dynamic-slice_fusion.9), channel_id=1, source_target_pairs={{0,4},{2,6},{4,0},{6,2},{1,5},{3,7},{5,1},{7,3},{8,12},{10,14},{12... | collective-permute-start | bytes 264200 | tf_op jit(solution)/shard_map/ppermute | solution.py:77
  43.8 0.0 collective-permute-done.10
  43.8 0.1 dynamic-slice_add_fusion.1
  43.9 0.1 collective-permute-start.11
  44.0 0.8 %collective-permute-done.14 = f32[2,1,2,2,1,43,128]{6,3,5,4,2,1,0:T(2,128)S(1)} collective-permute-done((f32[2,1,2,2,1,43,128]{6,3,5,4,2,1,0:T(2,128)S(1)}, f32[2,1,2,2,1,43,128]{6,3,5,4,2,1,0:T(2,128)S(1)}, u32[]{:S(2)}, u32[]{:S(2)}) %collective-permute-start.14) | collective-permute-done | bytes 176160 | tf_op jit(solution)/shard_map/ppermute | solution.py:77
  44.8 0.1 dynamic-slice_add_fusion
  44.9 0.1 constant_dynamic-slice_fusion.1
  45.0 1.0 %collective-permute-start.15 = (f32[2,1,2,1,1,43,128]{6,3,5,4,2,1,0:T(1,128)S(1)}, f32[2,1,2,1,1,43,128]{6,3,5,4,2,1,0:T(1,128)S(1)}, u32[]{:S(2)}, u32[]{:S(2)}) collective-permute-start(f32[2,1,2,1,1,43,128]{6,3,5,4,2,1,0:T(1,128)S(1)} %constant_dynamic-slice_fusion.1), channel_id=1, source_target_pairs={{0,2},{2,0},{4,6},{6,4},{1,3},{3,1},{5,7},{7,5},{8,10},{10,8},{12,... | collective-permute-start | bytes 264200 | tf_op jit(solution)/shard_map/ppermute | solution.py:77
  46.0 0.9 %collective-permute-done.7 = f32[2,2,1,1,1,43,128]{6,3,5,4,2,1,0:T(1,128)S(1)} collective-permute-done((f32[2,2,1,1,1,43,128]{6,3,5,4,2,1,0:T(1,128)S(1)}, f32[2,2,1,1,1,43,128]{6,3,5,4,2,1,0:T(1,128)S(1)}, u32[]{:S(2)}, u32[]{:S(2)}) %collective-permute-start.7) | collective-permute-done | bytes 88096 | tf_op jit(solution)/shard_map/ppermute | solution.py:77
  46.9 0.1 dynamic-slice_add_fusion.5
  47.0 1.2 %collective-permute-start.8 = (f32[2,1,1,1,1,43,128]{6,3,5,4,2,1,0:T(1,128)S(1)}, f32[2,1,1,1,1,43,128]{6,3,5,4,2,1,0:T(1,128)S(1)}, u32[]{:S(2)}, u32[]{:S(2)}) collective-permute-start(f32[2,1,1,1,1,43,128]{6,3,5,4,2,1,0:T(1,128)S(1)} %constant_dynamic-slice_fusion.8), channel_id=1, source_target_pairs={{0,8},{8,0},{16,24},{24,16},{1,9},{9,1},{17,25},{25,17},{2,10},{10... | collective-permute-start | bytes 132104 | tf_op jit(solution)/shard_map/ppermute | solution.py:77
  48.2 0.8 %collective-permute-done.11 = f32[2,1,1,2,1,43,128]{6,3,5,4,2,1,0:T(2,128)S(1)} collective-permute-done((f32[2,1,1,2,1,43,128]{6,3,5,4,2,1,0:T(2,128)S(1)}, f32[2,1,1,2,1,43,128]{6,3,5,4,2,1,0:T(2,128)S(1)}, u32[]{:S(2)}, u32[]{:S(2)}) %collective-permute-start.11) | collective-permute-done | bytes 88096 | tf_op jit(solution)/shard_map/ppermute | solution.py:77
  49.1 1.8 %collective-permute-start.12 = (f32[2,1,1,1,1,43,128]{6,3,5,4,2,1,0:T(1,128)S(1)}, f32[2,1,1,1,1,43,128]{6,3,5,4,2,1,0:T(1,128)S(1)}, u32[]{:S(2)}, u32[]{:S(2)}) collective-permute-start(f32[2,1,1,1,1,43,128]{6,3,5,4,2,1,0:T(1,128)S(1)} %constant_dynamic-slice_fusion.4), channel_id=1, source_target_pairs={{0,2},{2,0},{4,6},{6,4},{1,3},{3,1},{5,7},{7,5},{8,10},{10,8},{12,... | collective-permute-start | bytes 132104 | tf_op jit(solution)/shard_map/ppermute | solution.py:77
  50.9 0.0 collective-permute-done.15
  50.9 0.1 dynamic-slice_add_fusion.3
  51.0 0.1 collective-permute-start.16
  51.2 4.0 %collective-permute-start.9 = (f32[1,1,1,1,1,43,128]{6,3,5,4,2,1,0:T(1,128)S(1)}, f32[1,1,1,1,1,43,128]{6,3,5,4,2,1,0:T(1,128)S(1)}, u32[]{:S(2)}, u32[]{:S(2)}) collective-permute-start(f32[1,1,1,1,1,43,128]{6,3,5,4,2,1,0:T(1,128)S(1)} %constant_dynamic-slice_fusion.7), channel_id=1, source_target_pairs={{0,16},{8,24},{16,0},{24,8},{1,17},{9,25},{17,1},{25,9},{2,18},{10... | collective-permute-start | bytes 66056 | tf_op jit(solution)/shard_map/ppermute | solution.py:77
  55.2 0.1 dynamic-slice_add_fusion.7
  55.3 0.5 collective-permute-start.13
  55.8 0.0 collective-permute-done.16
  55.9 2.5 %collective-permute-start.17 = (f32[1,1,1,1,1,43,128]{6,3,5,4,2,1,0:T(1,128)S(1)}, f32[1,1,1,1,1,43,128]{6,3,5,4,2,1,0:T(1,128)S(1)}, u32[]{:S(2)}, u32[]{:S(2)}) collective-permute-start(f32[1,1,1,1,1,43,128]{6,3,5,4,2,1,0:T(1,128)S(1)} %constant_dynamic-slice_fusion.13), channel_id=1, source_target_pairs={{0,16},{8,24},{16,0},{24,8},{1,17},{9,25},{17,1},{25,9},{2,18},{10... | collective-permute-start | bytes 66056 | tf_op jit(solution)/shard_map/ppermute | solution.py:77
  58.4 2.2 %collective-permute-done.17 = f32[1,1,1,1,1,43,128]{6,3,5,4,2,1,0:T(1,128)S(1)} collective-permute-done((f32[1,1,1,1,1,43,128]{6,3,5,4,2,1,0:T(1,128)S(1)}, f32[1,1,1,1,1,43,128]{6,3,5,4,2,1,0:T(1,128)S(1)}, u32[]{:S(2)}, u32[]{:S(2)}) %collective-permute-start.17) | collective-permute-done | bytes 22048 | tf_op jit(solution)/shard_map/ppermute | solution.py:77
  60.7 0.1 pad_maximum_fusion.8
  60.8 0.1 reshape_squeeze.3
  60.9 0.1 copy.29
  61.0 0.6 %pad_maximum_fusion.7 = f32[64,258]{1,0:T(8,128)} fusion(f32[64,2]{1,0:T(8,128)S(1)} %copy.29, f32[64,256]{1,0:T(8,128)S(1)} %bitcast.26), kind=kLoop, calls=%fused_computation.19 | loop fusion | flops 16512 | bytes 132096 | tf_op jit(solution)/shard_map/concatenate | solution.py:210
  (25 shorter events, 0.5 us)
Async XLA Ops:
  1.1 13.5 %collective-permute-start.4 = (f32[3,4,8,1,128]{4,3,2,1,0:T(1,128)S(1)}, f32[3,4,8,1,128]{4,3,2,1,0:T(1,128)S(1)}, u32[]{:S(2)}, u32[]{:S(2)}) collective-permute-start(f32[3,4,8,1,128]{4,3,2,1,0:T(1,128)S(1)} %broadcast_select_fusion.2), channel_id=1, source_target_pairs={{0,1},{1,0},{2,3},{3,2},{4,5},{5,4},{6,7},{7,6},{8,9},{9,8},{10,11... | collective-permute-start | bytes 147464 | tf_op jit(solution)/shard_map/ppermute | solution.py:44
  2.5 12.6 %copy-start = (f32[3,4,8,4,128]{4,3,2,1,0:T(4,128)S(1)}, f32[3,4,8,4,128]{4,3,2,1,0:T(4,128)}, u32[]{:S(2)}) copy-start(f32[3,4,8,4,128]{4,3,2,1,0:T(4,128)} %param.3) | copy-start | bytes 589828
  2.5 12.6 %collective-permute-start = (f32[3,1,8,4,128]{4,3,2,1,0:T(4,128)S(1)}, f32[3,1,8,4,128]{4,3,2,1,0:T(4,128)S(1)}, u32[]{:S(2)}, u32[]{:S(2)}) collective-permute-start(f32[3,1,8,4,128]{4,3,2,1,0:T(4,128)S(1)} %get-tuple-element.13), channel_id=1, source_target_pairs={{8,0},{16,8},{24,16},{0,24},{9,1},{17,9},{25,17},{1,25},{10,2},{18... | collective-permute-start | bytes 147464 | tf_op jit(solution)/shard_map/ppermute | solution.py:49
  7.1 7.9 %collective-permute-start.1 = (f32[3,1,8,4,128]{4,3,2,1,0:T(4,128)S(1)}, f32[3,1,8,4,128]{4,3,2,1,0:T(4,128)S(1)}, u32[]{:S(2)}, u32[]{:S(2)}) collective-permute-start(f32[3,1,8,4,128]{4,3,2,1,0:T(4,128)S(1)} %get-tuple-element.14), channel_id=1, source_target_pairs={{0,8},{8,16},{16,24},{24,0},{1,9},{9,17},{17,25},{25,1},{2,10},{10... | collective-permute-start | bytes 147464 | tf_op jit(solution)/shard_map/ppermute | solution.py:48
  7.9 6.8 %collective-permute-start.2 = (f32[3,4,1,4,128]{4,3,2,1,0:T(4,128)S(1)}, f32[3,4,1,4,128]{4,3,2,1,0:T(4,128)S(1)}, u32[]{:S(2)}, u32[]{:S(2)}) collective-permute-start(f32[3,4,1,4,128]{4,3,2,1,0:T(4,128)S(1)} %get-tuple-element.15), channel_id=1, source_target_pairs={{2,0},{4,2},{6,4},{0,6},{3,1},{5,3},{7,5},{1,7},{10,8},{12,10},{14... | collective-permute-start | bytes 73736 | tf_op jit(solution)/shard_map/ppermute | solution.py:49
  10.3 4.7 %collective-permute-start.3 = (f32[3,4,1,4,128]{4,3,2,1,0:T(4,128)S(1)}, f32[3,4,1,4,128]{4,3,2,1,0:T(4,128)S(1)}, u32[]{:S(2)}, u32[]{:S(2)}) collective-permute-start(f32[3,4,1,4,128]{4,3,2,1,0:T(4,128)S(1)} %get-tuple-element.16), channel_id=1, source_target_pairs={{0,2},{2,4},{4,6},{6,0},{1,3},{3,5},{5,7},{7,1},{8,10},{10,12},{12... | collective-permute-start | bytes 73736 | tf_op jit(solution)/shard_map/ppermute | solution.py:48
  31.8 2.7 %collective-permute-start.5 = (f32[2,2,2,2,1,129,128]{6,3,5,4,2,1,0:T(2,128)S(1)}, f32[2,2,2,2,1,129,128]{6,3,5,4,2,1,0:T(2,128)S(1)}, u32[]{:S(2)}, u32[]{:S(2)}) collective-permute-start(f32[2,2,2,2,1,129,128]{6,3,5,4,2,1,0:T(2,128)S(1)} %copy.31), channel_id=1, source_target_pairs={{0,1},{1,0},{2,3},{3,2},{4,5},{5,4},{6,7},{7,6},{8,9},{9,8},{10,11... | collective-permute-start | bytes 3170312 | tf_op jit(solution)/shard_map/ppermute | solution.py:77
  35.5 6.6 %collective-permute-start.6 = (f32[2,2,2,1,1,43,128]{6,3,5,4,2,1,0:T(1,128)S(1)}, f32[2,2,2,1,1,43,128]{6,3,5,4,2,1,0:T(1,128)S(1)}, u32[]{:S(2)}, u32[]{:S(2)}) collective-permute-start(f32[2,2,2,1,1,43,128]{6,3,5,4,2,1,0:T(1,128)S(1)} %constant_dynamic-slice_fusion.10), channel_id=1, source_target_pairs={{0,2},{2,0},{4,6},{6,4},{1,3},{3,1},{5,7},{7,5},{8,10},{10,8},{12,... | collective-permute-start | bytes 528392 | tf_op jit(solution)/shard_map/ppermute | solution.py:77
  37.2 6.6 %collective-permute-start.10 = (f32[2,2,1,2,1,43,128]{6,3,5,4,2,1,0:T(2,128)S(1)}, f32[2,2,1,2,1,43,128]{6,3,5,4,2,1,0:T(2,128)S(1)}, u32[]{:S(2)}, u32[]{:S(2)}) collective-permute-start(f32[2,2,1,2,1,43,128]{6,3,5,4,2,1,0:T(2,128)S(1)} %constant_dynamic-slice_fusion.6), channel_id=1, source_target_pairs={{0,4},{2,6},{4,0},{6,2},{1,5},{3,7},{5,1},{7,3},{8,12},{10,14},{12... | collective-permute-start | bytes 528392 | tf_op jit(solution)/shard_map/ppermute | solution.py:77
  38.8 6.0 %collective-permute-start.14 = (f32[2,1,2,2,1,43,128]{6,3,5,4,2,1,0:T(2,128)S(1)}, f32[2,1,2,2,1,43,128]{6,3,5,4,2,1,0:T(2,128)S(1)}, u32[]{:S(2)}, u32[]{:S(2)}) collective-permute-start(f32[2,1,2,2,1,43,128]{6,3,5,4,2,1,0:T(2,128)S(1)} %constant_dynamic-slice_fusion.2), channel_id=1, source_target_pairs={{0,8},{8,0},{16,24},{24,16},{1,9},{9,1},{17,25},{25,17},{2,10},{10... | collective-permute-start | bytes 528392 | tf_op jit(solution)/shard_map/ppermute | solution.py:77
  42.3 4.6 %collective-permute-start.7 = (f32[2,2,1,1,1,43,128]{6,3,5,4,2,1,0:T(1,128)S(1)}, f32[2,2,1,1,1,43,128]{6,3,5,4,2,1,0:T(1,128)S(1)}, u32[]{:S(2)}, u32[]{:S(2)}) collective-permute-start(f32[2,2,1,1,1,43,128]{6,3,5,4,2,1,0:T(1,128)S(1)} %constant_dynamic-slice_fusion.9), channel_id=1, source_target_pairs={{0,4},{2,6},{4,0},{6,2},{1,5},{3,7},{5,1},{7,3},{8,12},{10,14},{12... | collective-permute-start | bytes 264200 | tf_op jit(solution)/shard_map/ppermute | solution.py:77
  43.9 5.0 %collective-permute-start.11 = (f32[2,1,1,2,1,43,128]{6,3,5,4,2,1,0:T(2,128)S(1)}, f32[2,1,1,2,1,43,128]{6,3,5,4,2,1,0:T(2,128)S(1)}, u32[]{:S(2)}, u32[]{:S(2)}) collective-permute-start(f32[2,1,1,2,1,43,128]{6,3,5,4,2,1,0:T(2,128)S(1)} %constant_dynamic-slice_fusion.5), channel_id=1, source_target_pairs={{0,8},{8,0},{16,24},{24,16},{1,9},{9,1},{17,25},{25,17},{2,10},{10... | collective-permute-start | bytes 264200 | tf_op jit(solution)/shard_map/ppermute | solution.py:77
  45.0 5.9 %collective-permute-start.15 = (f32[2,1,2,1,1,43,128]{6,3,5,4,2,1,0:T(1,128)S(1)}, f32[2,1,2,1,1,43,128]{6,3,5,4,2,1,0:T(1,128)S(1)}, u32[]{:S(2)}, u32[]{:S(2)}) collective-permute-start(f32[2,1,2,1,1,43,128]{6,3,5,4,2,1,0:T(1,128)S(1)} %constant_dynamic-slice_fusion.1), channel_id=1, source_target_pairs={{0,2},{2,0},{4,6},{6,4},{1,3},{3,1},{5,7},{7,5},{8,10},{10,8},{12,... | collective-permute-start | bytes 264200 | tf_op jit(solution)/shard_map/ppermute | solution.py:77
  47.0 4.1 %collective-permute-start.8 = (f32[2,1,1,1,1,43,128]{6,3,5,4,2,1,0:T(1,128)S(1)}, f32[2,1,1,1,1,43,128]{6,3,5,4,2,1,0:T(1,128)S(1)}, u32[]{:S(2)}, u32[]{:S(2)}) collective-permute-start(f32[2,1,1,1,1,43,128]{6,3,5,4,2,1,0:T(1,128)S(1)} %constant_dynamic-slice_fusion.8), channel_id=1, source_target_pairs={{0,8},{8,0},{16,24},{24,16},{1,9},{9,1},{17,25},{25,17},{2,10},{10... | collective-permute-start | bytes 132104 | tf_op jit(solution)/shard_map/ppermute | solution.py:77
  49.1 6.1 %collective-permute-start.12 = (f32[2,1,1,1,1,43,128]{6,3,5,4,2,1,0:T(1,128)S(1)}, f32[2,1,1,1,1,43,128]{6,3,5,4,2,1,0:T(1,128)S(1)}, u32[]{:S(2)}, u32[]{:S(2)}) collective-permute-start(f32[2,1,1,1,1,43,128]{6,3,5,4,2,1,0:T(1,128)S(1)} %constant_dynamic-slice_fusion.4), channel_id=1, source_target_pairs={{0,2},{2,0},{4,6},{6,4},{1,3},{3,1},{5,7},{7,5},{8,10},{10,8},{12,... | collective-permute-start | bytes 132104 | tf_op jit(solution)/shard_map/ppermute | solution.py:77
  51.0 4.8 %collective-permute-start.16 = (f32[2,1,1,1,1,43,128]{6,3,5,4,2,1,0:T(1,128)S(1)}, f32[2,1,1,1,1,43,128]{6,3,5,4,2,1,0:T(1,128)S(1)}, u32[]{:S(2)}, u32[]{:S(2)}) collective-permute-start(f32[2,1,1,1,1,43,128]{6,3,5,4,2,1,0:T(1,128)S(1)} %constant_dynamic-slice_fusion), channel_id=1, source_target_pairs={{0,4},{2,6},{4,0},{6,2},{1,5},{3,7},{5,1},{7,3},{8,12},{10,14},{12... | collective-permute-start | bytes 132104 | tf_op jit(solution)/shard_map/ppermute | solution.py:77
  51.2 7.2 %collective-permute-start.9 = (f32[1,1,1,1,1,43,128]{6,3,5,4,2,1,0:T(1,128)S(1)}, f32[1,1,1,1,1,43,128]{6,3,5,4,2,1,0:T(1,128)S(1)}, u32[]{:S(2)}, u32[]{:S(2)}) collective-permute-start(f32[1,1,1,1,1,43,128]{6,3,5,4,2,1,0:T(1,128)S(1)} %constant_dynamic-slice_fusion.7), channel_id=1, source_target_pairs={{0,16},{8,24},{16,0},{24,8},{1,17},{9,25},{17,1},{25,9},{2,18},{10... | collective-permute-start | bytes 66056 | tf_op jit(solution)/shard_map/ppermute | solution.py:77
  55.3 5.4 %collective-permute-start.13 = (f32[1,1,1,1,1,43,128]{6,3,5,4,2,1,0:T(1,128)S(1)}, f32[1,1,1,1,1,43,128]{6,3,5,4,2,1,0:T(1,128)S(1)}, u32[]{:S(2)}, u32[]{:S(2)}) collective-permute-start(f32[1,1,1,1,1,43,128]{6,3,5,4,2,1,0:T(1,128)S(1)} %constant_dynamic-slice_fusion.3), channel_id=1, source_target_pairs={{0,16},{8,24},{16,0},{24,8},{1,17},{9,25},{17,1},{25,9},{2,18},{10... | collective-permute-start | bytes 66056 | tf_op jit(solution)/shard_map/ppermute | solution.py:77
  55.9 4.8 %collective-permute-start.17 = (f32[1,1,1,1,1,43,128]{6,3,5,4,2,1,0:T(1,128)S(1)}, f32[1,1,1,1,1,43,128]{6,3,5,4,2,1,0:T(1,128)S(1)}, u32[]{:S(2)}, u32[]{:S(2)}) collective-permute-start(f32[1,1,1,1,1,43,128]{6,3,5,4,2,1,0:T(1,128)S(1)} %constant_dynamic-slice_fusion.13), channel_id=1, source_target_pairs={{0,16},{8,24},{16,0},{24,8},{1,17},{9,25},{17,1},{25,9},{2,18},{10... | collective-permute-start | bytes 66056 | tf_op jit(solution)/shard_map/ppermute | solution.py:77

commit v16 on v15

--- a/solution.py
+++ b/solution.py
@@ -105,7 +105,7 @@
 
 def triangle_kernel(block_len, dense, slot_ref, w_ref, g_ref, m_ref, out_ref, sym_ref, rest_ref):
     test, width = w_ref.shape[1], m_ref.shape[1]
-    group = 32
+    group = 64
     full = block_len // 128 if dense else out_ref.shape[2] // 128
     out_ref[...] = jnp.zeros(out_ref.shape, out_ref.dtype)
     rest_ref[...] = jnp.zeros(rest_ref.shape, rest_ref.dtype)

time: 62 us -> 62.8 us (1.013)
  no operation moved by 1% of the time
where the time goes in v16:
time: 62.8 us; the launch traced here: 62.4 us
  starting transfers between devices  23.8 us (38%)
  Pallas kernels  13.6 us (22%)
  waiting for transfers between devices  10.8 us (17%)
  local copies, waits for them, and re-layouts  7.08 us (11%)
  other arithmetic  6.83 us (11%)
    ppermute x13, starting transfers between devices, halve(): return keep + lax.ppermute(other, axis, pairs)  16.1 us
    pallas_call x1, Pallas kernels, triangle(): pl.pallas_call(functools.partial(triangle_kernel, block_len, dense), out_...  13.6 us
    ppermute x13, waiting for transfers between devices, halve(): return keep + lax.ppermute(other, axis, pairs)  10.4 us
    ppermute x2, starting transfers between devices, face_gradients(): after = lax.ppermute(leading, axis, down)  7.12 us
    dynamic_slice x1, local copies, waits for them, and re-layouts, halve(): keep = lax.dynamic_index_in_dim(value, mine, dim, keepdims=True)  1.91 us
    add x13, other arithmetic, halve(): return keep + lax.ppermute(other, axis, pairs)  1.64 us
    slice x2, local copies, waits for them, and re-layouts, face_gradients(): leading = lax.slice_in_dim(value, 0, 1, axis=dim)  1.59 us
  transfers between devices with their start and end apart: 18, of which 7 were waited for; matrix products, arithmetic and copies ran while one was open for 11% of the time, Pallas kernels for 0%

profile of v16, /device:TPU:0, one launch (start us, length us, event | category | flops | bytes accessed | tf_op | source)
XLA Modules:
  0.0 62.4 jit_solution(6734881909923383079)
XLA Ops:
  0.0 1.1 %broadcast_select_fusion.2 = f32[3,4,8,1,128]{4,3,2,1,0:T(1,128)S(1)} fusion(pred[]{:T(512)S(6)} %eq.37, f32[3,4,8,4,128]{4,3,2,1,0:T(4,128)} %param.3), kind=kLoop, calls=%fused_computation.22 | loop fusion | flops 12288 | bytes 147457 | tf_op jit(solution)/shard_map/jit(_where)/select_n | solution.py:44
  1.1 0.5 collective-permute-start.4
  1.6 0.8 %fusion.8 = (f32[3,1,8,4,128]{4,3,2,1,0:T(4,128)S(1)}, f32[3,1,8,4,128]{4,3,2,1,0:T(4,128)S(1)}) fusion(f32[3,4,8,4,128]{4,3,2,1,0:T(4,128)} %param.3), kind=kLoop, calls=%fused_computation.55 | loop fusion | bytes 196608 | tf_op jit(solution)/shard_map/slice | solution.py:41
  2.5 4.7 %collective-permute-start = (f32[3,1,8,4,128]{4,3,2,1,0:T(4,128)S(1)}, f32[3,1,8,4,128]{4,3,2,1,0:T(4,128)S(1)}, u32[]{:S(2)}, u32[]{:S(2)}) collective-permute-start(f32[3,1,8,4,128]{4,3,2,1,0:T(4,128)S(1)} %get-tuple-element.13), channel_id=1, source_target_pairs={{8,0},{16,8},{24,16},{0,24},{9,1},{17,9},{25,17},{1,25},{10,2},{18... | collective-permute-start | bytes 147464 | tf_op jit(solution)/shard_map/ppermute | solution.py:49
  7.1 0.0 collective-permute-start.1
  7.1 0.8 %fusion.9 = (f32[3,4,1,4,128]{4,3,2,1,0:T(4,128)S(1)}, f32[3,4,1,4,128]{4,3,2,1,0:T(4,128)S(1)}) fusion(f32[3,4,8,4,128]{4,3,2,1,0:T(4,128)} %param.3), kind=kLoop, calls=%fused_computation.56 | loop fusion | bytes 98304 | tf_op jit(solution)/shard_map/slice | solution.py:41
  7.9 2.4 %collective-permute-start.2 = (f32[3,4,1,4,128]{4,3,2,1,0:T(4,128)S(1)}, f32[3,4,1,4,128]{4,3,2,1,0:T(4,128)S(1)}, u32[]{:S(2)}, u32[]{:S(2)}) collective-permute-start(f32[3,4,1,4,128]{4,3,2,1,0:T(4,128)S(1)} %get-tuple-element.15), channel_id=1, source_target_pairs={{2,0},{4,2},{6,4},{0,6},{3,1},{5,3},{7,5},{1,7},{10,8},{12,10},{14... | collective-permute-start | bytes 73736 | tf_op jit(solution)/shard_map/ppermute | solution.py:49
  10.3 0.7 %broadcast_multiply_fusion = f32[4,8,4]{1,2,0:T(4,128)S(1)} fusion(f32[4,8,4]{1,2,0:T(4,128)} %param.4), kind=kLoop, calls=%fused_computation.51 | loop fusion | flops 128 | bytes 1024 | tf_op jit(solution)/shard_map/mul | solution.py:195
  11.0 0.1 copy.23
  11.1 0.1 mul.32
  11.2 0.8 %select_reduce_fusion = s32[32]{0:T(128)S(1)} fusion(s32[32]{0:T(128)} %param.5), kind=kLoop, calls=%fused_computation.35 | loop fusion | flops 3040 | bytes 256 | tf_op jit(solution)/shard_map/reduce_sum | solution.py:201
  12.0 1.0 %fusion.6 = f32[3,64,128]{1,2,0:T(8,128)S(1)} fusion(f32[3,128,128]{2,1,0:T(8,128)} %bitcast.20, f32[128]{0:T(128)S(1)} %mul.32), kind=kLoop, calls=%fused_computation.15 | loop fusion | flops 24576 | bytes 197120 | tf_op jit(solution)/shard_map/transpose | solution.py:196
  13.0 0.5 broadcast_clamp_fusion.slot_ref
  13.6 0.1 copy.24
  13.7 0.1 tile.4
  13.7 0.9 %tile.10.w_ref = f32[3,64,384]{2,1,0:T(8,128)} reshape(f32[3,64,3,128]{3,2,1,0:T(4,128)S(1)} %tile.4) | data formatting | bytes 589824 | tf_op jit(solution)/shard_map/tile | solution.py:196
  14.6 0.1 broadcast_select_fusion.1
  14.7 0.0 collective-permute-done.2
  14.7 0.4 collective-permute-done.3
  15.1 0.0 collective-permute-done
  15.1 0.0 collective-permute-done.1
  15.1 0.3 fusion.5
  15.4 1.1 %copy.25.g_ref = f32[3,128,384]{2,1,0:T(8,128)} copy(f32[3,128,384]{1,2,0:T(8,128)S(1)} %bitcast.22) | data formatting | bytes 1179648 | tf_op jit(solution)/shard_map/reshape | solution.py:197
  16.5 13.6 %shard_map.37 = f32[32,129,128]{2,1,0:T(8,128)} custom-call(s32[32]{0:T(128)} %broadcast_clamp_fusion.slot_ref, f32[3,64,384]{2,1,0:T(8,128)} %tile.10.w_ref, f32[3,128,384]{2,1,0:T(8,128)} %copy.25.g_ref, f32[384,128]{1,0:T(8,128)} %bitcast.21), custom_call_target="tpu_custom_call" | custom-call | tf_op jit(solution)/shard_map/pallas_call | solution.py:170
  30.1 1.9 %constant_dynamic-slice_fusion.12 = (f32[2,2,2,2,1,129,128]{6,5,4,3,2,1,0:T(8,128)S(1)}, f32[2,2,2,2,1,129,128]{6,5,4,3,2,1,0:T(8,128)S(1)}) fusion(f32[2,2,2,2,2,129,128]{6,5,4,3,2,1,0:T(8,128)} %bitcast.19, s32[]{:T(128)S(6)} %select_n.145, s32[]{:T(128)S(6)} %select_n.146), kind=kLoop, calls=%fused_computation.49 | loop fusion | bytes 4227080 | tf_op jit(solution)/shard_map/jit(dynamic_index_in_dim)/dynamic_slice | solution.py:75
  32.0 0.5 copy.31
  32.6 0.1 collective-permute-start.5
  32.7 2.6 %collective-permute-done.5 = f32[2,2,2,2,1,129,128]{6,3,5,4,2,1,0:T(2,128)S(1)} collective-permute-done((f32[2,2,2,2,1,129,128]{6,3,5,4,2,1,0:T(2,128)S(1)}, f32[2,2,2,2,1,129,128]{6,3,5,4,2,1,0:T(2,128)S(1)}, u32[]{:S(2)}, u32[]{:S(2)}) %collective-permute-start.5) | collective-permute-done | bytes 1056800 | tf_op jit(solution)/shard_map/ppermute | solution.py:77
  35.3 0.7 %copy_add_fusion = f32[2,2,2,2,1,129,128]{6,3,5,4,2,1,0:T(2,128)S(1)} fusion(f32[2,2,2,2,1,129,128]{6,3,5,4,2,1,0:T(2,128)S(1)} %collective-permute-done.5, f32[2,2,2,2,1,129,128]{6,5,4,3,2,1,0:T(8,128)S(1)} %get-tuple-element.5), kind=kLoop, calls=%fused_computation | loop fusion | flops 264192 | bytes 3170304 | tf_op jit(solution)/shard_map/add | solution.py:77
  36.0 0.1 fusion.7
  36.1 0.2 constant_dynamic-slice_fusion.10
  36.3 1.7 %collective-permute-start.6 = (f32[2,2,2,1,1,43,128]{6,3,5,4,2,1,0:T(1,128)S(1)}, f32[2,2,2,1,1,43,128]{6,3,5,4,2,1,0:T(1,128)S(1)}, u32[]{:S(2)}, u32[]{:S(2)}) collective-permute-start(f32[2,2,2,1,1,43,128]{6,3,5,4,2,1,0:T(1,128)S(1)} %constant_dynamic-slice_fusion.10), channel_id=1, source_target_pairs={{0,2},{2,0},{4,6},{6,4},{1,3},{3,1},{5,7},{7,5},{8,10},{10,8},{12,... | collective-permute-start | bytes 528392 | tf_op jit(solution)/shard_map/ppermute | solution.py:77
  38.0 1.6 %collective-permute-start.10 = (f32[2,2,1,2,1,43,128]{6,3,5,4,2,1,0:T(2,128)S(1)}, f32[2,2,1,2,1,43,128]{6,3,5,4,2,1,0:T(2,128)S(1)}, u32[]{:S(2)}, u32[]{:S(2)}) collective-permute-start(f32[2,2,1,2,1,43,128]{6,3,5,4,2,1,0:T(2,128)S(1)} %constant_dynamic-slice_fusion.6), channel_id=1, source_target_pairs={{0,4},{2,6},{4,0},{6,2},{1,5},{3,7},{5,1},{7,3},{8,12},{10,14},{12... | collective-permute-start | bytes 528392 | tf_op jit(solution)/shard_map/ppermute | solution.py:77
  39.6 0.1 collective-permute-start.14
  39.7 3.2 %collective-permute-done.6 = f32[2,2,2,1,1,43,128]{6,3,5,4,2,1,0:T(1,128)S(1)} collective-permute-done((f32[2,2,2,1,1,43,128]{6,3,5,4,2,1,0:T(1,128)S(1)}, f32[2,2,2,1,1,43,128]{6,3,5,4,2,1,0:T(1,128)S(1)}, u32[]{:S(2)}, u32[]{:S(2)}) %collective-permute-start.6) | collective-permute-done | bytes 176160 | tf_op jit(solution)/shard_map/ppermute | solution.py:77
  42.8 0.2 dynamic-slice_add_fusion.2
  43.1 1.5 %collective-permute-start.7 = (f32[2,2,1,1,1,43,128]{6,3,5,4,2,1,0:T(1,128)S(1)}, f32[2,2,1,1,1,43,128]{6,3,5,4,2,1,0:T(1,128)S(1)}, u32[]{:S(2)}, u32[]{:S(2)}) collective-permute-start(f32[2,2,1,1,1,43,128]{6,3,5,4,2,1,0:T(1,128)S(1)} %constant_dynamic-slice_fusion.9), channel_id=1, source_target_pairs={{0,4},{2,6},{4,0},{6,2},{1,5},{3,7},{5,1},{7,3},{8,12},{10,14},{12... | collective-permute-start | bytes 264200 | tf_op jit(solution)/shard_map/ppermute | solution.py:77
  44.6 0.0 collective-permute-done.10
  44.6 0.1 dynamic-slice_add_fusion.1
  44.7 0.1 collective-permute-start.11
  44.8 0.8 %collective-permute-done.14 = f32[2,1,2,2,1,43,128]{6,3,5,4,2,1,0:T(2,128)S(1)} collective-permute-done((f32[2,1,2,2,1,43,128]{6,3,5,4,2,1,0:T(2,128)S(1)}, f32[2,1,2,2,1,43,128]{6,3,5,4,2,1,0:T(2,128)S(1)}, u32[]{:S(2)}, u32[]{:S(2)}) %collective-permute-start.14) | collective-permute-done | bytes 176160 | tf_op jit(solution)/shard_map/ppermute | solution.py:77
  45.6 0.1 dynamic-slice_add_fusion
  45.7 0.1 constant_dynamic-slice_fusion.1
  45.8 1.0 %collective-permute-start.15 = (f32[2,1,2,1,1,43,128]{6,3,5,4,2,1,0:T(1,128)S(1)}, f32[2,1,2,1,1,43,128]{6,3,5,4,2,1,0:T(1,128)S(1)}, u32[]{:S(2)}, u32[]{:S(2)}) collective-permute-start(f32[2,1,2,1,1,43,128]{6,3,5,4,2,1,0:T(1,128)S(1)} %constant_dynamic-slice_fusion.1), channel_id=1, source_target_pairs={{0,2},{2,0},{4,6},{6,4},{1,3},{3,1},{5,7},{7,5},{8,10},{10,8},{12,... | collective-permute-start | bytes 264200 | tf_op jit(solution)/shard_map/ppermute | solution.py:77
  46.8 0.9 %collective-permute-done.7 = f32[2,2,1,1,1,43,128]{6,3,5,4,2,1,0:T(1,128)S(1)} collective-permute-done((f32[2,2,1,1,1,43,128]{6,3,5,4,2,1,0:T(1,128)S(1)}, f32[2,2,1,1,1,43,128]{6,3,5,4,2,1,0:T(1,128)S(1)}, u32[]{:S(2)}, u32[]{:S(2)}) %collective-permute-start.7) | collective-permute-done | bytes 88096 | tf_op jit(solution)/shard_map/ppermute | solution.py:77
  47.7 0.1 dynamic-slice_add_fusion.5
  47.8 1.2 %collective-permute-start.8 = (f32[2,1,1,1,1,43,128]{6,3,5,4,2,1,0:T(1,128)S(1)}, f32[2,1,1,1,1,43,128]{6,3,5,4,2,1,0:T(1,128)S(1)}, u32[]{:S(2)}, u32[]{:S(2)}) collective-permute-start(f32[2,1,1,1,1,43,128]{6,3,5,4,2,1,0:T(1,128)S(1)} %constant_dynamic-slice_fusion.8), channel_id=1, source_target_pairs={{0,8},{8,0},{16,24},{24,16},{1,9},{9,1},{17,25},{25,17},{2,10},{10... | collective-permute-start | bytes 132104 | tf_op jit(solution)/shard_map/ppermute | solution.py:77
  49.0 0.8 %collective-permute-done.11 = f32[2,1,1,2,1,43,128]{6,3,5,4,2,1,0:T(2,128)S(1)} collective-permute-done((f32[2,1,1,2,1,43,128]{6,3,5,4,2,1,0:T(2,128)S(1)}, f32[2,1,1,2,1,43,128]{6,3,5,4,2,1,0:T(2,128)S(1)}, u32[]{:S(2)}, u32[]{:S(2)}) %collective-permute-start.11) | collective-permute-done | bytes 88096 | tf_op jit(solution)/shard_map/ppermute | solution.py:77
  49.9 1.8 %collective-permute-start.12 = (f32[2,1,1,1,1,43,128]{6,3,5,4,2,1,0:T(1,128)S(1)}, f32[2,1,1,1,1,43,128]{6,3,5,4,2,1,0:T(1,128)S(1)}, u32[]{:S(2)}, u32[]{:S(2)}) collective-permute-start(f32[2,1,1,1,1,43,128]{6,3,5,4,2,1,0:T(1,128)S(1)} %constant_dynamic-slice_fusion.4), channel_id=1, source_target_pairs={{0,2},{2,0},{4,6},{6,4},{1,3},{3,1},{5,7},{7,5},{8,10},{10,8},{12,... | collective-permute-start | bytes 132104 | tf_op jit(solution)/shard_map/ppermute | solution.py:77
  51.7 0.0 collective-permute-done.15
  51.7 0.1 dynamic-slice_add_fusion.3
  51.8 0.1 collective-permute-start.16
  52.0 4.0 %collective-permute-start.9 = (f32[1,1,1,1,1,43,128]{6,3,5,4,2,1,0:T(1,128)S(1)}, f32[1,1,1,1,1,43,128]{6,3,5,4,2,1,0:T(1,128)S(1)}, u32[]{:S(2)}, u32[]{:S(2)}) collective-permute-start(f32[1,1,1,1,1,43,128]{6,3,5,4,2,1,0:T(1,128)S(1)} %constant_dynamic-slice_fusion.7), channel_id=1, source_target_pairs={{0,16},{8,24},{16,0},{24,8},{1,17},{9,25},{17,1},{25,9},{2,18},{10... | collective-permute-start | bytes 66056 | tf_op jit(solution)/shard_map/ppermute | solution.py:77
  56.0 0.0 collective-permute-done.12
  56.0 0.1 dynamic-slice_add_fusion.7
  56.1 0.5 collective-permute-start.13
  56.7 2.5 %collective-permute-start.17 = (f32[1,1,1,1,1,43,128]{6,3,5,4,2,1,0:T(1,128)S(1)}, f32[1,1,1,1,1,43,128]{6,3,5,4,2,1,0:T(1,128)S(1)}, u32[]{:S(2)}, u32[]{:S(2)}) collective-permute-start(f32[1,1,1,1,1,43,128]{6,3,5,4,2,1,0:T(1,128)S(1)} %constant_dynamic-slice_fusion.13), channel_id=1, source_target_pairs={{0,16},{8,24},{16,0},{24,8},{1,17},{9,25},{17,1},{25,9},{2,18},{10... | collective-permute-start | bytes 66056 | tf_op jit(solution)/shard_map/ppermute | solution.py:77
  59.2 0.0 collective-permute-done.9
  59.2 2.2 %collective-permute-done.17 = f32[1,1,1,1,1,43,128]{6,3,5,4,2,1,0:T(1,128)S(1)} collective-permute-done((f32[1,1,1,1,1,43,128]{6,3,5,4,2,1,0:T(1,128)S(1)}, f32[1,1,1,1,1,43,128]{6,3,5,4,2,1,0:T(1,128)S(1)}, u32[]{:S(2)}, u32[]{:S(2)}) %collective-permute-start.17) | collective-permute-done | bytes 22048 | tf_op jit(solution)/shard_map/ppermute | solution.py:77
  61.5 0.0 collective-permute-done.13
  61.5 0.1 pad_maximum_fusion.8
  61.6 0.1 reshape_squeeze.3
  61.7 0.1 copy.29
  61.8 0.6 %pad_maximum_fusion.7 = f32[64,258]{1,0:T(8,128)} fusion(f32[64,2]{1,0:T(8,128)S(1)} %copy.29, f32[64,256]{1,0:T(8,128)S(1)} %bitcast.26), kind=kLoop, calls=%fused_computation.19 | loop fusion | flops 16512 | bytes 132096 | tf_op jit(solution)/shard_map/concatenate | solution.py:210
  (25 shorter events, 0.5 us)
Async XLA Ops:
  1.1 13.5 %collective-permute-start.4 = (f32[3,4,8,1,128]{4,3,2,1,0:T(1,128)S(1)}, f32[3,4,8,1,128]{4,3,2,1,0:T(1,128)S(1)}, u32[]{:S(2)}, u32[]{:S(2)}) collective-permute-start(f32[3,4,8,1,128]{4,3,2,1,0:T(1,128)S(1)} %broadcast_select_fusion.2), channel_id=1, source_target_pairs={{0,1},{1,0},{2,3},{3,2},{4,5},{5,4},{6,7},{7,6},{8,9},{9,8},{10,11... | collective-permute-start | bytes 147464 | tf_op jit(solution)/shard_map/ppermute | solution.py:44
  2.5 12.6 %copy-start = (f32[3,4,8,4,128]{4,3,2,1,0:T(4,128)S(1)}, f32[3,4,8,4,128]{4,3,2,1,0:T(4,128)}, u32[]{:S(2)}) copy-start(f32[3,4,8,4,128]{4,3,2,1,0:T(4,128)} %param.3) | copy-start | bytes 589828
  2.5 12.6 %collective-permute-start = (f32[3,1,8,4,128]{4,3,2,1,0:T(4,128)S(1)}, f32[3,1,8,4,128]{4,3,2,1,0:T(4,128)S(1)}, u32[]{:S(2)}, u32[]{:S(2)}) collective-permute-start(f32[3,1,8,4,128]{4,3,2,1,0:T(4,128)S(1)} %get-tuple-element.13), channel_id=1, source_target_pairs={{8,0},{16,8},{24,16},{0,24},{9,1},{17,9},{25,17},{1,25},{10,2},{18... | collective-permute-start | bytes 147464 | tf_op jit(solution)/shard_map/ppermute | solution.py:49
  7.1 7.9 %collective-permute-start.1 = (f32[3,1,8,4,128]{4,3,2,1,0:T(4,128)S(1)}, f32[3,1,8,4,128]{4,3,2,1,0:T(4,128)S(1)}, u32[]{:S(2)}, u32[]{:S(2)}) collective-permute-start(f32[3,1,8,4,128]{4,3,2,1,0:T(4,128)S(1)} %get-tuple-element.14), channel_id=1, source_target_pairs={{0,8},{8,16},{16,24},{24,0},{1,9},{9,17},{17,25},{25,1},{2,10},{10... | collective-permute-start | bytes 147464 | tf_op jit(solution)/shard_map/ppermute | solution.py:48
  7.9 6.8 %collective-permute-start.2 = (f32[3,4,1,4,128]{4,3,2,1,0:T(4,128)S(1)}, f32[3,4,1,4,128]{4,3,2,1,0:T(4,128)S(1)}, u32[]{:S(2)}, u32[]{:S(2)}) collective-permute-start(f32[3,4,1,4,128]{4,3,2,1,0:T(4,128)S(1)} %get-tuple-element.15), channel_id=1, source_target_pairs={{2,0},{4,2},{6,4},{0,6},{3,1},{5,3},{7,5},{1,7},{10,8},{12,10},{14... | collective-permute-start | bytes 73736 | tf_op jit(solution)/shard_map/ppermute | solution.py:49
  10.3 4.7 %collective-permute-start.3 = (f32[3,4,1,4,128]{4,3,2,1,0:T(4,128)S(1)}, f32[3,4,1,4,128]{4,3,2,1,0:T(4,128)S(1)}, u32[]{:S(2)}, u32[]{:S(2)}) collective-permute-start(f32[3,4,1,4,128]{4,3,2,1,0:T(4,128)S(1)} %get-tuple-element.16), channel_id=1, source_target_pairs={{0,2},{2,4},{4,6},{6,0},{1,3},{3,5},{5,7},{7,1},{8,10},{10,12},{12... | collective-permute-start | bytes 73736 | tf_op jit(solution)/shard_map/ppermute | solution.py:48
  32.6 2.7 %collective-permute-start.5 = (f32[2,2,2,2,1,129,128]{6,3,5,4,2,1,0:T(2,128)S(1)}, f32[2,2,2,2,1,129,128]{6,3,5,4,2,1,0:T(2,128)S(1)}, u32[]{:S(2)}, u32[]{:S(2)}) collective-permute-start(f32[2,2,2,2,1,129,128]{6,3,5,4,2,1,0:T(2,128)S(1)} %copy.31), channel_id=1, source_target_pairs={{0,1},{1,0},{2,3},{3,2},{4,5},{5,4},{6,7},{7,6},{8,9},{9,8},{10,11... | collective-permute-start | bytes 3170312 | tf_op jit(solution)/shard_map/ppermute | solution.py:77
  36.3 6.6 %collective-permute-start.6 = (f32[2,2,2,1,1,43,128]{6,3,5,4,2,1,0:T(1,128)S(1)}, f32[2,2,2,1,1,43,128]{6,3,5,4,2,1,0:T(1,128)S(1)}, u32[]{:S(2)}, u32[]{:S(2)}) collective-permute-start(f32[2,2,2,1,1,43,128]{6,3,5,4,2,1,0:T(1,128)S(1)} %constant_dynamic-slice_fusion.10), channel_id=1, source_target_pairs={{0,2},{2,0},{4,6},{6,4},{1,3},{3,1},{5,7},{7,5},{8,10},{10,8},{12,... | collective-permute-start | bytes 528392 | tf_op jit(solution)/shard_map/ppermute | solution.py:77
  38.0 6.6 %collective-permute-start.10 = (f32[2,2,1,2,1,43,128]{6,3,5,4,2,1,0:T(2,128)S(1)}, f32[2,2,1,2,1,43,128]{6,3,5,4,2,1,0:T(2,128)S(1)}, u32[]{:S(2)}, u32[]{:S(2)}) collective-permute-start(f32[2,2,1,2,1,43,128]{6,3,5,4,2,1,0:T(2,128)S(1)} %constant_dynamic-slice_fusion.6), channel_id=1, source_target_pairs={{0,4},{2,6},{4,0},{6,2},{1,5},{3,7},{5,1},{7,3},{8,12},{10,14},{12... | collective-permute-start | bytes 528392 | tf_op jit(solution)/shard_map/ppermute | solution.py:77
  39.6 6.0 %collective-permute-start.14 = (f32[2,1,2,2,1,43,128]{6,3,5,4,2,1,0:T(2,128)S(1)}, f32[2,1,2,2,1,43,128]{6,3,5,4,2,1,0:T(2,128)S(1)}, u32[]{:S(2)}, u32[]{:S(2)}) collective-permute-start(f32[2,1,2,2,1,43,128]{6,3,5,4,2,1,0:T(2,128)S(1)} %constant_dynamic-slice_fusion.2), channel_id=1, source_target_pairs={{0,8},{8,0},{16,24},{24,16},{1,9},{9,1},{17,25},{25,17},{2,10},{10... | collective-permute-start | bytes 528392 | tf_op jit(solution)/shard_map/ppermute | solution.py:77
  43.1 4.6 %collective-permute-start.7 = (f32[2,2,1,1,1,43,128]{6,3,5,4,2,1,0:T(1,128)S(1)}, f32[2,2,1,1,1,43,128]{6,3,5,4,2,1,0:T(1,128)S(1)}, u32[]{:S(2)}, u32[]{:S(2)}) collective-permute-start(f32[2,2,1,1,1,43,128]{6,3,5,4,2,1,0:T(1,128)S(1)} %constant_dynamic-slice_fusion.9), channel_id=1, source_target_pairs={{0,4},{2,6},{4,0},{6,2},{1,5},{3,7},{5,1},{7,3},{8,12},{10,14},{12... | collective-permute-start | bytes 264200 | tf_op jit(solution)/shard_map/ppermute | solution.py:77
  44.7 5.0 %collective-permute-start.11 = (f32[2,1,1,2,1,43,128]{6,3,5,4,2,1,0:T(2,128)S(1)}, f32[2,1,1,2,1,43,128]{6,3,5,4,2,1,0:T(2,128)S(1)}, u32[]{:S(2)}, u32[]{:S(2)}) collective-permute-start(f32[2,1,1,2,1,43,128]{6,3,5,4,2,1,0:T(2,128)S(1)} %constant_dynamic-slice_fusion.5), channel_id=1, source_target_pairs={{0,8},{8,0},{16,24},{24,16},{1,9},{9,1},{17,25},{25,17},{2,10},{10... | collective-permute-start | bytes 264200 | tf_op jit(solution)/shard_map/ppermute | solution.py:77
  45.8 5.9 %collective-permute-start.15 = (f32[2,1,2,1,1,43,128]{6,3,5,4,2,1,0:T(1,128)S(1)}, f32[2,1,2,1,1,43,128]{6,3,5,4,2,1,0:T(1,128)S(1)}, u32[]{:S(2)}, u32[]{:S(2)}) collective-permute-start(f32[2,1,2,1,1,43,128]{6,3,5,4,2,1,0:T(1,128)S(1)} %constant_dynamic-slice_fusion.1), channel_id=1, source_target_pairs={{0,2},{2,0},{4,6},{6,4},{1,3},{3,1},{5,7},{7,5},{8,10},{10,8},{12,... | collective-permute-start | bytes 264200 | tf_op jit(solution)/shard_map/ppermute | solution.py:77
  47.8 4.1 %collective-permute-start.8 = (f32[2,1,1,1,1,43,128]{6,3,5,4,2,1,0:T(1,128)S(1)}, f32[2,1,1,1,1,43,128]{6,3,5,4,2,1,0:T(1,128)S(1)}, u32[]{:S(2)}, u32[]{:S(2)}) collective-permute-start(f32[2,1,1,1,1,43,128]{6,3,5,4,2,1,0:T(1,128)S(1)} %constant_dynamic-slice_fusion.8), channel_id=1, source_target_pairs={{0,8},{8,0},{16,24},{24,16},{1,9},{9,1},{17,25},{25,17},{2,10},{10... | collective-permute-start | bytes 132104 | tf_op jit(solution)/shard_map/ppermute | solution.py:77
  49.9 6.1 %collective-permute-start.12 = (f32[2,1,1,1,1,43,128]{6,3,5,4,2,1,0:T(1,128)S(1)}, f32[2,1,1,1,1,43,128]{6,3,5,4,2,1,0:T(1,128)S(1)}, u32[]{:S(2)}, u32[]{:S(2)}) collective-permute-start(f32[2,1,1,1,1,43,128]{6,3,5,4,2,1,0:T(1,128)S(1)} %constant_dynamic-slice_fusion.4), channel_id=1, source_target_pairs={{0,2},{2,0},{4,6},{6,4},{1,3},{3,1},{5,7},{7,5},{8,10},{10,8},{12,... | collective-permute-start | bytes 132104 | tf_op jit(solution)/shard_map/ppermute | solution.py:77
  51.8 4.8 %collective-permute-start.16 = (f32[2,1,1,1,1,43,128]{6,3,5,4,2,1,0:T(1,128)S(1)}, f32[2,1,1,1,1,43,128]{6,3,5,4,2,1,0:T(1,128)S(1)}, u32[]{:S(2)}, u32[]{:S(2)}) collective-permute-start(f32[2,1,1,1,1,43,128]{6,3,5,4,2,1,0:T(1,128)S(1)} %constant_dynamic-slice_fusion), channel_id=1, source_target_pairs={{0,4},{2,6},{4,0},{6,2},{1,5},{3,7},{5,1},{7,3},{8,12},{10,14},{12... | collective-permute-start | bytes 132104 | tf_op jit(solution)/shard_map/ppermute | solution.py:77
  52.0 7.2 %collective-permute-start.9 = (f32[1,1,1,1,1,43,128]{6,3,5,4,2,1,0:T(1,128)S(1)}, f32[1,1,1,1,1,43,128]{6,3,5,4,2,1,0:T(1,128)S(1)}, u32[]{:S(2)}, u32[]{:S(2)}) collective-permute-start(f32[1,1,1,1,1,43,128]{6,3,5,4,2,1,0:T(1,128)S(1)} %constant_dynamic-slice_fusion.7), channel_id=1, source_target_pairs={{0,16},{8,24},{16,0},{24,8},{1,17},{9,25},{17,1},{25,9},{2,18},{10... | collective-permute-start | bytes 66056 | tf_op jit(solution)/shard_map/ppermute | solution.py:77
  56.1 5.4 %collective-permute-start.13 = (f32[1,1,1,1,1,43,128]{6,3,5,4,2,1,0:T(1,128)S(1)}, f32[1,1,1,1,1,43,128]{6,3,5,4,2,1,0:T(1,128)S(1)}, u32[]{:S(2)}, u32[]{:S(2)}) collective-permute-start(f32[1,1,1,1,1,43,128]{6,3,5,4,2,1,0:T(1,128)S(1)} %constant_dynamic-slice_fusion.3), channel_id=1, source_target_pairs={{0,16},{8,24},{16,0},{24,8},{1,17},{9,25},{17,1},{25,9},{2,18},{10... | collective-permute-start | bytes 66056 | tf_op jit(solution)/shard_map/ppermute | solution.py:77
  56.7 4.8 %collective-permute-start.17 = (f32[1,1,1,1,1,43,128]{6,3,5,4,2,1,0:T(1,128)S(1)}, f32[1,1,1,1,1,43,128]{6,3,5,4,2,1,0:T(1,128)S(1)}, u32[]{:S(2)}, u32[]{:S(2)}) collective-permute-start(f32[1,1,1,1,1,43,128]{6,3,5,4,2,1,0:T(1,128)S(1)} %constant_dynamic-slice_fusion.13), channel_id=1, source_target_pairs={{0,16},{8,24},{16,0},{24,8},{1,17},{9,25},{17,1},{25,9},{2,18},{10... | collective-permute-start | bytes 66056 | tf_op jit(solution)/shard_map/ppermute | solution.py:77

commit v17 on v15

--- a/solution.py
+++ b/solution.py
@@ -103,8 +103,12 @@
     return value.reshape(1, rows, lanes)
 
 
-def triangle_kernel(block_len, dense, slot_ref, w_ref, g_ref, m_ref, out_ref, sym_ref, rest_ref):
+def triangle_kernel(block_len, dense, slot_ref, w_ref, grad_ref, m_ref, out_ref, sym_ref, rest_ref, g_ref):
     test, width = w_ref.shape[1], m_ref.shape[1]
+    cells = grad_ref.shape[2]
+    for a in range(3):
+        for b in range(3):
+            g_ref[a, :, pl.ds(b * cells, cells)] = grad_ref[a, b].T
     group = 32
     full = block_len // 128 if dense else out_ref.shape[2] // 128
     out_ref[...] = jnp.zeros(out_ref.shape, out_ref.dtype)
@@ -175,6 +179,7 @@
         scratch_shapes=[
             pltpu.VMEM((test * width, width), jnp.float32),
             pltpu.VMEM((owners if dense else 1, test, 128), jnp.float32),
+            pltpu.VMEM((3, width, 3 * grads.shape[2]), jnp.float32),
         ],
     )(slots, weighted, grads, modes_flat)
 
@@ -194,7 +199,6 @@
     cells = mode_flat.shape[1]
     weighted = mode_flat[:, :, :TEST] * (weight_flat * scale)[None, :, None]
     weighted = jnp.tile(jnp.swapaxes(weighted, 1, 2), (1, 1, 3))
-    grads_t = grad_flat.transpose(0, 3, 1, 2).reshape(3, width, 3 * cells)
     pair_total = width * (width + 1) // 2
     block_len = (pair_total + owners - 1) // owners
     ranks = jnp.arange(owners, dtype=jnp.int32)
@@ -202,7 +206,7 @@
     slots = jnp.clip(slots, 0, owners - 1).astype(jnp.int32)
     full, spare = block_len // 128, block_len % 128
     dense = 0 < spare and spare * TEST <= 128
-    placed = triangle(slots, weighted, grads_t, mode_flat.reshape(3 * cells, width), block_len, dense)
+    placed = triangle(slots, weighted, grad_flat, mode_flat.reshape(3 * cells, width), block_len, dense)
     if dense:
         owned = scatter_sum(placed, ("gx", "gy", "gz"))[0]
         main = owned[: full * TEST].reshape(full, TEST, 128).transpose(1, 0, 2).reshape(TEST, full * 128)

time: 62 us -> 61.9 us (level)
  local copies, waits for them, and re-layouts: 6.9 us -> 5.83 us
  other arithmetic: 6.83 us -> 7.67 us
    reshape x1 -> x0, local copies, waits for them, and re-layouts: 1.07 us -> none  [shards(): grads_t = grad_flat.transpose(0, 3, 1, 2).reshape(3, width, 3 * cells)]
    another operation x1, other arithmetic: 0.04 us -> 0.88 us  [face_gradients(): return jnp.stack(steps, axis=1)]
  transfers between devices with their start and end apart: 18 -> 18, of which waited for: 7 -> 7; matrix products, arithmetic and copies ran while one was open for 11% -> 12% of each run, Pallas kernels for 0% -> 0%
where the time goes in v17:
time: 61.9 us; the launch traced here: 61.5 us
  starting transfers between devices  23.8 us (38%)
  Pallas kernels  13.1 us (21%)
  waiting for transfers between devices  10.8 us (17%)
  other arithmetic  7.67 us (12%)
  local copies, waits for them, and re-layouts  5.83 us (9%)
    ppermute x13, starting transfers between devices, halve(): return keep + lax.ppermute(other, axis, pairs)  16.1 us
    pallas_call x1, Pallas kernels, triangle(): pl.pallas_call(functools.partial(triangle_kernel, block_len, dense), out_...  13.1 us
    ppermute x13, waiting for transfers between devices, halve(): return keep + lax.ppermute(other, axis, pairs)  10.4 us
    ppermute x2, starting transfers between devices, face_gradients(): after = lax.ppermute(leading, axis, down)  7.12 us
    dynamic_slice x1, local copies, waits for them, and re-layouts, halve(): keep = lax.dynamic_index_in_dim(value, mine, dim, keepdims=True)  1.73 us
    add x13, other arithmetic, halve(): return keep + lax.ppermute(other, axis, pairs)  1.64 us
    slice x2, local copies, waits for them, and re-layouts, face_gradients(): leading = lax.slice_in_dim(value, 0, 1, axis=dim)  1.59 us
  transfers between devices with their start and end apart: 18, of which 7 were waited for; matrix products, arithmetic and copies ran while one was open for 12% of the time, Pallas kernels for 0%

profile of v17, /device:TPU:0, one launch (start us, length us, event | category | flops | bytes accessed | tf_op | source)
XLA Modules:
  0.0 61.5 jit_solution(953800933219880621)
XLA Ops:
  0.0 1.1 %broadcast_select_fusion.2 = f32[3,4,8,1,128]{4,3,2,1,0:T(1,128)S(1)} fusion(pred[]{:T(512)S(6)} %eq.37, f32[3,4,8,4,128]{4,3,2,1,0:T(4,128)} %param.3), kind=kLoop, calls=%fused_computation.22 | loop fusion | flops 12288 | bytes 147457 | tf_op jit(solution)/shard_map/jit(_where)/select_n | solution.py:44
  1.1 0.5 collective-permute-start.4
  1.6 0.8 %fusion.8 = (f32[3,1,8,4,128]{4,3,2,1,0:T(4,128)S(1)}, f32[3,1,8,4,128]{4,3,2,1,0:T(4,128)S(1)}) fusion(f32[3,4,8,4,128]{4,3,2,1,0:T(4,128)} %param.3), kind=kLoop, calls=%fused_computation.55 | loop fusion | bytes 196608 | tf_op jit(solution)/shard_map/slice | solution.py:41
  2.5 4.7 %collective-permute-start = (f32[3,1,8,4,128]{4,3,2,1,0:T(4,128)S(1)}, f32[3,1,8,4,128]{4,3,2,1,0:T(4,128)S(1)}, u32[]{:S(2)}, u32[]{:S(2)}) collective-permute-start(f32[3,1,8,4,128]{4,3,2,1,0:T(4,128)S(1)} %get-tuple-element.13), channel_id=1, source_target_pairs={{8,0},{16,8},{24,16},{0,24},{9,1},{17,9},{25,17},{1,25},{10,2},{18... | collective-permute-start | bytes 147464 | tf_op jit(solution)/shard_map/ppermute | solution.py:49
  7.1 0.0 collective-permute-start.1
  7.1 0.8 %fusion.9 = (f32[3,4,1,4,128]{4,3,2,1,0:T(4,128)S(1)}, f32[3,4,1,4,128]{4,3,2,1,0:T(4,128)S(1)}) fusion(f32[3,4,8,4,128]{4,3,2,1,0:T(4,128)} %param.3), kind=kLoop, calls=%fused_computation.56 | loop fusion | bytes 98304 | tf_op jit(solution)/shard_map/slice | solution.py:41
  7.9 2.4 %collective-permute-start.2 = (f32[3,4,1,4,128]{4,3,2,1,0:T(4,128)S(1)}, f32[3,4,1,4,128]{4,3,2,1,0:T(4,128)S(1)}, u32[]{:S(2)}, u32[]{:S(2)}) collective-permute-start(f32[3,4,1,4,128]{4,3,2,1,0:T(4,128)S(1)} %get-tuple-element.15), channel_id=1, source_target_pairs={{2,0},{4,2},{6,4},{0,6},{3,1},{5,3},{7,5},{1,7},{10,8},{12,10},{14... | collective-permute-start | bytes 73736 | tf_op jit(solution)/shard_map/ppermute | solution.py:49
  10.3 0.0 collective-permute-start.3
  10.3 0.7 %broadcast_multiply_fusion = f32[4,8,4]{1,2,0:T(4,128)S(1)} fusion(f32[4,8,4]{1,2,0:T(4,128)} %param.4), kind=kLoop, calls=%fused_computation.51 | loop fusion | flops 128 | bytes 1024 | tf_op jit(solution)/shard_map/mul | solution.py:200
  11.0 0.1 copy.18
  11.1 0.1 mul.32
  11.2 0.8 %select_reduce_fusion = s32[32]{0:T(128)S(1)} fusion(s32[32]{0:T(128)} %param.5), kind=kLoop, calls=%fused_computation.35 | loop fusion | flops 3040 | bytes 256 | tf_op jit(solution)/shard_map/reduce_sum | solution.py:205
  12.0 1.0 %fusion.6 = f32[3,64,128]{1,2,0:T(8,128)S(1)} fusion(f32[3,128,128]{2,1,0:T(8,128)} %bitcast.17, f32[128]{0:T(128)S(1)} %mul.32), kind=kLoop, calls=%fused_computation.15 | loop fusion | flops 24576 | bytes 197120 | tf_op jit(solution)/shard_map/transpose | solution.py:201
  13.0 0.5 broadcast_clamp_fusion.slot_ref
  13.6 0.1 copy.19
  13.7 0.1 tile.4
  13.7 0.9 %tile.10.w_ref = f32[3,64,384]{2,1,0:T(8,128)} reshape(f32[3,64,3,128]{3,2,1,0:T(4,128)S(1)} %tile.4) | data formatting | bytes 589824 | tf_op jit(solution)/shard_map/tile | solution.py:201
  14.6 0.0 collective-permute-done.4
  14.6 0.1 broadcast_select_fusion.1
  14.7 0.0 collective-permute-done.2
  14.7 0.4 collective-permute-done.3
  15.1 0.0 collective-permute-done
  15.1 0.0 collective-permute-done.1
  15.1 0.3 fusion.5
  15.4 0.9 %pad_maximum_fusion.grad_ref = f32[3,3,128,128]{3,2,1,0:T(8,128)} fusion(f32[3,1,128,128]{3,2,1,0:T(8,128)S(1)} %bitcast.21, f32[3,1,128,128]{3,2,1,0:T(8,128)S(1)} %bitcast.20, f32[3,1,128,128]{3,2,1,0:T(8,128)S(1)} %bitcast.19), kind=kLoop, calls=%fused_computation.1 | loop fusion | flops 294912 | bytes 1179648 | tf_op jit(solution)/shard_map/stack | solution.py:58
  16.2 13.1 %shard_map.37 = f32[32,129,128]{2,1,0:T(8,128)} custom-call(s32[32]{0:T(128)} %broadcast_clamp_fusion.slot_ref, f32[3,64,384]{2,1,0:T(8,128)} %tile.10.w_ref, f32[3,3,128,128]{3,2,1,0:T(8,128)} %pad_maximum_fusion.grad_ref, f32[384,128]{1,0:T(8,128)} %bitcast.18), custom_call_target="tpu_custom_call" | custom-call | tf_op jit(solution)/shard_map/pallas_call | solution.py:174
  29.3 1.7 %constant_dynamic-slice_fusion.12 = (f32[2,2,2,2,1,129,128]{6,5,4,3,2,1,0:T(8,128)S(1)}, f32[2,2,2,2,1,129,128]{6,5,4,3,2,1,0:T(8,128)S(1)}) fusion(f32[2,2,2,2,2,129,128]{6,5,4,3,2,1,0:T(8,128)} %bitcast.16, s32[]{:T(128)S(6)} %select_n.145, s32[]{:T(128)S(6)} %select_n.146), kind=kLoop, calls=%fused_computation.49 | loop fusion | bytes 4227080 | tf_op jit(solution)/shard_map/jit(dynamic_index_in_dim)/dynamic_slice | solution.py:75
  31.1 0.5 copy.25
  31.6 0.1 collective-permute-start.5
  31.8 2.6 %collective-permute-done.5 = f32[2,2,2,2,1,129,128]{6,3,5,4,2,1,0:T(2,128)S(1)} collective-permute-done((f32[2,2,2,2,1,129,128]{6,3,5,4,2,1,0:T(2,128)S(1)}, f32[2,2,2,2,1,129,128]{6,3,5,4,2,1,0:T(2,128)S(1)}, u32[]{:S(2)}, u32[]{:S(2)}) %collective-permute-start.5) | collective-permute-done | bytes 1056800 | tf_op jit(solution)/shard_map/ppermute | solution.py:77
  34.4 0.7 %copy_add_fusion = f32[2,2,2,2,1,129,128]{6,3,5,4,2,1,0:T(2,128)S(1)} fusion(f32[2,2,2,2,1,129,128]{6,3,5,4,2,1,0:T(2,128)S(1)} %collective-permute-done.5, f32[2,2,2,2,1,129,128]{6,5,4,3,2,1,0:T(8,128)S(1)} %get-tuple-element.5), kind=kLoop, calls=%fused_computation | loop fusion | flops 264192 | bytes 3170304 | tf_op jit(solution)/shard_map/add | solution.py:77
  35.1 0.1 fusion.7
  35.2 0.2 constant_dynamic-slice_fusion.10
  35.3 1.7 %collective-permute-start.6 = (f32[2,2,2,1,1,43,128]{6,3,5,4,2,1,0:T(1,128)S(1)}, f32[2,2,2,1,1,43,128]{6,3,5,4,2,1,0:T(1,128)S(1)}, u32[]{:S(2)}, u32[]{:S(2)}) collective-permute-start(f32[2,2,2,1,1,43,128]{6,3,5,4,2,1,0:T(1,128)S(1)} %constant_dynamic-slice_fusion.10), channel_id=1, source_target_pairs={{0,2},{2,0},{4,6},{6,4},{1,3},{3,1},{5,7},{7,5},{8,10},{10,8},{12,... | collective-permute-start | bytes 528392 | tf_op jit(solution)/shard_map/ppermute | solution.py:77
  37.1 1.6 %collective-permute-start.10 = (f32[2,2,1,2,1,43,128]{6,3,5,4,2,1,0:T(2,128)S(1)}, f32[2,2,1,2,1,43,128]{6,3,5,4,2,1,0:T(2,128)S(1)}, u32[]{:S(2)}, u32[]{:S(2)}) collective-permute-start(f32[2,2,1,2,1,43,128]{6,3,5,4,2,1,0:T(2,128)S(1)} %constant_dynamic-slice_fusion.6), channel_id=1, source_target_pairs={{0,4},{2,6},{4,0},{6,2},{1,5},{3,7},{5,1},{7,3},{8,12},{10,14},{12... | collective-permute-start | bytes 528392 | tf_op jit(solution)/shard_map/ppermute | solution.py:77
  38.7 0.1 collective-permute-start.14
  38.8 3.2 %collective-permute-done.6 = f32[2,2,2,1,1,43,128]{6,3,5,4,2,1,0:T(1,128)S(1)} collective-permute-done((f32[2,2,2,1,1,43,128]{6,3,5,4,2,1,0:T(1,128)S(1)}, f32[2,2,2,1,1,43,128]{6,3,5,4,2,1,0:T(1,128)S(1)}, u32[]{:S(2)}, u32[]{:S(2)}) %collective-permute-start.6) | collective-permute-done | bytes 176160 | tf_op jit(solution)/shard_map/ppermute | solution.py:77
  41.9 0.2 dynamic-slice_add_fusion.2
  42.2 1.5 %collective-permute-start.7 = (f32[2,2,1,1,1,43,128]{6,3,5,4,2,1,0:T(1,128)S(1)}, f32[2,2,1,1,1,43,128]{6,3,5,4,2,1,0:T(1,128)S(1)}, u32[]{:S(2)}, u32[]{:S(2)}) collective-permute-start(f32[2,2,1,1,1,43,128]{6,3,5,4,2,1,0:T(1,128)S(1)} %constant_dynamic-slice_fusion.9), channel_id=1, source_target_pairs={{0,4},{2,6},{4,0},{6,2},{1,5},{3,7},{5,1},{7,3},{8,12},{10,14},{12... | collective-permute-start | bytes 264200 | tf_op jit(solution)/shard_map/ppermute | solution.py:77
  43.7 0.0 collective-permute-done.10
  43.7 0.1 dynamic-slice_add_fusion.1
  43.8 0.1 collective-permute-start.11
  43.9 0.8 %collective-permute-done.14 = f32[2,1,2,2,1,43,128]{6,3,5,4,2,1,0:T(2,128)S(1)} collective-permute-done((f32[2,1,2,2,1,43,128]{6,3,5,4,2,1,0:T(2,128)S(1)}, f32[2,1,2,2,1,43,128]{6,3,5,4,2,1,0:T(2,128)S(1)}, u32[]{:S(2)}, u32[]{:S(2)}) %collective-permute-start.14) | collective-permute-done | bytes 176160 | tf_op jit(solution)/shard_map/ppermute | solution.py:77
  44.7 0.1 dynamic-slice_add_fusion
  44.8 0.1 constant_dynamic-slice_fusion.1
  44.9 1.0 %collective-permute-start.15 = (f32[2,1,2,1,1,43,128]{6,3,5,4,2,1,0:T(1,128)S(1)}, f32[2,1,2,1,1,43,128]{6,3,5,4,2,1,0:T(1,128)S(1)}, u32[]{:S(2)}, u32[]{:S(2)}) collective-permute-start(f32[2,1,2,1,1,43,128]{6,3,5,4,2,1,0:T(1,128)S(1)} %constant_dynamic-slice_fusion.1), channel_id=1, source_target_pairs={{0,2},{2,0},{4,6},{6,4},{1,3},{3,1},{5,7},{7,5},{8,10},{10,8},{12,... | collective-permute-start | bytes 264200 | tf_op jit(solution)/shard_map/ppermute | solution.py:77
  45.9 0.9 %collective-permute-done.7 = f32[2,2,1,1,1,43,128]{6,3,5,4,2,1,0:T(1,128)S(1)} collective-permute-done((f32[2,2,1,1,1,43,128]{6,3,5,4,2,1,0:T(1,128)S(1)}, f32[2,2,1,1,1,43,128]{6,3,5,4,2,1,0:T(1,128)S(1)}, u32[]{:S(2)}, u32[]{:S(2)}) %collective-permute-start.7) | collective-permute-done | bytes 88096 | tf_op jit(solution)/shard_map/ppermute | solution.py:77
  46.7 0.1 dynamic-slice_add_fusion.5
  46.9 1.2 %collective-permute-start.8 = (f32[2,1,1,1,1,43,128]{6,3,5,4,2,1,0:T(1,128)S(1)}, f32[2,1,1,1,1,43,128]{6,3,5,4,2,1,0:T(1,128)S(1)}, u32[]{:S(2)}, u32[]{:S(2)}) collective-permute-start(f32[2,1,1,1,1,43,128]{6,3,5,4,2,1,0:T(1,128)S(1)} %constant_dynamic-slice_fusion.8), channel_id=1, source_target_pairs={{0,8},{8,0},{16,24},{24,16},{1,9},{9,1},{17,25},{25,17},{2,10},{10... | collective-permute-start | bytes 132104 | tf_op jit(solution)/shard_map/ppermute | solution.py:77
  48.1 0.8 %collective-permute-done.11 = f32[2,1,1,2,1,43,128]{6,3,5,4,2,1,0:T(2,128)S(1)} collective-permute-done((f32[2,1,1,2,1,43,128]{6,3,5,4,2,1,0:T(2,128)S(1)}, f32[2,1,1,2,1,43,128]{6,3,5,4,2,1,0:T(2,128)S(1)}, u32[]{:S(2)}, u32[]{:S(2)}) %collective-permute-start.11) | collective-permute-done | bytes 88096 | tf_op jit(solution)/shard_map/ppermute | solution.py:77
  48.9 1.8 %collective-permute-start.12 = (f32[2,1,1,1,1,43,128]{6,3,5,4,2,1,0:T(1,128)S(1)}, f32[2,1,1,1,1,43,128]{6,3,5,4,2,1,0:T(1,128)S(1)}, u32[]{:S(2)}, u32[]{:S(2)}) collective-permute-start(f32[2,1,1,1,1,43,128]{6,3,5,4,2,1,0:T(1,128)S(1)} %constant_dynamic-slice_fusion.4), channel_id=1, source_target_pairs={{0,2},{2,0},{4,6},{6,4},{1,3},{3,1},{5,7},{7,5},{8,10},{10,8},{12,... | collective-permute-start | bytes 132104 | tf_op jit(solution)/shard_map/ppermute | solution.py:77
  50.8 0.1 dynamic-slice_add_fusion.3
  50.9 0.1 collective-permute-start.16
  51.1 4.0 %collective-permute-start.9 = (f32[1,1,1,1,1,43,128]{6,3,5,4,2,1,0:T(1,128)S(1)}, f32[1,1,1,1,1,43,128]{6,3,5,4,2,1,0:T(1,128)S(1)}, u32[]{:S(2)}, u32[]{:S(2)}) collective-permute-start(f32[1,1,1,1,1,43,128]{6,3,5,4,2,1,0:T(1,128)S(1)} %constant_dynamic-slice_fusion.7), channel_id=1, source_target_pairs={{0,16},{8,24},{16,0},{24,8},{1,17},{9,25},{17,1},{25,9},{2,18},{10... | collective-permute-start | bytes 66056 | tf_op jit(solution)/shard_map/ppermute | solution.py:77
  55.0 0.1 dynamic-slice_add_fusion.7
  55.1 0.5 collective-permute-start.13
  55.7 2.5 %collective-permute-start.17 = (f32[1,1,1,1,1,43,128]{6,3,5,4,2,1,0:T(1,128)S(1)}, f32[1,1,1,1,1,43,128]{6,3,5,4,2,1,0:T(1,128)S(1)}, u32[]{:S(2)}, u32[]{:S(2)}) collective-permute-start(f32[1,1,1,1,1,43,128]{6,3,5,4,2,1,0:T(1,128)S(1)} %constant_dynamic-slice_fusion.13), channel_id=1, source_target_pairs={{0,16},{8,24},{16,0},{24,8},{1,17},{9,25},{17,1},{25,9},{2,18},{10... | collective-permute-start | bytes 66056 | tf_op jit(solution)/shard_map/ppermute | solution.py:77
  58.3 0.0 collective-permute-done.9
  58.3 2.2 %collective-permute-done.17 = f32[1,1,1,1,1,43,128]{6,3,5,4,2,1,0:T(1,128)S(1)} collective-permute-done((f32[1,1,1,1,1,43,128]{6,3,5,4,2,1,0:T(1,128)S(1)}, f32[1,1,1,1,1,43,128]{6,3,5,4,2,1,0:T(1,128)S(1)}, u32[]{:S(2)}, u32[]{:S(2)}) %collective-permute-start.17) | collective-permute-done | bytes 22048 | tf_op jit(solution)/shard_map/ppermute | solution.py:77
  60.6 0.0 collective-permute-done.13
  60.6 0.1 pad_maximum_fusion.8
  60.7 0.1 reshape_squeeze.3
  60.8 0.1 copy.23
  60.9 0.6 %pad_maximum_fusion.7 = f32[64,258]{1,0:T(8,128)} fusion(f32[64,2]{1,0:T(8,128)S(1)} %copy.23, f32[64,256]{1,0:T(8,128)S(1)} %bitcast.22), kind=kLoop, calls=%fused_computation.19 | loop fusion | flops 16512 | bytes 132096 | tf_op jit(solution)/shard_map/concatenate | solution.py:214
  (24 shorter events, 0.4 us)
Async XLA Ops:
  1.1 13.5 %collective-permute-start.4 = (f32[3,4,8,1,128]{4,3,2,1,0:T(1,128)S(1)}, f32[3,4,8,1,128]{4,3,2,1,0:T(1,128)S(1)}, u32[]{:S(2)}, u32[]{:S(2)}) collective-permute-start(f32[3,4,8,1,128]{4,3,2,1,0:T(1,128)S(1)} %broadcast_select_fusion.2), channel_id=1, source_target_pairs={{0,1},{1,0},{2,3},{3,2},{4,5},{5,4},{6,7},{7,6},{8,9},{9,8},{10,11... | collective-permute-start | bytes 147464 | tf_op jit(solution)/shard_map/ppermute | solution.py:44
  2.5 12.6 %copy-start = (f32[3,4,8,4,128]{4,3,2,1,0:T(4,128)S(1)}, f32[3,4,8,4,128]{4,3,2,1,0:T(4,128)}, u32[]{:S(2)}) copy-start(f32[3,4,8,4,128]{4,3,2,1,0:T(4,128)} %param.3) | copy-start | bytes 589828
  2.5 12.6 %collective-permute-start = (f32[3,1,8,4,128]{4,3,2,1,0:T(4,128)S(1)}, f32[3,1,8,4,128]{4,3,2,1,0:T(4,128)S(1)}, u32[]{:S(2)}, u32[]{:S(2)}) collective-permute-start(f32[3,1,8,4,128]{4,3,2,1,0:T(4,128)S(1)} %get-tuple-element.13), channel_id=1, source_target_pairs={{8,0},{16,8},{24,16},{0,24},{9,1},{17,9},{25,17},{1,25},{10,2},{18... | collective-permute-start | bytes 147464 | tf_op jit(solution)/shard_map/ppermute | solution.py:49
  7.1 7.9 %collective-permute-start.1 = (f32[3,1,8,4,128]{4,3,2,1,0:T(4,128)S(1)}, f32[3,1,8,4,128]{4,3,2,1,0:T(4,128)S(1)}, u32[]{:S(2)}, u32[]{:S(2)}) collective-permute-start(f32[3,1,8,4,128]{4,3,2,1,0:T(4,128)S(1)} %get-tuple-element.14), channel_id=1, source_target_pairs={{0,8},{8,16},{16,24},{24,0},{1,9},{9,17},{17,25},{25,1},{2,10},{10... | collective-permute-start | bytes 147464 | tf_op jit(solution)/shard_map/ppermute | solution.py:48
  7.9 6.8 %collective-permute-start.2 = (f32[3,4,1,4,128]{4,3,2,1,0:T(4,128)S(1)}, f32[3,4,1,4,128]{4,3,2,1,0:T(4,128)S(1)}, u32[]{:S(2)}, u32[]{:S(2)}) collective-permute-start(f32[3,4,1,4,128]{4,3,2,1,0:T(4,128)S(1)} %get-tuple-element.15), channel_id=1, source_target_pairs={{2,0},{4,2},{6,4},{0,6},{3,1},{5,3},{7,5},{1,7},{10,8},{12,10},{14... | collective-permute-start | bytes 73736 | tf_op jit(solution)/shard_map/ppermute | solution.py:49
  10.3 4.7 %collective-permute-start.3 = (f32[3,4,1,4,128]{4,3,2,1,0:T(4,128)S(1)}, f32[3,4,1,4,128]{4,3,2,1,0:T(4,128)S(1)}, u32[]{:S(2)}, u32[]{:S(2)}) collective-permute-start(f32[3,4,1,4,128]{4,3,2,1,0:T(4,128)S(1)} %get-tuple-element.16), channel_id=1, source_target_pairs={{0,2},{2,4},{4,6},{6,0},{1,3},{3,5},{5,7},{7,1},{8,10},{10,12},{12... | collective-permute-start | bytes 73736 | tf_op jit(solution)/shard_map/ppermute | solution.py:48
  31.6 2.7 %collective-permute-start.5 = (f32[2,2,2,2,1,129,128]{6,3,5,4,2,1,0:T(2,128)S(1)}, f32[2,2,2,2,1,129,128]{6,3,5,4,2,1,0:T(2,128)S(1)}, u32[]{:S(2)}, u32[]{:S(2)}) collective-permute-start(f32[2,2,2,2,1,129,128]{6,3,5,4,2,1,0:T(2,128)S(1)} %copy.25), channel_id=1, source_target_pairs={{0,1},{1,0},{2,3},{3,2},{4,5},{5,4},{6,7},{7,6},{8,9},{9,8},{10,11... | collective-permute-start | bytes 3170312 | tf_op jit(solution)/shard_map/ppermute | solution.py:77
  35.3 6.6 %collective-permute-start.6 = (f32[2,2,2,1,1,43,128]{6,3,5,4,2,1,0:T(1,128)S(1)}, f32[2,2,2,1,1,43,128]{6,3,5,4,2,1,0:T(1,128)S(1)}, u32[]{:S(2)}, u32[]{:S(2)}) collective-permute-start(f32[2,2,2,1,1,43,128]{6,3,5,4,2,1,0:T(1,128)S(1)} %constant_dynamic-slice_fusion.10), channel_id=1, source_target_pairs={{0,2},{2,0},{4,6},{6,4},{1,3},{3,1},{5,7},{7,5},{8,10},{10,8},{12,... | collective-permute-start | bytes 528392 | tf_op jit(solution)/shard_map/ppermute | solution.py:77
  37.1 6.6 %collective-permute-start.10 = (f32[2,2,1,2,1,43,128]{6,3,5,4,2,1,0:T(2,128)S(1)}, f32[2,2,1,2,1,43,128]{6,3,5,4,2,1,0:T(2,128)S(1)}, u32[]{:S(2)}, u32[]{:S(2)}) collective-permute-start(f32[2,2,1,2,1,43,128]{6,3,5,4,2,1,0:T(2,128)S(1)} %constant_dynamic-slice_fusion.6), channel_id=1, source_target_pairs={{0,4},{2,6},{4,0},{6,2},{1,5},{3,7},{5,1},{7,3},{8,12},{10,14},{12... | collective-permute-start | bytes 528392 | tf_op jit(solution)/shard_map/ppermute | solution.py:77
  38.7 6.0 %collective-permute-start.14 = (f32[2,1,2,2,1,43,128]{6,3,5,4,2,1,0:T(2,128)S(1)}, f32[2,1,2,2,1,43,128]{6,3,5,4,2,1,0:T(2,128)S(1)}, u32[]{:S(2)}, u32[]{:S(2)}) collective-permute-start(f32[2,1,2,2,1,43,128]{6,3,5,4,2,1,0:T(2,128)S(1)} %constant_dynamic-slice_fusion.2), channel_id=1, source_target_pairs={{0,8},{8,0},{16,24},{24,16},{1,9},{9,1},{17,25},{25,17},{2,10},{10... | collective-permute-start | bytes 528392 | tf_op jit(solution)/shard_map/ppermute | solution.py:77
  42.2 4.6 %collective-permute-start.7 = (f32[2,2,1,1,1,43,128]{6,3,5,4,2,1,0:T(1,128)S(1)}, f32[2,2,1,1,1,43,128]{6,3,5,4,2,1,0:T(1,128)S(1)}, u32[]{:S(2)}, u32[]{:S(2)}) collective-permute-start(f32[2,2,1,1,1,43,128]{6,3,5,4,2,1,0:T(1,128)S(1)} %constant_dynamic-slice_fusion.9), channel_id=1, source_target_pairs={{0,4},{2,6},{4,0},{6,2},{1,5},{3,7},{5,1},{7,3},{8,12},{10,14},{12... | collective-permute-start | bytes 264200 | tf_op jit(solution)/shard_map/ppermute | solution.py:77
  43.8 5.0 %collective-permute-start.11 = (f32[2,1,1,2,1,43,128]{6,3,5,4,2,1,0:T(2,128)S(1)}, f32[2,1,1,2,1,43,128]{6,3,5,4,2,1,0:T(2,128)S(1)}, u32[]{:S(2)}, u32[]{:S(2)}) collective-permute-start(f32[2,1,1,2,1,43,128]{6,3,5,4,2,1,0:T(2,128)S(1)} %constant_dynamic-slice_fusion.5), channel_id=1, source_target_pairs={{0,8},{8,0},{16,24},{24,16},{1,9},{9,1},{17,25},{25,17},{2,10},{10... | collective-permute-start | bytes 264200 | tf_op jit(solution)/shard_map/ppermute | solution.py:77
  44.9 5.9 %collective-permute-start.15 = (f32[2,1,2,1,1,43,128]{6,3,5,4,2,1,0:T(1,128)S(1)}, f32[2,1,2,1,1,43,128]{6,3,5,4,2,1,0:T(1,128)S(1)}, u32[]{:S(2)}, u32[]{:S(2)}) collective-permute-start(f32[2,1,2,1,1,43,128]{6,3,5,4,2,1,0:T(1,128)S(1)} %constant_dynamic-slice_fusion.1), channel_id=1, source_target_pairs={{0,2},{2,0},{4,6},{6,4},{1,3},{3,1},{5,7},{7,5},{8,10},{10,8},{12,... | collective-permute-start | bytes 264200 | tf_op jit(solution)/shard_map/ppermute | solution.py:77
  46.9 4.1 %collective-permute-start.8 = (f32[2,1,1,1,1,43,128]{6,3,5,4,2,1,0:T(1,128)S(1)}, f32[2,1,1,1,1,43,128]{6,3,5,4,2,1,0:T(1,128)S(1)}, u32[]{:S(2)}, u32[]{:S(2)}) collective-permute-start(f32[2,1,1,1,1,43,128]{6,3,5,4,2,1,0:T(1,128)S(1)} %constant_dynamic-slice_fusion.8), channel_id=1, source_target_pairs={{0,8},{8,0},{16,24},{24,16},{1,9},{9,1},{17,25},{25,17},{2,10},{10... | collective-permute-start | bytes 132104 | tf_op jit(solution)/shard_map/ppermute | solution.py:77
  48.9 6.1 %collective-permute-start.12 = (f32[2,1,1,1,1,43,128]{6,3,5,4,2,1,0:T(1,128)S(1)}, f32[2,1,1,1,1,43,128]{6,3,5,4,2,1,0:T(1,128)S(1)}, u32[]{:S(2)}, u32[]{:S(2)}) collective-permute-start(f32[2,1,1,1,1,43,128]{6,3,5,4,2,1,0:T(1,128)S(1)} %constant_dynamic-slice_fusion.4), channel_id=1, source_target_pairs={{0,2},{2,0},{4,6},{6,4},{1,3},{3,1},{5,7},{7,5},{8,10},{10,8},{12,... | collective-permute-start | bytes 132104 | tf_op jit(solution)/shard_map/ppermute | solution.py:77
  50.9 4.8 %collective-permute-start.16 = (f32[2,1,1,1,1,43,128]{6,3,5,4,2,1,0:T(1,128)S(1)}, f32[2,1,1,1,1,43,128]{6,3,5,4,2,1,0:T(1,128)S(1)}, u32[]{:S(2)}, u32[]{:S(2)}) collective-permute-start(f32[2,1,1,1,1,43,128]{6,3,5,4,2,1,0:T(1,128)S(1)} %constant_dynamic-slice_fusion), channel_id=1, source_target_pairs={{0,4},{2,6},{4,0},{6,2},{1,5},{3,7},{5,1},{7,3},{8,12},{10,14},{12... | collective-permute-start | bytes 132104 | tf_op jit(solution)/shard_map/ppermute | solution.py:77
  51.1 7.2 %collective-permute-start.9 = (f32[1,1,1,1,1,43,128]{6,3,5,4,2,1,0:T(1,128)S(1)}, f32[1,1,1,1,1,43,128]{6,3,5,4,2,1,0:T(1,128)S(1)}, u32[]{:S(2)}, u32[]{:S(2)}) collective-permute-start(f32[1,1,1,1,1,43,128]{6,3,5,4,2,1,0:T(1,128)S(1)} %constant_dynamic-slice_fusion.7), channel_id=1, source_target_pairs={{0,16},{8,24},{16,0},{24,8},{1,17},{9,25},{17,1},{25,9},{2,18},{10... | collective-permute-start | bytes 66056 | tf_op jit(solution)/shard_map/ppermute | solution.py:77
  55.1 5.4 %collective-permute-start.13 = (f32[1,1,1,1,1,43,128]{6,3,5,4,2,1,0:T(1,128)S(1)}, f32[1,1,1,1,1,43,128]{6,3,5,4,2,1,0:T(1,128)S(1)}, u32[]{:S(2)}, u32[]{:S(2)}) collective-permute-start(f32[1,1,1,1,1,43,128]{6,3,5,4,2,1,0:T(1,128)S(1)} %constant_dynamic-slice_fusion.3), channel_id=1, source_target_pairs={{0,16},{8,24},{16,0},{24,8},{1,17},{9,25},{17,1},{25,9},{2,18},{10... | collective-permute-start | bytes 66056 | tf_op jit(solution)/shard_map/ppermute | solution.py:77
  55.7 4.8 %collective-permute-start.17 = (f32[1,1,1,1,1,43,128]{6,3,5,4,2,1,0:T(1,128)S(1)}, f32[1,1,1,1,1,43,128]{6,3,5,4,2,1,0:T(1,128)S(1)}, u32[]{:S(2)}, u32[]{:S(2)}) collective-permute-start(f32[1,1,1,1,1,43,128]{6,3,5,4,2,1,0:T(1,128)S(1)} %constant_dynamic-slice_fusion.13), channel_id=1, source_target_pairs={{0,16},{8,24},{16,0},{24,8},{1,17},{9,25},{17,1},{25,9},{2,18},{10... | collective-permute-start | bytes 66056 | tf_op jit(solution)/shard_map/ppermute | solution.py:77

commit v18 on v12

--- a/solution.py
+++ b/solution.py
@@ -103,12 +103,19 @@
     return value.reshape(1, rows, lanes)
 
 
-def triangle_kernel(block_len, dense, slot_ref, side_ref, w_ref, g_ref, m_ref, out_ref, sym_ref, rest_ref):
+def triangle_kernel(block_len, dense, slot_ref, side_ref, w_ref, grad_ref, m_ref, out_ref, send_ref, sym_ref, rest_ref, g_ref, buf_ref):
     test, width = w_ref.shape[1], m_ref.shape[1]
-    group = 4
+    cells = grad_ref.shape[2]
+    for a in range(3):
+        for b in range(3):
+            g_ref[a, :, pl.ds(b * cells, cells)] = grad_ref[a, b].T
+    group = 32
     full = block_len // 128 if dense else out_ref.shape[2] // 128
     out_ref[...] = jnp.zeros(out_ref.shape, out_ref.dtype)
     rest_ref[...] = jnp.zeros(rest_ref.shape, rest_ref.dtype)
+    buf_ref[...] = jnp.zeros(buf_ref.shape, buf_ref.dtype)
+    if not dense:
+        send_ref[...] = jnp.zeros(send_ref.shape, send_ref.dtype)
 
     def contract(step, carry):
         slabs = []
@@ -141,7 +148,7 @@
                 rolled = pltpu.roll(slab, (offset - j - base) % 128, 1)
                 keep = (lane >= lo - u * 128) & (lane < hi - u * 128)
                 if u < full and dense:
-                    target = out_ref.at[(slot + side_ref[0]) % 2, slot // 2, pl.ds(u * test, test), :]
+                    target = buf_ref.at[(slot + side_ref[0]) % 2, slot // 2, pl.ds(u * test, test), :]
                 elif u < full:
                     target = out_ref.at[slot, :, pl.ds(u * 128, 128)]
                 else:
@@ -156,7 +163,9 @@
             for r in range(spare):
                 hit = (lane >= r * test) & (lane < (r + 1) * test) & (lane - r * test == row)
                 picked = jnp.where(hit, jnp.broadcast_to(tail[:, r : r + 1], (test, 128)), picked)
-            out_ref[(s + side_ref[0]) % 2, s // 2, pl.ds(full * test, 1), :] = jnp.sum(picked, axis=0, keepdims=True)
+            buf_ref[(s + side_ref[0]) % 2, s // 2, pl.ds(full * test, 1), :] = jnp.sum(picked, axis=0, keepdims=True)
+        out_ref[...] = buf_ref[0]
+        send_ref[...] = buf_ref[1]
 
 
 def triangle(slots, side, weighted, grads, modes_flat, block_len, dense):
@@ -164,17 +173,21 @@
     test, width = weighted.shape[1], modes_flat.shape[1]
     tiles = -(-block_len // 128)
     if dense:
-        shape = (2, owners // 2, (block_len // 128) * test + 1, 128)
+        shape = (owners // 2, (block_len // 128) * test + 1, 128)
+        spare = (2,) + shape
     else:
         shape = (owners, test, tiles * 128)
+        spare = (1, 1, 8, 128)
     return pl.pallas_call(
         functools.partial(triangle_kernel, block_len, dense),
-        out_shape=jax.ShapeDtypeStruct(shape, jnp.float32),
+        out_shape=(jax.ShapeDtypeStruct(shape, jnp.float32), jax.ShapeDtypeStruct(shape if dense else (8, 128), jnp.float32)),
         in_specs=[pl.BlockSpec(memory_space=pltpu.SMEM)] * 2 + [pl.BlockSpec(memory_space=pltpu.VMEM)] * 3,
-        out_specs=pl.BlockSpec(memory_space=pltpu.VMEM),
+        out_specs=(pl.BlockSpec(memory_space=pltpu.VMEM), pl.BlockSpec(memory_space=pltpu.VMEM)),
         scratch_shapes=[
             pltpu.VMEM((test * width, width), jnp.float32),
             pltpu.VMEM((owners if dense else 1, test, 128), jnp.float32),
+            pltpu.VMEM((3, width, 3 * grads.shape[2]), jnp.float32),
+            pltpu.VMEM(spare, jnp.float32),
         ],
     )(slots, side, weighted, grads, modes_flat)
 
@@ -194,7 +207,6 @@
     cells = mode_flat.shape[1]
     weighted = mode_flat[:, :, :TEST] * (weight_flat * scale)[None, :, None]
     weighted = jnp.tile(jnp.swapaxes(weighted, 1, 2), (1, 1, 3))
-    grads_t = grad_flat.transpose(0, 3, 1, 2).reshape(3, width, 3 * cells)
     pair_total = width * (width + 1) // 2
     block_len = (pair_total + owners - 1) // owners
     ranks = jnp.arange(owners, dtype=jnp.int32)
@@ -203,9 +215,9 @@
     full, spare = block_len // 128, block_len % 128
     dense = 0 < spare and spare * TEST <= 128 and size_z == 2
     side = lax.axis_index("gz").astype(jnp.int32).reshape(1)
-    placed = triangle(slots, side, weighted, grads_t, mode_flat.reshape(3 * cells, width), block_len, dense)
+    placed, sent = triangle(slots, side, weighted, grad_flat, mode_flat.reshape(3 * cells, width), block_len, dense)
     if dense:
-        merged = placed[0] + lax.ppermute(placed[1], "gz", [(0, 1), (1, 0)])
+        merged = placed + lax.ppermute(sent, "gz", [(0, 1), (1, 0)])
         owned = scatter_sum(merged, ("gx", "gy"), local=False)[0]
         main = owned[: full * TEST].reshape(full, TEST, 128).transpose(1, 0, 2).reshape(TEST, full * 128)
         tail = owned[full * TEST, : spare * TEST].reshape(spare, TEST).T

time: 65.4 us -> 60.1 us (0.919)
  Pallas kernels: 16.3 us -> 13.3 us
  local copies, waits for them, and re-layouts: 7 us -> 4.97 us
  waiting for transfers between devices: 12.7 us -> 11.7 us
  other arithmetic: 5.65 us -> 6.54 us
    ppermute x2, starting transfers between devices: 0.01 us -> 4.71 us  [face_gradients(): before = lax.ppermute(last, axis, up)]
    ppermute x2, starting transfers between devices: 7.12 us -> 3.37 us  [face_gradients(): after = lax.ppermute(leading, axis, down)]
    pallas_call x1, Pallas kernels: 16.3 us -> 13.3 us  [triangle(): pl.pallas_call(functools.partial(triangle_kernel, block_len, dense), out_...]
    squeeze x2 -> x0, local copies, waits for them, and re-layouts: 2.51 us -> none  [shards(): merged = placed[0] + lax.ppermute(placed[1], 'gz', [(0, 1), (1, 0)])]
    pallas_call x0 -> x1, local copies, waits for them, and re-layouts: none -> 1.54 us  [triangle(): pl.pallas_call(functools.partial(triangle_kernel, block_len, dense), out_...]
    ppermute x12, starting transfers between devices: 15.4 us -> 14.3 us  [halve(): return keep + lax.ppermute(other, axis, pairs)]
    reshape x1 -> x0, local copies, waits for them, and re-layouts: 1.07 us -> none  [shards(): grads_t = grad_flat.transpose(0, 3, 1, 2).reshape(3, width, 3 * cells)]
    another operation x1, other arithmetic: 0.04 us -> 0.88 us  [face_gradients(): return jnp.stack(steps, axis=1)]
  transfers between devices with their start and end apart: 18 -> 18, of which waited for: 8 -> 7; matrix products, arithmetic and copies ran while one was open for 10% -> 11% of each run, Pallas kernels for 0% -> 0%
where the time goes in v18:
time: 60.1 us; the launch traced here: 59.8 us
  starting transfers between devices  23 us (38%)
  Pallas kernels  13.3 us (22%)
  waiting for transfers between devices  11.7 us (19%)
  other arithmetic  6.54 us (11%)
  local copies, waits for them, and re-layouts  4.97 us (8%)
    ppermute x12, starting transfers between devices, halve(): return keep + lax.ppermute(other, axis, pairs)  14.3 us
    pallas_call x1, Pallas kernels, triangle(): pl.pallas_call(functools.partial(triangle_kernel, block_len, dense), out_...  13.3 us
    ppermute x12, waiting for transfers between devices, halve(): return keep + lax.ppermute(other, axis, pairs)  9.4 us
    ppermute x2, starting transfers between devices, face_gradients(): before = lax.ppermute(last, axis, up)  4.71 us
    ppermute x2, starting transfers between devices, face_gradients(): after = lax.ppermute(leading, axis, down)  3.37 us
    ppermute x1, waiting for transfers between devices, shards(): merged = placed + lax.ppermute(sent, 'gz', [(0, 1), (1, 0)])  2.3 us
    slice x2, local copies, waits for them, and re-layouts, face_gradients(): leading = lax.slice_in_dim(value, 0, 1, axis=dim)  1.59 us
    pallas_call x1, local copies, waits for them, and re-layouts, triangle(): pl.pallas_call(functools.partial(triangle_kernel, block_len, dense), out_...  1.54 us
  transfers between devices with their start and end apart: 18, of which 7 were waited for; matrix products, arithmetic and copies ran while one was open for 11% of the time, Pallas kernels for 0%

profile of v18, /device:TPU:0, one launch (start us, length us, event | category | flops | bytes accessed | tf_op | source)
XLA Modules:
  0.0 59.8 jit_solution(5282868331541282582)
XLA Ops:
  0.0 0.8 %fusion.8 = (f32[3,1,8,4,128]{4,3,2,1,0:T(4,128)S(1)}, f32[3,1,8,4,128]{4,3,2,1,0:T(4,128)S(1)}) fusion(f32[3,4,8,4,128]{4,3,2,1,0:T(4,128)} %param.3), kind=kLoop, calls=%fused_computation.53 | loop fusion | bytes 196608 | tf_op jit(solution)/shard_map/slice | solution.py:41
  0.8 3.1 %collective-permute-start.1 = (f32[3,1,8,4,128]{4,3,2,1,0:T(4,128)S(1)}, f32[3,1,8,4,128]{4,3,2,1,0:T(4,128)S(1)}, u32[]{:S(2)}, u32[]{:S(2)}) collective-permute-start(f32[3,1,8,4,128]{4,3,2,1,0:T(4,128)S(1)} %get-tuple-element.16), channel_id=1, source_target_pairs={{0,8},{8,16},{16,24},{24,0},{1,9},{9,17},{17,25},{25,1},{2,10},{10... | collective-permute-start | bytes 147464 | tf_op jit(solution)/shard_map/ppermute | solution.py:48
  3.9 2.1 %collective-permute-start = (f32[3,1,8,4,128]{4,3,2,1,0:T(4,128)S(1)}, f32[3,1,8,4,128]{4,3,2,1,0:T(4,128)S(1)}, u32[]{:S(2)}, u32[]{:S(2)}) collective-permute-start(f32[3,1,8,4,128]{4,3,2,1,0:T(4,128)S(1)} %get-tuple-element.15), channel_id=1, source_target_pairs={{8,0},{16,8},{24,16},{0,24},{9,1},{17,9},{25,17},{1,25},{10,2},{18... | collective-permute-start | bytes 147464 | tf_op jit(solution)/shard_map/ppermute | solution.py:49
  6.0 0.8 %fusion.9 = (f32[3,4,1,4,128]{4,3,2,1,0:T(4,128)S(1)}, f32[3,4,1,4,128]{4,3,2,1,0:T(4,128)S(1)}) fusion(f32[3,4,8,4,128]{4,3,2,1,0:T(4,128)} %param.3), kind=kLoop, calls=%fused_computation.54 | loop fusion | bytes 98304 | tf_op jit(solution)/shard_map/slice | solution.py:41
  6.7 1.6 %collective-permute-start.3 = (f32[3,4,1,4,128]{4,3,2,1,0:T(4,128)S(1)}, f32[3,4,1,4,128]{4,3,2,1,0:T(4,128)S(1)}, u32[]{:S(2)}, u32[]{:S(2)}) collective-permute-start(f32[3,4,1,4,128]{4,3,2,1,0:T(4,128)S(1)} %get-tuple-element.18), channel_id=1, source_target_pairs={{0,2},{2,4},{4,6},{6,0},{1,3},{3,5},{5,7},{7,1},{8,10},{10,12},{12... | collective-permute-start | bytes 73736 | tf_op jit(solution)/shard_map/ppermute | solution.py:48
  8.4 1.3 %collective-permute-start.2 = (f32[3,4,1,4,128]{4,3,2,1,0:T(4,128)S(1)}, f32[3,4,1,4,128]{4,3,2,1,0:T(4,128)S(1)}, u32[]{:S(2)}, u32[]{:S(2)}) collective-permute-start(f32[3,4,1,4,128]{4,3,2,1,0:T(4,128)S(1)} %get-tuple-element.17), channel_id=1, source_target_pairs={{2,0},{4,2},{6,4},{0,6},{3,1},{5,3},{7,5},{1,7},{10,8},{12,10},{14... | collective-permute-start | bytes 73736 | tf_op jit(solution)/shard_map/ppermute | solution.py:49
  9.7 0.0 copy-start
  9.7 1.2 %broadcast_select_fusion.2 = f32[3,4,8,1,128]{4,3,2,1,0:T(1,128)S(1)} fusion(pred[]{:T(512)S(6)} %eq.36, f32[3,4,8,4,128]{4,3,2,1,0:T(4,128)} %param.3), kind=kLoop, calls=%fused_computation.25 | loop fusion | flops 12288 | bytes 147457 | tf_op jit(solution)/shard_map/jit(_where)/select_n | solution.py:44
  10.8 0.1 collective-permute-start.4
  10.9 0.8 %select_reduce_fusion = s32[32]{0:T(128)S(1)} fusion(s32[32]{0:T(128)} %param.5), kind=kLoop, calls=%fused_computation.35 | loop fusion | flops 3040 | bytes 256 | tf_op jit(solution)/shard_map/reduce_sum | solution.py:213
  11.7 0.7 %broadcast_multiply_fusion = f32[4,8,4]{1,2,0:T(4,128)S(1)} fusion(f32[4,8,4]{1,2,0:T(4,128)} %param.4), kind=kLoop, calls=%fused_computation.49 | loop fusion | flops 128 | bytes 1024 | tf_op jit(solution)/shard_map/mul | solution.py:208
  12.4 0.1 copy.18
  12.5 0.1 mul.32
  12.6 1.0 %fusion.6 = f32[3,64,128]{1,2,0:T(8,128)S(1)} fusion(f32[3,128,128]{2,1,0:T(8,128)} %bitcast.17, f32[128]{0:T(128)S(1)} %mul.32), kind=kLoop, calls=%fused_computation.15 | loop fusion | flops 24576 | bytes 197120 | tf_op jit(solution)/shard_map/transpose | solution.py:209
  13.6 0.5 broadcast_clamp_fusion.slot_ref
  14.1 0.1 copy.19
  14.2 0.1 tile.4
  14.3 0.9 %tile.10.w_ref = f32[3,64,384]{2,1,0:T(8,128)} reshape(f32[3,64,3,128]{3,2,1,0:T(4,128)S(1)} %tile.4) | data formatting | bytes 589824 | tf_op jit(solution)/shard_map/tile | solution.py:209
  15.2 0.0 collective-permute-done.4
  15.2 0.1 broadcast_select_fusion.1
  15.3 0.0 collective-permute-done.3
  15.3 0.0 collective-permute-done.2
  15.3 0.0 collective-permute-done.1
  15.3 0.0 collective-permute-done
  15.3 0.0 copy-done
  15.3 0.3 fusion.5
  15.6 0.9 %pad_maximum_fusion.grad_ref = f32[3,3,128,128]{3,2,1,0:T(8,128)} fusion(f32[3,1,128,128]{3,2,1,0:T(8,128)S(1)} %bitcast.21, f32[3,1,128,128]{3,2,1,0:T(8,128)S(1)} %bitcast.20, f32[3,1,128,128]{3,2,1,0:T(8,128)S(1)} %bitcast.19), kind=kLoop, calls=%fused_computation.1 | loop fusion | flops 294912 | bytes 1179648 | tf_op jit(solution)/shard_map/stack | solution.py:58
  16.5 13.3 %shard_map.37 = (f32[16,129,128]{2,1,0:T(8,128)}, f32[16,129,128]{2,1,0:T(8,128)}) custom-call(s32[32]{0:T(128)} %broadcast_clamp_fusion.slot_ref, s32[1]{0:T(128)} %bitcast.side_ref, f32[3,64,384]{2,1,0:T(8,128)} %tile.10.w_ref, f32[3,3,128,128]{3,2,1,0:T(8,128)} %pad_maximum_fusion.grad_ref, f32[384,128]{1,0:T(8,128)} %bitcast.18), custom_call_target="tpu_custom_call" | custom-call | tf_op jit(solution)/shard_map/pallas_call | solution.py:181
  29.8 0.0 copy-start.1
  29.8 1.5 %copy.20 = f32[16,129,128]{2,0,1:T(8,128)S(1)} copy(f32[16,129,128]{2,1,0:T(8,128)} %get-tuple-element.8) | data formatting | bytes 2113536 | tf_op jit(solution)/shard_map/pallas_call | solution.py:181
  31.3 0.6 collective-permute-start.5
  31.9 2.3 %collective-permute-done.5 = f32[16,129,128]{2,0,1:T(8,128)S(1)} collective-permute-done((f32[16,129,128]{2,0,1:T(8,128)S(1)}, f32[16,129,128]{2,0,1:T(8,128)S(1)}, u32[]{:S(2)}, u32[]{:S(2)}) %collective-permute-start.5) | collective-permute-done | bytes 1056800 | tf_op jit(solution)/shard_map/ppermute | solution.py:220
  34.2 0.0 copy-done.1
  34.2 0.4 copy_add_fusion
  34.5 0.1 fusion.7
  34.7 0.1 collective-permute-start.14
  34.8 1.8 %collective-permute-start.10 = (f32[2,2,1,2,43,128]{5,4,3,2,1,0:T(8,128)S(1)}, f32[2,2,1,2,43,128]{5,4,3,2,1,0:T(8,128)S(1)}, u32[]{:S(2)}, u32[]{:S(2)}) collective-permute-start(f32[2,2,1,2,43,128]{5,4,3,2,1,0:T(8,128)S(1)} %constant_dynamic-slice_fusion.6), channel_id=1, source_target_pairs={{0,4},{2,6},{4,0},{6,2},{1,5},{3,7},{5,1},{7,3},{8,12},{10,14},{12... | collective-permute-start | bytes 528392 | tf_op jit(solution)/shard_map/ppermute | solution.py:77
  36.6 0.7 %collective-permute-start.6 = (f32[2,2,2,1,43,128]{5,4,3,2,1,0:T(8,128)S(1)}, f32[2,2,2,1,43,128]{5,4,3,2,1,0:T(8,128)S(1)}, u32[]{:S(2)}, u32[]{:S(2)}) collective-permute-start(f32[2,2,2,1,43,128]{5,4,3,2,1,0:T(8,128)S(1)} %constant_dynamic-slice_fusion.10), channel_id=1, source_target_pairs={{0,2},{2,0},{4,6},{6,4},{1,3},{3,1},{5,7},{7,5},{8,10},{10,8},{12,... | collective-permute-start | bytes 528392 | tf_op jit(solution)/shard_map/ppermute | solution.py:77
  37.2 4.7 %collective-permute-done.14 = f32[2,1,2,2,43,128]{5,4,3,2,1,0:T(8,128)S(1)} collective-permute-done((f32[2,1,2,2,43,128]{5,4,3,2,1,0:T(8,128)S(1)}, f32[2,1,2,2,43,128]{5,4,3,2,1,0:T(8,128)S(1)}, u32[]{:S(2)}, u32[]{:S(2)}) %collective-permute-start.14) | collective-permute-done | bytes 176160 | tf_op jit(solution)/shard_map/ppermute | solution.py:77
  42.0 0.8 %collective-permute-start.15 = (f32[2,1,2,1,43,128]{5,4,3,2,1,0:T(8,128)S(1)}, f32[2,1,2,1,43,128]{5,4,3,2,1,0:T(8,128)S(1)}, u32[]{:S(2)}, u32[]{:S(2)}) collective-permute-start(f32[2,1,2,1,43,128]{5,4,3,2,1,0:T(8,128)S(1)} %constant_dynamic-slice_fusion.1), channel_id=1, source_target_pairs={{0,2},{2,0},{4,6},{6,4},{1,3},{3,1},{5,7},{7,5},{8,10},{10,8},{12,... | collective-permute-start | bytes 264200 | tf_op jit(solution)/shard_map/ppermute | solution.py:77
  42.8 0.0 collective-permute-done.10
  42.9 1.0 %collective-permute-start.11 = (f32[2,1,1,2,43,128]{5,4,3,2,1,0:T(8,128)S(1)}, f32[2,1,1,2,43,128]{5,4,3,2,1,0:T(8,128)S(1)}, u32[]{:S(2)}, u32[]{:S(2)}) collective-permute-start(f32[2,1,1,2,43,128]{5,4,3,2,1,0:T(8,128)S(1)} %constant_dynamic-slice_fusion.5), channel_id=1, source_target_pairs={{0,8},{8,0},{16,24},{24,16},{1,9},{9,1},{17,25},{25,17},{2,10},{10... | collective-permute-start | bytes 264200 | tf_op jit(solution)/shard_map/ppermute | solution.py:77
  43.9 0.0 collective-permute-done.6
  44.0 1.7 %collective-permute-start.7 = (f32[2,2,1,1,43,128]{5,4,3,2,1,0:T(8,128)S(1)}, f32[2,2,1,1,43,128]{5,4,3,2,1,0:T(8,128)S(1)}, u32[]{:S(2)}, u32[]{:S(2)}) collective-permute-start(f32[2,2,1,1,43,128]{5,4,3,2,1,0:T(8,128)S(1)} %constant_dynamic-slice_fusion.9), channel_id=1, source_target_pairs={{0,4},{2,6},{4,0},{6,2},{1,5},{3,7},{5,1},{7,3},{8,12},{10,14},{12... | collective-permute-start | bytes 264200 | tf_op jit(solution)/shard_map/ppermute | solution.py:77
  45.7 1.0 %collective-permute-done.15 = f32[2,1,2,1,43,128]{5,4,3,2,1,0:T(8,128)S(1)} collective-permute-done((f32[2,1,2,1,43,128]{5,4,3,2,1,0:T(8,128)S(1)}, f32[2,1,2,1,43,128]{5,4,3,2,1,0:T(8,128)S(1)}, u32[]{:S(2)}, u32[]{:S(2)}) %collective-permute-start.15) | collective-permute-done | bytes 88096 | tf_op jit(solution)/shard_map/ppermute | solution.py:77
  46.7 1.7 %collective-permute-start.16 = (f32[2,1,1,1,43,128]{5,4,3,2,1,0:T(8,128)S(1)}, f32[2,1,1,1,43,128]{5,4,3,2,1,0:T(8,128)S(1)}, u32[]{:S(2)}, u32[]{:S(2)}) collective-permute-start(f32[2,1,1,1,43,128]{5,4,3,2,1,0:T(8,128)S(1)} %constant_dynamic-slice_fusion), channel_id=1, source_target_pairs={{0,4},{2,6},{4,0},{6,2},{1,5},{3,7},{5,1},{7,3},{8,12},{10,14},{12... | collective-permute-start | bytes 132104 | tf_op jit(solution)/shard_map/ppermute | solution.py:77
  48.5 0.0 collective-permute-done.11
  48.5 0.7 %collective-permute-start.12 = (f32[2,1,1,1,43,128]{5,4,3,2,1,0:T(8,128)S(1)}, f32[2,1,1,1,43,128]{5,4,3,2,1,0:T(8,128)S(1)}, u32[]{:S(2)}, u32[]{:S(2)}) collective-permute-start(f32[2,1,1,1,43,128]{5,4,3,2,1,0:T(8,128)S(1)} %constant_dynamic-slice_fusion.4), channel_id=1, source_target_pairs={{0,2},{2,0},{4,6},{6,4},{1,3},{3,1},{5,7},{7,5},{8,10},{10,8},{12,... | collective-permute-start | bytes 132104 | tf_op jit(solution)/shard_map/ppermute | solution.py:77
  49.2 0.0 collective-permute-done.7
  49.2 1.9 %collective-permute-start.8 = (f32[2,1,1,1,43,128]{5,4,3,2,1,0:T(8,128)S(1)}, f32[2,1,1,1,43,128]{5,4,3,2,1,0:T(8,128)S(1)}, u32[]{:S(2)}, u32[]{:S(2)}) collective-permute-start(f32[2,1,1,1,43,128]{5,4,3,2,1,0:T(8,128)S(1)} %constant_dynamic-slice_fusion.8), channel_id=1, source_target_pairs={{0,8},{8,0},{16,24},{24,16},{1,9},{9,1},{17,25},{25,17},{2,10},{10... | collective-permute-start | bytes 132104 | tf_op jit(solution)/shard_map/ppermute | solution.py:77
  51.1 0.0 collective-permute-done.16
  51.1 0.9 %collective-permute-start.17 = (f32[1,1,1,1,43,128]{5,4,3,2,1,0:T(8,128)S(1)}, f32[1,1,1,1,43,128]{5,4,3,2,1,0:T(8,128)S(1)}, u32[]{:S(2)}, u32[]{:S(2)}) collective-permute-start(f32[1,1,1,1,43,128]{5,4,3,2,1,0:T(8,128)S(1)} %constant_dynamic-slice_fusion.11), channel_id=1, source_target_pairs={{0,16},{8,24},{16,0},{24,8},{1,17},{9,25},{17,1},{25,9},{2,18},{10... | collective-permute-start | bytes 66056 | tf_op jit(solution)/shard_map/ppermute | solution.py:77
  52.0 0.7 %collective-permute-done.12 = f32[2,1,1,1,43,128]{5,4,3,2,1,0:T(8,128)S(1)} collective-permute-done((f32[2,1,1,1,43,128]{5,4,3,2,1,0:T(8,128)S(1)}, f32[2,1,1,1,43,128]{5,4,3,2,1,0:T(8,128)S(1)}, u32[]{:S(2)}, u32[]{:S(2)}) %collective-permute-start.12) | collective-permute-done | bytes 44064 | tf_op jit(solution)/shard_map/ppermute | solution.py:77
  52.7 1.5 %collective-permute-start.13 = (f32[1,1,1,1,43,128]{5,4,3,2,1,0:T(8,128)S(1)}, f32[1,1,1,1,43,128]{5,4,3,2,1,0:T(8,128)S(1)}, u32[]{:S(2)}, u32[]{:S(2)}) collective-permute-start(f32[1,1,1,1,43,128]{5,4,3,2,1,0:T(8,128)S(1)} %constant_dynamic-slice_fusion.3), channel_id=1, source_target_pairs={{0,16},{8,24},{16,0},{24,8},{1,17},{9,25},{17,1},{25,9},{2,18},{10... | collective-permute-start | bytes 66056 | tf_op jit(solution)/shard_map/ppermute | solution.py:77
  54.2 0.0 collective-permute-done.8
  54.2 1.6 %collective-permute-start.9 = (f32[1,1,1,1,43,128]{5,4,3,2,1,0:T(8,128)S(1)}, f32[1,1,1,1,43,128]{5,4,3,2,1,0:T(8,128)S(1)}, u32[]{:S(2)}, u32[]{:S(2)}) collective-permute-start(f32[1,1,1,1,43,128]{5,4,3,2,1,0:T(8,128)S(1)} %constant_dynamic-slice_fusion.7), channel_id=1, source_target_pairs={{0,16},{8,24},{16,0},{24,8},{1,17},{9,25},{17,1},{25,9},{2,18},{10... | collective-permute-start | bytes 66056 | tf_op jit(solution)/shard_map/ppermute | solution.py:77
  55.8 0.3 collective-permute-done.17
  56.1 1.4 %collective-permute-done.13 = f32[1,1,1,1,43,128]{5,4,3,2,1,0:T(8,128)S(1)} collective-permute-done((f32[1,1,1,1,43,128]{5,4,3,2,1,0:T(8,128)S(1)}, f32[1,1,1,1,43,128]{5,4,3,2,1,0:T(8,128)S(1)}, u32[]{:S(2)}, u32[]{:S(2)}) %collective-permute-start.13) | collective-permute-done | bytes 22048 | tf_op jit(solution)/shard_map/ppermute | solution.py:77
  57.5 0.1 reshape_squeeze.3
  57.6 0.1 copy.23
  57.7 1.3 %collective-permute-done.9 = f32[1,1,1,1,43,128]{5,4,3,2,1,0:T(8,128)S(1)} collective-permute-done((f32[1,1,1,1,43,128]{5,4,3,2,1,0:T(8,128)S(1)}, f32[1,1,1,1,43,128]{5,4,3,2,1,0:T(8,128)S(1)}, u32[]{:S(2)}, u32[]{:S(2)}) %collective-permute-start.9) | collective-permute-done | bytes 22048 | tf_op jit(solution)/shard_map/ppermute | solution.py:77
  59.0 0.1 copy.22
  59.1 0.7 %pad_maximum_fusion.7 = f32[64,258]{1,0:T(8,128)} fusion(f32[64,2]{1,0:T(8,128)S(1)} %copy.23, f32[64,256]{1,0:T(8,128)S(1)} %bitcast.22), kind=kLoop, calls=%fused_computation.19 | loop fusion | flops 16512 | bytes 132096 | tf_op jit(solution)/shard_map/concatenate | solution.py:224
  (27 shorter events, 0.4 us)
Async XLA Ops:
  0.8 14.5 %collective-permute-start.1 = (f32[3,1,8,4,128]{4,3,2,1,0:T(4,128)S(1)}, f32[3,1,8,4,128]{4,3,2,1,0:T(4,128)S(1)}, u32[]{:S(2)}, u32[]{:S(2)}) collective-permute-start(f32[3,1,8,4,128]{4,3,2,1,0:T(4,128)S(1)} %get-tuple-element.16), channel_id=1, source_target_pairs={{0,8},{8,16},{16,24},{24,0},{1,9},{9,17},{17,25},{25,1},{2,10},{10... | collective-permute-start | bytes 147464 | tf_op jit(solution)/shard_map/ppermute | solution.py:48
  3.9 11.4 %collective-permute-start = (f32[3,1,8,4,128]{4,3,2,1,0:T(4,128)S(1)}, f32[3,1,8,4,128]{4,3,2,1,0:T(4,128)S(1)}, u32[]{:S(2)}, u32[]{:S(2)}) collective-permute-start(f32[3,1,8,4,128]{4,3,2,1,0:T(4,128)S(1)} %get-tuple-element.15), channel_id=1, source_target_pairs={{8,0},{16,8},{24,16},{0,24},{9,1},{17,9},{25,17},{1,25},{10,2},{18... | collective-permute-start | bytes 147464 | tf_op jit(solution)/shard_map/ppermute | solution.py:49
  6.7 8.5 %collective-permute-start.3 = (f32[3,4,1,4,128]{4,3,2,1,0:T(4,128)S(1)}, f32[3,4,1,4,128]{4,3,2,1,0:T(4,128)S(1)}, u32[]{:S(2)}, u32[]{:S(2)}) collective-permute-start(f32[3,4,1,4,128]{4,3,2,1,0:T(4,128)S(1)} %get-tuple-element.18), channel_id=1, source_target_pairs={{0,2},{2,4},{4,6},{6,0},{1,3},{3,5},{5,7},{7,1},{8,10},{10,12},{12... | collective-permute-start | bytes 73736 | tf_op jit(solution)/shard_map/ppermute | solution.py:48
  8.4 6.9 %collective-permute-start.2 = (f32[3,4,1,4,128]{4,3,2,1,0:T(4,128)S(1)}, f32[3,4,1,4,128]{4,3,2,1,0:T(4,128)S(1)}, u32[]{:S(2)}, u32[]{:S(2)}) collective-permute-start(f32[3,4,1,4,128]{4,3,2,1,0:T(4,128)S(1)} %get-tuple-element.17), channel_id=1, source_target_pairs={{2,0},{4,2},{6,4},{0,6},{3,1},{5,3},{7,5},{1,7},{10,8},{12,10},{14... | collective-permute-start | bytes 73736 | tf_op jit(solution)/shard_map/ppermute | solution.py:49
  9.7 5.6 %copy-start = (f32[3,4,8,4,128]{4,3,2,1,0:T(4,128)S(1)}, f32[3,4,8,4,128]{4,3,2,1,0:T(4,128)}, u32[]{:S(2)}) copy-start(f32[3,4,8,4,128]{4,3,2,1,0:T(4,128)} %param.3) | copy-start | bytes 589828
  10.8 4.4 %collective-permute-start.4 = (f32[3,4,8,1,128]{4,3,2,1,0:T(1,128)S(1)}, f32[3,4,8,1,128]{4,3,2,1,0:T(1,128)S(1)}, u32[]{:S(2)}, u32[]{:S(2)}) collective-permute-start(f32[3,4,8,1,128]{4,3,2,1,0:T(1,128)S(1)} %broadcast_select_fusion.2), channel_id=1, source_target_pairs={{0,1},{1,0},{2,3},{3,2},{4,5},{5,4},{6,7},{7,6},{8,9},{9,8},{10,11... | collective-permute-start | bytes 147464 | tf_op jit(solution)/shard_map/ppermute | solution.py:44
  29.8 4.4 %copy-start.1 = (f32[16,129,128]{2,1,0:T(8,128)S(1)}, f32[16,129,128]{2,1,0:T(8,128)}, u32[]{:S(2)}) copy-start(f32[16,129,128]{2,1,0:T(8,128)} %get-tuple-element.7) | copy-start | bytes 3170308
  31.3 2.9 %collective-permute-start.5 = (f32[16,129,128]{2,0,1:T(8,128)S(1)}, f32[16,129,128]{2,0,1:T(8,128)S(1)}, u32[]{:S(2)}, u32[]{:S(2)}) collective-permute-start(f32[16,129,128]{2,0,1:T(8,128)S(1)} %copy.20), channel_id=1, source_target_pairs={{0,1},{1,0},{2,3},{3,2},{4,5},{5,4},{6,7},{7,6},{8,9},{9,8},{10,11... | collective-permute-start | bytes 3170312 | tf_op jit(solution)/shard_map/ppermute | solution.py:220
  34.7 7.2 %collective-permute-start.14 = (f32[2,1,2,2,43,128]{5,4,3,2,1,0:T(8,128)S(1)}, f32[2,1,2,2,43,128]{5,4,3,2,1,0:T(8,128)S(1)}, u32[]{:S(2)}, u32[]{:S(2)}) collective-permute-start(f32[2,1,2,2,43,128]{5,4,3,2,1,0:T(8,128)S(1)} %constant_dynamic-slice_fusion.2), channel_id=1, source_target_pairs={{0,8},{8,0},{16,24},{24,16},{1,9},{9,1},{17,25},{25,17},{2,10},{10... | collective-permute-start | bytes 528392 | tf_op jit(solution)/shard_map/ppermute | solution.py:77
  34.8 8.0 %collective-permute-start.10 = (f32[2,2,1,2,43,128]{5,4,3,2,1,0:T(8,128)S(1)}, f32[2,2,1,2,43,128]{5,4,3,2,1,0:T(8,128)S(1)}, u32[]{:S(2)}, u32[]{:S(2)}) collective-permute-start(f32[2,2,1,2,43,128]{5,4,3,2,1,0:T(8,128)S(1)} %constant_dynamic-slice_fusion.6), channel_id=1, source_target_pairs={{0,4},{2,6},{4,0},{6,2},{1,5},{3,7},{5,1},{7,3},{8,12},{10,14},{12... | collective-permute-start | bytes 528392 | tf_op jit(solution)/shard_map/ppermute | solution.py:77
  36.6 7.3 %collective-permute-start.6 = (f32[2,2,2,1,43,128]{5,4,3,2,1,0:T(8,128)S(1)}, f32[2,2,2,1,43,128]{5,4,3,2,1,0:T(8,128)S(1)}, u32[]{:S(2)}, u32[]{:S(2)}) collective-permute-start(f32[2,2,2,1,43,128]{5,4,3,2,1,0:T(8,128)S(1)} %constant_dynamic-slice_fusion.10), channel_id=1, source_target_pairs={{0,2},{2,0},{4,6},{6,4},{1,3},{3,1},{5,7},{7,5},{8,10},{10,8},{12,... | collective-permute-start | bytes 528392 | tf_op jit(solution)/shard_map/ppermute | solution.py:77
  42.0 4.7 %collective-permute-start.15 = (f32[2,1,2,1,43,128]{5,4,3,2,1,0:T(8,128)S(1)}, f32[2,1,2,1,43,128]{5,4,3,2,1,0:T(8,128)S(1)}, u32[]{:S(2)}, u32[]{:S(2)}) collective-permute-start(f32[2,1,2,1,43,128]{5,4,3,2,1,0:T(8,128)S(1)} %constant_dynamic-slice_fusion.1), channel_id=1, source_target_pairs={{0,2},{2,0},{4,6},{6,4},{1,3},{3,1},{5,7},{7,5},{8,10},{10,8},{12,... | collective-permute-start | bytes 264200 | tf_op jit(solution)/shard_map/ppermute | solution.py:77
  42.9 5.6 %collective-permute-start.11 = (f32[2,1,1,2,43,128]{5,4,3,2,1,0:T(8,128)S(1)}, f32[2,1,1,2,43,128]{5,4,3,2,1,0:T(8,128)S(1)}, u32[]{:S(2)}, u32[]{:S(2)}) collective-permute-start(f32[2,1,1,2,43,128]{5,4,3,2,1,0:T(8,128)S(1)} %constant_dynamic-slice_fusion.5), channel_id=1, source_target_pairs={{0,8},{8,0},{16,24},{24,16},{1,9},{9,1},{17,25},{25,17},{2,10},{10... | collective-permute-start | bytes 264200 | tf_op jit(solution)/shard_map/ppermute | solution.py:77
  44.0 5.2 %collective-permute-start.7 = (f32[2,2,1,1,43,128]{5,4,3,2,1,0:T(8,128)S(1)}, f32[2,2,1,1,43,128]{5,4,3,2,1,0:T(8,128)S(1)}, u32[]{:S(2)}, u32[]{:S(2)}) collective-permute-start(f32[2,2,1,1,43,128]{5,4,3,2,1,0:T(8,128)S(1)} %constant_dynamic-slice_fusion.9), channel_id=1, source_target_pairs={{0,4},{2,6},{4,0},{6,2},{1,5},{3,7},{5,1},{7,3},{8,12},{10,14},{12... | collective-permute-start | bytes 264200 | tf_op jit(solution)/shard_map/ppermute | solution.py:77
  46.7 4.4 %collective-permute-start.16 = (f32[2,1,1,1,43,128]{5,4,3,2,1,0:T(8,128)S(1)}, f32[2,1,1,1,43,128]{5,4,3,2,1,0:T(8,128)S(1)}, u32[]{:S(2)}, u32[]{:S(2)}) collective-permute-start(f32[2,1,1,1,43,128]{5,4,3,2,1,0:T(8,128)S(1)} %constant_dynamic-slice_fusion), channel_id=1, source_target_pairs={{0,4},{2,6},{4,0},{6,2},{1,5},{3,7},{5,1},{7,3},{8,12},{10,14},{12... | collective-permute-start | bytes 132104 | tf_op jit(solution)/shard_map/ppermute | solution.py:77
  48.5 4.2 %collective-permute-start.12 = (f32[2,1,1,1,43,128]{5,4,3,2,1,0:T(8,128)S(1)}, f32[2,1,1,1,43,128]{5,4,3,2,1,0:T(8,128)S(1)}, u32[]{:S(2)}, u32[]{:S(2)}) collective-permute-start(f32[2,1,1,1,43,128]{5,4,3,2,1,0:T(8,128)S(1)} %constant_dynamic-slice_fusion.4), channel_id=1, source_target_pairs={{0,2},{2,0},{4,6},{6,4},{1,3},{3,1},{5,7},{7,5},{8,10},{10,8},{12,... | collective-permute-start | bytes 132104 | tf_op jit(solution)/shard_map/ppermute | solution.py:77
  49.2 5.0 %collective-permute-start.8 = (f32[2,1,1,1,43,128]{5,4,3,2,1,0:T(8,128)S(1)}, f32[2,1,1,1,43,128]{5,4,3,2,1,0:T(8,128)S(1)}, u32[]{:S(2)}, u32[]{:S(2)}) collective-permute-start(f32[2,1,1,1,43,128]{5,4,3,2,1,0:T(8,128)S(1)} %constant_dynamic-slice_fusion.8), channel_id=1, source_target_pairs={{0,8},{8,0},{16,24},{24,16},{1,9},{9,1},{17,25},{25,17},{2,10},{10... | collective-permute-start | bytes 132104 | tf_op jit(solution)/shard_map/ppermute | solution.py:77
  51.1 5.0 %collective-permute-start.17 = (f32[1,1,1,1,43,128]{5,4,3,2,1,0:T(8,128)S(1)}, f32[1,1,1,1,43,128]{5,4,3,2,1,0:T(8,128)S(1)}, u32[]{:S(2)}, u32[]{:S(2)}) collective-permute-start(f32[1,1,1,1,43,128]{5,4,3,2,1,0:T(8,128)S(1)} %constant_dynamic-slice_fusion.11), channel_id=1, source_target_pairs={{0,16},{8,24},{16,0},{24,8},{1,17},{9,25},{17,1},{25,9},{2,18},{10... | collective-permute-start | bytes 66056 | tf_op jit(solution)/shard_map/ppermute | solution.py:77
  52.7 4.8 %collective-permute-start.13 = (f32[1,1,1,1,43,128]{5,4,3,2,1,0:T(8,128)S(1)}, f32[1,1,1,1,43,128]{5,4,3,2,1,0:T(8,128)S(1)}, u32[]{:S(2)}, u32[]{:S(2)}) collective-permute-start(f32[1,1,1,1,43,128]{5,4,3,2,1,0:T(8,128)S(1)} %constant_dynamic-slice_fusion.3), channel_id=1, source_target_pairs={{0,16},{8,24},{16,0},{24,8},{1,17},{9,25},{17,1},{25,9},{2,18},{10... | collective-permute-start | bytes 66056 | tf_op jit(solution)/shard_map/ppermute | solution.py:77
  54.2 4.8 %collective-permute-start.9 = (f32[1,1,1,1,43,128]{5,4,3,2,1,0:T(8,128)S(1)}, f32[1,1,1,1,43,128]{5,4,3,2,1,0:T(8,128)S(1)}, u32[]{:S(2)}, u32[]{:S(2)}) collective-permute-start(f32[1,1,1,1,43,128]{5,4,3,2,1,0:T(8,128)S(1)} %constant_dynamic-slice_fusion.7), channel_id=1, source_target_pairs={{0,16},{8,24},{16,0},{24,8},{1,17},{9,25},{17,1},{25,9},{2,18},{10... | collective-permute-start | bytes 66056 | tf_op jit(solution)/shard_map/ppermute | solution.py:77

commit v19 on v18

--- a/solution.py
+++ b/solution.py
@@ -111,10 +111,10 @@
             g_ref[a, :, pl.ds(b * cells, cells)] = grad_ref[a, b].T
     group = 32
     full = block_len // 128 if dense else out_ref.shape[2] // 128
-    out_ref[...] = jnp.zeros(out_ref.shape, out_ref.dtype)
     rest_ref[...] = jnp.zeros(rest_ref.shape, rest_ref.dtype)
     buf_ref[...] = jnp.zeros(buf_ref.shape, buf_ref.dtype)
     if not dense:
+        out_ref[...] = jnp.zeros(out_ref.shape, out_ref.dtype)
         send_ref[...] = jnp.zeros(send_ref.shape, send_ref.dtype)
 
     def contract(step, carry):

time: 60.1 us -> 60.1 us (level)
  no operation moved by 1% of the time
where the time goes in v19:
time: 60.1 us; the launch traced here: 59.7 us
  starting transfers between devices  23 us (38%)
  Pallas kernels  13.2 us (22%)
  waiting for transfers between devices  11.7 us (19%)
  other arithmetic  6.54 us (11%)
  local copies, waits for them, and re-layouts  4.97 us (8%)
    ppermute x12, starting transfers between devices, halve(): return keep + lax.ppermute(other, axis, pairs)  14.3 us
    pallas_call x1, Pallas kernels, triangle(): pl.pallas_call(functools.partial(triangle_kernel, block_len, dense), out_...  13.2 us
    ppermute x12, waiting for transfers between devices, halve(): return keep + lax.ppermute(other, axis, pairs)  9.4 us
    ppermute x2, starting transfers between devices, face_gradients(): before = lax.ppermute(last, axis, up)  4.71 us
    ppermute x2, starting transfers between devices, face_gradients(): after = lax.ppermute(leading, axis, down)  3.37 us
    ppermute x1, waiting for transfers between devices, shards(): merged = placed + lax.ppermute(sent, 'gz', [(0, 1), (1, 0)])  2.3 us
    slice x2, local copies, waits for them, and re-layouts, face_gradients(): leading = lax.slice_in_dim(value, 0, 1, axis=dim)  1.59 us
    pallas_call x1, local copies, waits for them, and re-layouts, triangle(): pl.pallas_call(functools.partial(triangle_kernel, block_len, dense), out_...  1.54 us
  transfers between devices with their start and end apart: 18, of which 7 were waited for; matrix products, arithmetic and copies ran while one was open for 11% of the time, Pallas kernels for 0%

profile of v19, /device:TPU:0, one launch (start us, length us, event | category | flops | bytes accessed | tf_op | source)
XLA Modules:
  0.0 59.7 jit_solution(14866914751831733297)
XLA Ops:
  0.0 0.8 %fusion.8 = (f32[3,1,8,4,128]{4,3,2,1,0:T(4,128)S(1)}, f32[3,1,8,4,128]{4,3,2,1,0:T(4,128)S(1)}) fusion(f32[3,4,8,4,128]{4,3,2,1,0:T(4,128)} %param.3), kind=kLoop, calls=%fused_computation.53 | loop fusion | bytes 196608 | tf_op jit(solution)/shard_map/slice | solution.py:41
  0.8 3.1 %collective-permute-start.1 = (f32[3,1,8,4,128]{4,3,2,1,0:T(4,128)S(1)}, f32[3,1,8,4,128]{4,3,2,1,0:T(4,128)S(1)}, u32[]{:S(2)}, u32[]{:S(2)}) collective-permute-start(f32[3,1,8,4,128]{4,3,2,1,0:T(4,128)S(1)} %get-tuple-element.16), channel_id=1, source_target_pairs={{0,8},{8,16},{16,24},{24,0},{1,9},{9,17},{17,25},{25,1},{2,10},{10... | collective-permute-start | bytes 147464 | tf_op jit(solution)/shard_map/ppermute | solution.py:48
  3.9 2.1 %collective-permute-start = (f32[3,1,8,4,128]{4,3,2,1,0:T(4,128)S(1)}, f32[3,1,8,4,128]{4,3,2,1,0:T(4,128)S(1)}, u32[]{:S(2)}, u32[]{:S(2)}) collective-permute-start(f32[3,1,8,4,128]{4,3,2,1,0:T(4,128)S(1)} %get-tuple-element.15), channel_id=1, source_target_pairs={{8,0},{16,8},{24,16},{0,24},{9,1},{17,9},{25,17},{1,25},{10,2},{18... | collective-permute-start | bytes 147464 | tf_op jit(solution)/shard_map/ppermute | solution.py:49
  6.0 0.8 %fusion.9 = (f32[3,4,1,4,128]{4,3,2,1,0:T(4,128)S(1)}, f32[3,4,1,4,128]{4,3,2,1,0:T(4,128)S(1)}) fusion(f32[3,4,8,4,128]{4,3,2,1,0:T(4,128)} %param.3), kind=kLoop, calls=%fused_computation.54 | loop fusion | bytes 98304 | tf_op jit(solution)/shard_map/slice | solution.py:41
  6.7 1.6 %collective-permute-start.3 = (f32[3,4,1,4,128]{4,3,2,1,0:T(4,128)S(1)}, f32[3,4,1,4,128]{4,3,2,1,0:T(4,128)S(1)}, u32[]{:S(2)}, u32[]{:S(2)}) collective-permute-start(f32[3,4,1,4,128]{4,3,2,1,0:T(4,128)S(1)} %get-tuple-element.18), channel_id=1, source_target_pairs={{0,2},{2,4},{4,6},{6,0},{1,3},{3,5},{5,7},{7,1},{8,10},{10,12},{12... | collective-permute-start | bytes 73736 | tf_op jit(solution)/shard_map/ppermute | solution.py:48
  8.4 1.3 %collective-permute-start.2 = (f32[3,4,1,4,128]{4,3,2,1,0:T(4,128)S(1)}, f32[3,4,1,4,128]{4,3,2,1,0:T(4,128)S(1)}, u32[]{:S(2)}, u32[]{:S(2)}) collective-permute-start(f32[3,4,1,4,128]{4,3,2,1,0:T(4,128)S(1)} %get-tuple-element.17), channel_id=1, source_target_pairs={{2,0},{4,2},{6,4},{0,6},{3,1},{5,3},{7,5},{1,7},{10,8},{12,10},{14... | collective-permute-start | bytes 73736 | tf_op jit(solution)/shard_map/ppermute | solution.py:49
  9.7 0.0 copy-start
  9.7 1.2 %broadcast_select_fusion.2 = f32[3,4,8,1,128]{4,3,2,1,0:T(1,128)S(1)} fusion(pred[]{:T(512)S(6)} %eq.36, f32[3,4,8,4,128]{4,3,2,1,0:T(4,128)} %param.3), kind=kLoop, calls=%fused_computation.25 | loop fusion | flops 12288 | bytes 147457 | tf_op jit(solution)/shard_map/jit(_where)/select_n | solution.py:44
  10.8 0.1 collective-permute-start.4
  10.9 0.8 %select_reduce_fusion = s32[32]{0:T(128)S(1)} fusion(s32[32]{0:T(128)} %param.5), kind=kLoop, calls=%fused_computation.35 | loop fusion | flops 3040 | bytes 256 | tf_op jit(solution)/shard_map/reduce_sum | solution.py:213
  11.7 0.7 %broadcast_multiply_fusion = f32[4,8,4]{1,2,0:T(4,128)S(1)} fusion(f32[4,8,4]{1,2,0:T(4,128)} %param.4), kind=kLoop, calls=%fused_computation.49 | loop fusion | flops 128 | bytes 1024 | tf_op jit(solution)/shard_map/mul | solution.py:208
  12.4 0.1 copy.18
  12.5 0.1 mul.32
  12.6 1.0 %fusion.6 = f32[3,64,128]{1,2,0:T(8,128)S(1)} fusion(f32[3,128,128]{2,1,0:T(8,128)} %bitcast.17, f32[128]{0:T(128)S(1)} %mul.32), kind=kLoop, calls=%fused_computation.15 | loop fusion | flops 24576 | bytes 197120 | tf_op jit(solution)/shard_map/transpose | solution.py:209
  13.6 0.5 broadcast_clamp_fusion.slot_ref
  14.1 0.1 copy.19
  14.2 0.1 tile.4
  14.3 0.9 %tile.10.w_ref = f32[3,64,384]{2,1,0:T(8,128)} reshape(f32[3,64,3,128]{3,2,1,0:T(4,128)S(1)} %tile.4) | data formatting | bytes 589824 | tf_op jit(solution)/shard_map/tile | solution.py:209
  15.2 0.0 collective-permute-done.4
  15.2 0.1 broadcast_select_fusion.1
  15.3 0.0 collective-permute-done.3
  15.3 0.0 collective-permute-done.2
  15.3 0.0 collective-permute-done.1
  15.3 0.0 collective-permute-done
  15.3 0.0 copy-done
  15.3 0.3 fusion.5
  15.6 0.9 %pad_maximum_fusion.grad_ref = f32[3,3,128,128]{3,2,1,0:T(8,128)} fusion(f32[3,1,128,128]{3,2,1,0:T(8,128)S(1)} %bitcast.21, f32[3,1,128,128]{3,2,1,0:T(8,128)S(1)} %bitcast.20, f32[3,1,128,128]{3,2,1,0:T(8,128)S(1)} %bitcast.19), kind=kLoop, calls=%fused_computation.1 | loop fusion | flops 294912 | bytes 1179648 | tf_op jit(solution)/shard_map/stack | solution.py:58
  16.5 13.2 %shard_map.37 = (f32[16,129,128]{2,1,0:T(8,128)}, f32[16,129,128]{2,1,0:T(8,128)}) custom-call(s32[32]{0:T(128)} %broadcast_clamp_fusion.slot_ref, s32[1]{0:T(128)} %bitcast.side_ref, f32[3,64,384]{2,1,0:T(8,128)} %tile.10.w_ref, f32[3,3,128,128]{3,2,1,0:T(8,128)} %pad_maximum_fusion.grad_ref, f32[384,128]{1,0:T(8,128)} %bitcast.18), custom_call_target="tpu_custom_call" | custom-call | tf_op jit(solution)/shard_map/pallas_call | solution.py:181
  29.7 0.0 copy-start.1
  29.7 1.5 %copy.20 = f32[16,129,128]{2,0,1:T(8,128)S(1)} copy(f32[16,129,128]{2,1,0:T(8,128)} %get-tuple-element.8) | data formatting | bytes 2113536 | tf_op jit(solution)/shard_map/pallas_call | solution.py:181
  31.2 0.6 collective-permute-start.5
  31.8 2.3 %collective-permute-done.5 = f32[16,129,128]{2,0,1:T(8,128)S(1)} collective-permute-done((f32[16,129,128]{2,0,1:T(8,128)S(1)}, f32[16,129,128]{2,0,1:T(8,128)S(1)}, u32[]{:S(2)}, u32[]{:S(2)}) %collective-permute-start.5) | collective-permute-done | bytes 1056800 | tf_op jit(solution)/shard_map/ppermute | solution.py:220
  34.1 0.0 copy-done.1
  34.1 0.4 copy_add_fusion
  34.5 0.1 fusion.7
  34.6 0.1 collective-permute-start.14
  34.7 1.8 %collective-permute-start.10 = (f32[2,2,1,2,43,128]{5,4,3,2,1,0:T(8,128)S(1)}, f32[2,2,1,2,43,128]{5,4,3,2,1,0:T(8,128)S(1)}, u32[]{:S(2)}, u32[]{:S(2)}) collective-permute-start(f32[2,2,1,2,43,128]{5,4,3,2,1,0:T(8,128)S(1)} %constant_dynamic-slice_fusion.6), channel_id=1, source_target_pairs={{0,4},{2,6},{4,0},{6,2},{1,5},{3,7},{5,1},{7,3},{8,12},{10,14},{12... | collective-permute-start | bytes 528392 | tf_op jit(solution)/shard_map/ppermute | solution.py:77
  36.5 0.7 %collective-permute-start.6 = (f32[2,2,2,1,43,128]{5,4,3,2,1,0:T(8,128)S(1)}, f32[2,2,2,1,43,128]{5,4,3,2,1,0:T(8,128)S(1)}, u32[]{:S(2)}, u32[]{:S(2)}) collective-permute-start(f32[2,2,2,1,43,128]{5,4,3,2,1,0:T(8,128)S(1)} %constant_dynamic-slice_fusion.10), channel_id=1, source_target_pairs={{0,2},{2,0},{4,6},{6,4},{1,3},{3,1},{5,7},{7,5},{8,10},{10,8},{12,... | collective-permute-start | bytes 528392 | tf_op jit(solution)/shard_map/ppermute | solution.py:77
  37.2 4.7 %collective-permute-done.14 = f32[2,1,2,2,43,128]{5,4,3,2,1,0:T(8,128)S(1)} collective-permute-done((f32[2,1,2,2,43,128]{5,4,3,2,1,0:T(8,128)S(1)}, f32[2,1,2,2,43,128]{5,4,3,2,1,0:T(8,128)S(1)}, u32[]{:S(2)}, u32[]{:S(2)}) %collective-permute-start.14) | collective-permute-done | bytes 176160 | tf_op jit(solution)/shard_map/ppermute | solution.py:77
  41.9 0.8 %collective-permute-start.15 = (f32[2,1,2,1,43,128]{5,4,3,2,1,0:T(8,128)S(1)}, f32[2,1,2,1,43,128]{5,4,3,2,1,0:T(8,128)S(1)}, u32[]{:S(2)}, u32[]{:S(2)}) collective-permute-start(f32[2,1,2,1,43,128]{5,4,3,2,1,0:T(8,128)S(1)} %constant_dynamic-slice_fusion.1), channel_id=1, source_target_pairs={{0,2},{2,0},{4,6},{6,4},{1,3},{3,1},{5,7},{7,5},{8,10},{10,8},{12,... | collective-permute-start | bytes 264200 | tf_op jit(solution)/shard_map/ppermute | solution.py:77
  42.7 0.0 collective-permute-done.10
  42.8 1.0 %collective-permute-start.11 = (f32[2,1,1,2,43,128]{5,4,3,2,1,0:T(8,128)S(1)}, f32[2,1,1,2,43,128]{5,4,3,2,1,0:T(8,128)S(1)}, u32[]{:S(2)}, u32[]{:S(2)}) collective-permute-start(f32[2,1,1,2,43,128]{5,4,3,2,1,0:T(8,128)S(1)} %constant_dynamic-slice_fusion.5), channel_id=1, source_target_pairs={{0,8},{8,0},{16,24},{24,16},{1,9},{9,1},{17,25},{25,17},{2,10},{10... | collective-permute-start | bytes 264200 | tf_op jit(solution)/shard_map/ppermute | solution.py:77
  43.8 0.0 collective-permute-done.6
  43.9 1.7 %collective-permute-start.7 = (f32[2,2,1,1,43,128]{5,4,3,2,1,0:T(8,128)S(1)}, f32[2,2,1,1,43,128]{5,4,3,2,1,0:T(8,128)S(1)}, u32[]{:S(2)}, u32[]{:S(2)}) collective-permute-start(f32[2,2,1,1,43,128]{5,4,3,2,1,0:T(8,128)S(1)} %constant_dynamic-slice_fusion.9), channel_id=1, source_target_pairs={{0,4},{2,6},{4,0},{6,2},{1,5},{3,7},{5,1},{7,3},{8,12},{10,14},{12... | collective-permute-start | bytes 264200 | tf_op jit(solution)/shard_map/ppermute | solution.py:77
  45.6 1.0 %collective-permute-done.15 = f32[2,1,2,1,43,128]{5,4,3,2,1,0:T(8,128)S(1)} collective-permute-done((f32[2,1,2,1,43,128]{5,4,3,2,1,0:T(8,128)S(1)}, f32[2,1,2,1,43,128]{5,4,3,2,1,0:T(8,128)S(1)}, u32[]{:S(2)}, u32[]{:S(2)}) %collective-permute-start.15) | collective-permute-done | bytes 88096 | tf_op jit(solution)/shard_map/ppermute | solution.py:77
  46.7 1.7 %collective-permute-start.16 = (f32[2,1,1,1,43,128]{5,4,3,2,1,0:T(8,128)S(1)}, f32[2,1,1,1,43,128]{5,4,3,2,1,0:T(8,128)S(1)}, u32[]{:S(2)}, u32[]{:S(2)}) collective-permute-start(f32[2,1,1,1,43,128]{5,4,3,2,1,0:T(8,128)S(1)} %constant_dynamic-slice_fusion), channel_id=1, source_target_pairs={{0,4},{2,6},{4,0},{6,2},{1,5},{3,7},{5,1},{7,3},{8,12},{10,14},{12... | collective-permute-start | bytes 132104 | tf_op jit(solution)/shard_map/ppermute | solution.py:77
  48.4 0.0 collective-permute-done.11
  48.4 0.7 %collective-permute-start.12 = (f32[2,1,1,1,43,128]{5,4,3,2,1,0:T(8,128)S(1)}, f32[2,1,1,1,43,128]{5,4,3,2,1,0:T(8,128)S(1)}, u32[]{:S(2)}, u32[]{:S(2)}) collective-permute-start(f32[2,1,1,1,43,128]{5,4,3,2,1,0:T(8,128)S(1)} %constant_dynamic-slice_fusion.4), channel_id=1, source_target_pairs={{0,2},{2,0},{4,6},{6,4},{1,3},{3,1},{5,7},{7,5},{8,10},{10,8},{12,... | collective-permute-start | bytes 132104 | tf_op jit(solution)/shard_map/ppermute | solution.py:77
  49.1 0.0 collective-permute-done.7
  49.1 1.9 %collective-permute-start.8 = (f32[2,1,1,1,43,128]{5,4,3,2,1,0:T(8,128)S(1)}, f32[2,1,1,1,43,128]{5,4,3,2,1,0:T(8,128)S(1)}, u32[]{:S(2)}, u32[]{:S(2)}) collective-permute-start(f32[2,1,1,1,43,128]{5,4,3,2,1,0:T(8,128)S(1)} %constant_dynamic-slice_fusion.8), channel_id=1, source_target_pairs={{0,8},{8,0},{16,24},{24,16},{1,9},{9,1},{17,25},{25,17},{2,10},{10... | collective-permute-start | bytes 132104 | tf_op jit(solution)/shard_map/ppermute | solution.py:77
  51.0 0.0 collective-permute-done.16
  51.0 0.9 %collective-permute-start.17 = (f32[1,1,1,1,43,128]{5,4,3,2,1,0:T(8,128)S(1)}, f32[1,1,1,1,43,128]{5,4,3,2,1,0:T(8,128)S(1)}, u32[]{:S(2)}, u32[]{:S(2)}) collective-permute-start(f32[1,1,1,1,43,128]{5,4,3,2,1,0:T(8,128)S(1)} %constant_dynamic-slice_fusion.11), channel_id=1, source_target_pairs={{0,16},{8,24},{16,0},{24,8},{1,17},{9,25},{17,1},{25,9},{2,18},{10... | collective-permute-start | bytes 66056 | tf_op jit(solution)/shard_map/ppermute | solution.py:77
  51.9 0.7 %collective-permute-done.12 = f32[2,1,1,1,43,128]{5,4,3,2,1,0:T(8,128)S(1)} collective-permute-done((f32[2,1,1,1,43,128]{5,4,3,2,1,0:T(8,128)S(1)}, f32[2,1,1,1,43,128]{5,4,3,2,1,0:T(8,128)S(1)}, u32[]{:S(2)}, u32[]{:S(2)}) %collective-permute-start.12) | collective-permute-done | bytes 44064 | tf_op jit(solution)/shard_map/ppermute | solution.py:77
  52.6 1.5 %collective-permute-start.13 = (f32[1,1,1,1,43,128]{5,4,3,2,1,0:T(8,128)S(1)}, f32[1,1,1,1,43,128]{5,4,3,2,1,0:T(8,128)S(1)}, u32[]{:S(2)}, u32[]{:S(2)}) collective-permute-start(f32[1,1,1,1,43,128]{5,4,3,2,1,0:T(8,128)S(1)} %constant_dynamic-slice_fusion.3), channel_id=1, source_target_pairs={{0,16},{8,24},{16,0},{24,8},{1,17},{9,25},{17,1},{25,9},{2,18},{10... | collective-permute-start | bytes 66056 | tf_op jit(solution)/shard_map/ppermute | solution.py:77
  54.1 0.0 collective-permute-done.8
  54.2 1.6 %collective-permute-start.9 = (f32[1,1,1,1,43,128]{5,4,3,2,1,0:T(8,128)S(1)}, f32[1,1,1,1,43,128]{5,4,3,2,1,0:T(8,128)S(1)}, u32[]{:S(2)}, u32[]{:S(2)}) collective-permute-start(f32[1,1,1,1,43,128]{5,4,3,2,1,0:T(8,128)S(1)} %constant_dynamic-slice_fusion.7), channel_id=1, source_target_pairs={{0,16},{8,24},{16,0},{24,8},{1,17},{9,25},{17,1},{25,9},{2,18},{10... | collective-permute-start | bytes 66056 | tf_op jit(solution)/shard_map/ppermute | solution.py:77
  55.7 0.3 collective-permute-done.17
  56.0 1.4 %collective-permute-done.13 = f32[1,1,1,1,43,128]{5,4,3,2,1,0:T(8,128)S(1)} collective-permute-done((f32[1,1,1,1,43,128]{5,4,3,2,1,0:T(8,128)S(1)}, f32[1,1,1,1,43,128]{5,4,3,2,1,0:T(8,128)S(1)}, u32[]{:S(2)}, u32[]{:S(2)}) %collective-permute-start.13) | collective-permute-done | bytes 22048 | tf_op jit(solution)/shard_map/ppermute | solution.py:77
  57.4 0.1 reshape_squeeze.3
  57.5 0.1 copy.23
  57.6 1.3 %collective-permute-done.9 = f32[1,1,1,1,43,128]{5,4,3,2,1,0:T(8,128)S(1)} collective-permute-done((f32[1,1,1,1,43,128]{5,4,3,2,1,0:T(8,128)S(1)}, f32[1,1,1,1,43,128]{5,4,3,2,1,0:T(8,128)S(1)}, u32[]{:S(2)}, u32[]{:S(2)}) %collective-permute-start.9) | collective-permute-done | bytes 22048 | tf_op jit(solution)/shard_map/ppermute | solution.py:77
  59.0 0.1 copy.22
  59.0 0.7 %pad_maximum_fusion.7 = f32[64,258]{1,0:T(8,128)} fusion(f32[64,2]{1,0:T(8,128)S(1)} %copy.23, f32[64,256]{1,0:T(8,128)S(1)} %bitcast.22), kind=kLoop, calls=%fused_computation.19 | loop fusion | flops 16512 | bytes 132096 | tf_op jit(solution)/shard_map/concatenate | solution.py:224
  (27 shorter events, 0.4 us)
Async XLA Ops:
  0.8 14.5 %collective-permute-start.1 = (f32[3,1,8,4,128]{4,3,2,1,0:T(4,128)S(1)}, f32[3,1,8,4,128]{4,3,2,1,0:T(4,128)S(1)}, u32[]{:S(2)}, u32[]{:S(2)}) collective-permute-start(f32[3,1,8,4,128]{4,3,2,1,0:T(4,128)S(1)} %get-tuple-element.16), channel_id=1, source_target_pairs={{0,8},{8,16},{16,24},{24,0},{1,9},{9,17},{17,25},{25,1},{2,10},{10... | collective-permute-start | bytes 147464 | tf_op jit(solution)/shard_map/ppermute | solution.py:48
  3.9 11.4 %collective-permute-start = (f32[3,1,8,4,128]{4,3,2,1,0:T(4,128)S(1)}, f32[3,1,8,4,128]{4,3,2,1,0:T(4,128)S(1)}, u32[]{:S(2)}, u32[]{:S(2)}) collective-permute-start(f32[3,1,8,4,128]{4,3,2,1,0:T(4,128)S(1)} %get-tuple-element.15), channel_id=1, source_target_pairs={{8,0},{16,8},{24,16},{0,24},{9,1},{17,9},{25,17},{1,25},{10,2},{18... | collective-permute-start | bytes 147464 | tf_op jit(solution)/shard_map/ppermute | solution.py:49
  6.7 8.5 %collective-permute-start.3 = (f32[3,4,1,4,128]{4,3,2,1,0:T(4,128)S(1)}, f32[3,4,1,4,128]{4,3,2,1,0:T(4,128)S(1)}, u32[]{:S(2)}, u32[]{:S(2)}) collective-permute-start(f32[3,4,1,4,128]{4,3,2,1,0:T(4,128)S(1)} %get-tuple-element.18), channel_id=1, source_target_pairs={{0,2},{2,4},{4,6},{6,0},{1,3},{3,5},{5,7},{7,1},{8,10},{10,12},{12... | collective-permute-start | bytes 73736 | tf_op jit(solution)/shard_map/ppermute | solution.py:48
  8.4 6.9 %collective-permute-start.2 = (f32[3,4,1,4,128]{4,3,2,1,0:T(4,128)S(1)}, f32[3,4,1,4,128]{4,3,2,1,0:T(4,128)S(1)}, u32[]{:S(2)}, u32[]{:S(2)}) collective-permute-start(f32[3,4,1,4,128]{4,3,2,1,0:T(4,128)S(1)} %get-tuple-element.17), channel_id=1, source_target_pairs={{2,0},{4,2},{6,4},{0,6},{3,1},{5,3},{7,5},{1,7},{10,8},{12,10},{14... | collective-permute-start | bytes 73736 | tf_op jit(solution)/shard_map/ppermute | solution.py:49
  9.7 5.6 %copy-start = (f32[3,4,8,4,128]{4,3,2,1,0:T(4,128)S(1)}, f32[3,4,8,4,128]{4,3,2,1,0:T(4,128)}, u32[]{:S(2)}) copy-start(f32[3,4,8,4,128]{4,3,2,1,0:T(4,128)} %param.3) | copy-start | bytes 589828
  10.8 4.4 %collective-permute-start.4 = (f32[3,4,8,1,128]{4,3,2,1,0:T(1,128)S(1)}, f32[3,4,8,1,128]{4,3,2,1,0:T(1,128)S(1)}, u32[]{:S(2)}, u32[]{:S(2)}) collective-permute-start(f32[3,4,8,1,128]{4,3,2,1,0:T(1,128)S(1)} %broadcast_select_fusion.2), channel_id=1, source_target_pairs={{0,1},{1,0},{2,3},{3,2},{4,5},{5,4},{6,7},{7,6},{8,9},{9,8},{10,11... | collective-permute-start | bytes 147464 | tf_op jit(solution)/shard_map/ppermute | solution.py:44
  29.7 4.4 %copy-start.1 = (f32[16,129,128]{2,1,0:T(8,128)S(1)}, f32[16,129,128]{2,1,0:T(8,128)}, u32[]{:S(2)}) copy-start(f32[16,129,128]{2,1,0:T(8,128)} %get-tuple-element.7) | copy-start | bytes 3170308
  31.2 2.9 %collective-permute-start.5 = (f32[16,129,128]{2,0,1:T(8,128)S(1)}, f32[16,129,128]{2,0,1:T(8,128)S(1)}, u32[]{:S(2)}, u32[]{:S(2)}) collective-permute-start(f32[16,129,128]{2,0,1:T(8,128)S(1)} %copy.20), channel_id=1, source_target_pairs={{0,1},{1,0},{2,3},{3,2},{4,5},{5,4},{6,7},{7,6},{8,9},{9,8},{10,11... | collective-permute-start | bytes 3170312 | tf_op jit(solution)/shard_map/ppermute | solution.py:220
  34.6 7.2 %collective-permute-start.14 = (f32[2,1,2,2,43,128]{5,4,3,2,1,0:T(8,128)S(1)}, f32[2,1,2,2,43,128]{5,4,3,2,1,0:T(8,128)S(1)}, u32[]{:S(2)}, u32[]{:S(2)}) collective-permute-start(f32[2,1,2,2,43,128]{5,4,3,2,1,0:T(8,128)S(1)} %constant_dynamic-slice_fusion.2), channel_id=1, source_target_pairs={{0,8},{8,0},{16,24},{24,16},{1,9},{9,1},{17,25},{25,17},{2,10},{10... | collective-permute-start | bytes 528392 | tf_op jit(solution)/shard_map/ppermute | solution.py:77
  34.7 8.0 %collective-permute-start.10 = (f32[2,2,1,2,43,128]{5,4,3,2,1,0:T(8,128)S(1)}, f32[2,2,1,2,43,128]{5,4,3,2,1,0:T(8,128)S(1)}, u32[]{:S(2)}, u32[]{:S(2)}) collective-permute-start(f32[2,2,1,2,43,128]{5,4,3,2,1,0:T(8,128)S(1)} %constant_dynamic-slice_fusion.6), channel_id=1, source_target_pairs={{0,4},{2,6},{4,0},{6,2},{1,5},{3,7},{5,1},{7,3},{8,12},{10,14},{12... | collective-permute-start | bytes 528392 | tf_op jit(solution)/shard_map/ppermute | solution.py:77
  36.5 7.3 %collective-permute-start.6 = (f32[2,2,2,1,43,128]{5,4,3,2,1,0:T(8,128)S(1)}, f32[2,2,2,1,43,128]{5,4,3,2,1,0:T(8,128)S(1)}, u32[]{:S(2)}, u32[]{:S(2)}) collective-permute-start(f32[2,2,2,1,43,128]{5,4,3,2,1,0:T(8,128)S(1)} %constant_dynamic-slice_fusion.10), channel_id=1, source_target_pairs={{0,2},{2,0},{4,6},{6,4},{1,3},{3,1},{5,7},{7,5},{8,10},{10,8},{12,... | collective-permute-start | bytes 528392 | tf_op jit(solution)/shard_map/ppermute | solution.py:77
  41.9 4.7 %collective-permute-start.15 = (f32[2,1,2,1,43,128]{5,4,3,2,1,0:T(8,128)S(1)}, f32[2,1,2,1,43,128]{5,4,3,2,1,0:T(8,128)S(1)}, u32[]{:S(2)}, u32[]{:S(2)}) collective-permute-start(f32[2,1,2,1,43,128]{5,4,3,2,1,0:T(8,128)S(1)} %constant_dynamic-slice_fusion.1), channel_id=1, source_target_pairs={{0,2},{2,0},{4,6},{6,4},{1,3},{3,1},{5,7},{7,5},{8,10},{10,8},{12,... | collective-permute-start | bytes 264200 | tf_op jit(solution)/shard_map/ppermute | solution.py:77
  42.8 5.6 %collective-permute-start.11 = (f32[2,1,1,2,43,128]{5,4,3,2,1,0:T(8,128)S(1)}, f32[2,1,1,2,43,128]{5,4,3,2,1,0:T(8,128)S(1)}, u32[]{:S(2)}, u32[]{:S(2)}) collective-permute-start(f32[2,1,1,2,43,128]{5,4,3,2,1,0:T(8,128)S(1)} %constant_dynamic-slice_fusion.5), channel_id=1, source_target_pairs={{0,8},{8,0},{16,24},{24,16},{1,9},{9,1},{17,25},{25,17},{2,10},{10... | collective-permute-start | bytes 264200 | tf_op jit(solution)/shard_map/ppermute | solution.py:77
  43.9 5.2 %collective-permute-start.7 = (f32[2,2,1,1,43,128]{5,4,3,2,1,0:T(8,128)S(1)}, f32[2,2,1,1,43,128]{5,4,3,2,1,0:T(8,128)S(1)}, u32[]{:S(2)}, u32[]{:S(2)}) collective-permute-start(f32[2,2,1,1,43,128]{5,4,3,2,1,0:T(8,128)S(1)} %constant_dynamic-slice_fusion.9), channel_id=1, source_target_pairs={{0,4},{2,6},{4,0},{6,2},{1,5},{3,7},{5,1},{7,3},{8,12},{10,14},{12... | collective-permute-start | bytes 264200 | tf_op jit(solution)/shard_map/ppermute | solution.py:77
  46.7 4.3 %collective-permute-start.16 = (f32[2,1,1,1,43,128]{5,4,3,2,1,0:T(8,128)S(1)}, f32[2,1,1,1,43,128]{5,4,3,2,1,0:T(8,128)S(1)}, u32[]{:S(2)}, u32[]{:S(2)}) collective-permute-start(f32[2,1,1,1,43,128]{5,4,3,2,1,0:T(8,128)S(1)} %constant_dynamic-slice_fusion), channel_id=1, source_target_pairs={{0,4},{2,6},{4,0},{6,2},{1,5},{3,7},{5,1},{7,3},{8,12},{10,14},{12... | collective-permute-start | bytes 132104 | tf_op jit(solution)/shard_map/ppermute | solution.py:77
  48.4 4.2 %collective-permute-start.12 = (f32[2,1,1,1,43,128]{5,4,3,2,1,0:T(8,128)S(1)}, f32[2,1,1,1,43,128]{5,4,3,2,1,0:T(8,128)S(1)}, u32[]{:S(2)}, u32[]{:S(2)}) collective-permute-start(f32[2,1,1,1,43,128]{5,4,3,2,1,0:T(8,128)S(1)} %constant_dynamic-slice_fusion.4), channel_id=1, source_target_pairs={{0,2},{2,0},{4,6},{6,4},{1,3},{3,1},{5,7},{7,5},{8,10},{10,8},{12,... | collective-permute-start | bytes 132104 | tf_op jit(solution)/shard_map/ppermute | solution.py:77
  49.1 5.0 %collective-permute-start.8 = (f32[2,1,1,1,43,128]{5,4,3,2,1,0:T(8,128)S(1)}, f32[2,1,1,1,43,128]{5,4,3,2,1,0:T(8,128)S(1)}, u32[]{:S(2)}, u32[]{:S(2)}) collective-permute-start(f32[2,1,1,1,43,128]{5,4,3,2,1,0:T(8,128)S(1)} %constant_dynamic-slice_fusion.8), channel_id=1, source_target_pairs={{0,8},{8,0},{16,24},{24,16},{1,9},{9,1},{17,25},{25,17},{2,10},{10... | collective-permute-start | bytes 132104 | tf_op jit(solution)/shard_map/ppermute | solution.py:77
  51.0 5.0 %collective-permute-start.17 = (f32[1,1,1,1,43,128]{5,4,3,2,1,0:T(8,128)S(1)}, f32[1,1,1,1,43,128]{5,4,3,2,1,0:T(8,128)S(1)}, u32[]{:S(2)}, u32[]{:S(2)}) collective-permute-start(f32[1,1,1,1,43,128]{5,4,3,2,1,0:T(8,128)S(1)} %constant_dynamic-slice_fusion.11), channel_id=1, source_target_pairs={{0,16},{8,24},{16,0},{24,8},{1,17},{9,25},{17,1},{25,9},{2,18},{10... | collective-permute-start | bytes 66056 | tf_op jit(solution)/shard_map/ppermute | solution.py:77
  52.6 4.8 %collective-permute-start.13 = (f32[1,1,1,1,43,128]{5,4,3,2,1,0:T(8,128)S(1)}, f32[1,1,1,1,43,128]{5,4,3,2,1,0:T(8,128)S(1)}, u32[]{:S(2)}, u32[]{:S(2)}) collective-permute-start(f32[1,1,1,1,43,128]{5,4,3,2,1,0:T(8,128)S(1)} %constant_dynamic-slice_fusion.3), channel_id=1, source_target_pairs={{0,16},{8,24},{16,0},{24,8},{1,17},{9,25},{17,1},{25,9},{2,18},{10... | collective-permute-start | bytes 66056 | tf_op jit(solution)/shard_map/ppermute | solution.py:77
  54.2 4.8 %collective-permute-start.9 = (f32[1,1,1,1,43,128]{5,4,3,2,1,0:T(8,128)S(1)}, f32[1,1,1,1,43,128]{5,4,3,2,1,0:T(8,128)S(1)}, u32[]{:S(2)}, u32[]{:S(2)}) collective-permute-start(f32[1,1,1,1,43,128]{5,4,3,2,1,0:T(8,128)S(1)} %constant_dynamic-slice_fusion.7), channel_id=1, source_target_pairs={{0,16},{8,24},{16,0},{24,8},{1,17},{9,25},{17,1},{25,9},{2,18},{10... | collective-permute-start | bytes 66056 | tf_op jit(solution)/shard_map/ppermute | solution.py:77
